TPU v7x, 256 devices: a whole 4x4x8 slice. The times are simulated.
256 devices in a mesh: gz: 8 (over x, z_lo), gy: 32 (over z_hi, y, core).
Axes of the slice: x: 4, y: 4, z: 8 (z_hi: 4, z_lo: 2; z = z_hi * 2 + z_lo), core: 2. Of those that a mesh axis runs over, the one named last changes fastest.
Arguments:
- observed: float32 [256, 1024, 768], P('gz', 'gy'), may hold values from 0.2 to 5
- estimate: float32 [256, 1024, 768], P('gz', 'gy'), may hold values from 0.5 to 2
- taps_z: float32 [9], replicated, may hold values from 0.05 to 1
- taps_y: float32 [9], replicated, may hold values from 0.05 to 1
- taps_x: float32 [9], replicated, may hold values from 0.05 to 1
Outputs:
- updated: float32 [256, 1024, 768], P('gz', 'gy')
- projection: float32 [1024, 768], P('gy')
All inputs are finite; a program needn't handle non-finite values.
Results may differ from a plain program's by a relative error of at most 0.00002.
Values sent between devices are 32-bit elements; how exact they have to be, the bound alone decides.
No kernel may reach another device: no remote copies, remote signals or barrier semaphores. Data moves between devices by JAX's collectives and lax.ppermute only.
A program may use at most 64 MiB of HBM per device.

v0:
```python
import jax
import jax.numpy as jnp
from jax import lax
from jax.sharding import PartitionSpec as P


def with_halo(shard, sides, width):
    for axis, dim in sides:
        peers, length = (lax.axis_size(axis), shard.shape[dim])
        up = [(i, (i + 1) % peers) for i in range(peers - 1)]
        down = [(j, i) for i, j in up]
        last = lax.slice_in_dim(shard, length - width, length, axis=dim)
        first = lax.slice_in_dim(shard, 0, width, axis=dim)
        before = lax.ppermute(last, axis, up)
        after = lax.ppermute(first, axis, down)
        shard = jnp.concatenate([before, shard, after], axis=dim)
    return shard


def valid_pass(padded, taps, axis):
    count = padded.shape[axis] - (taps.shape[0] - 1)
    total = taps[0] * lax.slice_in_dim(padded, 0, count, axis=axis)
    for index in range(1, taps.shape[0]):
        total = total + taps[index] * lax.slice_in_dim(padded, index, index + count, axis=axis)
    return total


def blur_along_x(volume, taps):
    radius = (taps.shape[0] - 1) // 2
    padded = jnp.pad(volume, ((0, 0), (0, 0), (radius, radius)))
    return valid_pass(padded, taps, 2)


def blur_padded(padded, taps_z, taps_y, taps_x):
    volume = valid_pass(padded, taps_z, 0)
    volume = valid_pass(volume, taps_y, 1)
    return blur_along_x(volume, taps_x)


def per_device(observed, estimate, taps_z, taps_y, taps_x):
    radius = (taps_z.shape[0] - 1) // 2
    back_z = taps_z[::-1]
    back_y = taps_y[::-1]
    back_x = taps_x[::-1]
    padded = with_halo(estimate, (("gz", 0), ("gy", 1)), radius)
    blurred = blur_padded(padded, taps_z, taps_y, taps_x)
    ratio = observed / blurred
    ratio_padded = with_halo(ratio, (("gz", 0), ("gy", 1)), radius)
    correction = blur_padded(ratio_padded, back_z, back_y, back_x)
    updated = estimate * correction
    local_max = jnp.max(updated, axis=0)
    projection = lax.pmax(local_max, "gz")
    return (updated, projection)


def solution(mesh):
    return jax.shard_map(
        per_device,
        mesh=mesh,
        in_specs=(P("gz", "gy", None), P("gz", "gy", None), P(), P(), P()),
        out_specs=(P("gz", "gy", None), P("gy", None)),
        check_vma=False,
    )
```

profile of v0, /device:TPU:160, one launch (start us, length us, event | category | flops | bytes accessed | tf_op | source)
XLA Modules:
  0.0 239.6 jit_solution(2137631412528973655)
XLA Ops:
  7.2 0.0 all-reduce.4.cloned.1.call-start
  7.2 1.2 fusion.69
  8.4 3.8 %collective-permute-start = (f32[4,32,768]{2,1,0:T(8,128)S(1)}, f32[4,32,768]{2,1,0:T(8,128)S(1)}, u32[]{:S(2)}, u32[]{:S(2)}) collective-permute-start(f32[4,32,768]{2,1,0:T(8,128)S(1)} %get-tuple-element.14), channel_id=1, source_target_pairs={{0,32},{32,64},{64,96},{96,128},{128,160},{160,192},{192,224},{1,3... | collective-permute-start | bytes 1179656 | tf_op jit(solution)/shard_map/ppermute | solution.py:14
  12.2 2.0 collective-permute-start.1
  14.3 3.7 %copy.21 = f32[32,32,768]{2,0,1:T(8,128)S(1)} copy(f32[32,32,768]{2,1,0:T(8,128)} %param.6) | data formatting | bytes 6291456 | tf_op args[1]
  18.0 0.0 copy-start.2
  18.0 0.0 copy-start.3
  18.0 0.0 copy-start.4
  18.0 3.7 %collective-permute-done = f32[4,32,768]{2,1,0:T(8,128)S(1)} collective-permute-done((f32[4,32,768]{2,1,0:T(8,128)S(1)}, f32[4,32,768]{2,1,0:T(8,128)S(1)}, u32[]{:S(2)}, u32[]{:S(2)}) %collective-permute-start) | collective-permute-done | bytes 393248 | tf_op jit(solution)/shard_map/ppermute | solution.py:14
  21.7 0.3 copy.13
  22.0 8.5 %collective-permute-done.1 = f32[4,32,768]{2,1,0:T(8,128)S(1)} collective-permute-done((f32[4,32,768]{2,1,0:T(8,128)S(1)}, f32[4,32,768]{2,1,0:T(8,128)S(1)}, u32[]{:S(2)}, u32[]{:S(2)}) %collective-permute-start.1) | collective-permute-done | bytes 393248 | tf_op jit(solution)/shard_map/ppermute | solution.py:15
  30.5 0.3 copy.15
  30.8 0.1 pad_maximum_fusion.7
  30.9 1.9 collective-permute-start.2
  32.8 7.9 %collective-permute-start.3 = (f32[40,4,768]{2,0,1:T(8,128)S(1)}, f32[40,4,768]{2,0,1:T(8,128)S(1)}, u32[]{:S(2)}, u32[]{:S(2)}) collective-permute-start(f32[40,4,768]{2,0,1:T(8,128)S(1)} %get-tuple-element.11), channel_id=1, source_target_pairs={{1,0},{2,1},{3,2},{4,3},{5,4},{6,5},{7,6},{8,7},{9,8},{10,9},{11,1... | collective-permute-start | bytes 1474568 | tf_op jit(solution)/shard_map/ppermute | solution.py:15
  40.7 0.0 copy-done.2
  40.7 0.7 fusion.72
  41.4 0.0 copy-done.3
  41.4 0.7 fusion.71
  42.0 0.0 copy-done.4
  42.1 0.7 fusion.70
  42.7 5.9 %collective-permute-done.2 = f32[40,4,768]{2,0,1:T(8,128)S(1)} collective-permute-done((f32[40,4,768]{2,0,1:T(8,128)S(1)}, f32[40,4,768]{2,0,1:T(8,128)S(1)}, u32[]{:S(2)}, u32[]{:S(2)}) %collective-permute-start.2) | collective-permute-done | bytes 491552 | tf_op jit(solution)/shard_map/ppermute | solution.py:14
  48.6 0.0 collective-permute-done.3
  48.7 0.7 pad_maximum_fusion
  49.4 9.8 %fusion.8 = f32[32,40,768]{2,0,1:T(8,128)S(1)} fusion(f32[40,40,768]{2,0,1:T(8,128)S(1)} %pad_maximum_fusion, f32[]{:T(128)} %bitcast.12, f32[]{:T(128)} %bitcast.11, f32[]{:T(128)} %bitcast.10, f32[]{:T(128)} %bitcast.9, f32[]{:T(128)} %bitcast.8, f32[]{:T(128)} %bitcast.7, f32[]{:T(128)} %bitcast.6, f32[]{:T(128)} %bitcast.5, f32[]{:T(128)} %bitcast.2), kind=kLoop, calls=%fused_computation.36 | loop fusion | flops 16711680 | bytes 39321636 | tf_op jit(solution)/shard_map/add | solution.py:24
  59.1 0.0 copy-start.1
  59.2 9.0 %fusion.58 = f32[32,32,768]{2,0,1:T(8,128)S(1)} fusion(f32[32,40,768]{2,0,1:T(8,128)S(1)} %fusion.8, f32[]{:T(128)} %bitcast.19, f32[]{:T(128)} %bitcast.18, f32[]{:T(128)} %bitcast.17, f32[]{:T(128)} %bitcast.16, f32[]{:T(128)} %bitcast.15, f32[]{:T(128)} %bitcast.14, f32[]{:T(128)} %bitcast.13, f32[]{:T(128)} %bitcast.4, f32[]{:T(128)} %bitcast.1), kind=kLoop, calls=%fused_computation.104 | loop fusion | flops 13369344 | bytes 31457316 | tf_op jit(solution)/shard_map/add | solution.py:24
  68.2 0.0 copy-done.1
  68.2 12.6 %fusion.25 = f32[32,32,768]{2,0,1:T(8,128)S(1)} fusion(f32[32,32,768]{2,0,1:T(8,128)S(1)} %fusion.58, f32[32,32,768]{2,1,0:T(8,128)S(1)} %copy-done.1, f32[]{:T(128)} %bitcast.26, f32[]{:T(128)} %bitcast.25, f32[]{:T(128)} %bitcast.24, f32[]{:T(128)} %bitcast.23, f32[]{:T(128)} %bitcast.22, f32[]{:T(128)} %bitcast.21, f32[]{:T(128)} %bitcast.20, f32[]{:T(128)} %bitcast.3, ...), kind=kLoop, calls=%fused_computation.61 | loop fusion | flops 14155776 | bytes 9437220 | tf_op jit(solution)/shard_map/div | solution.py:47
  80.8 0.1 fusion.68
  81.0 0.1 copy.18
  81.0 6.4 %collective-permute-start.5 = (f32[4,32,768]{2,1,0:T(8,128)S(1)}, f32[4,32,768]{2,1,0:T(8,128)S(1)}, u32[]{:S(2)}, u32[]{:S(2)}) collective-permute-start(f32[4,32,768]{2,1,0:T(8,128)S(1)} %copy.18), channel_id=1, source_target_pairs={{32,0},{64,32},{96,64},{128,96},{160,128},{192,160},{224,192},{33,... | collective-permute-start | bytes 1179656 | tf_op jit(solution)/shard_map/ppermute | solution.py:15
  87.4 0.1 copy.17
  87.5 2.8 %collective-permute-start.4 = (f32[4,32,768]{2,1,0:T(8,128)S(1)}, f32[4,32,768]{2,1,0:T(8,128)S(1)}, u32[]{:S(2)}, u32[]{:S(2)}) collective-permute-start(f32[4,32,768]{2,1,0:T(8,128)S(1)} %copy.17), channel_id=1, source_target_pairs={{0,32},{32,64},{64,96},{96,128},{128,160},{160,192},{192,224},{1,3... | collective-permute-start | bytes 1179656 | tf_op jit(solution)/shard_map/ppermute | solution.py:14
  90.4 5.0 %collective-permute-done.5 = f32[4,32,768]{2,1,0:T(8,128)S(1)} collective-permute-done((f32[4,32,768]{2,1,0:T(8,128)S(1)}, f32[4,32,768]{2,1,0:T(8,128)S(1)}, u32[]{:S(2)}, u32[]{:S(2)}) %collective-permute-start.5) | collective-permute-done | bytes 393248 | tf_op jit(solution)/shard_map/ppermute | solution.py:15
  95.3 0.3 copy.20
  95.6 1.6 collective-permute-done.4
  97.2 0.3 copy.19
  97.5 0.1 pad_maximum_fusion.4
  97.6 1.9 collective-permute-start.6
  99.5 8.0 %collective-permute-start.7 = (f32[40,4,768]{2,0,1:T(8,128)S(1)}, f32[40,4,768]{2,0,1:T(8,128)S(1)}, u32[]{:S(2)}, u32[]{:S(2)}) collective-permute-start(f32[40,4,768]{2,0,1:T(8,128)S(1)} %get-tuple-element.9), channel_id=1, source_target_pairs={{1,0},{2,1},{3,2},{4,3},{5,4},{6,5},{7,6},{8,7},{9,8},{10,9},{11,1... | collective-permute-start | bytes 1474568 | tf_op jit(solution)/shard_map/ppermute | solution.py:15
  107.6 6.0 %collective-permute-done.6 = f32[40,4,768]{2,0,1:T(8,128)S(1)} collective-permute-done((f32[40,4,768]{2,0,1:T(8,128)S(1)}, f32[40,4,768]{2,0,1:T(8,128)S(1)}, u32[]{:S(2)}, u32[]{:S(2)}) %collective-permute-start.6) | collective-permute-done | bytes 491552 | tf_op jit(solution)/shard_map/ppermute | solution.py:14
  113.6 0.2 collective-permute-done.7
  113.8 0.7 pad_maximum_fusion.1
  114.5 9.8 %fusion = f32[32,40,768]{2,0,1:T(8,128)S(1)} fusion(f32[40,40,768]{2,0,1:T(8,128)S(1)} %pad_maximum_fusion.1, f32[]{:T(128)} %bitcast.12, f32[]{:T(128)} %bitcast.11, f32[]{:T(128)} %bitcast.10, f32[]{:T(128)} %bitcast.9, f32[]{:T(128)} %bitcast.8, f32[]{:T(128)} %bitcast.7, f32[]{:T(128)} %bitcast.6, f32[]{:T(128)} %bitcast.5, f32[]{:T(128)} %bitcast.2), kind=kLoop, calls=%fused_computation.19 | loop fusion | flops 16711680 | bytes 39321636 | tf_op jit(solution)/shard_map/add | solution.py:24
  124.3 0.0 copy-start
  124.3 9.0 %fusion.50 = f32[32,32,768]{2,0,1:T(8,128)S(1)} fusion(f32[32,40,768]{2,0,1:T(8,128)S(1)} %fusion, f32[]{:T(128)} %bitcast.19, f32[]{:T(128)} %bitcast.18, f32[]{:T(128)} %bitcast.17, f32[]{:T(128)} %bitcast.16, f32[]{:T(128)} %bitcast.15, f32[]{:T(128)} %bitcast.14, f32[]{:T(128)} %bitcast.13, f32[]{:T(128)} %bitcast.4, f32[]{:T(128)} %bitcast.1), kind=kLoop, calls=%fused_computation.87 | loop fusion | flops 13369344 | bytes 31457316 | tf_op jit(solution)/shard_map/add | solution.py:24
  133.3 0.0 copy-done
  133.3 13.9 %fusion.66 = (f32[32,768]{1,0:T(8,128)}, f32[32,32,768]{2,0,1:T(8,128)S(1)}) fusion(f32[]{:T(128)} %bitcast.3, f32[]{:T(128)} %bitcast.20, f32[]{:T(128)} %bitcast.21, f32[]{:T(128)} %bitcast.22, f32[32,32,768]{2,0,1:T(8,128)S(1)} %fusion.50, f32[]{:T(128)} %bitcast.23, f32[]{:T(128)} %bitcast.24, f32[]{:T(128)} %bitcast.25, f32[]{:T(128)} %bitcast.26, ...), kind=kLoop, calls=%fused_computation.126 | loop fusion | flops 14917632 | bytes 9535524 | tf_op jit(solution)/shard_map/reduce_max | solution.py:51
  147.2 0.0 all-reduce.4.cloned.1.call-update
  147.3 3.5 %copy.22 = f32[32,32,768]{2,1,0:T(8,128)} copy(f32[32,32,768]{2,0,1:T(8,128)S(1)} %get-tuple-element.7) | data formatting | bytes 6291456
  150.8 80.5 %all-reduce.4.cloned.1.call-done = f32[32,768]{1,0:T(8,128)} async-done(((f32[32,768]{1,0:T(8,128)}), f32[32,768]{1,0:T(8,128)}) %all-reduce.4.cloned.1.call-update) | async-done | bytes 98320 | tf_op jit(solution)/shard_map/pmax | solution.py:52
  231.3 1.5 copy.27
Async XLA Ops:
  7.2 224.1 %all-reduce.4.cloned.1.call-start = ((), (), s32[]{:S(2)}) async-start(), calls=%async_computation | async-start | bytes 196608 | tf_op jit(solution)/shard_map/pmax | solution.py:52
  8.4 13.3 %collective-permute-start = (f32[4,32,768]{2,1,0:T(8,128)S(1)}, f32[4,32,768]{2,1,0:T(8,128)S(1)}, u32[]{:S(2)}, u32[]{:S(2)}) collective-permute-start(f32[4,32,768]{2,1,0:T(8,128)S(1)} %get-tuple-element.14), channel_id=1, source_target_pairs={{0,32},{32,64},{64,96},{96,128},{128,160},{160,192},{192,224},{1,3... | collective-permute-start | bytes 1179656 | tf_op jit(solution)/shard_map/ppermute | solution.py:14
  12.2 18.3 %collective-permute-start.1 = (f32[4,32,768]{2,1,0:T(8,128)S(1)}, f32[4,32,768]{2,1,0:T(8,128)S(1)}, u32[]{:S(2)}, u32[]{:S(2)}) collective-permute-start(f32[4,32,768]{2,1,0:T(8,128)S(1)} %get-tuple-element.15), channel_id=1, source_target_pairs={{32,0},{64,32},{96,64},{128,96},{160,128},{192,160},{224,192},{33,... | collective-permute-start | bytes 1179656 | tf_op jit(solution)/shard_map/ppermute | solution.py:15
  18.0 22.7 %copy-start.2 = (f32[9]{0:T(128)S(1)}, f32[9]{0:T(128)}, u32[]{:S(2)}) copy-start(f32[9]{0:T(128)} %param.7) | copy-start | bytes 112
  18.0 23.4 %copy-start.3 = (f32[9]{0:T(128)S(1)}, f32[9]{0:T(128)}, u32[]{:S(2)}) copy-start(f32[9]{0:T(128)} %param.8) | copy-start | bytes 112
  18.0 24.0 %copy-start.4 = (f32[9]{0:T(128)S(1)}, f32[9]{0:T(128)}, u32[]{:S(2)}) copy-start(f32[9]{0:T(128)} %param.9) | copy-start | bytes 112
  30.9 17.8 %collective-permute-start.2 = (f32[40,4,768]{2,0,1:T(8,128)S(1)}, f32[40,4,768]{2,0,1:T(8,128)S(1)}, u32[]{:S(2)}, u32[]{:S(2)}) collective-permute-start(f32[40,4,768]{2,0,1:T(8,128)S(1)} %get-tuple-element.10), channel_id=1, source_target_pairs={{0,1},{1,2},{2,3},{3,4},{4,5},{5,6},{6,7},{7,8},{8,9},{9,10},{10,1... | collective-permute-start | bytes 1474568 | tf_op jit(solution)/shard_map/ppermute | solution.py:14
  32.8 15.8 %collective-permute-start.3 = (f32[40,4,768]{2,0,1:T(8,128)S(1)}, f32[40,4,768]{2,0,1:T(8,128)S(1)}, u32[]{:S(2)}, u32[]{:S(2)}) collective-permute-start(f32[40,4,768]{2,0,1:T(8,128)S(1)} %get-tuple-element.11), channel_id=1, source_target_pairs={{1,0},{2,1},{3,2},{4,3},{5,4},{6,5},{7,6},{8,7},{9,8},{10,9},{11,1... | collective-permute-start | bytes 1474568 | tf_op jit(solution)/shard_map/ppermute | solution.py:15
  59.1 9.0 %copy-start.1 = (f32[32,32,768]{2,1,0:T(8,128)S(1)}, f32[32,32,768]{2,1,0:T(8,128)}, u32[]{:S(2)}) copy-start(f32[32,32,768]{2,1,0:T(8,128)} %param.5) | copy-start | bytes 9437188
  81.0 14.3 %collective-permute-start.5 = (f32[4,32,768]{2,1,0:T(8,128)S(1)}, f32[4,32,768]{2,1,0:T(8,128)S(1)}, u32[]{:S(2)}, u32[]{:S(2)}) collective-permute-start(f32[4,32,768]{2,1,0:T(8,128)S(1)} %copy.18), channel_id=1, source_target_pairs={{32,0},{64,32},{96,64},{128,96},{160,128},{192,160},{224,192},{33,... | collective-permute-start | bytes 1179656 | tf_op jit(solution)/shard_map/ppermute | solution.py:15
  87.5 9.7 %collective-permute-start.4 = (f32[4,32,768]{2,1,0:T(8,128)S(1)}, f32[4,32,768]{2,1,0:T(8,128)S(1)}, u32[]{:S(2)}, u32[]{:S(2)}) collective-permute-start(f32[4,32,768]{2,1,0:T(8,128)S(1)} %copy.17), channel_id=1, source_target_pairs={{0,32},{32,64},{64,96},{96,128},{128,160},{160,192},{192,224},{1,3... | collective-permute-start | bytes 1179656 | tf_op jit(solution)/shard_map/ppermute | solution.py:14
  97.6 16.0 %collective-permute-start.6 = (f32[40,4,768]{2,0,1:T(8,128)S(1)}, f32[40,4,768]{2,0,1:T(8,128)S(1)}, u32[]{:S(2)}, u32[]{:S(2)}) collective-permute-start(f32[40,4,768]{2,0,1:T(8,128)S(1)} %get-tuple-element.8), channel_id=1, source_target_pairs={{0,1},{1,2},{2,3},{3,4},{4,5},{5,6},{6,7},{7,8},{8,9},{9,10},{10,1... | collective-permute-start | bytes 1474568 | tf_op jit(solution)/shard_map/ppermute | solution.py:14
  99.5 14.3 %collective-permute-start.7 = (f32[40,4,768]{2,0,1:T(8,128)S(1)}, f32[40,4,768]{2,0,1:T(8,128)S(1)}, u32[]{:S(2)}, u32[]{:S(2)}) collective-permute-start(f32[40,4,768]{2,0,1:T(8,128)S(1)} %get-tuple-element.9), channel_id=1, source_target_pairs={{1,0},{2,1},{3,2},{4,3},{5,4},{6,5},{7,6},{8,7},{9,8},{10,9},{11,1... | collective-permute-start | bytes 1474568 | tf_op jit(solution)/shard_map/ppermute | solution.py:15
  124.3 9.0 %copy-start = (f32[32,32,768]{2,1,0:T(8,128)S(1)}, f32[32,32,768]{2,1,0:T(8,128)}, u32[]{:S(2)}) copy-start(f32[32,32,768]{2,1,0:T(8,128)} %param.6) | copy-start | bytes 9437188
Sparse Core Ops, SparseCore 0:
  147.4 83.8 all-reduce.3
where the time goes:
time: 244 us; the launch traced here: 240 us
  waiting for transfers between devices  111 us (45%)
  other arithmetic  65.7 us (27%)
  starting transfers between devices  34.9 us (14%)
  between operations  14.3 us (6%)
  local copies, waits for them, and re-layouts  13.3 us (5%)
    pmax x1, waiting for transfers between devices, per_device(): projection = lax.pmax(local_max, 'gz')  80.5 us
    add x4, other arithmetic, valid_pass(): total + taps[index] * lax.slice_in_dim(padded, index, index + count, axis...  37.5 us
    ppermute x4, starting transfers between devices, with_halo(): after = lax.ppermute(first, axis, down)  24.3 us
    ppermute x4, waiting for transfers between devices, with_halo(): before = lax.ppermute(last, axis, up)  17.2 us
    reduce_max x1, other arithmetic, per_device(): local_max = jnp.max(updated, axis=0)  13.9 us
    ppermute x4, waiting for transfers between devices, with_halo(): after = lax.ppermute(first, axis, down)  13.7 us
    div x1, other arithmetic, per_device(): ratio = observed / blurred  12.6 us
    ppermute x4, starting transfers between devices, with_halo(): before = lax.ppermute(last, axis, up)  10.5 us
  transfers between devices with their start and end apart: 9, of which 8 were waited for; matrix products, arithmetic and copies ran while one was open for 4% of the time, Pallas kernels for 0%

commit v1 on v0

--- a/solution.py
+++ b/solution.py
@@ -37,6 +37,16 @@
     return blur_along_x(volume, taps_x)
 
 
+def butterfly_max(value, axis):
+    peers = lax.axis_size(axis)
+    step = 1
+    while step < peers:
+        pairs = [(i, i ^ step) for i in range(peers)]
+        value = jnp.maximum(value, lax.ppermute(value, axis, pairs))
+        step *= 2
+    return value
+
+
 def per_device(observed, estimate, taps_z, taps_y, taps_x):
     radius = (taps_z.shape[0] - 1) // 2
     back_z = taps_z[::-1]
@@ -49,7 +59,7 @@
     correction = blur_padded(ratio_padded, back_z, back_y, back_x)
     updated = estimate * correction
     local_max = jnp.max(updated, axis=0)
-    projection = lax.pmax(local_max, "gz")
+    projection = butterfly_max(local_max, "gz")
     return (updated, projection)
 
 

time: 244 us -> 166 us (0.68)
  the two profiles are of different devices: /device:TPU:160 before, /device:TPU:89 now
where the time goes in v1:
time: 166 us
  other arithmetic  65.8 us (40%)
  waiting for transfers between devices  55.3 us (33%)
  starting transfers between devices  31.8 us (19%)
  local copies, waits for them, and re-layouts  11.8 us (7%)
    add x4, other arithmetic, valid_pass(): total + taps[index] * lax.slice_in_dim(padded, index, index + count, axis...  37.6 us
    ppermute x4, waiting for transfers between devices, with_halo(): after = lax.ppermute(first, axis, down)  30.3 us
    ppermute x4, waiting for transfers between devices, with_halo(): before = lax.ppermute(last, axis, up)  19.6 us
    ppermute x4, starting transfers between devices, with_halo(): before = lax.ppermute(last, axis, up)  17.6 us
    reduce_max x1, other arithmetic, per_device(): local_max = jnp.max(updated, axis=0)  13.3 us
    div x1, other arithmetic, per_device(): ratio = observed / blurred  12.6 us
    ppermute x3, starting transfers between devices, butterfly_max(): value = jnp.maximum(value, lax.ppermute(value, axis, pairs))  7.53 us
    unnamed x12, local copies, waits for them, and re-layouts  7.23 us
  transfers between devices with their start and end apart: 11, of which 10 were waited for; matrix products, arithmetic and copies ran while one was open for 6% of the time, Pallas kernels for 0%

profile of v1, /device:TPU:89, one launch (start us, length us, event | category | flops | bytes accessed | tf_op | source)
XLA Modules:
  0.0 165.5 jit_solution(16763586636478509946)
XLA Ops:
  0.6 1.2 fusion.69
  1.8 3.6 %collective-permute-start = (f32[4,32,768]{2,1,0:T(8,128)S(1)}, f32[4,32,768]{2,1,0:T(8,128)S(1)}, u32[]{:S(2)}, u32[]{:S(2)}) collective-permute-start(f32[4,32,768]{2,1,0:T(8,128)S(1)} %get-tuple-element.14), channel_id=1, source_target_pairs={{0,32},{32,64},{64,96},{96,128},{128,160},{160,192},{192,224},{1,3... | collective-permute-start | bytes 1179656 | tf_op jit(solution)/shard_map/ppermute | solution.py:14
  5.4 1.3 collective-permute-start.1
  6.7 3.7 %copy.21 = f32[32,32,768]{2,0,1:T(8,128)S(1)} copy(f32[32,32,768]{2,1,0:T(8,128)} %param.6) | data formatting | bytes 6291456 | tf_op args[1]
  10.4 0.0 copy-start.2
  10.4 0.0 copy-start.3
  10.4 0.0 copy-start.4
  10.4 2.7 %collective-permute-done = f32[4,32,768]{2,1,0:T(8,128)S(1)} collective-permute-done((f32[4,32,768]{2,1,0:T(8,128)S(1)}, f32[4,32,768]{2,1,0:T(8,128)S(1)}, u32[]{:S(2)}, u32[]{:S(2)}) %collective-permute-start) | collective-permute-done | bytes 393248 | tf_op jit(solution)/shard_map/ppermute | solution.py:14
  13.1 0.3 copy.13
  13.4 9.7 %collective-permute-done.1 = f32[4,32,768]{2,1,0:T(8,128)S(1)} collective-permute-done((f32[4,32,768]{2,1,0:T(8,128)S(1)}, f32[4,32,768]{2,1,0:T(8,128)S(1)}, u32[]{:S(2)}, u32[]{:S(2)}) %collective-permute-start.1) | collective-permute-done | bytes 393248 | tf_op jit(solution)/shard_map/ppermute | solution.py:15
  23.1 0.3 copy.15
  23.3 0.1 pad_maximum_fusion.7
  23.4 7.2 %collective-permute-start.2 = (f32[40,4,768]{2,0,1:T(8,128)S(1)}, f32[40,4,768]{2,0,1:T(8,128)S(1)}, u32[]{:S(2)}, u32[]{:S(2)}) collective-permute-start(f32[40,4,768]{2,0,1:T(8,128)S(1)} %get-tuple-element.10), channel_id=1, source_target_pairs={{0,1},{1,2},{2,3},{3,4},{4,5},{5,6},{6,7},{7,8},{8,9},{9,10},{10,1... | collective-permute-start | bytes 1474568 | tf_op jit(solution)/shard_map/ppermute | solution.py:14
  30.6 1.9 %collective-permute-start.3 = (f32[40,4,768]{2,0,1:T(8,128)S(1)}, f32[40,4,768]{2,0,1:T(8,128)S(1)}, u32[]{:S(2)}, u32[]{:S(2)}) collective-permute-start(f32[40,4,768]{2,0,1:T(8,128)S(1)} %get-tuple-element.11), channel_id=1, source_target_pairs={{1,0},{2,1},{3,2},{4,3},{5,4},{6,5},{7,6},{8,7},{9,8},{10,9},{11,1... | collective-permute-start | bytes 1474568 | tf_op jit(solution)/shard_map/ppermute | solution.py:15
  32.6 0.0 copy-done.2
  32.6 0.7 fusion.72
  33.3 0.0 copy-done.3
  33.3 0.7 fusion.71
  33.9 0.0 copy-done.4
  34.0 0.7 fusion.70
  34.6 7.0 %collective-permute-done.2 = f32[40,4,768]{2,0,1:T(8,128)S(1)} collective-permute-done((f32[40,4,768]{2,0,1:T(8,128)S(1)}, f32[40,4,768]{2,0,1:T(8,128)S(1)}, u32[]{:S(2)}, u32[]{:S(2)}) %collective-permute-start.2) | collective-permute-done | bytes 491552 | tf_op jit(solution)/shard_map/ppermute | solution.py:14
  41.6 8.5 %collective-permute-done.3 = f32[40,4,768]{2,0,1:T(8,128)S(1)} collective-permute-done((f32[40,4,768]{2,0,1:T(8,128)S(1)}, f32[40,4,768]{2,0,1:T(8,128)S(1)}, u32[]{:S(2)}, u32[]{:S(2)}) %collective-permute-start.3) | collective-permute-done | bytes 491552 | tf_op jit(solution)/shard_map/ppermute | solution.py:15
  50.1 0.7 pad_maximum_fusion
  50.8 9.7 %fusion.8 = f32[32,40,768]{2,0,1:T(8,128)S(1)} fusion(f32[40,40,768]{2,0,1:T(8,128)S(1)} %pad_maximum_fusion, f32[]{:T(128)} %bitcast.12, f32[]{:T(128)} %bitcast.11, f32[]{:T(128)} %bitcast.10, f32[]{:T(128)} %bitcast.9, f32[]{:T(128)} %bitcast.8, f32[]{:T(128)} %bitcast.7, f32[]{:T(128)} %bitcast.6, f32[]{:T(128)} %bitcast.5, f32[]{:T(128)} %bitcast.2), kind=kLoop, calls=%fused_computation.36 | loop fusion | flops 16711680 | bytes 39321636 | tf_op jit(solution)/shard_map/add | solution.py:24
  60.6 0.0 copy-start.1
  60.6 9.1 %fusion.58 = f32[32,32,768]{2,0,1:T(8,128)S(1)} fusion(f32[32,40,768]{2,0,1:T(8,128)S(1)} %fusion.8, f32[]{:T(128)} %bitcast.19, f32[]{:T(128)} %bitcast.18, f32[]{:T(128)} %bitcast.17, f32[]{:T(128)} %bitcast.16, f32[]{:T(128)} %bitcast.15, f32[]{:T(128)} %bitcast.14, f32[]{:T(128)} %bitcast.13, f32[]{:T(128)} %bitcast.4, f32[]{:T(128)} %bitcast.1), kind=kLoop, calls=%fused_computation.104 | loop fusion | flops 13369344 | bytes 31457316 | tf_op jit(solution)/shard_map/add | solution.py:24
  69.7 0.0 copy-done.1
  69.7 12.6 %fusion.25 = f32[32,32,768]{2,0,1:T(8,128)S(1)} fusion(f32[32,32,768]{2,0,1:T(8,128)S(1)} %fusion.58, f32[32,32,768]{2,1,0:T(8,128)S(1)} %copy-done.1, f32[]{:T(128)} %bitcast.26, f32[]{:T(128)} %bitcast.25, f32[]{:T(128)} %bitcast.24, f32[]{:T(128)} %bitcast.23, f32[]{:T(128)} %bitcast.22, f32[]{:T(128)} %bitcast.21, f32[]{:T(128)} %bitcast.20, f32[]{:T(128)} %bitcast.3, ...), kind=kLoop, calls=%fused_computation.61 | loop fusion | flops 14155776 | bytes 9437220 | tf_op jit(solution)/shard_map/div | solution.py:57
  82.3 0.1 fusion.68
  82.4 0.1 copy.18
  82.5 1.3 collective-permute-start.5
  83.8 0.1 copy.17
  83.9 4.0 %collective-permute-start.4 = (f32[4,32,768]{2,1,0:T(8,128)S(1)}, f32[4,32,768]{2,1,0:T(8,128)S(1)}, u32[]{:S(2)}, u32[]{:S(2)}) collective-permute-start(f32[4,32,768]{2,1,0:T(8,128)S(1)} %copy.17), channel_id=1, source_target_pairs={{0,32},{32,64},{64,96},{96,128},{128,160},{160,192},{192,224},{1,3... | collective-permute-start | bytes 1179656 | tf_op jit(solution)/shard_map/ppermute | solution.py:14
  87.9 3.4 %collective-permute-done.5 = f32[4,32,768]{2,1,0:T(8,128)S(1)} collective-permute-done((f32[4,32,768]{2,1,0:T(8,128)S(1)}, f32[4,32,768]{2,1,0:T(8,128)S(1)}, u32[]{:S(2)}, u32[]{:S(2)}) %collective-permute-start.5) | collective-permute-done | bytes 393248 | tf_op jit(solution)/shard_map/ppermute | solution.py:15
  91.3 0.3 copy.20
  91.6 1.0 collective-permute-done.4
  92.6 0.3 copy.19
  92.9 0.1 pad_maximum_fusion.4
  93.0 2.9 %collective-permute-start.6 = (f32[40,4,768]{2,0,1:T(8,128)S(1)}, f32[40,4,768]{2,0,1:T(8,128)S(1)}, u32[]{:S(2)}, u32[]{:S(2)}) collective-permute-start(f32[40,4,768]{2,0,1:T(8,128)S(1)} %get-tuple-element.8), channel_id=1, source_target_pairs={{0,1},{1,2},{2,3},{3,4},{4,5},{5,6},{6,7},{7,8},{8,9},{9,10},{10,1... | collective-permute-start | bytes 1474568 | tf_op jit(solution)/shard_map/ppermute | solution.py:14
  95.9 2.1 %collective-permute-start.7 = (f32[40,4,768]{2,0,1:T(8,128)S(1)}, f32[40,4,768]{2,0,1:T(8,128)S(1)}, u32[]{:S(2)}, u32[]{:S(2)}) collective-permute-start(f32[40,4,768]{2,0,1:T(8,128)S(1)} %get-tuple-element.9), channel_id=1, source_target_pairs={{1,0},{2,1},{3,2},{4,3},{5,4},{6,5},{7,6},{8,7},{9,8},{10,9},{11,1... | collective-permute-start | bytes 1474568 | tf_op jit(solution)/shard_map/ppermute | solution.py:15
  98.0 8.9 %collective-permute-done.6 = f32[40,4,768]{2,0,1:T(8,128)S(1)} collective-permute-done((f32[40,4,768]{2,0,1:T(8,128)S(1)}, f32[40,4,768]{2,0,1:T(8,128)S(1)}, u32[]{:S(2)}, u32[]{:S(2)}) %collective-permute-start.6) | collective-permute-done | bytes 491552 | tf_op jit(solution)/shard_map/ppermute | solution.py:14
  106.8 8.6 %collective-permute-done.7 = f32[40,4,768]{2,0,1:T(8,128)S(1)} collective-permute-done((f32[40,4,768]{2,0,1:T(8,128)S(1)}, f32[40,4,768]{2,0,1:T(8,128)S(1)}, u32[]{:S(2)}, u32[]{:S(2)}) %collective-permute-start.7) | collective-permute-done | bytes 491552 | tf_op jit(solution)/shard_map/ppermute | solution.py:15
  115.5 0.7 pad_maximum_fusion.1
  116.2 9.7 %fusion = f32[32,40,768]{2,0,1:T(8,128)S(1)} fusion(f32[40,40,768]{2,0,1:T(8,128)S(1)} %pad_maximum_fusion.1, f32[]{:T(128)} %bitcast.12, f32[]{:T(128)} %bitcast.11, f32[]{:T(128)} %bitcast.10, f32[]{:T(128)} %bitcast.9, f32[]{:T(128)} %bitcast.8, f32[]{:T(128)} %bitcast.7, f32[]{:T(128)} %bitcast.6, f32[]{:T(128)} %bitcast.5, f32[]{:T(128)} %bitcast.2), kind=kLoop, calls=%fused_computation.19 | loop fusion | flops 16711680 | bytes 39321636 | tf_op jit(solution)/shard_map/add | solution.py:24
  125.9 0.0 copy-start
  125.9 9.1 %fusion.50 = f32[32,32,768]{2,0,1:T(8,128)S(1)} fusion(f32[32,40,768]{2,0,1:T(8,128)S(1)} %fusion, f32[]{:T(128)} %bitcast.19, f32[]{:T(128)} %bitcast.18, f32[]{:T(128)} %bitcast.17, f32[]{:T(128)} %bitcast.16, f32[]{:T(128)} %bitcast.15, f32[]{:T(128)} %bitcast.14, f32[]{:T(128)} %bitcast.13, f32[]{:T(128)} %bitcast.4, f32[]{:T(128)} %bitcast.1), kind=kLoop, calls=%fused_computation.87 | loop fusion | flops 13369344 | bytes 31457316 | tf_op jit(solution)/shard_map/add | solution.py:24
  135.0 0.0 copy-done
  135.0 13.3 %fusion.66 = (f32[32,768]{1,0:T(8,128)S(1)}, f32[32,32,768]{2,0,1:T(8,128)S(1)}) fusion(f32[]{:T(128)} %bitcast.3, f32[]{:T(128)} %bitcast.20, f32[]{:T(128)} %bitcast.21, f32[]{:T(128)} %bitcast.22, f32[32,32,768]{2,0,1:T(8,128)S(1)} %fusion.50, f32[]{:T(128)} %bitcast.23, f32[]{:T(128)} %bitcast.24, f32[]{:T(128)} %bitcast.25, f32[]{:T(128)} %bitcast.26, ...), kind=kLoop, calls=%fused_computation.126 | loop fusion | flops 14917632 | bytes 9535524 | tf_op jit(solution)/shard_map/reduce_max | solution.py:61
  148.3 0.1 collective-permute-start.8
  148.4 3.5 %collective-permute-done.8 = f32[32,768]{1,0:T(8,128)S(1)} collective-permute-done((f32[32,768]{1,0:T(8,128)S(1)}, f32[32,768]{1,0:T(8,128)S(1)}, u32[]{:S(2)}, u32[]{:S(2)}) %collective-permute-start.8) | collective-permute-done | bytes 98336 | tf_op jit(solution)/shard_map/ppermute | solution.py:45
  151.9 4.1 %collective-permute-start.9 = (f32[32,768]{1,0:T(8,128)S(1)}, f32[32,768]{1,0:T(8,128)S(1)}, u32[]{:S(2)}, u32[]{:S(2)}) collective-permute-start(f32[32,768]{1,0:T(8,128)S(1)} %max.9), channel_id=1, source_target_pairs={{0,64},{32,96},{64,0},{96,32},{128,192},{160,224},{192,128},{224,1... | collective-permute-start | bytes 294920 | tf_op jit(solution)/shard_map/ppermute | solution.py:45
  156.0 2.0 %collective-permute-done.9 = f32[32,768]{1,0:T(8,128)S(1)} collective-permute-done((f32[32,768]{1,0:T(8,128)S(1)}, f32[32,768]{1,0:T(8,128)S(1)}, u32[]{:S(2)}, u32[]{:S(2)}) %collective-permute-start.9) | collective-permute-done | bytes 98336 | tf_op jit(solution)/shard_map/ppermute | solution.py:45
  158.0 3.4 %collective-permute-start.10 = (f32[32,768]{1,0:T(8,128)S(1)}, f32[32,768]{1,0:T(8,128)S(1)}, u32[]{:S(2)}, u32[]{:S(2)}) collective-permute-start(f32[32,768]{1,0:T(8,128)S(1)} %max.10), channel_id=1, source_target_pairs={{0,128},{32,160},{64,192},{96,224},{128,0},{160,32},{192,64},{224,... | collective-permute-start | bytes 294920 | tf_op jit(solution)/shard_map/ppermute | solution.py:45
  161.4 3.5 %copy.22 = f32[32,32,768]{2,1,0:T(8,128)} copy(f32[32,32,768]{2,0,1:T(8,128)S(1)} %get-tuple-element.7) | data formatting | bytes 6291456
  164.9 0.0 collective-permute-done.10
  164.9 0.7 max.11
  (2 shorter events, 0.0 us)
Async XLA Ops:
  1.8 11.3 %collective-permute-start = (f32[4,32,768]{2,1,0:T(8,128)S(1)}, f32[4,32,768]{2,1,0:T(8,128)S(1)}, u32[]{:S(2)}, u32[]{:S(2)}) collective-permute-start(f32[4,32,768]{2,1,0:T(8,128)S(1)} %get-tuple-element.14), channel_id=1, source_target_pairs={{0,32},{32,64},{64,96},{96,128},{128,160},{160,192},{192,224},{1,3... | collective-permute-start | bytes 1179656 | tf_op jit(solution)/shard_map/ppermute | solution.py:14
  5.4 17.7 %collective-permute-start.1 = (f32[4,32,768]{2,1,0:T(8,128)S(1)}, f32[4,32,768]{2,1,0:T(8,128)S(1)}, u32[]{:S(2)}, u32[]{:S(2)}) collective-permute-start(f32[4,32,768]{2,1,0:T(8,128)S(1)} %get-tuple-element.15), channel_id=1, source_target_pairs={{32,0},{64,32},{96,64},{128,96},{160,128},{192,160},{224,192},{33,... | collective-permute-start | bytes 1179656 | tf_op jit(solution)/shard_map/ppermute | solution.py:15
  10.4 22.2 %copy-start.2 = (f32[9]{0:T(128)S(1)}, f32[9]{0:T(128)}, u32[]{:S(2)}) copy-start(f32[9]{0:T(128)} %param.7) | copy-start | bytes 112
  10.4 22.8 %copy-start.3 = (f32[9]{0:T(128)S(1)}, f32[9]{0:T(128)}, u32[]{:S(2)}) copy-start(f32[9]{0:T(128)} %param.8) | copy-start | bytes 112
  10.4 23.5 %copy-start.4 = (f32[9]{0:T(128)S(1)}, f32[9]{0:T(128)}, u32[]{:S(2)}) copy-start(f32[9]{0:T(128)} %param.9) | copy-start | bytes 112
  23.4 18.2 %collective-permute-start.2 = (f32[40,4,768]{2,0,1:T(8,128)S(1)}, f32[40,4,768]{2,0,1:T(8,128)S(1)}, u32[]{:S(2)}, u32[]{:S(2)}) collective-permute-start(f32[40,4,768]{2,0,1:T(8,128)S(1)} %get-tuple-element.10), channel_id=1, source_target_pairs={{0,1},{1,2},{2,3},{3,4},{4,5},{5,6},{6,7},{7,8},{8,9},{9,10},{10,1... | collective-permute-start | bytes 1474568 | tf_op jit(solution)/shard_map/ppermute | solution.py:14
  30.6 19.5 %collective-permute-start.3 = (f32[40,4,768]{2,0,1:T(8,128)S(1)}, f32[40,4,768]{2,0,1:T(8,128)S(1)}, u32[]{:S(2)}, u32[]{:S(2)}) collective-permute-start(f32[40,4,768]{2,0,1:T(8,128)S(1)} %get-tuple-element.11), channel_id=1, source_target_pairs={{1,0},{2,1},{3,2},{4,3},{5,4},{6,5},{7,6},{8,7},{9,8},{10,9},{11,1... | collective-permute-start | bytes 1474568 | tf_op jit(solution)/shard_map/ppermute | solution.py:15
  60.6 9.1 %copy-start.1 = (f32[32,32,768]{2,1,0:T(8,128)S(1)}, f32[32,32,768]{2,1,0:T(8,128)}, u32[]{:S(2)}) copy-start(f32[32,32,768]{2,1,0:T(8,128)} %param.5) | copy-start | bytes 9437188
  82.5 8.8 %collective-permute-start.5 = (f32[4,32,768]{2,1,0:T(8,128)S(1)}, f32[4,32,768]{2,1,0:T(8,128)S(1)}, u32[]{:S(2)}, u32[]{:S(2)}) collective-permute-start(f32[4,32,768]{2,1,0:T(8,128)S(1)} %copy.18), channel_id=1, source_target_pairs={{32,0},{64,32},{96,64},{128,96},{160,128},{192,160},{224,192},{33,... | collective-permute-start | bytes 1179656 | tf_op jit(solution)/shard_map/ppermute | solution.py:15
  83.9 8.7 %collective-permute-start.4 = (f32[4,32,768]{2,1,0:T(8,128)S(1)}, f32[4,32,768]{2,1,0:T(8,128)S(1)}, u32[]{:S(2)}, u32[]{:S(2)}) collective-permute-start(f32[4,32,768]{2,1,0:T(8,128)S(1)} %copy.17), channel_id=1, source_target_pairs={{0,32},{32,64},{64,96},{96,128},{128,160},{160,192},{192,224},{1,3... | collective-permute-start | bytes 1179656 | tf_op jit(solution)/shard_map/ppermute | solution.py:14
  93.0 13.9 %collective-permute-start.6 = (f32[40,4,768]{2,0,1:T(8,128)S(1)}, f32[40,4,768]{2,0,1:T(8,128)S(1)}, u32[]{:S(2)}, u32[]{:S(2)}) collective-permute-start(f32[40,4,768]{2,0,1:T(8,128)S(1)} %get-tuple-element.8), channel_id=1, source_target_pairs={{0,1},{1,2},{2,3},{3,4},{4,5},{5,6},{6,7},{7,8},{8,9},{9,10},{10,1... | collective-permute-start | bytes 1474568 | tf_op jit(solution)/shard_map/ppermute | solution.py:14
  95.9 19.6 %collective-permute-start.7 = (f32[40,4,768]{2,0,1:T(8,128)S(1)}, f32[40,4,768]{2,0,1:T(8,128)S(1)}, u32[]{:S(2)}, u32[]{:S(2)}) collective-permute-start(f32[40,4,768]{2,0,1:T(8,128)S(1)} %get-tuple-element.9), channel_id=1, source_target_pairs={{1,0},{2,1},{3,2},{4,3},{5,4},{6,5},{7,6},{8,7},{9,8},{10,9},{11,1... | collective-permute-start | bytes 1474568 | tf_op jit(solution)/shard_map/ppermute | solution.py:15
  125.9 9.1 %copy-start = (f32[32,32,768]{2,1,0:T(8,128)S(1)}, f32[32,32,768]{2,1,0:T(8,128)}, u32[]{:S(2)}) copy-start(f32[32,32,768]{2,1,0:T(8,128)} %param.6) | copy-start | bytes 9437188
  148.3 3.6 %collective-permute-start.8 = (f32[32,768]{1,0:T(8,128)S(1)}, f32[32,768]{1,0:T(8,128)S(1)}, u32[]{:S(2)}, u32[]{:S(2)}) collective-permute-start(f32[32,768]{1,0:T(8,128)S(1)} %get-tuple-element.6), channel_id=1, source_target_pairs={{0,32},{32,0},{64,96},{96,64},{128,160},{160,128},{192,224},{224,1... | collective-permute-start | bytes 294920 | tf_op jit(solution)/shard_map/ppermute | solution.py:45
  151.9 6.1 %collective-permute-start.9 = (f32[32,768]{1,0:T(8,128)S(1)}, f32[32,768]{1,0:T(8,128)S(1)}, u32[]{:S(2)}, u32[]{:S(2)}) collective-permute-start(f32[32,768]{1,0:T(8,128)S(1)} %max.9), channel_id=1, source_target_pairs={{0,64},{32,96},{64,0},{96,32},{128,192},{160,224},{192,128},{224,1... | collective-permute-start | bytes 294920 | tf_op jit(solution)/shard_map/ppermute | solution.py:45
  158.0 6.9 %collective-permute-start.10 = (f32[32,768]{1,0:T(8,128)S(1)}, f32[32,768]{1,0:T(8,128)S(1)}, u32[]{:S(2)}, u32[]{:S(2)}) collective-permute-start(f32[32,768]{1,0:T(8,128)S(1)} %max.10), channel_id=1, source_target_pairs={{0,128},{32,160},{64,192},{96,224},{128,0},{160,32},{192,64},{224,... | collective-permute-start | bytes 294920 | tf_op jit(solution)/shard_map/ppermute | solution.py:45

commit v2 on v1

--- a/solution.py
+++ b/solution.py
@@ -4,17 +4,32 @@
 from jax.sharding import PartitionSpec as P
 
 
-def with_halo(shard, sides, width):
-    for axis, dim in sides:
-        peers, length = (lax.axis_size(axis), shard.shape[dim])
-        up = [(i, (i + 1) % peers) for i in range(peers - 1)]
-        down = [(j, i) for i, j in up]
-        last = lax.slice_in_dim(shard, length - width, length, axis=dim)
-        first = lax.slice_in_dim(shard, 0, width, axis=dim)
-        before = lax.ppermute(last, axis, up)
-        after = lax.ppermute(first, axis, down)
-        shard = jnp.concatenate([before, shard, after], axis=dim)
-    return shard
+def shift_from(piece, axes, offsets):
+    sizes = [lax.axis_size(a) for a in axes]
+    pairs = []
+    for src in range(sizes[0] * sizes[1]):
+        coords = (src // sizes[1], src % sizes[1])
+        dst = [c + o for c, o in zip(coords, offsets)]
+        if all(0 <= d < n for d, n in zip(dst, sizes)):
+            pairs.append((src, dst[0] * sizes[1] + dst[1]))
+    return lax.ppermute(piece, axes, pairs)
+
+
+def with_halo(shard, width):
+    axes = ("gz", "gy")
+    nz, ny = shard.shape[0], shard.shape[1]
+    zs = {-1: slice(0, width), 0: slice(0, nz), 1: slice(nz - width, nz)}
+    ys = {-1: slice(0, width), 0: slice(0, ny), 1: slice(ny - width, ny)}
+    grid = {}
+    for dz in (-1, 0, 1):
+        for dy in (-1, 0, 1):
+            if dz == 0 and dy == 0:
+                grid[(dz, dy)] = shard
+                continue
+            piece = shard[zs[-dz], ys[-dy]]
+            grid[(dz, dy)] = shift_from(piece, axes, (-dz, -dy))
+    rows = [jnp.concatenate([grid[(dz, -1)], grid[(dz, 0)], grid[(dz, 1)]], axis=1) for dz in (-1, 0, 1)]
+    return jnp.concatenate(rows, axis=0)
 
 
 def valid_pass(padded, taps, axis):
@@ -52,10 +67,10 @@
     back_z = taps_z[::-1]
     back_y = taps_y[::-1]
     back_x = taps_x[::-1]
-    padded = with_halo(estimate, (("gz", 0), ("gy", 1)), radius)
+    padded = with_halo(estimate, radius)
     blurred = blur_padded(padded, taps_z, taps_y, taps_x)
     ratio = observed / blurred
-    ratio_padded = with_halo(ratio, (("gz", 0), ("gy", 1)), radius)
+    ratio_padded = with_halo(ratio, radius)
     correction = blur_padded(ratio_padded, back_z, back_y, back_x)
     updated = estimate * correction
     local_max = jnp.max(updated, axis=0)

time: 166 us -> 198 us (1.19)
  the two profiles are of different devices: /device:TPU:89 before, /device:TPU:160 now
where the time goes in v2:
time: 198 us; the launch traced here: 196 us
  starting transfers between devices  79.9 us (40%)
  other arithmetic  68.2 us (34%)
  waiting for transfers between devices  41.3 us (21%)
  local copies, waits for them, and re-layouts  5.41 us (3%)
    ppermute x16, starting transfers between devices, shift_from(): return lax.ppermute(piece, axes, pairs)  68.9 us
    add x4, other arithmetic, valid_pass(): total + taps[index] * lax.slice_in_dim(padded, index, index + count, axis...  38.6 us
    ppermute x16, waiting for transfers between devices, shift_from(): return lax.ppermute(piece, axes, pairs)  28.7 us
    reduce_max x1, other arithmetic, per_device(): local_max = jnp.max(updated, axis=0)  13.4 us
    ppermute x3, waiting for transfers between devices, butterfly_max(): value = jnp.maximum(value, lax.ppermute(value, axis, pairs))  12.6 us
    div x1, other arithmetic, per_device(): ratio = observed / blurred  12.3 us
    ppermute x3, starting transfers between devices, butterfly_max(): value = jnp.maximum(value, lax.ppermute(value, axis, pairs))  11 us
  transfers between devices with their start and end apart: 19, of which 7 were waited for; matrix products, arithmetic and copies ran while one was open for 2% of the time, Pallas kernels for 0%

profile of v2, /device:TPU:160, one launch (start us, length us, event | category | flops | bytes accessed | tf_op | source)
XLA Modules:
  0.0 195.9 jit_solution(17706111591609984822)
XLA Ops:
  0.7 1.7 fusion.73
  2.3 0.1 copy.28
  2.4 4.4 %collective-permute-start.4 = (f32[32,4,768]{2,0,1:T(8,128)S(1)}, f32[32,4,768]{2,0,1:T(8,128)S(1)}, u32[]{:S(2)}, u32[]{:S(2)}) collective-permute-start(f32[32,4,768]{2,0,1:T(8,128)S(1)} %copy.28), channel_id=1, source_target_pairs={{1,0},{2,1},{3,2},{4,3},{5,4},{6,5},{7,6},{8,7},{9,8},{10,9},{11,1... | collective-permute-start | bytes 1179656 | tf_op jit(solution)/shard_map/ppermute | solution.py:15
  6.8 0.1 copy.27
  6.9 1.9 collective-permute-start.3
  8.8 0.1 fusion.72
  8.9 2.9 %collective-permute-start.1 = (f32[4,32,768]{2,1,0:T(8,128)S(1)}, f32[4,32,768]{2,1,0:T(8,128)S(1)}, u32[]{:S(2)}, u32[]{:S(2)}) collective-permute-start(f32[4,32,768]{2,1,0:T(8,128)S(1)} %get-tuple-element.22), channel_id=1, source_target_pairs={{0,32},{1,33},{2,34},{3,35},{4,36},{5,37},{6,38},{7,39},{8,40},{9,... | collective-permute-start | bytes 1179656 | tf_op jit(solution)/shard_map/ppermute | solution.py:15
  11.8 2.9 %collective-permute-start.6 = (f32[4,32,768]{2,1,0:T(8,128)S(1)}, f32[4,32,768]{2,1,0:T(8,128)S(1)}, u32[]{:S(2)}, u32[]{:S(2)}) collective-permute-start(f32[4,32,768]{2,1,0:T(8,128)S(1)} %get-tuple-element.23), channel_id=1, source_target_pairs={{32,0},{33,1},{34,2},{35,3},{36,4},{37,5},{38,6},{39,7},{40,8},{41... | collective-permute-start | bytes 1179656 | tf_op jit(solution)/shard_map/ppermute | solution.py:15
  14.8 3.0 %collective-permute-start = (f32[4,4,768]{2,1,0:T(4,128)S(1)}, f32[4,4,768]{2,1,0:T(4,128)S(1)}, u32[]{:S(2)}, u32[]{:S(2)}) collective-permute-start(f32[4,4,768]{2,1,0:T(4,128)S(1)} %get-tuple-element.18), channel_id=1, source_target_pairs={{0,33},{1,34},{2,35},{3,36},{4,37},{5,38},{6,39},{7,40},{8,41},{9,... | collective-permute-start | bytes 147464 | tf_op jit(solution)/shard_map/ppermute | solution.py:15
  17.8 0.7 fusion.76
  18.5 0.7 fusion.75
  19.2 15.0 %collective-permute-done = f32[4,4,768]{2,1,0:T(4,128)S(1)} collective-permute-done((f32[4,4,768]{2,1,0:T(4,128)S(1)}, f32[4,4,768]{2,1,0:T(4,128)S(1)}, u32[]{:S(2)}, u32[]{:S(2)}) %collective-permute-start) | collective-permute-done | bytes 49184 | tf_op jit(solution)/shard_map/ppermute | solution.py:15
  34.2 1.9 collective-permute-start.5
  36.1 0.0 collective-permute-done.4
  36.1 9.7 %collective-permute-start.2 = (f32[4,4,768]{2,1,0:T(4,128)S(1)}, f32[4,4,768]{2,1,0:T(4,128)S(1)}, u32[]{:S(2)}, u32[]{:S(2)}) collective-permute-start(f32[4,4,768]{2,1,0:T(4,128)S(1)} %get-tuple-element.20), channel_id=1, source_target_pairs={{1,32},{2,33},{3,34},{4,35},{5,36},{6,37},{7,38},{8,39},{9,40},{10... | collective-permute-start | bytes 147464 | tf_op jit(solution)/shard_map/ppermute | solution.py:15
  45.8 0.0 collective-permute-done.3
  45.8 1.9 collective-permute-start.7
  47.8 0.7 fusion.74
  48.4 0.3 copy.22
  48.7 0.0 copy-start.4
  48.7 0.3 copy.21
  49.0 0.0 collective-permute-done.5
  49.0 0.0 collective-permute-done.2
  49.0 3.1 %collective-permute-done.7 = f32[4,4,768]{2,1,0:T(4,128)S(1)} collective-permute-done((f32[4,4,768]{2,1,0:T(4,128)S(1)}, f32[4,4,768]{2,1,0:T(4,128)S(1)}, u32[]{:S(2)}, u32[]{:S(2)}) %collective-permute-start.7) | collective-permute-done | bytes 49184 | tf_op jit(solution)/shard_map/ppermute | solution.py:15
  52.1 0.0 collective-permute-done.1
  52.1 0.0 collective-permute-done.6
  52.1 1.5 maximum_maximum_fusion
  53.7 10.1 %fusion.8 = f32[32,40,768]{2,1,0:T(8,128)S(1)} fusion(f32[36,40,768]{2,1,0:T(8,128)S(1)} %get-tuple-element.9, f32[36,40,768]{2,1,0:T(8,128)S(1)} %get-tuple-element.8, f32[32,4,768]{2,1,0:T(4,128)} %copy-done.4, f32[32,32,768]{2,1,0:T(8,128)S(1)} %copy-done, f32[32,4,768]{2,1,0:T(4,128)} %copy-done.5, f32[]{:T(128)} %bitcast.12, f32[]{:T(128)} %bitcast.11, ...), kind=kLoop, calls=%fused_computation.37 | loop fusion | flops 18677760 | bytes 39321636 | tf_op jit(solution)/shard_map/add | solution.py:39
  63.8 0.0 copy-start.6
  63.8 9.1 %fusion.58 = f32[32,32,768]{2,1,0:T(8,128)S(1)} fusion(f32[32,40,768]{2,1,0:T(8,128)S(1)} %fusion.8, f32[]{:T(128)} %bitcast.19, f32[]{:T(128)} %bitcast.18, f32[]{:T(128)} %bitcast.17, f32[]{:T(128)} %bitcast.16, f32[]{:T(128)} %bitcast.15, f32[]{:T(128)} %bitcast.14, f32[]{:T(128)} %bitcast.13, f32[]{:T(128)} %bitcast.4, f32[]{:T(128)} %bitcast.1), kind=kLoop, calls=%fused_computation.106 | loop fusion | flops 13369344 | bytes 31457316 | tf_op jit(solution)/shard_map/add | solution.py:39
  73.0 12.3 %fusion.25 = f32[32,32,768]{2,1,0:T(8,128)S(1)} fusion(f32[32,32,768]{2,1,0:T(8,128)S(1)} %copy-done.6, f32[32,32,768]{2,1,0:T(8,128)S(1)} %fusion.58, f32[]{:T(128)} %bitcast.26, f32[]{:T(128)} %bitcast.25, f32[]{:T(128)} %bitcast.24, f32[]{:T(128)} %bitcast.23, f32[]{:T(128)} %bitcast.22, f32[]{:T(128)} %bitcast.21, f32[]{:T(128)} %bitcast.20, f32[]{:T(128)} %bitcast.3, ...), kind=kLoop, calls=%fused_computation.63 | loop fusion | flops 14155776 | bytes 9437220 | tf_op jit(solution)/shard_map/div | solution.py:72
  85.3 0.0 copy-start.1
  85.3 0.1 fusion.70
  85.4 0.1 copy.23
  85.5 0.1 copy.24
  85.6 1.9 collective-permute-start.12
  87.5 2.4 %collective-permute-start.11 = (f32[32,4,768]{2,0,1:T(8,128)S(1)}, f32[32,4,768]{2,0,1:T(8,128)S(1)}, u32[]{:S(2)}, u32[]{:S(2)}) collective-permute-start(f32[32,4,768]{2,0,1:T(8,128)S(1)} %copy.23), channel_id=1, source_target_pairs={{0,1},{1,2},{2,3},{3,4},{4,5},{5,6},{6,7},{7,8},{8,9},{9,10},{10,1... | collective-permute-start | bytes 1179656 | tf_op jit(solution)/shard_map/ppermute | solution.py:15
  90.0 0.1 fusion.69
  90.0 14.8 %collective-permute-start.9 = (f32[4,32,768]{2,1,0:T(8,128)S(1)}, f32[4,32,768]{2,1,0:T(8,128)S(1)}, u32[]{:S(2)}, u32[]{:S(2)}) collective-permute-start(f32[4,32,768]{2,1,0:T(8,128)S(1)} %get-tuple-element.14), channel_id=1, source_target_pairs={{0,32},{1,33},{2,34},{3,35},{4,36},{5,37},{6,38},{7,39},{8,40},{9,... | collective-permute-start | bytes 1179656 | tf_op jit(solution)/shard_map/ppermute | solution.py:15
  104.8 1.9 collective-permute-start.14
  106.8 1.9 collective-permute-start.8
  108.7 9.5 %collective-permute-done.8 = f32[4,4,768]{2,1,0:T(4,128)S(1)} collective-permute-done((f32[4,4,768]{2,1,0:T(4,128)S(1)}, f32[4,4,768]{2,1,0:T(4,128)S(1)}, u32[]{:S(2)}, u32[]{:S(2)}) %collective-permute-start.8) | collective-permute-done | bytes 49184 | tf_op jit(solution)/shard_map/ppermute | solution.py:15
  118.2 1.9 collective-permute-start.15
  120.1 0.0 collective-permute-done.12
  120.2 1.9 collective-permute-start.13
  122.1 0.0 collective-permute-done.11
  122.1 13.5 %collective-permute-start.10 = (f32[4,4,768]{2,1,0:T(4,128)S(1)}, f32[4,4,768]{2,1,0:T(4,128)S(1)}, u32[]{:S(2)}, u32[]{:S(2)}) collective-permute-start(f32[4,4,768]{2,1,0:T(4,128)S(1)} %get-tuple-element.13), channel_id=1, source_target_pairs={{1,32},{2,33},{3,34},{4,35},{5,36},{6,37},{7,38},{8,39},{9,40},{10... | collective-permute-start | bytes 147464 | tf_op jit(solution)/shard_map/ppermute | solution.py:15
  135.6 0.3 copy.26
  135.9 0.3 copy.25
  136.2 0.0 collective-permute-done.15
  136.2 0.0 collective-permute-done.13
  136.2 1.0 collective-permute-done.10
  137.2 0.0 collective-permute-done.9
  137.2 1.6 maximum_maximum_fusion.2
  138.8 10.6 %fusion = f32[32,40,768]{2,1,0:T(8,128)S(1)} fusion(f32[36,40,768]{2,1,0:T(8,128)S(1)} %get-tuple-element.7, f32[36,40,768]{2,1,0:T(8,128)S(1)} %get-tuple-element.6, f32[32,4,768]{2,1,0:T(4,128)} %copy-done.2, f32[32,32,768]{2,1,0:T(8,128)} %copy-done.1, f32[32,4,768]{2,1,0:T(4,128)} %copy-done.3, f32[]{:T(128)} %bitcast.12, f32[]{:T(128)} %bitcast.11, ...), kind=kLoop, calls=%fused_computation.21 | loop fusion | flops 18677760 | bytes 39321636 | tf_op jit(solution)/shard_map/add | solution.py:39
  149.4 8.8 %fusion.50 = f32[32,32,768]{2,1,0:T(8,128)S(1)} fusion(f32[32,40,768]{2,1,0:T(8,128)S(1)} %fusion, f32[]{:T(128)} %bitcast.19, f32[]{:T(128)} %bitcast.18, f32[]{:T(128)} %bitcast.17, f32[]{:T(128)} %bitcast.16, f32[]{:T(128)} %bitcast.15, f32[]{:T(128)} %bitcast.14, f32[]{:T(128)} %bitcast.13, f32[]{:T(128)} %bitcast.4, f32[]{:T(128)} %bitcast.1), kind=kLoop, calls=%fused_computation.89 | loop fusion | flops 13369344 | bytes 31457316 | tf_op jit(solution)/shard_map/add | solution.py:39
  158.2 13.4 %fusion.66 = (f32[32,768]{1,0:T(8,128)S(1)}, f32[32,32,768]{2,1,0:T(8,128)}) fusion(f32[32,32,768]{2,1,0:T(8,128)S(1)} %copy-done, f32[]{:T(128)} %bitcast.3, f32[]{:T(128)} %bitcast.20, f32[]{:T(128)} %bitcast.21, f32[]{:T(128)} %bitcast.22, f32[32,32,768]{2,1,0:T(8,128)S(1)} %fusion.50, f32[]{:T(128)} %bitcast.23, f32[]{:T(128)} %bitcast.24, f32[]{:T(128)} %bitcast.25, ...), kind=kLoop, calls=%fused_computation.122 | loop fusion | flops 14917632 | bytes 9535524 | tf_op jit(solution)/shard_map/reduce_max | solution.py:76
  171.7 0.0 collective-permute-start.16
  171.7 4.6 %collective-permute-done.16 = f32[32,768]{1,0:T(8,128)S(1)} collective-permute-done((f32[32,768]{1,0:T(8,128)S(1)}, f32[32,768]{1,0:T(8,128)S(1)}, u32[]{:S(2)}, u32[]{:S(2)}) %collective-permute-start.16) | collective-permute-done | bytes 98336 | tf_op jit(solution)/shard_map/ppermute | solution.py:60
  176.3 9.2 %collective-permute-start.17 = (f32[32,768]{1,0:T(8,128)S(1)}, f32[32,768]{1,0:T(8,128)S(1)}, u32[]{:S(2)}, u32[]{:S(2)}) collective-permute-start(f32[32,768]{1,0:T(8,128)S(1)} %max.9), channel_id=1, source_target_pairs={{0,64},{32,96},{64,0},{96,32},{128,192},{160,224},{192,128},{224,1... | collective-permute-start | bytes 294920 | tf_op jit(solution)/shard_map/ppermute | solution.py:60
  185.5 3.5 %collective-permute-done.17 = f32[32,768]{1,0:T(8,128)S(1)} collective-permute-done((f32[32,768]{1,0:T(8,128)S(1)}, f32[32,768]{1,0:T(8,128)S(1)}, u32[]{:S(2)}, u32[]{:S(2)}) %collective-permute-start.17) | collective-permute-done | bytes 98336 | tf_op jit(solution)/shard_map/ppermute | solution.py:60
  189.0 1.7 collective-permute-start.18
  190.7 4.5 %collective-permute-done.18 = f32[32,768]{1,0:T(8,128)S(1)} collective-permute-done((f32[32,768]{1,0:T(8,128)S(1)}, f32[32,768]{1,0:T(8,128)S(1)}, u32[]{:S(2)}, u32[]{:S(2)}) %collective-permute-start.18) | collective-permute-done | bytes 98336 | tf_op jit(solution)/shard_map/ppermute | solution.py:60
  195.2 0.7 max.11
  (22 shorter events, 0.1 us)
Async XLA Ops:
  0.6 8.2 %copy-start = (f32[32,32,768]{2,1,0:T(8,128)S(1)}, f32[32,32,768]{2,1,0:T(8,128)}, u32[]{:S(2)}) copy-start(f32[32,32,768]{2,1,0:T(8,128)} %param.6) | copy-start | bytes 9437188
  0.6 17.2 %copy-start.7 = (f32[9]{0:T(128)S(1)}, f32[9]{0:T(128)}, u32[]{:S(2)}) copy-start(f32[9]{0:T(128)} %param.7) | copy-start | bytes 112
  0.7 17.9 %copy-start.8 = (f32[9]{0:T(128)S(1)}, f32[9]{0:T(128)}, u32[]{:S(2)}) copy-start(f32[9]{0:T(128)} %param.8) | copy-start | bytes 112
  0.7 47.1 %copy-start.9 = (f32[9]{0:T(128)S(1)}, f32[9]{0:T(128)}, u32[]{:S(2)}) copy-start(f32[9]{0:T(128)} %param.9) | copy-start | bytes 112
  2.4 33.7 %collective-permute-start.4 = (f32[32,4,768]{2,0,1:T(8,128)S(1)}, f32[32,4,768]{2,0,1:T(8,128)S(1)}, u32[]{:S(2)}, u32[]{:S(2)}) collective-permute-start(f32[32,4,768]{2,0,1:T(8,128)S(1)} %copy.28), channel_id=1, source_target_pairs={{1,0},{2,1},{3,2},{4,3},{5,4},{6,5},{7,6},{8,7},{9,8},{10,9},{11,1... | collective-permute-start | bytes 1179656 | tf_op jit(solution)/shard_map/ppermute | solution.py:15
  6.9 38.9 %collective-permute-start.3 = (f32[32,4,768]{2,0,1:T(8,128)S(1)}, f32[32,4,768]{2,0,1:T(8,128)S(1)}, u32[]{:S(2)}, u32[]{:S(2)}) collective-permute-start(f32[32,4,768]{2,0,1:T(8,128)S(1)} %copy.27), channel_id=1, source_target_pairs={{0,1},{1,2},{2,3},{3,4},{4,5},{5,6},{6,7},{7,8},{8,9},{9,10},{10,1... | collective-permute-start | bytes 1179656 | tf_op jit(solution)/shard_map/ppermute | solution.py:15
  8.9 43.3 %collective-permute-start.1 = (f32[4,32,768]{2,1,0:T(8,128)S(1)}, f32[4,32,768]{2,1,0:T(8,128)S(1)}, u32[]{:S(2)}, u32[]{:S(2)}) collective-permute-start(f32[4,32,768]{2,1,0:T(8,128)S(1)} %get-tuple-element.22), channel_id=1, source_target_pairs={{0,32},{1,33},{2,34},{3,35},{4,36},{5,37},{6,38},{7,39},{8,40},{9,... | collective-permute-start | bytes 1179656 | tf_op jit(solution)/shard_map/ppermute | solution.py:15
  11.8 40.3 %collective-permute-start.6 = (f32[4,32,768]{2,1,0:T(8,128)S(1)}, f32[4,32,768]{2,1,0:T(8,128)S(1)}, u32[]{:S(2)}, u32[]{:S(2)}) collective-permute-start(f32[4,32,768]{2,1,0:T(8,128)S(1)} %get-tuple-element.23), channel_id=1, source_target_pairs={{32,0},{33,1},{34,2},{35,3},{36,4},{37,5},{38,6},{39,7},{40,8},{41... | collective-permute-start | bytes 1179656 | tf_op jit(solution)/shard_map/ppermute | solution.py:15
  14.8 19.4 %collective-permute-start = (f32[4,4,768]{2,1,0:T(4,128)S(1)}, f32[4,4,768]{2,1,0:T(4,128)S(1)}, u32[]{:S(2)}, u32[]{:S(2)}) collective-permute-start(f32[4,4,768]{2,1,0:T(4,128)S(1)} %get-tuple-element.18), channel_id=1, source_target_pairs={{0,33},{1,34},{2,35},{3,36},{4,37},{5,38},{6,39},{7,40},{8,41},{9,... | collective-permute-start | bytes 147464 | tf_op jit(solution)/shard_map/ppermute | solution.py:15
  34.2 14.8 %collective-permute-start.5 = (f32[4,4,768]{2,1,0:T(4,128)S(1)}, f32[4,4,768]{2,1,0:T(4,128)S(1)}, u32[]{:S(2)}, u32[]{:S(2)}) collective-permute-start(f32[4,4,768]{2,1,0:T(4,128)S(1)} %get-tuple-element.19), channel_id=1, source_target_pairs={{32,1},{33,2},{34,3},{35,4},{36,5},{37,6},{38,7},{39,8},{40,9},{41... | collective-permute-start | bytes 147464 | tf_op jit(solution)/shard_map/ppermute | solution.py:15
  36.1 12.8 %collective-permute-start.2 = (f32[4,4,768]{2,1,0:T(4,128)S(1)}, f32[4,4,768]{2,1,0:T(4,128)S(1)}, u32[]{:S(2)}, u32[]{:S(2)}) collective-permute-start(f32[4,4,768]{2,1,0:T(4,128)S(1)} %get-tuple-element.20), channel_id=1, source_target_pairs={{1,32},{2,33},{3,34},{4,35},{5,36},{6,37},{7,38},{8,39},{9,40},{10... | collective-permute-start | bytes 147464 | tf_op jit(solution)/shard_map/ppermute | solution.py:15
  45.8 6.3 %collective-permute-start.7 = (f32[4,4,768]{2,1,0:T(4,128)S(1)}, f32[4,4,768]{2,1,0:T(4,128)S(1)}, u32[]{:S(2)}, u32[]{:S(2)}) collective-permute-start(f32[4,4,768]{2,1,0:T(4,128)S(1)} %get-tuple-element.21), channel_id=1, source_target_pairs={{33,0},{34,1},{35,2},{36,3},{37,4},{38,5},{39,6},{40,7},{41,8},{42... | collective-permute-start | bytes 147464 | tf_op jit(solution)/shard_map/ppermute | solution.py:15
  48.7 5.0 %copy-start.4 = (f32[32,4,768]{2,1,0:T(4,128)}, f32[32,4,768]{2,1,0:T(4,128)S(1)}, u32[]{:S(2)}) copy-start(f32[32,4,768]{2,1,0:T(4,128)S(1)} %copy.22) | copy-start | bytes 1179652
  49.0 4.7 %copy-start.5 = (f32[32,4,768]{2,1,0:T(4,128)}, f32[32,4,768]{2,1,0:T(4,128)S(1)}, u32[]{:S(2)}) copy-start(f32[32,4,768]{2,1,0:T(4,128)S(1)} %copy.21) | copy-start | bytes 1179652
  63.8 9.1 %copy-start.6 = (f32[32,32,768]{2,1,0:T(8,128)S(1)}, f32[32,32,768]{2,1,0:T(8,128)}, u32[]{:S(2)}) copy-start(f32[32,32,768]{2,1,0:T(8,128)} %param.5) | copy-start | bytes 9437188
  85.3 51.9 %copy-start.1 = (f32[32,32,768]{2,1,0:T(8,128)}, f32[32,32,768]{2,1,0:T(8,128)S(1)}, u32[]{:S(2)}) copy-start(f32[32,32,768]{2,1,0:T(8,128)S(1)} %fusion.25) | copy-start | bytes 9437188
  85.6 34.5 %collective-permute-start.12 = (f32[32,4,768]{2,0,1:T(8,128)S(1)}, f32[32,4,768]{2,0,1:T(8,128)S(1)}, u32[]{:S(2)}, u32[]{:S(2)}) collective-permute-start(f32[32,4,768]{2,0,1:T(8,128)S(1)} %copy.24), channel_id=1, source_target_pairs={{1,0},{2,1},{3,2},{4,3},{5,4},{6,5},{7,6},{8,7},{9,8},{10,9},{11,1... | collective-permute-start | bytes 1179656 | tf_op jit(solution)/shard_map/ppermute | solution.py:15
  87.5 34.5 %collective-permute-start.11 = (f32[32,4,768]{2,0,1:T(8,128)S(1)}, f32[32,4,768]{2,0,1:T(8,128)S(1)}, u32[]{:S(2)}, u32[]{:S(2)}) collective-permute-start(f32[32,4,768]{2,0,1:T(8,128)S(1)} %copy.23), channel_id=1, source_target_pairs={{0,1},{1,2},{2,3},{3,4},{4,5},{5,6},{6,7},{7,8},{8,9},{9,10},{10,1... | collective-permute-start | bytes 1179656 | tf_op jit(solution)/shard_map/ppermute | solution.py:15
  90.0 47.1 %collective-permute-start.9 = (f32[4,32,768]{2,1,0:T(8,128)S(1)}, f32[4,32,768]{2,1,0:T(8,128)S(1)}, u32[]{:S(2)}, u32[]{:S(2)}) collective-permute-start(f32[4,32,768]{2,1,0:T(8,128)S(1)} %get-tuple-element.14), channel_id=1, source_target_pairs={{0,32},{1,33},{2,34},{3,35},{4,36},{5,37},{6,38},{7,39},{8,40},{9,... | collective-permute-start | bytes 1179656 | tf_op jit(solution)/shard_map/ppermute | solution.py:15
  104.8 32.4 %collective-permute-start.14 = (f32[4,32,768]{2,1,0:T(8,128)S(1)}, f32[4,32,768]{2,1,0:T(8,128)S(1)}, u32[]{:S(2)}, u32[]{:S(2)}) collective-permute-start(f32[4,32,768]{2,1,0:T(8,128)S(1)} %get-tuple-element.15), channel_id=1, source_target_pairs={{32,0},{33,1},{34,2},{35,3},{36,4},{37,5},{38,6},{39,7},{40,8},{41... | collective-permute-start | bytes 1179656 | tf_op jit(solution)/shard_map/ppermute | solution.py:15
  106.8 11.4 %collective-permute-start.8 = (f32[4,4,768]{2,1,0:T(4,128)S(1)}, f32[4,4,768]{2,1,0:T(4,128)S(1)}, u32[]{:S(2)}, u32[]{:S(2)}) collective-permute-start(f32[4,4,768]{2,1,0:T(4,128)S(1)} %get-tuple-element.10), channel_id=1, source_target_pairs={{0,33},{1,34},{2,35},{3,36},{4,37},{5,38},{6,39},{7,40},{8,41},{9,... | collective-permute-start | bytes 147464 | tf_op jit(solution)/shard_map/ppermute | solution.py:15
  118.2 17.9 %collective-permute-start.15 = (f32[4,4,768]{2,1,0:T(4,128)S(1)}, f32[4,4,768]{2,1,0:T(4,128)S(1)}, u32[]{:S(2)}, u32[]{:S(2)}) collective-permute-start(f32[4,4,768]{2,1,0:T(4,128)S(1)} %get-tuple-element.11), channel_id=1, source_target_pairs={{33,0},{34,1},{35,2},{36,3},{37,4},{38,5},{39,6},{40,7},{41,8},{42... | collective-permute-start | bytes 147464 | tf_op jit(solution)/shard_map/ppermute | solution.py:15
  120.2 16.0 %collective-permute-start.13 = (f32[4,4,768]{2,1,0:T(4,128)S(1)}, f32[4,4,768]{2,1,0:T(4,128)S(1)}, u32[]{:S(2)}, u32[]{:S(2)}) collective-permute-start(f32[4,4,768]{2,1,0:T(4,128)S(1)} %get-tuple-element.12), channel_id=1, source_target_pairs={{32,1},{33,2},{34,3},{35,4},{36,5},{37,6},{38,7},{39,8},{40,9},{41... | collective-permute-start | bytes 147464 | tf_op jit(solution)/shard_map/ppermute | solution.py:15
  122.1 15.1 %collective-permute-start.10 = (f32[4,4,768]{2,1,0:T(4,128)S(1)}, f32[4,4,768]{2,1,0:T(4,128)S(1)}, u32[]{:S(2)}, u32[]{:S(2)}) collective-permute-start(f32[4,4,768]{2,1,0:T(4,128)S(1)} %get-tuple-element.13), channel_id=1, source_target_pairs={{1,32},{2,33},{3,34},{4,35},{5,36},{6,37},{7,38},{8,39},{9,40},{10... | collective-permute-start | bytes 147464 | tf_op jit(solution)/shard_map/ppermute | solution.py:15
  135.9 2.9 %copy-start.2 = (f32[32,4,768]{2,1,0:T(4,128)}, f32[32,4,768]{2,1,0:T(4,128)S(1)}, u32[]{:S(2)}) copy-start(f32[32,4,768]{2,1,0:T(4,128)S(1)} %copy.26) | copy-start | bytes 1179652
  136.2 2.7 %copy-start.3 = (f32[32,4,768]{2,1,0:T(4,128)}, f32[32,4,768]{2,1,0:T(4,128)S(1)}, u32[]{:S(2)}) copy-start(f32[32,4,768]{2,1,0:T(4,128)S(1)} %copy.25) | copy-start | bytes 1179652
  171.7 4.6 %collective-permute-start.16 = (f32[32,768]{1,0:T(8,128)S(1)}, f32[32,768]{1,0:T(8,128)S(1)}, u32[]{:S(2)}, u32[]{:S(2)}) collective-permute-start(f32[32,768]{1,0:T(8,128)S(1)} %get-tuple-element.4), channel_id=1, source_target_pairs={{0,32},{32,0},{64,96},{96,64},{128,160},{160,128},{192,224},{224,1... | collective-permute-start | bytes 294920 | tf_op jit(solution)/shard_map/ppermute | solution.py:60
  176.3 12.7 %collective-permute-start.17 = (f32[32,768]{1,0:T(8,128)S(1)}, f32[32,768]{1,0:T(8,128)S(1)}, u32[]{:S(2)}, u32[]{:S(2)}) collective-permute-start(f32[32,768]{1,0:T(8,128)S(1)} %max.9), channel_id=1, source_target_pairs={{0,64},{32,96},{64,0},{96,32},{128,192},{160,224},{192,128},{224,1... | collective-permute-start | bytes 294920 | tf_op jit(solution)/shard_map/ppermute | solution.py:60
  189.0 6.2 %collective-permute-start.18 = (f32[32,768]{1,0:T(8,128)S(1)}, f32[32,768]{1,0:T(8,128)S(1)}, u32[]{:S(2)}, u32[]{:S(2)}) collective-permute-start(f32[32,768]{1,0:T(8,128)S(1)} %max.10), channel_id=1, source_target_pairs={{0,128},{32,160},{64,192},{96,224},{128,0},{160,32},{192,64},{224,... | collective-permute-start | bytes 294920 | tf_op jit(solution)/shard_map/ppermute | solution.py:60

commit v3 on v1

--- a/solution.py
+++ b/solution.py
@@ -2,6 +2,9 @@
 import jax.numpy as jnp
 from jax import lax
 from jax.sharding import PartitionSpec as P
+import functools
+from jax.experimental import pallas as pl
+from jax.experimental.pallas import tpu as pltpu
 
 
 def with_halo(shard, sides, width):
@@ -37,6 +40,76 @@
     return blur_along_x(volume, taps_x)
 
 
+def blur_kernel(mode, taps_ref, pad_ref, other_ref, out_ref, *rest):
+    if mode == "update":
+        max_ref, zbuf, ybuf = rest
+    else:
+        zbuf, ybuf = rest
+    ntap = 9
+    r = 4
+    nz, ny, nx = out_ref.shape
+    py = ny + 2 * r
+    lanes = lax.broadcasted_iota(jnp.int32, (8, nx), 1)
+    if mode == "update":
+        max_ref[...] = jnp.full(max_ref.shape, -jnp.inf, max_ref.dtype)
+
+    def plane(zo, carry):
+        for c in range(py // 8):
+            rows = pl.ds(c * 8, 8)
+            acc = taps_ref[0] * pad_ref[zo, rows, :]
+            for k in range(1, ntap):
+                acc = acc + taps_ref[k] * pad_ref[zo + k, rows, :]
+            zbuf[rows, :] = acc
+        for c in range(ny // 8):
+            acc = taps_ref[ntap] * zbuf[pl.ds(c * 8, 8), :]
+            for k in range(1, ntap):
+                acc = acc + taps_ref[ntap + k] * zbuf[pl.ds(c * 8 + k, 8), :]
+            ybuf[pl.ds(c * 8, 8), :] = acc
+        for c in range(ny // 8):
+            rows = pl.ds(c * 8, 8)
+            v = ybuf[rows, :]
+            acc = None
+            for k in range(ntap):
+                d = k - r
+                if d == 0:
+                    s = v
+                else:
+                    s = pltpu.roll(v, (-d) % nx, 1)
+                    keep = (lanes >= -d) if d < 0 else (lanes < nx - d)
+                    s = jnp.where(keep, s, 0.0)
+                term = taps_ref[2 * ntap + k] * s
+                acc = term if acc is None else acc + term
+            if mode == "ratio":
+                out_ref[zo, rows, :] = other_ref[zo, rows, :] / acc
+            else:
+                upd = other_ref[zo, rows, :] * acc
+                out_ref[zo, rows, :] = upd
+                max_ref[rows, :] = jnp.maximum(max_ref[rows, :], upd)
+        return carry
+
+    lax.fori_loop(0, nz, plane, 0)
+
+
+def fused_blur(mode, taps, padded, other):
+    nz, ny, nx = other.shape
+    vmem = pltpu.VMEM
+    outs = [jax.ShapeDtypeStruct((nz, ny, nx), jnp.float32)]
+    out_specs = [pl.BlockSpec(memory_space=vmem)]
+    if mode == "update":
+        outs.append(jax.ShapeDtypeStruct((ny, nx), jnp.float32))
+        out_specs.append(pl.BlockSpec(memory_space=vmem))
+    elems = nz * ny * nx
+    return pl.pallas_call(
+        functools.partial(blur_kernel, mode),
+        out_shape=tuple(outs),
+        in_specs=[pl.BlockSpec(memory_space=pltpu.SMEM), pl.BlockSpec(memory_space=vmem), pl.BlockSpec(memory_space=vmem)],
+        out_specs=tuple(out_specs),
+        scratch_shapes=[pltpu.VMEM((ny + 8, nx), jnp.float32), pltpu.VMEM((ny, nx), jnp.float32)],
+        compiler_params=pltpu.CompilerParams(vmem_limit_bytes=48 * 1024 * 1024),
+        cost_estimate=pl.CostEstimate(flops=elems * 60, bytes_accessed=elems * 4 * 4, transcendentals=0),
+    )(taps, padded, other)
+
+
 def butterfly_max(value, axis):
     peers = lax.axis_size(axis)
     step = 1
@@ -49,16 +122,12 @@
 
 def per_device(observed, estimate, taps_z, taps_y, taps_x):
     radius = (taps_z.shape[0] - 1) // 2
-    back_z = taps_z[::-1]
-    back_y = taps_y[::-1]
-    back_x = taps_x[::-1]
+    forward = jnp.concatenate([taps_z, taps_y, taps_x])
+    backward = jnp.concatenate([taps_z[::-1], taps_y[::-1], taps_x[::-1]])
     padded = with_halo(estimate, (("gz", 0), ("gy", 1)), radius)
-    blurred = blur_padded(padded, taps_z, taps_y, taps_x)
-    ratio = observed / blurred
+    (ratio,) = fused_blur("ratio", forward, padded, observed)
     ratio_padded = with_halo(ratio, (("gz", 0), ("gy", 1)), radius)
-    correction = blur_padded(ratio_padded, back_z, back_y, back_x)
-    updated = estimate * correction
-    local_max = jnp.max(updated, axis=0)
+    updated, local_max = fused_blur("update", backward, ratio_padded, estimate)
     projection = butterfly_max(local_max, "gz")
     return (updated, projection)
 

time: 166 us -> 145 us (0.87)
  the two profiles are of different devices: /device:TPU:89 before, /device:TPU:160 now
where the time goes in v3:
time: 145 us; the launch traced here: 144 us
  waiting for transfers between devices  47.4 us (33%)
  starting transfers between devices  45.1 us (31%)
  Pallas kernels  37 us (26%)
  other arithmetic  8.63 us (6%)
  local copies, waits for them, and re-layouts  4.64 us (3%)
    pallas_call x2, Pallas kernels, fused_blur(): pl.pallas_call(functools.partial(blur_kernel, mode), out_shape=tuple(outs...  37 us
    ppermute x4, waiting for transfers between devices, with_halo(): before = lax.ppermute(last, axis, up)  26.5 us
    ppermute x4, starting transfers between devices, with_halo(): after = lax.ppermute(first, axis, down)  19.7 us
    ppermute x4, starting transfers between devices, with_halo(): before = lax.ppermute(last, axis, up)  15 us
    ppermute x4, waiting for transfers between devices, with_halo(): after = lax.ppermute(first, axis, down)  12.3 us
    ppermute x3, starting transfers between devices, butterfly_max(): value = jnp.maximum(value, lax.ppermute(value, axis, pairs))  10.5 us
    ppermute x3, waiting for transfers between devices, butterfly_max(): value = jnp.maximum(value, lax.ppermute(value, axis, pairs))  8.61 us
    concatenate x2, other arithmetic, with_halo(): shard = jnp.concatenate([before, shard, after], axis=dim)  6.68 us
  transfers between devices with their start and end apart: 11, of which 9 were waited for; matrix products, arithmetic and copies ran while one was open for 2% of the time, Pallas kernels for 0%

profile of v3, /device:TPU:160, one launch (start us, length us, event | category | flops | bytes accessed | tf_op | source)
XLA Modules:
  0.0 143.6 jit_solution(1201879281783050875)
XLA Ops:
  0.6 1.2 fusion.2
  1.8 3.8 %collective-permute-start = (f32[4,32,768]{2,1,0:T(8,128)S(1)}, f32[4,32,768]{2,1,0:T(8,128)S(1)}, u32[]{:S(2)}, u32[]{:S(2)}) collective-permute-start(f32[4,32,768]{2,1,0:T(8,128)S(1)} %get-tuple-element.13), channel_id=1, source_target_pairs={{0,32},{32,64},{64,96},{96,128},{128,160},{160,192},{192,224},{1,3... | collective-permute-start | bytes 1179656 | tf_op jit(solution)/shard_map/ppermute | solution.py:17
  5.7 2.0 %collective-permute-start.1 = (f32[4,32,768]{2,1,0:T(8,128)S(1)}, f32[4,32,768]{2,1,0:T(8,128)S(1)}, u32[]{:S(2)}, u32[]{:S(2)}) collective-permute-start(f32[4,32,768]{2,1,0:T(8,128)S(1)} %get-tuple-element.12), channel_id=1, source_target_pairs={{32,0},{64,32},{96,64},{128,96},{160,128},{192,160},{224,192},{33,... | collective-permute-start | bytes 1179656 | tf_op jit(solution)/shard_map/ppermute | solution.py:18
  7.7 7.5 %collective-permute-done = f32[4,32,768]{2,1,0:T(8,128)S(1)} collective-permute-done((f32[4,32,768]{2,1,0:T(8,128)S(1)}, f32[4,32,768]{2,1,0:T(8,128)S(1)}, u32[]{:S(2)}, u32[]{:S(2)}) %collective-permute-start) | collective-permute-done | bytes 393248 | tf_op jit(solution)/shard_map/ppermute | solution.py:17
  15.2 0.0 copy-start.2
  15.2 0.0 copy-start.3
  15.2 0.0 copy-start.4
  15.2 2.1 %constant_dynamic-update-slice_fusion.1 = f32[40,32,768]{2,1,0:T(8,128)S(1)} fusion(f32[40,32,768]{2,1,0:T(8,128)S(1)} %constant_dynamic-update-slice_fusion.2, f32[32,32,768]{2,1,0:T(8,128)} %other_ref.3), kind=kLoop, calls=%fused_computation.6 | loop fusion | bytes 6291456
  17.3 6.6 %collective-permute-done.1 = f32[4,32,768]{2,1,0:T(8,128)S(1)} collective-permute-done((f32[4,32,768]{2,1,0:T(8,128)S(1)}, f32[4,32,768]{2,1,0:T(8,128)S(1)}, u32[]{:S(2)}, u32[]{:S(2)}) %collective-permute-start.1) | collective-permute-done | bytes 393248 | tf_op jit(solution)/shard_map/ppermute | solution.py:18
  23.9 0.2 fusion
  24.1 1.9 %collective-permute-start.2 = (f32[40,4,768]{2,1,0:T(4,128)S(1)}, f32[40,4,768]{2,1,0:T(4,128)S(1)}, u32[]{:S(2)}, u32[]{:S(2)}) collective-permute-start(f32[40,4,768]{2,1,0:T(4,128)S(1)} %get-tuple-element.8), channel_id=1, source_target_pairs={{0,1},{1,2},{2,3},{3,4},{4,5},{5,6},{6,7},{7,8},{8,9},{9,10},{10,1... | collective-permute-start | bytes 1474568 | tf_op jit(solution)/shard_map/ppermute | solution.py:17
  26.0 7.9 %collective-permute-start.3 = (f32[40,4,768]{2,1,0:T(4,128)S(1)}, f32[40,4,768]{2,1,0:T(4,128)S(1)}, u32[]{:S(2)}, u32[]{:S(2)}) collective-permute-start(f32[40,4,768]{2,1,0:T(4,128)S(1)} %get-tuple-element.9), channel_id=1, source_target_pairs={{1,0},{2,1},{3,2},{4,3},{5,4},{6,5},{7,6},{8,7},{9,8},{10,9},{11,1... | collective-permute-start | bytes 1474568 | tf_op jit(solution)/shard_map/ppermute | solution.py:18
  33.9 0.0 copy-done.2
  33.9 0.0 copy-done.3
  33.9 0.0 copy-done.4
  33.9 0.1 pad_maximum_fusion.6.taps_ref
  34.0 7.9 %collective-permute-done.2 = f32[40,4,768]{2,1,0:T(4,128)S(1)} collective-permute-done((f32[40,4,768]{2,1,0:T(4,128)S(1)}, f32[40,4,768]{2,1,0:T(4,128)S(1)}, u32[]{:S(2)}, u32[]{:S(2)}) %collective-permute-start.2) | collective-permute-done | bytes 491552 | tf_op jit(solution)/shard_map/ppermute | solution.py:17
  41.9 0.0 collective-permute-done.3
  41.9 2.8 %pad_maximum_fusion.pad_ref = f32[40,40,768]{2,1,0:T(8,128)} fusion(f32[40,4,768]{2,1,0:T(4,128)S(1)} %collective-permute-done.3, f32[40,32,768]{2,1,0:T(8,128)S(1)} %constant_dynamic-update-slice_fusion, f32[40,4,768]{2,1,0:T(4,128)S(1)} %collective-permute-done.2), kind=kLoop, calls=%fused_computation | loop fusion | flops 2457600 | bytes 9830400 | tf_op jit(solution)/shard_map/concatenate | solution.py:19
  44.7 18.2 %shard_map.68 = f32[32,32,768]{2,1,0:T(8,128)S(1)} custom-call(f32[27]{0:T(128)S(1)} %pad_maximum_fusion.6.taps_ref, f32[40,40,768]{2,1,0:T(8,128)} %pad_maximum_fusion.pad_ref, f32[32,32,768]{2,1,0:T(8,128)} %other_ref.2), custom_call_target="tpu_custom_call" | custom-call | flops 47185920 | bytes 12582912 | tf_op jit(solution)/shard_map/pallas_call | solution.py:102
  62.9 0.1 fusion.1
  63.0 7.3 %collective-permute-start.4 = (f32[4,32,768]{2,1,0:T(8,128)S(1)}, f32[4,32,768]{2,1,0:T(8,128)S(1)}, u32[]{:S(2)}, u32[]{:S(2)}) collective-permute-start(f32[4,32,768]{2,1,0:T(8,128)S(1)} %get-tuple-element.10), channel_id=1, source_target_pairs={{0,32},{32,64},{64,96},{96,128},{128,160},{160,192},{192,224},{1,3... | collective-permute-start | bytes 1179656 | tf_op jit(solution)/shard_map/ppermute | solution.py:17
  70.3 1.9 %collective-permute-start.5 = (f32[4,32,768]{2,1,0:T(8,128)S(1)}, f32[4,32,768]{2,1,0:T(8,128)S(1)}, u32[]{:S(2)}, u32[]{:S(2)}) collective-permute-start(f32[4,32,768]{2,1,0:T(8,128)S(1)} %get-tuple-element.11), channel_id=1, source_target_pairs={{32,0},{64,32},{96,64},{128,96},{160,128},{192,160},{224,192},{33,... | collective-permute-start | bytes 1179656 | tf_op jit(solution)/shard_map/ppermute | solution.py:18
  72.2 3.6 %collective-permute-done.4 = f32[4,32,768]{2,1,0:T(8,128)S(1)} collective-permute-done((f32[4,32,768]{2,1,0:T(8,128)S(1)}, f32[4,32,768]{2,1,0:T(8,128)S(1)}, u32[]{:S(2)}, u32[]{:S(2)}) %collective-permute-start.4) | collective-permute-done | bytes 393248 | tf_op jit(solution)/shard_map/ppermute | solution.py:17
  75.8 5.7 %collective-permute-done.5 = f32[4,32,768]{2,1,0:T(8,128)S(1)} collective-permute-done((f32[4,32,768]{2,1,0:T(8,128)S(1)}, f32[4,32,768]{2,1,0:T(8,128)S(1)}, u32[]{:S(2)}, u32[]{:S(2)}) %collective-permute-start.5) | collective-permute-done | bytes 393248 | tf_op jit(solution)/shard_map/ppermute | solution.py:18
  81.5 0.0 copy-start.1
  81.5 0.8 copy-done.1
  82.3 1.1 pad_maximum_fusion.4
  83.4 1.9 %collective-permute-start.6 = (f32[40,4,768]{2,1,0:T(4,128)}, f32[40,4,768]{2,1,0:T(4,128)}, u32[]{:S(2)}, u32[]{:S(2)}) collective-permute-start(f32[40,4,768]{2,1,0:T(4,128)} %get-tuple-element.6), channel_id=1, source_target_pairs={{0,1},{1,2},{2,3},{3,4},{4,5},{5,6},{6,7},{7,8},{8,9},{9,10},{10,1... | collective-permute-start | bytes 1474568 | tf_op jit(solution)/shard_map/ppermute | solution.py:17
  85.3 7.9 %collective-permute-start.7 = (f32[40,4,768]{2,1,0:T(4,128)}, f32[40,4,768]{2,1,0:T(4,128)}, u32[]{:S(2)}, u32[]{:S(2)}) collective-permute-start(f32[40,4,768]{2,1,0:T(4,128)} %get-tuple-element.7), channel_id=1, source_target_pairs={{1,0},{2,1},{3,2},{4,3},{5,4},{6,5},{7,6},{8,7},{9,8},{10,9},{11,1... | collective-permute-start | bytes 1474568 | tf_op jit(solution)/shard_map/ppermute | solution.py:18
  93.2 0.1 rev.10
  93.3 0.1 rev.11
  93.4 0.1 rev.9
  93.5 0.1 pad_maximum_fusion.5.taps_ref
  93.6 0.0 copy-start
  93.6 7.6 %collective-permute-done.6 = f32[40,4,768]{2,1,0:T(4,128)} collective-permute-done((f32[40,4,768]{2,1,0:T(4,128)}, f32[40,4,768]{2,1,0:T(4,128)}, u32[]{:S(2)}, u32[]{:S(2)}) %collective-permute-start.6) | collective-permute-done | bytes 491552 | tf_op jit(solution)/shard_map/ppermute | solution.py:17
  101.2 0.0 collective-permute-done.7
  101.2 3.9 %pad_maximum_fusion.1.pad_ref = f32[40,40,768]{2,1,0:T(8,128)} fusion(f32[40,4,768]{2,1,0:T(4,128)} %collective-permute-done.7, f32[4,32,768]{2,1,0:T(8,128)} %copy-done.1, f32[32,32,768]{2,1,0:T(8,128)S(1)} %shard_map.68, f32[4,32,768]{2,1,0:T(8,128)S(1)} %collective-permute-done.4, f32[40,4,768]{2,1,0:T(4,128)} %collective-permute-done.6), kind=kLoop, calls=%fused_computation.1 | loop fusion | flops 4915200 | bytes 9830400 | tf_op jit(solution)/shard_map/concatenate | solution.py:19
  105.0 0.0 copy-done
  105.0 18.8 %shard_map.69 = (f32[32,32,768]{2,1,0:T(8,128)}, f32[32,768]{1,0:T(8,128)S(1)}) custom-call(f32[27]{0:T(128)S(1)} %pad_maximum_fusion.5.taps_ref, f32[40,40,768]{2,1,0:T(8,128)} %pad_maximum_fusion.1.pad_ref, f32[32,32,768]{2,1,0:T(8,128)S(1)} %copy-done), custom_call_target="tpu_custom_call" | custom-call | flops 47185920 | bytes 12582912 | tf_op jit(solution)/shard_map/pallas_call | solution.py:102
  123.9 4.9 %collective-permute-start.8 = (f32[32,768]{1,0:T(8,128)S(1)}, f32[32,768]{1,0:T(8,128)S(1)}, u32[]{:S(2)}, u32[]{:S(2)}) collective-permute-start(f32[32,768]{1,0:T(8,128)S(1)} %get-tuple-element.5), channel_id=1, source_target_pairs={{0,32},{32,0},{64,96},{96,64},{128,160},{160,128},{192,224},{224,1... | collective-permute-start | bytes 294920 | tf_op jit(solution)/shard_map/ppermute | solution.py:118
  128.8 2.6 %collective-permute-done.8 = f32[32,768]{1,0:T(8,128)S(1)} collective-permute-done((f32[32,768]{1,0:T(8,128)S(1)}, f32[32,768]{1,0:T(8,128)S(1)}, u32[]{:S(2)}, u32[]{:S(2)}) %collective-permute-start.8) | collective-permute-done | bytes 98336 | tf_op jit(solution)/shard_map/ppermute | solution.py:118
  131.4 1.3 collective-permute-start.9
  132.7 3.4 %collective-permute-done.9 = f32[32,768]{1,0:T(8,128)S(1)} collective-permute-done((f32[32,768]{1,0:T(8,128)S(1)}, f32[32,768]{1,0:T(8,128)S(1)}, u32[]{:S(2)}, u32[]{:S(2)}) %collective-permute-start.9) | collective-permute-done | bytes 98336 | tf_op jit(solution)/shard_map/ppermute | solution.py:118
  136.1 4.3 %collective-permute-start.10 = (f32[32,768]{1,0:T(8,128)S(1)}, f32[32,768]{1,0:T(8,128)S(1)}, u32[]{:S(2)}, u32[]{:S(2)}) collective-permute-start(f32[32,768]{1,0:T(8,128)S(1)} %max.10), channel_id=1, source_target_pairs={{0,128},{32,160},{64,192},{96,224},{128,0},{160,32},{192,64},{224,... | collective-permute-start | bytes 294920 | tf_op jit(solution)/shard_map/ppermute | solution.py:118
  140.4 2.6 %collective-permute-done.10 = f32[32,768]{1,0:T(8,128)S(1)} collective-permute-done((f32[32,768]{1,0:T(8,128)S(1)}, f32[32,768]{1,0:T(8,128)S(1)}, u32[]{:S(2)}, u32[]{:S(2)}) %collective-permute-start.10) | collective-permute-done | bytes 98336 | tf_op jit(solution)/shard_map/ppermute | solution.py:118
  143.0 0.7 max.11
  (4 shorter events, 0.1 us)
Async XLA Ops:
  1.8 13.3 %collective-permute-start = (f32[4,32,768]{2,1,0:T(8,128)S(1)}, f32[4,32,768]{2,1,0:T(8,128)S(1)}, u32[]{:S(2)}, u32[]{:S(2)}) collective-permute-start(f32[4,32,768]{2,1,0:T(8,128)S(1)} %get-tuple-element.13), channel_id=1, source_target_pairs={{0,32},{32,64},{64,96},{96,128},{128,160},{160,192},{192,224},{1,3... | collective-permute-start | bytes 1179656 | tf_op jit(solution)/shard_map/ppermute | solution.py:17
  5.7 18.3 %collective-permute-start.1 = (f32[4,32,768]{2,1,0:T(8,128)S(1)}, f32[4,32,768]{2,1,0:T(8,128)S(1)}, u32[]{:S(2)}, u32[]{:S(2)}) collective-permute-start(f32[4,32,768]{2,1,0:T(8,128)S(1)} %get-tuple-element.12), channel_id=1, source_target_pairs={{32,0},{64,32},{96,64},{128,96},{160,128},{192,160},{224,192},{33,... | collective-permute-start | bytes 1179656 | tf_op jit(solution)/shard_map/ppermute | solution.py:18
  15.2 18.8 %copy-start.2 = (f32[9]{0:T(128)S(1)}, f32[9]{0:T(128)}, u32[]{:S(2)}) copy-start(f32[9]{0:T(128)} %param.8) | copy-start | bytes 112
  15.2 18.7 %copy-start.3 = (f32[9]{0:T(128)S(1)}, f32[9]{0:T(128)}, u32[]{:S(2)}) copy-start(f32[9]{0:T(128)} %param.9) | copy-start | bytes 112
  15.2 18.7 %copy-start.4 = (f32[9]{0:T(128)S(1)}, f32[9]{0:T(128)}, u32[]{:S(2)}) copy-start(f32[9]{0:T(128)} %param.7) | copy-start | bytes 112
  24.1 17.8 %collective-permute-start.2 = (f32[40,4,768]{2,1,0:T(4,128)S(1)}, f32[40,4,768]{2,1,0:T(4,128)S(1)}, u32[]{:S(2)}, u32[]{:S(2)}) collective-permute-start(f32[40,4,768]{2,1,0:T(4,128)S(1)} %get-tuple-element.8), channel_id=1, source_target_pairs={{0,1},{1,2},{2,3},{3,4},{4,5},{5,6},{6,7},{7,8},{8,9},{9,10},{10,1... | collective-permute-start | bytes 1474568 | tf_op jit(solution)/shard_map/ppermute | solution.py:17
  26.0 15.8 %collective-permute-start.3 = (f32[40,4,768]{2,1,0:T(4,128)S(1)}, f32[40,4,768]{2,1,0:T(4,128)S(1)}, u32[]{:S(2)}, u32[]{:S(2)}) collective-permute-start(f32[40,4,768]{2,1,0:T(4,128)S(1)} %get-tuple-element.9), channel_id=1, source_target_pairs={{1,0},{2,1},{3,2},{4,3},{5,4},{6,5},{7,6},{8,7},{9,8},{10,9},{11,1... | collective-permute-start | bytes 1474568 | tf_op jit(solution)/shard_map/ppermute | solution.py:18
  63.0 12.9 %collective-permute-start.4 = (f32[4,32,768]{2,1,0:T(8,128)S(1)}, f32[4,32,768]{2,1,0:T(8,128)S(1)}, u32[]{:S(2)}, u32[]{:S(2)}) collective-permute-start(f32[4,32,768]{2,1,0:T(8,128)S(1)} %get-tuple-element.10), channel_id=1, source_target_pairs={{0,32},{32,64},{64,96},{96,128},{128,160},{160,192},{192,224},{1,3... | collective-permute-start | bytes 1179656 | tf_op jit(solution)/shard_map/ppermute | solution.py:17
  70.3 11.2 %collective-permute-start.5 = (f32[4,32,768]{2,1,0:T(8,128)S(1)}, f32[4,32,768]{2,1,0:T(8,128)S(1)}, u32[]{:S(2)}, u32[]{:S(2)}) collective-permute-start(f32[4,32,768]{2,1,0:T(8,128)S(1)} %get-tuple-element.11), channel_id=1, source_target_pairs={{32,0},{64,32},{96,64},{128,96},{160,128},{192,160},{224,192},{33,... | collective-permute-start | bytes 1179656 | tf_op jit(solution)/shard_map/ppermute | solution.py:18
  81.5 0.8 copy-start.1
  83.4 17.8 %collective-permute-start.6 = (f32[40,4,768]{2,1,0:T(4,128)}, f32[40,4,768]{2,1,0:T(4,128)}, u32[]{:S(2)}, u32[]{:S(2)}) collective-permute-start(f32[40,4,768]{2,1,0:T(4,128)} %get-tuple-element.6), channel_id=1, source_target_pairs={{0,1},{1,2},{2,3},{3,4},{4,5},{5,6},{6,7},{7,8},{8,9},{9,10},{10,1... | collective-permute-start | bytes 1474568 | tf_op jit(solution)/shard_map/ppermute | solution.py:17
  85.3 15.9 %collective-permute-start.7 = (f32[40,4,768]{2,1,0:T(4,128)}, f32[40,4,768]{2,1,0:T(4,128)}, u32[]{:S(2)}, u32[]{:S(2)}) collective-permute-start(f32[40,4,768]{2,1,0:T(4,128)} %get-tuple-element.7), channel_id=1, source_target_pairs={{1,0},{2,1},{3,2},{4,3},{5,4},{6,5},{7,6},{8,7},{9,8},{10,9},{11,1... | collective-permute-start | bytes 1474568 | tf_op jit(solution)/shard_map/ppermute | solution.py:18
  93.6 11.5 %copy-start = (f32[32,32,768]{2,1,0:T(8,128)S(1)}, f32[32,32,768]{2,1,0:T(8,128)}, u32[]{:S(2)}) copy-start(f32[32,32,768]{2,1,0:T(8,128)} %other_ref.3) | copy-start | bytes 9437188
  123.9 7.5 %collective-permute-start.8 = (f32[32,768]{1,0:T(8,128)S(1)}, f32[32,768]{1,0:T(8,128)S(1)}, u32[]{:S(2)}, u32[]{:S(2)}) collective-permute-start(f32[32,768]{1,0:T(8,128)S(1)} %get-tuple-element.5), channel_id=1, source_target_pairs={{0,32},{32,0},{64,96},{96,64},{128,160},{160,128},{192,224},{224,1... | collective-permute-start | bytes 294920 | tf_op jit(solution)/shard_map/ppermute | solution.py:118
  131.4 4.7 %collective-permute-start.9 = (f32[32,768]{1,0:T(8,128)S(1)}, f32[32,768]{1,0:T(8,128)S(1)}, u32[]{:S(2)}, u32[]{:S(2)}) collective-permute-start(f32[32,768]{1,0:T(8,128)S(1)} %max.9), channel_id=1, source_target_pairs={{0,64},{32,96},{64,0},{96,32},{128,192},{160,224},{192,128},{224,1... | collective-permute-start | bytes 294920 | tf_op jit(solution)/shard_map/ppermute | solution.py:118
  136.1 6.9 %collective-permute-start.10 = (f32[32,768]{1,0:T(8,128)S(1)}, f32[32,768]{1,0:T(8,128)S(1)}, u32[]{:S(2)}, u32[]{:S(2)}) collective-permute-start(f32[32,768]{1,0:T(8,128)S(1)} %max.10), channel_id=1, source_target_pairs={{0,128},{32,160},{64,192},{96,224},{128,0},{160,32},{192,64},{224,... | collective-permute-start | bytes 294920 | tf_op jit(solution)/shard_map/ppermute | solution.py:118

commit v4 on v3

v4 whole, which is shorter than its diff:
```python
import jax
import jax.numpy as jnp
from jax import lax
from jax.sharding import PartitionSpec as P
import functools
from jax.experimental import pallas as pl
from jax.experimental.pallas import tpu as pltpu


def blur_kernel(mode, segments, taps_ref, pad_ref, other_ref, out_ref, *rest):
    if mode == "update":
        max_ref, zbuf, ybuf = rest
    else:
        zbuf, ybuf = rest
    ntap = 9
    r = 4
    ny, nx = out_ref.shape[1], out_ref.shape[2]
    py = ny + 2 * r
    lanes = lax.broadcasted_iota(jnp.int32, (8, nx), 1)
    if mode == "update":
        max_ref[...] = jnp.full(max_ref.shape, -jnp.inf, max_ref.dtype)

    def plane(zo, zs, zt):
        for c in range(py // 8):
            rows = pl.ds(c * 8, 8)
            acc = taps_ref[0] * pad_ref[zs, rows, :]
            for k in range(1, ntap):
                acc = acc + taps_ref[k] * pad_ref[zs + k, rows, :]
            zbuf[rows, :] = acc
        for c in range(ny // 8):
            acc = taps_ref[ntap] * zbuf[pl.ds(c * 8, 8), :]
            for k in range(1, ntap):
                acc = acc + taps_ref[ntap + k] * zbuf[pl.ds(c * 8 + k, 8), :]
            ybuf[pl.ds(c * 8, 8), :] = acc
        for c in range(ny // 8):
            rows = pl.ds(c * 8, 8)
            v = ybuf[rows, :]
            acc = None
            for k in range(ntap):
                d = k - r
                if d == 0:
                    s = v
                else:
                    s = pltpu.roll(v, (-d) % nx, 1)
                    keep = (lanes >= -d) if d < 0 else (lanes < nx - d)
                    s = jnp.where(keep, s, 0.0)
                term = taps_ref[2 * ntap + k] * s
                acc = term if acc is None else acc + term
            if mode == "ratio":
                out_ref[zo, rows, :] = other_ref[zt, rows, :] / acc
            else:
                upd = other_ref[zt, rows, :] * acc
                out_ref[zo, rows, :] = upd
                max_ref[rows, :] = jnp.maximum(max_ref[rows, :], upd)

    for out_start, count, src_start, other_start in segments:
        def body(j, carry, out_start=out_start, src_start=src_start, other_start=other_start):
            plane(out_start + j, src_start + j, other_start + j)
            return carry

        lax.fori_loop(0, count, body, 0)


def fused_blur(mode, segments, taps, padded, other):
    nzo = sum(seg[1] for seg in segments)
    ny, nx = other.shape[1], other.shape[2]
    vmem = pltpu.VMEM
    outs = [jax.ShapeDtypeStruct((nzo, ny, nx), jnp.float32)]
    out_specs = [pl.BlockSpec(memory_space=vmem)]
    if mode == "update":
        outs.append(jax.ShapeDtypeStruct((ny, nx), jnp.float32))
        out_specs.append(pl.BlockSpec(memory_space=vmem))
    elems = nzo * ny * nx
    return pl.pallas_call(
        functools.partial(blur_kernel, mode, tuple(segments)),
        out_shape=tuple(outs),
        in_specs=[pl.BlockSpec(memory_space=pltpu.SMEM), pl.BlockSpec(memory_space=vmem), pl.BlockSpec(memory_space=vmem)],
        out_specs=tuple(out_specs),
        scratch_shapes=[pltpu.VMEM((ny + 8, nx), jnp.float32), pltpu.VMEM((ny, nx), jnp.float32)],
        compiler_params=pltpu.CompilerParams(vmem_limit_bytes=48 * 1024 * 1024),
        cost_estimate=pl.CostEstimate(flops=elems * 60, bytes_accessed=elems * 4 * 4, transcendentals=0),
    )(taps, padded, other)


def halo_pair(shard, axis, dim, width):
    peers, length = (lax.axis_size(axis), shard.shape[dim])
    up = [(i, (i + 1) % peers) for i in range(peers - 1)]
    down = [(j, i) for i, j in up]
    last = lax.slice_in_dim(shard, length - width, length, axis=dim)
    first = lax.slice_in_dim(shard, 0, width, axis=dim)
    before = lax.ppermute(last, axis, up)
    after = lax.ppermute(first, axis, down)
    return before, after


def split_blur(mode, taps, shard, other, width):
    nz = shard.shape[0]
    before, after = halo_pair(shard, "gy", 1, width)
    rows_padded = jnp.concatenate([before, shard, after], axis=1)
    below, above = halo_pair(rows_padded, "gz", 0, width)
    inner = fused_blur(mode, [(0, nz - 2 * width, 0, width)], taps, rows_padded, other)
    slabs = jnp.concatenate([below, rows_padded[: 2 * width], rows_padded[nz - 2 * width :], above], axis=0)
    edges = fused_blur(mode, [(0, width, 0, 0), (width, width, 3 * width, nz - width)], taps, slabs, other)
    volume = jnp.concatenate([edges[0][:width], inner[0], edges[0][width:]], axis=0)
    if mode == "update":
        return volume, jnp.maximum(inner[1], edges[1])
    return volume


def butterfly_max(value, axis):
    peers = lax.axis_size(axis)
    step = 1
    while step < peers:
        pairs = [(i, i ^ step) for i in range(peers)]
        value = jnp.maximum(value, lax.ppermute(value, axis, pairs))
        step *= 2
    return value


def per_device(observed, estimate, taps_z, taps_y, taps_x):
    radius = (taps_z.shape[0] - 1) // 2
    forward = jnp.concatenate([taps_z, taps_y, taps_x])
    backward = jnp.concatenate([taps_z[::-1], taps_y[::-1], taps_x[::-1]])
    ratio = split_blur("ratio", forward, estimate, observed, radius)
    updated, local_max = split_blur("update", backward, ratio, estimate, radius)
    projection = butterfly_max(local_max, "gz")
    return (updated, projection)


def solution(mesh):
    return jax.shard_map(
        per_device,
        mesh=mesh,
        in_specs=(P("gz", "gy", None), P("gz", "gy", None), P(), P(), P()),
        out_specs=(P("gz", "gy", None), P("gy", None)),
        check_vma=False,
    )
```

time: 145 us -> 120 us (0.83)
  waiting for transfers between devices: 47.4 us -> 24.7 us
  starting transfers between devices: 45.1 us -> 40.5 us
  local copies, waits for them, and re-layouts: 4.64 us -> 6.7 us
    ppermute x8, waiting for transfers between devices: 38.8 us -> 15.3 us  [the longest x4 13 us: halo_pair(): before = lax.ppermute(last, axis, up)]
    ppermute x3, starting transfers between devices: 10.5 us -> 4.09 us  [butterfly_max(): value = jnp.maximum(value, lax.ppermute(value, axis, pairs))]
    slice x3 -> x7, local copies, waits for them, and re-layouts: 1.39 us -> 4.51 us  [the longest x3 2.61 us: halo_pair(): last = lax.slice_in_dim(shard, length - width, length, axis=dim)]
    ppermute x8, starting transfers between devices: 34.7 us -> 36.4 us  [the longest x4 21.3 us: halo_pair(): after = lax.ppermute(first, axis, down)]
    unnamed x12 -> x16, local copies, waits for them, and re-layouts: 2.93 us -> 1.9 us
    pallas_call x2 -> x4, Pallas kernels: 37 us -> 37.8 us  [fused_blur(): pl.pallas_call(functools.partial(blur_kernel, mode, tuple(segments)), out...]
    concatenate x2 -> x5, other arithmetic: 6.68 us -> 6.41 us  [the longest x2 2.84 us: split_blur(): rows_padded = jnp.concatenate([before, shard, after], axis=1)]
  transfers between devices with their start and end apart: 11 -> 11, of which waited for: 9 -> 6; matrix products, arithmetic and copies ran while one was open for 2% -> 4% of each run, Pallas kernels for 0% -> 22%
where the time goes in v4:
time: 120 us; the launch traced here: 118 us
  starting transfers between devices  40.5 us (34%)
  Pallas kernels  37.8 us (31%)
  waiting for transfers between devices  24.7 us (21%)
  other arithmetic  7.4 us (6%)
  local copies, waits for them, and re-layouts  6.7 us (6%)
    pallas_call x4, Pallas kernels, fused_blur(): pl.pallas_call(functools.partial(blur_kernel, mode, tuple(segments)), out...  37.8 us
    ppermute x4, starting transfers between devices, halo_pair(): after = lax.ppermute(first, axis, down)  21.3 us
    ppermute x4, starting transfers between devices, halo_pair(): before = lax.ppermute(last, axis, up)  15.1 us
    ppermute x4, waiting for transfers between devices, halo_pair(): before = lax.ppermute(last, axis, up)  13 us
    ppermute x3, waiting for transfers between devices, butterfly_max(): value = jnp.maximum(value, lax.ppermute(value, axis, pairs))  9.45 us
    ppermute x3, starting transfers between devices, butterfly_max(): value = jnp.maximum(value, lax.ppermute(value, axis, pairs))  4.09 us
    concatenate x2, other arithmetic, split_blur(): rows_padded = jnp.concatenate([before, shard, after], axis=1)  2.84 us
    slice x3, local copies, waits for them, and re-layouts, halo_pair(): last = lax.slice_in_dim(shard, length - width, length, axis=dim)  2.61 us
  transfers between devices with their start and end apart: 11, of which 6 were waited for; matrix products, arithmetic and copies ran while one was open for 4% of the time, Pallas kernels for 22%

profile of v4, /device:TPU:160, one launch (start us, length us, event | category | flops | bytes accessed | tf_op | source)
XLA Modules:
  0.0 118.0 jit_solution(15173839539896312720)
XLA Ops:
  0.6 1.5 %fusion.4 = (f32[32,4,768]{2,1,0:T(4,128)S(1)}, f32[32,4,768]{2,1,0:T(4,128)S(1)}) fusion(f32[32,32,768]{2,1,0:T(8,128)} %other_ref.7), kind=kLoop, calls=%fused_computation.14 | loop fusion | bytes 1572864 | tf_op jit(solution)/shard_map/slice | solution.py:89
  2.1 1.9 %collective-permute-start = (f32[32,4,768]{2,1,0:T(4,128)S(1)}, f32[32,4,768]{2,1,0:T(4,128)S(1)}, u32[]{:S(2)}, u32[]{:S(2)}) collective-permute-start(f32[32,4,768]{2,1,0:T(4,128)S(1)} %get-tuple-element.20), channel_id=1, source_target_pairs={{0,1},{1,2},{2,3},{3,4},{4,5},{5,6},{6,7},{7,8},{8,9},{9,10},{10,1... | collective-permute-start | bytes 1179656 | tf_op jit(solution)/shard_map/ppermute | solution.py:91
  4.1 0.0 copy-start.5
  4.1 0.0 copy-start.6
  4.1 0.0 copy-start.7
  4.1 0.0 copy-start.1
  4.1 8.1 %collective-permute-start.1 = (f32[32,4,768]{2,1,0:T(4,128)S(1)}, f32[32,4,768]{2,1,0:T(4,128)S(1)}, u32[]{:S(2)}, u32[]{:S(2)}) collective-permute-start(f32[32,4,768]{2,1,0:T(4,128)S(1)} %get-tuple-element.21), channel_id=1, source_target_pairs={{1,0},{2,1},{3,2},{4,3},{5,4},{6,5},{7,6},{8,7},{9,8},{10,9},{11,1... | collective-permute-start | bytes 1179656 | tf_op jit(solution)/shard_map/ppermute | solution.py:92
  12.3 5.6 %collective-permute-done = f32[32,4,768]{2,1,0:T(4,128)S(1)} collective-permute-done((f32[32,4,768]{2,1,0:T(4,128)S(1)}, f32[32,4,768]{2,1,0:T(4,128)S(1)}, u32[]{:S(2)}, u32[]{:S(2)}) %collective-permute-start) | collective-permute-done | bytes 393248 | tf_op jit(solution)/shard_map/ppermute | solution.py:91
  17.8 0.0 collective-permute-done.1
  17.8 2.3 %pad_maximum_fusion.pad_ref = f32[32,40,768]{2,1,0:T(8,128)S(1)} fusion(f32[32,4,768]{2,1,0:T(4,128)S(1)} %collective-permute-done.1, f32[32,32,768]{2,1,0:T(8,128)} %other_ref.7, f32[32,4,768]{2,1,0:T(4,128)S(1)} %collective-permute-done), kind=kLoop, calls=%fused_computation | loop fusion | flops 1966080 | bytes 7864320 | tf_op jit(solution)/shard_map/concatenate | solution.py:99
  20.1 0.0 copy-start.4
  20.1 0.1 fusion.2
  20.2 7.8 %collective-permute-start.2 = (f32[4,40,768]{2,1,0:T(8,128)S(1)}, f32[4,40,768]{2,1,0:T(8,128)S(1)}, u32[]{:S(2)}, u32[]{:S(2)}) collective-permute-start(f32[4,40,768]{2,1,0:T(8,128)S(1)} %get-tuple-element.14), channel_id=1, source_target_pairs={{0,32},{32,64},{64,96},{96,128},{128,160},{160,192},{192,224},{1,3... | collective-permute-start | bytes 1474568 | tf_op jit(solution)/shard_map/ppermute | solution.py:91
  28.0 1.9 %collective-permute-start.3 = (f32[4,40,768]{2,1,0:T(8,128)S(1)}, f32[4,40,768]{2,1,0:T(8,128)S(1)}, u32[]{:S(2)}, u32[]{:S(2)}) collective-permute-start(f32[4,40,768]{2,1,0:T(8,128)S(1)} %get-tuple-element.15), channel_id=1, source_target_pairs={{32,0},{64,32},{96,64},{128,96},{160,128},{192,160},{224,192},{33,... | collective-permute-start | bytes 1474568 | tf_op jit(solution)/shard_map/ppermute | solution.py:92
  29.9 0.0 copy-done.5
  29.9 0.0 copy-done.6
  30.0 0.0 copy-done.7
  30.0 0.1 pad_maximum_fusion.9.taps_ref
  30.0 0.0 copy-done.4
  30.0 0.0 copy-done.1
  30.1 13.2 %shard_map.69 = f32[24,32,768]{2,1,0:T(8,128)S(1)} custom-call(f32[27]{0:T(128)S(1)} %pad_maximum_fusion.9.taps_ref, f32[32,40,768]{2,1,0:T(8,128)} %copy-done.4, f32[32,32,768]{2,1,0:T(8,128)S(1)} %copy-done.1), custom_call_target="tpu_custom_call" | custom-call | flops 35389440 | bytes 9437184 | tf_op jit(solution)/shard_map/pallas_call | solution.py:74
  43.2 1.6 %fusion.3 = (f32[8,40,768]{2,1,0:T(8,128)S(1)}, f32[8,40,768]{2,1,0:T(8,128)S(1)}) fusion(f32[32,40,768]{2,1,0:T(8,128)} %copy-done.4), kind=kLoop, calls=%fused_computation.13 | loop fusion | bytes 3932160 | tf_op jit(solution)/shard_map/slice | solution.py:102
  44.9 0.0 collective-permute-done.2
  44.9 0.0 collective-permute-done.3
  44.9 0.2 pad_maximum_fusion.3.pad_ref
  45.1 5.6 %shard_map.68 = f32[8,32,768]{2,1,0:T(8,128)S(1)} custom-call(f32[27]{0:T(128)S(1)} %pad_maximum_fusion.9.taps_ref, f32[24,40,768]{2,1,0:T(8,128)S(1)} %pad_maximum_fusion.3.pad_ref, f32[32,32,768]{2,1,0:T(8,128)} %other_ref.5), custom_call_target="tpu_custom_call" | custom-call | flops 11796480 | bytes 3145728 | tf_op jit(solution)/shard_map/pallas_call | solution.py:74
  50.7 0.1 fusion.6
  50.8 0.1 pad_maximum_fusion.7
  50.9 1.9 %collective-permute-start.4 = (f32[32,4,768]{2,1,0:T(4,128)S(1)}, f32[32,4,768]{2,1,0:T(4,128)S(1)}, u32[]{:S(2)}, u32[]{:S(2)}) collective-permute-start(f32[32,4,768]{2,1,0:T(4,128)S(1)} %get-tuple-element.18), channel_id=1, source_target_pairs={{0,1},{1,2},{2,3},{3,4},{4,5},{5,6},{6,7},{7,8},{8,9},{9,10},{10,1... | collective-permute-start | bytes 1179656 | tf_op jit(solution)/shard_map/ppermute | solution.py:91
  52.9 0.0 copy-start
  52.9 8.1 %collective-permute-start.5 = (f32[32,4,768]{2,1,0:T(4,128)S(1)}, f32[32,4,768]{2,1,0:T(4,128)S(1)}, u32[]{:S(2)}, u32[]{:S(2)}) collective-permute-start(f32[32,4,768]{2,1,0:T(4,128)S(1)} %get-tuple-element.19), channel_id=1, source_target_pairs={{1,0},{2,1},{3,2},{4,3},{5,4},{6,5},{7,6},{8,7},{9,8},{10,9},{11,1... | collective-permute-start | bytes 1179656 | tf_op jit(solution)/shard_map/ppermute | solution.py:92
  61.0 7.4 %collective-permute-done.4 = f32[32,4,768]{2,1,0:T(4,128)S(1)} collective-permute-done((f32[32,4,768]{2,1,0:T(4,128)S(1)}, f32[32,4,768]{2,1,0:T(4,128)S(1)}, u32[]{:S(2)}, u32[]{:S(2)}) %collective-permute-start.4) | collective-permute-done | bytes 393248 | tf_op jit(solution)/shard_map/ppermute | solution.py:91
  68.5 2.2 %collective-permute-done.5 = f32[32,4,768]{2,1,0:T(4,128)S(1)} collective-permute-done((f32[32,4,768]{2,1,0:T(4,128)S(1)}, f32[32,4,768]{2,1,0:T(4,128)S(1)}, u32[]{:S(2)}, u32[]{:S(2)}) %collective-permute-start.5) | collective-permute-done | bytes 393248 | tf_op jit(solution)/shard_map/ppermute | solution.py:92
  70.7 0.5 pad_maximum_fusion.1.pad_ref
  71.2 0.0 copy-start.2
  71.2 1.9 %copy-done.2 = f32[32,40,768]{2,1,0:T(8,128)} copy-done((f32[32,40,768]{2,1,0:T(8,128)}, f32[32,40,768]{2,1,0:T(8,128)S(1)}, u32[]{:S(2)}) %copy-start.2) | copy-done | bytes 3932184
  73.1 1.0 fusion
  74.1 3.4 %collective-permute-start.6 = (f32[4,40,768]{2,1,0:T(8,128)}, f32[4,40,768]{2,1,0:T(8,128)}, u32[]{:S(2)}, u32[]{:S(2)}) collective-permute-start(f32[4,40,768]{2,1,0:T(8,128)} %get-tuple-element.10), channel_id=1, source_target_pairs={{0,32},{32,64},{64,96},{96,128},{128,160},{160,192},{192,224},{1,3... | collective-permute-start | bytes 1474568 | tf_op jit(solution)/shard_map/ppermute | solution.py:91
  77.6 3.2 %collective-permute-start.7 = (f32[4,40,768]{2,1,0:T(8,128)}, f32[4,40,768]{2,1,0:T(8,128)}, u32[]{:S(2)}, u32[]{:S(2)}) collective-permute-start(f32[4,40,768]{2,1,0:T(8,128)} %get-tuple-element.11), channel_id=1, source_target_pairs={{32,0},{64,32},{96,64},{128,96},{160,128},{192,160},{224,192},{33,... | collective-permute-start | bytes 1474568 | tf_op jit(solution)/shard_map/ppermute | solution.py:92
  80.8 0.1 rev.9
  80.9 0.1 rev.10
  81.0 0.1 rev.11
  81.1 0.1 pad_maximum_fusion.8.taps_ref
  81.1 0.0 copy-done
  81.1 0.0 copy-start.3
  81.1 13.3 %shard_map.71 = (f32[24,32,768]{2,1,0:T(8,128)S(1)}, f32[32,768]{1,0:T(8,128)S(1)}) custom-call(f32[27]{0:T(128)S(1)} %pad_maximum_fusion.8.taps_ref, f32[32,40,768]{2,1,0:T(8,128)} %copy-done.2, f32[32,32,768]{2,1,0:T(8,128)S(1)} %copy-done), custom_call_target="tpu_custom_call" | custom-call | flops 35389440 | bytes 9437184 | tf_op jit(solution)/shard_map/pallas_call | solution.py:74
  94.5 0.0 copy-done.3
  94.5 0.1 fusion.1
  94.6 0.0 collective-permute-done.6
  94.7 0.0 collective-permute-done.7
  94.7 1.4 %pad_maximum_fusion.4.pad_ref = f32[24,40,768]{2,1,0:T(8,128)S(1)} fusion(f32[4,40,768]{2,1,0:T(8,128)} %collective-permute-done.7, f32[8,40,768]{2,1,0:T(8,128)S(1)} %get-tuple-element.13, f32[8,40,768]{2,1,0:T(8,128)S(1)} %get-tuple-element.12, f32[4,40,768]{2,1,0:T(8,128)} %collective-permute-done.6), kind=kLoop, calls=%fused_computation.4 | loop fusion | flops 2211840 | bytes 5898240 | tf_op jit(solution)/shard_map/concatenate | solution.py:102
  96.0 5.6 %shard_map.70 = (f32[8,32,768]{2,1,0:T(8,128)S(1)}, f32[32,768]{1,0:T(8,128)S(1)}) custom-call(f32[27]{0:T(128)S(1)} %pad_maximum_fusion.8.taps_ref, f32[24,40,768]{2,1,0:T(8,128)S(1)} %pad_maximum_fusion.4.pad_ref, f32[32,32,768]{2,1,0:T(8,128)} %other_ref.7), custom_call_target="tpu_custom_call" | custom-call | flops 11796480 | bytes 3145728 | tf_op jit(solution)/shard_map/pallas_call | solution.py:74
  101.7 0.1 collective-permute-start.8
  101.8 4.6 %collective-permute-done.8 = f32[32,768]{1,0:T(8,128)S(1)} collective-permute-done((f32[32,768]{1,0:T(8,128)S(1)}, f32[32,768]{1,0:T(8,128)S(1)}, u32[]{:S(2)}, u32[]{:S(2)}) %collective-permute-start.8) | collective-permute-done | bytes 98336 | tf_op jit(solution)/shard_map/ppermute | solution.py:115
  106.4 1.2 collective-permute-start.9
  107.6 0.1 fusion.5
  107.6 3.5 %collective-permute-done.9 = f32[32,768]{1,0:T(8,128)S(1)} collective-permute-done((f32[32,768]{1,0:T(8,128)S(1)}, f32[32,768]{1,0:T(8,128)S(1)}, u32[]{:S(2)}, u32[]{:S(2)}) %collective-permute-start.9) | collective-permute-done | bytes 98336 | tf_op jit(solution)/shard_map/ppermute | solution.py:115
  111.1 2.8 %collective-permute-start.10 = (f32[32,768]{1,0:T(8,128)S(1)}, f32[32,768]{1,0:T(8,128)S(1)}, u32[]{:S(2)}, u32[]{:S(2)}) collective-permute-start(f32[32,768]{1,0:T(8,128)S(1)} %max.14), channel_id=1, source_target_pairs={{0,128},{32,160},{64,192},{96,224},{128,0},{160,32},{192,64},{224,... | collective-permute-start | bytes 294920 | tf_op jit(solution)/shard_map/ppermute | solution.py:115
  114.0 2.0 %pad_maximum_fusion.2 = f32[32,32,768]{2,1,0:T(8,128)} fusion(f32[4,32,768]{2,1,0:T(8,128)S(1)} %get-tuple-element.23, f32[24,32,768]{2,1,0:T(8,128)S(1)} %get-tuple-element.7, f32[4,32,768]{2,1,0:T(8,128)S(1)} %get-tuple-element.22), kind=kLoop, calls=%fused_computation.2 | loop fusion | flops 1572864 | bytes 6291456 | tf_op jit(solution)/shard_map/concatenate | solution.py:104
  116.0 1.4 %collective-permute-done.10 = f32[32,768]{1,0:T(8,128)S(1)} collective-permute-done((f32[32,768]{1,0:T(8,128)S(1)}, f32[32,768]{1,0:T(8,128)S(1)}, u32[]{:S(2)}, u32[]{:S(2)}) %collective-permute-start.10) | collective-permute-done | bytes 98336 | tf_op jit(solution)/shard_map/ppermute | solution.py:115
  117.4 0.7 max.15
  (3 shorter events, 0.0 us)
Async XLA Ops:
  2.1 15.7 %collective-permute-start = (f32[32,4,768]{2,1,0:T(4,128)S(1)}, f32[32,4,768]{2,1,0:T(4,128)S(1)}, u32[]{:S(2)}, u32[]{:S(2)}) collective-permute-start(f32[32,4,768]{2,1,0:T(4,128)S(1)} %get-tuple-element.20), channel_id=1, source_target_pairs={{0,1},{1,2},{2,3},{3,4},{4,5},{5,6},{6,7},{7,8},{8,9},{9,10},{10,1... | collective-permute-start | bytes 1179656 | tf_op jit(solution)/shard_map/ppermute | solution.py:91
  4.1 25.9 %copy-start.5 = (f32[9]{0:T(128)S(1)}, f32[9]{0:T(128)}, u32[]{:S(2)}) copy-start(f32[9]{0:T(128)} %param.7) | copy-start | bytes 112
  4.1 25.9 %copy-start.6 = (f32[9]{0:T(128)S(1)}, f32[9]{0:T(128)}, u32[]{:S(2)}) copy-start(f32[9]{0:T(128)} %param.8) | copy-start | bytes 112
  4.1 25.9 %copy-start.7 = (f32[9]{0:T(128)S(1)}, f32[9]{0:T(128)}, u32[]{:S(2)}) copy-start(f32[9]{0:T(128)} %param.9) | copy-start | bytes 112
  4.1 25.9 %copy-start.1 = (f32[32,32,768]{2,1,0:T(8,128)S(1)}, f32[32,32,768]{2,1,0:T(8,128)}, u32[]{:S(2)}) copy-start(f32[32,32,768]{2,1,0:T(8,128)} %other_ref.5) | copy-start | bytes 9437188
  4.1 13.7 %collective-permute-start.1 = (f32[32,4,768]{2,1,0:T(4,128)S(1)}, f32[32,4,768]{2,1,0:T(4,128)S(1)}, u32[]{:S(2)}, u32[]{:S(2)}) collective-permute-start(f32[32,4,768]{2,1,0:T(4,128)S(1)} %get-tuple-element.21), channel_id=1, source_target_pairs={{1,0},{2,1},{3,2},{4,3},{5,4},{6,5},{7,6},{8,7},{9,8},{10,9},{11,1... | collective-permute-start | bytes 1179656 | tf_op jit(solution)/shard_map/ppermute | solution.py:92
  20.1 9.9 %copy-start.4 = (f32[32,40,768]{2,1,0:T(8,128)}, f32[32,40,768]{2,1,0:T(8,128)S(1)}, u32[]{:S(2)}) copy-start(f32[32,40,768]{2,1,0:T(8,128)S(1)} %pad_maximum_fusion.pad_ref) | copy-start | bytes 11796484
  20.2 24.7 %collective-permute-start.2 = (f32[4,40,768]{2,1,0:T(8,128)S(1)}, f32[4,40,768]{2,1,0:T(8,128)S(1)}, u32[]{:S(2)}, u32[]{:S(2)}) collective-permute-start(f32[4,40,768]{2,1,0:T(8,128)S(1)} %get-tuple-element.14), channel_id=1, source_target_pairs={{0,32},{32,64},{64,96},{96,128},{128,160},{160,192},{192,224},{1,3... | collective-permute-start | bytes 1474568 | tf_op jit(solution)/shard_map/ppermute | solution.py:91
  28.0 16.9 %collective-permute-start.3 = (f32[4,40,768]{2,1,0:T(8,128)S(1)}, f32[4,40,768]{2,1,0:T(8,128)S(1)}, u32[]{:S(2)}, u32[]{:S(2)}) collective-permute-start(f32[4,40,768]{2,1,0:T(8,128)S(1)} %get-tuple-element.15), channel_id=1, source_target_pairs={{32,0},{64,32},{96,64},{128,96},{160,128},{192,160},{224,192},{33,... | collective-permute-start | bytes 1474568 | tf_op jit(solution)/shard_map/ppermute | solution.py:92
  50.9 17.5 %collective-permute-start.4 = (f32[32,4,768]{2,1,0:T(4,128)S(1)}, f32[32,4,768]{2,1,0:T(4,128)S(1)}, u32[]{:S(2)}, u32[]{:S(2)}) collective-permute-start(f32[32,4,768]{2,1,0:T(4,128)S(1)} %get-tuple-element.18), channel_id=1, source_target_pairs={{0,1},{1,2},{2,3},{3,4},{4,5},{5,6},{6,7},{7,8},{8,9},{9,10},{10,1... | collective-permute-start | bytes 1179656 | tf_op jit(solution)/shard_map/ppermute | solution.py:91
  52.9 28.3 %copy-start = (f32[32,32,768]{2,1,0:T(8,128)S(1)}, f32[32,32,768]{2,1,0:T(8,128)}, u32[]{:S(2)}) copy-start(f32[32,32,768]{2,1,0:T(8,128)} %other_ref.7) | copy-start | bytes 9437188
  52.9 17.8 %collective-permute-start.5 = (f32[32,4,768]{2,1,0:T(4,128)S(1)}, f32[32,4,768]{2,1,0:T(4,128)S(1)}, u32[]{:S(2)}, u32[]{:S(2)}) collective-permute-start(f32[32,4,768]{2,1,0:T(4,128)S(1)} %get-tuple-element.19), channel_id=1, source_target_pairs={{1,0},{2,1},{3,2},{4,3},{5,4},{6,5},{7,6},{8,7},{9,8},{10,9},{11,1... | collective-permute-start | bytes 1179656 | tf_op jit(solution)/shard_map/ppermute | solution.py:92
  71.2 1.9 %copy-start.2 = (f32[32,40,768]{2,1,0:T(8,128)}, f32[32,40,768]{2,1,0:T(8,128)S(1)}, u32[]{:S(2)}) copy-start(f32[32,40,768]{2,1,0:T(8,128)S(1)} %pad_maximum_fusion.1.pad_ref) | copy-start | bytes 11796484
  74.1 20.5 %collective-permute-start.6 = (f32[4,40,768]{2,1,0:T(8,128)}, f32[4,40,768]{2,1,0:T(8,128)}, u32[]{:S(2)}, u32[]{:S(2)}) collective-permute-start(f32[4,40,768]{2,1,0:T(8,128)} %get-tuple-element.10), channel_id=1, source_target_pairs={{0,32},{32,64},{64,96},{96,128},{128,160},{160,192},{192,224},{1,3... | collective-permute-start | bytes 1474568 | tf_op jit(solution)/shard_map/ppermute | solution.py:91
  77.6 17.1 %collective-permute-start.7 = (f32[4,40,768]{2,1,0:T(8,128)}, f32[4,40,768]{2,1,0:T(8,128)}, u32[]{:S(2)}, u32[]{:S(2)}) collective-permute-start(f32[4,40,768]{2,1,0:T(8,128)} %get-tuple-element.11), channel_id=1, source_target_pairs={{32,0},{64,32},{96,64},{128,96},{160,128},{192,160},{224,192},{33,... | collective-permute-start | bytes 1474568 | tf_op jit(solution)/shard_map/ppermute | solution.py:92
  81.1 13.3 %copy-start.3 = (f32[32,40,768]{2,1,0:T(8,128)S(1)}, f32[32,40,768]{2,1,0:T(8,128)}, u32[]{:S(2)}) copy-start(f32[32,40,768]{2,1,0:T(8,128)} %copy-done.2) | copy-start | bytes 11796484
  101.7 4.7 %collective-permute-start.8 = (f32[32,768]{1,0:T(8,128)S(1)}, f32[32,768]{1,0:T(8,128)S(1)}, u32[]{:S(2)}, u32[]{:S(2)}) collective-permute-start(f32[32,768]{1,0:T(8,128)S(1)} %max.12), channel_id=1, source_target_pairs={{0,32},{32,0},{64,96},{96,64},{128,160},{160,128},{192,224},{224,1... | collective-permute-start | bytes 294920 | tf_op jit(solution)/shard_map/ppermute | solution.py:115
  106.4 4.7 %collective-permute-start.9 = (f32[32,768]{1,0:T(8,128)S(1)}, f32[32,768]{1,0:T(8,128)S(1)}, u32[]{:S(2)}, u32[]{:S(2)}) collective-permute-start(f32[32,768]{1,0:T(8,128)S(1)} %max.13), channel_id=1, source_target_pairs={{0,64},{32,96},{64,0},{96,32},{128,192},{160,224},{192,128},{224,1... | collective-permute-start | bytes 294920 | tf_op jit(solution)/shard_map/ppermute | solution.py:115
  111.1 6.2 %collective-permute-start.10 = (f32[32,768]{1,0:T(8,128)S(1)}, f32[32,768]{1,0:T(8,128)S(1)}, u32[]{:S(2)}, u32[]{:S(2)}) collective-permute-start(f32[32,768]{1,0:T(8,128)S(1)} %max.14), channel_id=1, source_target_pairs={{0,128},{32,160},{64,192},{96,224},{128,0},{160,32},{192,64},{224,... | collective-permute-start | bytes 294920 | tf_op jit(solution)/shard_map/ppermute | solution.py:115

commit v5 on v4

--- a/solution.py
+++ b/solution.py
@@ -96,10 +96,14 @@
 def split_blur(mode, taps, shard, other, width):
     nz = shard.shape[0]
     before, after = halo_pair(shard, "gy", 1, width)
+    below, above = halo_pair(shard, "gz", 0, width)
+    side_rows = jnp.concatenate([before, after], axis=1)
+    corner_below, corner_above = halo_pair(side_rows, "gz", 0, width)
     rows_padded = jnp.concatenate([before, shard, after], axis=1)
-    below, above = halo_pair(rows_padded, "gz", 0, width)
     inner = fused_blur(mode, [(0, nz - 2 * width, 0, width)], taps, rows_padded, other)
-    slabs = jnp.concatenate([below, rows_padded[: 2 * width], rows_padded[nz - 2 * width :], above], axis=0)
+    below_padded = jnp.concatenate([corner_below[:, :width], below, corner_below[:, width:]], axis=1)
+    above_padded = jnp.concatenate([corner_above[:, :width], above, corner_above[:, width:]], axis=1)
+    slabs = jnp.concatenate([below_padded, rows_padded[: 2 * width], rows_padded[nz - 2 * width :], above_padded], axis=0)
     edges = fused_blur(mode, [(0, width, 0, 0), (width, width, 3 * width, nz - width)], taps, slabs, other)
     volume = jnp.concatenate([edges[0][:width], inner[0], edges[0][width:]], axis=0)
     if mode == "update":

time: 120 us -> 126 us (1.050)
  starting transfers between devices: 40.5 us -> 51 us
  waiting for transfers between devices: 24.7 us -> 16.4 us
  local copies, waits for them, and re-layouts: 6.7 us -> 8.9 us
    ppermute x4 -> x6, waiting for transfers between devices: 13 us -> 0.02 us  [halo_pair(): before = lax.ppermute(last, axis, up)]
    ppermute x4 -> x6, waiting for transfers between devices: 2.26 us -> 8.66 us  [halo_pair(): after = lax.ppermute(first, axis, down)]
    ppermute x4 -> x6, starting transfers between devices: 21.3 us -> 26.6 us  [halo_pair(): after = lax.ppermute(first, axis, down)]
    unnamed x16 -> x18, local copies, waits for them, and re-layouts: 1.9 us -> 5.31 us
    ppermute x3, starting transfers between devices: 4.09 us -> 7.17 us  [butterfly_max(): value = jnp.maximum(value, lax.ppermute(value, axis, pairs))]
    ppermute x4 -> x6, starting transfers between devices: 15.1 us -> 17.3 us  [halo_pair(): before = lax.ppermute(last, axis, up)]
    slice x1 -> x3, other arithmetic: 0.14 us -> 2.01 us  [halo_pair(): last = lax.slice_in_dim(shard, length - width, length, axis=dim)]
    ppermute x3, waiting for transfers between devices: 9.45 us -> 7.73 us  [butterfly_max(): value = jnp.maximum(value, lax.ppermute(value, axis, pairs))]
  transfers between devices with their start and end apart: 11 -> 15, of which waited for: 6 -> 5; matrix products, arithmetic and copies ran while one was open for 4% -> 6% of each run, Pallas kernels for 22% -> 21%
where the time goes in v5:
time: 126 us; the launch traced here: 124 us
  starting transfers between devices  51 us (40%)
  Pallas kernels  38.1 us (30%)
  waiting for transfers between devices  16.4 us (13%)
  local copies, waits for them, and re-layouts  8.9 us (7%)
  other arithmetic  8.4 us (7%)
    pallas_call x4, Pallas kernels, fused_blur(): pl.pallas_call(functools.partial(blur_kernel, mode, tuple(segments)), out...  38.1 us
    ppermute x6, starting transfers between devices, halo_pair(): after = lax.ppermute(first, axis, down)  26.6 us
    ppermute x6, starting transfers between devices, halo_pair(): before = lax.ppermute(last, axis, up)  17.3 us
    ppermute x6, waiting for transfers between devices, halo_pair(): after = lax.ppermute(first, axis, down)  8.66 us
    ppermute x3, waiting for transfers between devices, butterfly_max(): value = jnp.maximum(value, lax.ppermute(value, axis, pairs))  7.73 us
    ppermute x3, starting transfers between devices, butterfly_max(): value = jnp.maximum(value, lax.ppermute(value, axis, pairs))  7.17 us
    unnamed x18, local copies, waits for them, and re-layouts  5.31 us
    concatenate x2, other arithmetic, split_blur(): rows_padded = jnp.concatenate([before, shard, after], axis=1)  2.89 us
  transfers between devices with their start and end apart: 15, of which 5 were waited for; matrix products, arithmetic and copies ran while one was open for 6% of the time, Pallas kernels for 21%

profile of v5, /device:TPU:160, one launch (start us, length us, event | category | flops | bytes accessed | tf_op | source)
XLA Modules:
  0.0 123.9 jit_solution(181527483673818889)
XLA Ops:
  0.6 0.0 copy-start
  0.6 0.0 copy-start.8
  0.7 0.0 copy-start.7
  0.7 0.0 copy-start.6
  0.7 1.7 %fusion.3 = (f32[32,4,768]{2,1,0:T(4,128)S(1)}, f32[32,4,768]{2,1,0:T(4,128)S(1)}) fusion(f32[32,32,768]{2,1,0:T(8,128)} %other_ref.7), kind=kLoop, calls=%fused_computation.17 | loop fusion | bytes 1572864 | tf_op jit(solution)/shard_map/slice | solution.py:89
  2.3 1.9 %collective-permute-start = (f32[32,4,768]{2,1,0:T(4,128)S(1)}, f32[32,4,768]{2,1,0:T(4,128)S(1)}, u32[]{:S(2)}, u32[]{:S(2)}) collective-permute-start(f32[32,4,768]{2,1,0:T(4,128)S(1)} %get-tuple-element.18), channel_id=1, source_target_pairs={{0,1},{1,2},{2,3},{3,4},{4,5},{5,6},{6,7},{7,8},{8,9},{9,10},{10,1... | collective-permute-start | bytes 1179656 | tf_op jit(solution)/shard_map/ppermute | solution.py:91
  4.3 7.9 %collective-permute-start.1 = (f32[32,4,768]{2,1,0:T(4,128)S(1)}, f32[32,4,768]{2,1,0:T(4,128)S(1)}, u32[]{:S(2)}, u32[]{:S(2)}) collective-permute-start(f32[32,4,768]{2,1,0:T(4,128)S(1)} %get-tuple-element.19), channel_id=1, source_target_pairs={{1,0},{2,1},{3,2},{4,3},{5,4},{6,5},{7,6},{8,7},{9,8},{10,9},{11,1... | collective-permute-start | bytes 1179656 | tf_op jit(solution)/shard_map/ppermute | solution.py:92
  12.1 1.2 fusion.2
  13.3 3.8 %collective-permute-start.3 = (f32[4,32,768]{2,1,0:T(8,128)S(1)}, f32[4,32,768]{2,1,0:T(8,128)S(1)}, u32[]{:S(2)}, u32[]{:S(2)}) collective-permute-start(f32[4,32,768]{2,1,0:T(8,128)S(1)} %get-tuple-element.16), channel_id=1, source_target_pairs={{0,32},{32,64},{64,96},{96,128},{128,160},{160,192},{192,224},{1,3... | collective-permute-start | bytes 1179656 | tf_op jit(solution)/shard_map/ppermute | solution.py:91
  17.2 2.0 %collective-permute-start.5 = (f32[4,32,768]{2,1,0:T(8,128)S(1)}, f32[4,32,768]{2,1,0:T(8,128)S(1)}, u32[]{:S(2)}, u32[]{:S(2)}) collective-permute-start(f32[4,32,768]{2,1,0:T(8,128)S(1)} %get-tuple-element.17), channel_id=1, source_target_pairs={{32,0},{64,32},{96,64},{128,96},{160,128},{192,160},{224,192},{33,... | collective-permute-start | bytes 1179656 | tf_op jit(solution)/shard_map/ppermute | solution.py:92
  19.2 0.0 copy-done.8
  19.2 0.0 copy-done.7
  19.2 0.0 copy-done.6
  19.2 0.1 pad_maximum_fusion.11.taps_ref
  19.3 0.0 collective-permute-done
  19.3 6.0 %collective-permute-done.1 = f32[32,4,768]{2,1,0:T(4,128)S(1)} collective-permute-done((f32[32,4,768]{2,1,0:T(4,128)S(1)}, f32[32,4,768]{2,1,0:T(4,128)S(1)}, u32[]{:S(2)}, u32[]{:S(2)}) %collective-permute-start.1) | collective-permute-done | bytes 393248 | tf_op jit(solution)/shard_map/ppermute | solution.py:92
  25.3 1.9 %collective-permute-start.2 = (f32[4,8,768]{2,1,0:T(8,128)S(1)}, f32[4,8,768]{2,1,0:T(8,128)S(1)}, u32[]{:S(2)}, u32[]{:S(2)}) collective-permute-start(f32[4,8,768]{2,1,0:T(8,128)S(1)} %get-tuple-element.26), channel_id=1, source_target_pairs={{0,32},{32,64},{64,96},{96,128},{128,160},{160,192},{192,224},{1,3... | collective-permute-start | bytes 294920 | tf_op jit(solution)/shard_map/ppermute | solution.py:91
  27.3 3.9 %collective-permute-start.4 = (f32[4,8,768]{2,1,0:T(8,128)S(1)}, f32[4,8,768]{2,1,0:T(8,128)S(1)}, u32[]{:S(2)}, u32[]{:S(2)}) collective-permute-start(f32[4,8,768]{2,1,0:T(8,128)S(1)} %get-tuple-element.27), channel_id=1, source_target_pairs={{32,0},{64,32},{96,64},{128,96},{160,128},{192,160},{224,192},{33,... | collective-permute-start | bytes 294920 | tf_op jit(solution)/shard_map/ppermute | solution.py:92
  31.2 0.5 pad_maximum_fusion.pad_ref
  31.7 1.9 %copy-done.4 = f32[32,40,768]{2,1,0:T(8,128)} copy-done((f32[32,40,768]{2,1,0:T(8,128)}, f32[32,40,768]{2,1,0:T(8,128)S(1)}, u32[]{:S(2)}) %copy-start.4) | copy-done | bytes 3932184
  33.6 0.1 fusion.1
  33.7 1.7 %copy-done.2 = f32[32,32,768]{2,1,0:T(8,128)S(1)} copy-done((f32[32,32,768]{2,1,0:T(8,128)S(1)}, f32[32,32,768]{2,1,0:T(8,128)}, u32[]{:S(2)}) %copy-start.2) | copy-done | bytes 3145752
  35.5 13.2 %shard_map.69 = f32[24,32,768]{2,1,0:T(8,128)S(1)} custom-call(f32[27]{0:T(128)S(1)} %pad_maximum_fusion.11.taps_ref, f32[32,40,768]{2,1,0:T(8,128)} %copy-done.4, f32[32,32,768]{2,1,0:T(8,128)S(1)} %copy-done.2), custom_call_target="tpu_custom_call" | custom-call | flops 35389440 | bytes 9437184 | tf_op jit(solution)/shard_map/pallas_call | solution.py:74
  48.7 0.0 copy-start.1
  48.7 0.0 collective-permute-done.2
  48.7 0.0 collective-permute-done.4
  48.8 0.0 collective-permute-done.3
  48.8 0.0 collective-permute-done.5
  48.8 0.3 maximum_maximum_fusion.pad_ref
  49.1 6.1 %shard_map.68 = f32[8,32,768]{2,1,0:T(8,128)S(1)} custom-call(f32[27]{0:T(128)S(1)} %pad_maximum_fusion.11.taps_ref, f32[24,40,768]{2,1,0:T(8,128)S(1)} %maximum_maximum_fusion.pad_ref, f32[32,32,768]{2,1,0:T(8,128)} %other_ref.5), custom_call_target="tpu_custom_call" | custom-call | flops 11796480 | bytes 3145728 | tf_op jit(solution)/shard_map/pallas_call | solution.py:74
  55.2 0.1 fusion.5
  55.3 1.1 pad_maximum_fusion.5
  56.3 1.9 %collective-permute-start.6 = (f32[32,4,768]{2,1,0:T(4,128)}, f32[32,4,768]{2,1,0:T(4,128)}, u32[]{:S(2)}, u32[]{:S(2)}) collective-permute-start(f32[32,4,768]{2,1,0:T(4,128)} %get-tuple-element.14), channel_id=1, source_target_pairs={{0,1},{1,2},{2,3},{3,4},{4,5},{5,6},{6,7},{7,8},{8,9},{9,10},{10,1... | collective-permute-start | bytes 1179656 | tf_op jit(solution)/shard_map/ppermute | solution.py:91
  58.3 7.9 %collective-permute-start.7 = (f32[32,4,768]{2,1,0:T(4,128)}, f32[32,4,768]{2,1,0:T(4,128)}, u32[]{:S(2)}, u32[]{:S(2)}) collective-permute-start(f32[32,4,768]{2,1,0:T(4,128)} %get-tuple-element.15), channel_id=1, source_target_pairs={{1,0},{2,1},{3,2},{4,3},{5,4},{6,5},{7,6},{8,7},{9,8},{10,9},{11,1... | collective-permute-start | bytes 1179656 | tf_op jit(solution)/shard_map/ppermute | solution.py:92
  66.1 0.1 rev.9
  66.2 0.1 rev.10
  66.3 0.1 rev.11
  66.4 0.1 pad_maximum_fusion.10.taps_ref
  66.5 1.9 %collective-permute-start.11 = (f32[4,32,768]{2,1,0:T(8,128)}, f32[4,32,768]{2,1,0:T(8,128)S(1)}, u32[]{:S(2)}, u32[]{:S(2)}) collective-permute-start(f32[4,32,768]{2,1,0:T(8,128)} %copy-done.5), channel_id=1, source_target_pairs={{32,0},{64,32},{96,64},{128,96},{160,128},{192,160},{224,192},{33,... | collective-permute-start | bytes 1179656 | tf_op jit(solution)/shard_map/ppermute | solution.py:92
  68.4 4.8 %collective-permute-start.9 = (f32[4,32,768]{2,1,0:T(8,128)S(1)}, f32[4,32,768]{2,1,0:T(8,128)S(1)}, u32[]{:S(2)}, u32[]{:S(2)}) collective-permute-start(f32[4,32,768]{2,1,0:T(8,128)S(1)} %get-tuple-element.25), channel_id=1, source_target_pairs={{0,32},{32,64},{64,96},{96,128},{128,160},{160,192},{192,224},{1,3... | collective-permute-start | bytes 1179656 | tf_op jit(solution)/shard_map/ppermute | solution.py:91
  73.2 0.0 collective-permute-done.6
  73.2 2.7 %collective-permute-done.7 = f32[32,4,768]{2,1,0:T(4,128)} collective-permute-done((f32[32,4,768]{2,1,0:T(4,128)}, f32[32,4,768]{2,1,0:T(4,128)}, u32[]{:S(2)}, u32[]{:S(2)}) %collective-permute-start.7) | collective-permute-done | bytes 393248 | tf_op jit(solution)/shard_map/ppermute | solution.py:92
  75.9 0.9 pad_maximum_fusion.7
  76.8 2.8 %collective-permute-start.8 = (f32[4,8,768]{2,1,0:T(8,128)S(1)}, f32[4,8,768]{2,1,0:T(8,128)S(1)}, u32[]{:S(2)}, u32[]{:S(2)}) collective-permute-start(f32[4,8,768]{2,1,0:T(8,128)S(1)} %get-tuple-element.22), channel_id=1, source_target_pairs={{0,32},{32,64},{64,96},{96,128},{128,160},{160,192},{192,224},{1,3... | collective-permute-start | bytes 294920 | tf_op jit(solution)/shard_map/ppermute | solution.py:91
  79.7 3.0 %collective-permute-start.10 = (f32[4,8,768]{2,1,0:T(8,128)S(1)}, f32[4,8,768]{2,1,0:T(8,128)S(1)}, u32[]{:S(2)}, u32[]{:S(2)}) collective-permute-start(f32[4,8,768]{2,1,0:T(8,128)S(1)} %get-tuple-element.23), channel_id=1, source_target_pairs={{32,0},{64,32},{96,64},{128,96},{160,128},{192,160},{224,192},{33,... | collective-permute-start | bytes 294920 | tf_op jit(solution)/shard_map/ppermute | solution.py:92
  82.7 2.4 %pad_maximum_fusion.1.pad_ref = f32[32,40,768]{2,1,0:T(8,128)S(1)} fusion(f32[32,4,768]{2,1,0:T(4,128)} %collective-permute-done.7, f32[4,32,768]{2,1,0:T(8,128)S(1)} %get-tuple-element.25, f32[24,32,768]{2,1,0:T(8,128)} %copy-done.1, f32[4,32,768]{2,1,0:T(8,128)} %copy-done.5, f32[32,4,768]{2,1,0:T(4,128)} %collective-permute-done.6), kind=kLoop, calls=%fused_computation.1 | loop fusion | flops 3932160 | bytes 7864320 | tf_op jit(solution)/shard_map/concatenate | solution.py:102
  85.1 0.2 fusion
  85.3 1.7 %copy-done.3 = f32[32,40,768]{2,1,0:T(8,128)} copy-done((f32[32,40,768]{2,1,0:T(8,128)}, f32[32,40,768]{2,1,0:T(8,128)S(1)}, u32[]{:S(2)}) %copy-start.3) | copy-done | bytes 3932184
  86.9 13.2 %shard_map.71 = (f32[24,32,768]{2,1,0:T(8,128)S(1)}, f32[32,768]{1,0:T(8,128)S(1)}) custom-call(f32[27]{0:T(128)S(1)} %pad_maximum_fusion.10.taps_ref, f32[32,40,768]{2,1,0:T(8,128)} %copy-done.3, f32[32,32,768]{2,1,0:T(8,128)S(1)} %copy-done), custom_call_target="tpu_custom_call" | custom-call | flops 35389440 | bytes 9437184 | tf_op jit(solution)/shard_map/pallas_call | solution.py:74
  100.2 0.0 collective-permute-done.8
  100.2 0.0 collective-permute-done.10
  100.2 0.0 collective-permute-done.11
  100.2 0.0 collective-permute-done.9
  100.2 0.3 maximum_maximum_fusion.1.pad_ref
  100.6 5.6 %shard_map.70 = (f32[8,32,768]{2,1,0:T(8,128)S(1)}, f32[32,768]{1,0:T(8,128)S(1)}) custom-call(f32[27]{0:T(128)S(1)} %pad_maximum_fusion.10.taps_ref, f32[24,40,768]{2,1,0:T(8,128)S(1)} %maximum_maximum_fusion.1.pad_ref, f32[32,32,768]{2,1,0:T(8,128)} %other_ref.7), custom_call_target="tpu_custom_call" | custom-call | flops 11796480 | bytes 3145728 | tf_op jit(solution)/shard_map/pallas_call | solution.py:74
  106.2 0.1 collective-permute-start.12
  106.3 4.6 %collective-permute-done.12 = f32[32,768]{1,0:T(8,128)S(1)} collective-permute-done((f32[32,768]{1,0:T(8,128)S(1)}, f32[32,768]{1,0:T(8,128)S(1)}, u32[]{:S(2)}, u32[]{:S(2)}) %collective-permute-start.12) | collective-permute-done | bytes 98336 | tf_op jit(solution)/shard_map/ppermute | solution.py:119
  111.0 3.4 %collective-permute-start.13 = (f32[32,768]{1,0:T(8,128)S(1)}, f32[32,768]{1,0:T(8,128)S(1)}, u32[]{:S(2)}, u32[]{:S(2)}) collective-permute-start(f32[32,768]{1,0:T(8,128)S(1)} %max.13), channel_id=1, source_target_pairs={{0,64},{32,96},{64,0},{96,32},{128,192},{160,224},{192,128},{224,1... | collective-permute-start | bytes 294920 | tf_op jit(solution)/shard_map/ppermute | solution.py:119
  114.4 0.1 fusion.4
  114.5 2.5 %collective-permute-done.13 = f32[32,768]{1,0:T(8,128)S(1)} collective-permute-done((f32[32,768]{1,0:T(8,128)S(1)}, f32[32,768]{1,0:T(8,128)S(1)}, u32[]{:S(2)}, u32[]{:S(2)}) %collective-permute-start.13) | collective-permute-done | bytes 98336 | tf_op jit(solution)/shard_map/ppermute | solution.py:119
  117.0 3.6 %collective-permute-start.14 = (f32[32,768]{1,0:T(8,128)S(1)}, f32[32,768]{1,0:T(8,128)S(1)}, u32[]{:S(2)}, u32[]{:S(2)}) collective-permute-start(f32[32,768]{1,0:T(8,128)S(1)} %max.14), channel_id=1, source_target_pairs={{0,128},{32,160},{64,192},{96,224},{128,0},{160,32},{192,64},{224,... | collective-permute-start | bytes 294920 | tf_op jit(solution)/shard_map/ppermute | solution.py:119
  120.7 2.0 %pad_maximum_fusion.2 = f32[32,32,768]{2,1,0:T(8,128)} fusion(f32[4,32,768]{2,1,0:T(8,128)S(1)} %get-tuple-element.21, f32[24,32,768]{2,1,0:T(8,128)S(1)} %get-tuple-element.7, f32[4,32,768]{2,1,0:T(8,128)S(1)} %get-tuple-element.20), kind=kLoop, calls=%fused_computation.2 | loop fusion | flops 1572864 | bytes 6291456 | tf_op jit(solution)/shard_map/concatenate | solution.py:108
  122.7 0.6 collective-permute-done.14
  123.3 0.7 max.15
  (15 shorter events, 0.2 us)
Async XLA Ops:
  0.6 30.6 %copy-start = (f32[32,32,768]{2,1,0:T(8,128)S(1)}, f32[32,32,768]{2,1,0:T(8,128)}, u32[]{:S(2)}) copy-start(f32[32,32,768]{2,1,0:T(8,128)} %other_ref.7) | copy-start | bytes 9437188
  0.6 18.6 %copy-start.8 = (f32[9]{0:T(128)S(1)}, f32[9]{0:T(128)}, u32[]{:S(2)}) copy-start(f32[9]{0:T(128)} %param.9) | copy-start | bytes 112
  0.7 18.6 %copy-start.7 = (f32[9]{0:T(128)S(1)}, f32[9]{0:T(128)}, u32[]{:S(2)}) copy-start(f32[9]{0:T(128)} %param.8) | copy-start | bytes 112
  0.7 18.6 %copy-start.6 = (f32[9]{0:T(128)S(1)}, f32[9]{0:T(128)}, u32[]{:S(2)}) copy-start(f32[9]{0:T(128)} %param.7) | copy-start | bytes 112
  2.3 17.0 %collective-permute-start = (f32[32,4,768]{2,1,0:T(4,128)S(1)}, f32[32,4,768]{2,1,0:T(4,128)S(1)}, u32[]{:S(2)}, u32[]{:S(2)}) collective-permute-start(f32[32,4,768]{2,1,0:T(4,128)S(1)} %get-tuple-element.18), channel_id=1, source_target_pairs={{0,1},{1,2},{2,3},{3,4},{4,5},{5,6},{6,7},{7,8},{8,9},{9,10},{10,1... | collective-permute-start | bytes 1179656 | tf_op jit(solution)/shard_map/ppermute | solution.py:91
  4.3 21.0 %collective-permute-start.1 = (f32[32,4,768]{2,1,0:T(4,128)S(1)}, f32[32,4,768]{2,1,0:T(4,128)S(1)}, u32[]{:S(2)}, u32[]{:S(2)}) collective-permute-start(f32[32,4,768]{2,1,0:T(4,128)S(1)} %get-tuple-element.19), channel_id=1, source_target_pairs={{1,0},{2,1},{3,2},{4,3},{5,4},{6,5},{7,6},{8,7},{9,8},{10,9},{11,1... | collective-permute-start | bytes 1179656 | tf_op jit(solution)/shard_map/ppermute | solution.py:92
  13.3 35.5 %collective-permute-start.3 = (f32[4,32,768]{2,1,0:T(8,128)S(1)}, f32[4,32,768]{2,1,0:T(8,128)S(1)}, u32[]{:S(2)}, u32[]{:S(2)}) collective-permute-start(f32[4,32,768]{2,1,0:T(8,128)S(1)} %get-tuple-element.16), channel_id=1, source_target_pairs={{0,32},{32,64},{64,96},{96,128},{128,160},{160,192},{192,224},{1,3... | collective-permute-start | bytes 1179656 | tf_op jit(solution)/shard_map/ppermute | solution.py:91
  17.2 31.6 %collective-permute-start.5 = (f32[4,32,768]{2,1,0:T(8,128)S(1)}, f32[4,32,768]{2,1,0:T(8,128)S(1)}, u32[]{:S(2)}, u32[]{:S(2)}) collective-permute-start(f32[4,32,768]{2,1,0:T(8,128)S(1)} %get-tuple-element.17), channel_id=1, source_target_pairs={{32,0},{64,32},{96,64},{128,96},{160,128},{192,160},{224,192},{33,... | collective-permute-start | bytes 1179656 | tf_op jit(solution)/shard_map/ppermute | solution.py:92
  25.3 23.4 %collective-permute-start.2 = (f32[4,8,768]{2,1,0:T(8,128)S(1)}, f32[4,8,768]{2,1,0:T(8,128)S(1)}, u32[]{:S(2)}, u32[]{:S(2)}) collective-permute-start(f32[4,8,768]{2,1,0:T(8,128)S(1)} %get-tuple-element.26), channel_id=1, source_target_pairs={{0,32},{32,64},{64,96},{96,128},{128,160},{160,192},{192,224},{1,3... | collective-permute-start | bytes 294920 | tf_op jit(solution)/shard_map/ppermute | solution.py:91
  27.3 21.5 %collective-permute-start.4 = (f32[4,8,768]{2,1,0:T(8,128)S(1)}, f32[4,8,768]{2,1,0:T(8,128)S(1)}, u32[]{:S(2)}, u32[]{:S(2)}) collective-permute-start(f32[4,8,768]{2,1,0:T(8,128)S(1)} %get-tuple-element.27), channel_id=1, source_target_pairs={{32,0},{64,32},{96,64},{128,96},{160,128},{192,160},{224,192},{33,... | collective-permute-start | bytes 294920 | tf_op jit(solution)/shard_map/ppermute | solution.py:92
  31.7 1.9 %copy-start.4 = (f32[32,40,768]{2,1,0:T(8,128)}, f32[32,40,768]{2,1,0:T(8,128)S(1)}, u32[]{:S(2)}) copy-start(f32[32,40,768]{2,1,0:T(8,128)S(1)} %pad_maximum_fusion.pad_ref) | copy-start | bytes 11796484
  33.6 1.9 %copy-start.2 = (f32[32,32,768]{2,1,0:T(8,128)S(1)}, f32[32,32,768]{2,1,0:T(8,128)}, u32[]{:S(2)}) copy-start(f32[32,32,768]{2,1,0:T(8,128)} %other_ref.5) | copy-start | bytes 9437188
  48.7 6.6 %copy-start.1 = (f32[24,32,768]{2,1,0:T(8,128)}, f32[24,32,768]{2,1,0:T(8,128)S(1)}, u32[]{:S(2)}) copy-start(f32[24,32,768]{2,1,0:T(8,128)S(1)} %shard_map.69) | copy-start | bytes 7077892
  55.3 1.1 copy-start.5
  56.3 16.9 %collective-permute-start.6 = (f32[32,4,768]{2,1,0:T(4,128)}, f32[32,4,768]{2,1,0:T(4,128)}, u32[]{:S(2)}, u32[]{:S(2)}) collective-permute-start(f32[32,4,768]{2,1,0:T(4,128)} %get-tuple-element.14), channel_id=1, source_target_pairs={{0,1},{1,2},{2,3},{3,4},{4,5},{5,6},{6,7},{7,8},{8,9},{9,10},{10,1... | collective-permute-start | bytes 1179656 | tf_op jit(solution)/shard_map/ppermute | solution.py:91
  58.3 17.7 %collective-permute-start.7 = (f32[32,4,768]{2,1,0:T(4,128)}, f32[32,4,768]{2,1,0:T(4,128)}, u32[]{:S(2)}, u32[]{:S(2)}) collective-permute-start(f32[32,4,768]{2,1,0:T(4,128)} %get-tuple-element.15), channel_id=1, source_target_pairs={{1,0},{2,1},{3,2},{4,3},{5,4},{6,5},{7,6},{8,7},{9,8},{10,9},{11,1... | collective-permute-start | bytes 1179656 | tf_op jit(solution)/shard_map/ppermute | solution.py:92
  66.5 33.7 %collective-permute-start.11 = (f32[4,32,768]{2,1,0:T(8,128)}, f32[4,32,768]{2,1,0:T(8,128)S(1)}, u32[]{:S(2)}, u32[]{:S(2)}) collective-permute-start(f32[4,32,768]{2,1,0:T(8,128)} %copy-done.5), channel_id=1, source_target_pairs={{32,0},{64,32},{96,64},{128,96},{160,128},{192,160},{224,192},{33,... | collective-permute-start | bytes 1179656 | tf_op jit(solution)/shard_map/ppermute | solution.py:92
  68.4 31.8 %collective-permute-start.9 = (f32[4,32,768]{2,1,0:T(8,128)S(1)}, f32[4,32,768]{2,1,0:T(8,128)S(1)}, u32[]{:S(2)}, u32[]{:S(2)}) collective-permute-start(f32[4,32,768]{2,1,0:T(8,128)S(1)} %get-tuple-element.25), channel_id=1, source_target_pairs={{0,32},{32,64},{64,96},{96,128},{128,160},{160,192},{192,224},{1,3... | collective-permute-start | bytes 1179656 | tf_op jit(solution)/shard_map/ppermute | solution.py:91
  76.8 23.3 %collective-permute-start.8 = (f32[4,8,768]{2,1,0:T(8,128)S(1)}, f32[4,8,768]{2,1,0:T(8,128)S(1)}, u32[]{:S(2)}, u32[]{:S(2)}) collective-permute-start(f32[4,8,768]{2,1,0:T(8,128)S(1)} %get-tuple-element.22), channel_id=1, source_target_pairs={{0,32},{32,64},{64,96},{96,128},{128,160},{160,192},{192,224},{1,3... | collective-permute-start | bytes 294920 | tf_op jit(solution)/shard_map/ppermute | solution.py:91
  79.7 20.5 %collective-permute-start.10 = (f32[4,8,768]{2,1,0:T(8,128)S(1)}, f32[4,8,768]{2,1,0:T(8,128)S(1)}, u32[]{:S(2)}, u32[]{:S(2)}) collective-permute-start(f32[4,8,768]{2,1,0:T(8,128)S(1)} %get-tuple-element.23), channel_id=1, source_target_pairs={{32,0},{64,32},{96,64},{128,96},{160,128},{192,160},{224,192},{33,... | collective-permute-start | bytes 294920 | tf_op jit(solution)/shard_map/ppermute | solution.py:92
  85.1 1.9 %copy-start.3 = (f32[32,40,768]{2,1,0:T(8,128)}, f32[32,40,768]{2,1,0:T(8,128)S(1)}, u32[]{:S(2)}) copy-start(f32[32,40,768]{2,1,0:T(8,128)S(1)} %pad_maximum_fusion.1.pad_ref) | copy-start | bytes 11796484
  106.2 4.7 %collective-permute-start.12 = (f32[32,768]{1,0:T(8,128)S(1)}, f32[32,768]{1,0:T(8,128)S(1)}, u32[]{:S(2)}, u32[]{:S(2)}) collective-permute-start(f32[32,768]{1,0:T(8,128)S(1)} %max.12), channel_id=1, source_target_pairs={{0,32},{32,0},{64,96},{96,64},{128,160},{160,128},{192,224},{224,1... | collective-permute-start | bytes 294920 | tf_op jit(solution)/shard_map/ppermute | solution.py:119
  111.0 6.0 %collective-permute-start.13 = (f32[32,768]{1,0:T(8,128)S(1)}, f32[32,768]{1,0:T(8,128)S(1)}, u32[]{:S(2)}, u32[]{:S(2)}) collective-permute-start(f32[32,768]{1,0:T(8,128)S(1)} %max.13), channel_id=1, source_target_pairs={{0,64},{32,96},{64,0},{96,32},{128,192},{160,224},{192,128},{224,1... | collective-permute-start | bytes 294920 | tf_op jit(solution)/shard_map/ppermute | solution.py:119
  117.0 6.2 %collective-permute-start.14 = (f32[32,768]{1,0:T(8,128)S(1)}, f32[32,768]{1,0:T(8,128)S(1)}, u32[]{:S(2)}, u32[]{:S(2)}) collective-permute-start(f32[32,768]{1,0:T(8,128)S(1)} %max.14), channel_id=1, source_target_pairs={{0,128},{32,160},{64,192},{96,224},{128,0},{160,32},{192,64},{224,... | collective-permute-start | bytes 294920 | tf_op jit(solution)/shard_map/ppermute | solution.py:119

commit v6 on v4

v6 whole, which is shorter than its diff:
```python
import jax
import jax.numpy as jnp
from jax import lax
from jax.sharding import PartitionSpec as P
import functools
from jax.experimental import pallas as pl
from jax.experimental.pallas import tpu as pltpu


def plane_blur(mode, taps_ref, load, zbuf, ybuf, lanes, store, other_plane, max_ref):
    ntap = 9
    r = 4
    ny, nx = ybuf.shape
    py = ny + 2 * r
    for c in range(py // 8):
        rows = pl.ds(c * 8, 8)
        acc = taps_ref[0] * load(0, rows)
        for k in range(1, ntap):
            acc = acc + taps_ref[k] * load(k, rows)
        zbuf[rows, :] = acc
    for c in range(ny // 8):
        acc = taps_ref[ntap] * zbuf[pl.ds(c * 8, 8), :]
        for k in range(1, ntap):
            acc = acc + taps_ref[ntap + k] * zbuf[pl.ds(c * 8 + k, 8), :]
        ybuf[pl.ds(c * 8, 8), :] = acc
    for c in range(ny // 8):
        rows = pl.ds(c * 8, 8)
        v = ybuf[rows, :]
        acc = None
        for k in range(ntap):
            d = k - r
            if d == 0:
                s = v
            else:
                s = pltpu.roll(v, (-d) % nx, 1)
                keep = (lanes >= -d) if d < 0 else (lanes < nx - d)
                s = jnp.where(keep, s, 0.0)
            term = taps_ref[2 * ntap + k] * s
            acc = term if acc is None else acc + term
        if mode == "ratio":
            store(rows, other_plane(rows) / acc)
        else:
            upd = other_plane(rows) * acc
            store(rows, upd)
            max_ref[rows, :] = jnp.maximum(max_ref[rows, :], upd)


def inner_kernel(mode, width, taps_ref, pad_ref, other_ref, out_ref, *rest):
    if mode == "update":
        max_ref, zbuf, ybuf = rest
        max_ref[...] = jnp.full(max_ref.shape, -jnp.inf, max_ref.dtype)
    else:
        (zbuf, ybuf), max_ref = rest, None
    nz, nx = out_ref.shape[0], out_ref.shape[2]
    lanes = lax.broadcasted_iota(jnp.int32, (8, nx), 1)

    def body(j, carry):
        zo = width + j

        def load(k, rows):
            return pad_ref[j + k, rows, :]

        def store(rows, value):
            out_ref[zo, rows, :] = value

        plane_blur(mode, taps_ref, load, zbuf, ybuf, lanes, store, lambda rows: other_ref[zo, rows, :], max_ref)
        return carry

    lax.fori_loop(0, nz - 2 * width, body, 0)


def edge_kernel(mode, width, taps_ref, below_ref, pad_ref, above_ref, other_ref, volume_in, volume_ref, *rest):
    if mode == "update":
        max_ref, planes, zbuf, ybuf, sems = rest
        max_ref[...] = jnp.full(max_ref.shape, -jnp.inf, max_ref.dtype)
    else:
        (planes, zbuf, ybuf, sems), max_ref = rest, None
    nz, nx = pad_ref.shape[0], pad_ref.shape[2]
    lanes = lax.broadcasted_iota(jnp.int32, (8, nx), 1)
    outs = list(range(width)) + list(range(nz - width, nz))
    for slot, zo in enumerate(outs):

        def load(k, rows, zo=zo):
            q = zo + k
            if q < width:
                return below_ref[q, rows, :]
            if q >= nz + width:
                return above_ref[q - nz - width, rows, :]
            return pad_ref[q - width, rows, :]

        def store(rows, value, slot=slot):
            planes[slot, rows, :] = value

        plane_blur(mode, taps_ref, load, zbuf, ybuf, lanes, store, lambda rows, zo=zo: other_ref[zo, rows, :], max_ref)
    low = pltpu.make_async_copy(planes.at[pl.ds(0, width)], volume_ref.at[pl.ds(0, width)], sems.at[0])
    high = pltpu.make_async_copy(planes.at[pl.ds(width, width)], volume_ref.at[pl.ds(nz - width, width)], sems.at[1])
    low.start()
    high.start()
    low.wait()
    high.wait()


def inner_blur(mode, width, taps, padded, other):
    nz, ny, nx = other.shape
    vmem = pltpu.VMEM
    outs = [jax.ShapeDtypeStruct((nz, ny, nx), jnp.float32)]
    out_specs = [pl.BlockSpec(memory_space=vmem)]
    if mode == "update":
        outs.append(jax.ShapeDtypeStruct((ny, nx), jnp.float32))
        out_specs.append(pl.BlockSpec(memory_space=vmem))
    elems = (nz - 2 * width) * ny * nx
    return pl.pallas_call(
        functools.partial(inner_kernel, mode, width),
        out_shape=tuple(outs),
        in_specs=[pl.BlockSpec(memory_space=pltpu.SMEM), pl.BlockSpec(memory_space=vmem), pl.BlockSpec(memory_space=vmem)],
        out_specs=tuple(out_specs),
        scratch_shapes=[pltpu.VMEM((ny + 8, nx), jnp.float32), pltpu.VMEM((ny, nx), jnp.float32)],
        compiler_params=pltpu.CompilerParams(vmem_limit_bytes=48 * 1024 * 1024),
        cost_estimate=pl.CostEstimate(flops=elems * 60, bytes_accessed=elems * 4 * 4, transcendentals=0),
    )(taps, padded, other)


def edge_blur(mode, width, taps, below, padded, above, other, volume):
    nz, ny, nx = other.shape
    vmem = pltpu.VMEM
    outs = [jax.ShapeDtypeStruct((nz, ny, nx), jnp.float32)]
    out_specs = [pl.BlockSpec(memory_space=pl.ANY)]
    if mode == "update":
        outs.append(jax.ShapeDtypeStruct((ny, nx), jnp.float32))
        out_specs.append(pl.BlockSpec(memory_space=vmem))
    elems = 2 * width * ny * nx
    return pl.pallas_call(
        functools.partial(edge_kernel, mode, width),
        out_shape=tuple(outs),
        in_specs=[pl.BlockSpec(memory_space=pltpu.SMEM)] + [pl.BlockSpec(memory_space=vmem)] * 4 + [pl.BlockSpec(memory_space=pl.ANY)],
        out_specs=tuple(out_specs),
        scratch_shapes=[
            pltpu.VMEM((2 * width, ny, nx), jnp.float32),
            pltpu.VMEM((ny + 8, nx), jnp.float32),
            pltpu.VMEM((ny, nx), jnp.float32),
            pltpu.SemaphoreType.DMA((2,)),
        ],
        input_output_aliases={5: 0},
        compiler_params=pltpu.CompilerParams(vmem_limit_bytes=48 * 1024 * 1024),
        cost_estimate=pl.CostEstimate(flops=elems * 60, bytes_accessed=elems * 4 * 4, transcendentals=0),
    )(taps, below, padded, above, other, volume)


def halo_pair(shard, axis, dim, width):
    peers, length = (lax.axis_size(axis), shard.shape[dim])
    up = [(i, (i + 1) % peers) for i in range(peers - 1)]
    down = [(j, i) for i, j in up]
    last = lax.slice_in_dim(shard, length - width, length, axis=dim)
    first = lax.slice_in_dim(shard, 0, width, axis=dim)
    before = lax.ppermute(last, axis, up)
    after = lax.ppermute(first, axis, down)
    return before, after


def split_blur(mode, taps, shard, other, width):
    before, after = halo_pair(shard, "gy", 1, width)
    rows_padded = jnp.concatenate([before, shard, after], axis=1)
    below, above = halo_pair(rows_padded, "gz", 0, width)
    inner = inner_blur(mode, width, taps, rows_padded, other)
    edges = edge_blur(mode, width, taps, below, rows_padded, above, other, inner[0])
    if mode == "update":
        return edges[0], jnp.maximum(inner[1], edges[1])
    return edges[0]


def butterfly_max(value, axis):
    peers = lax.axis_size(axis)
    step = 1
    while step < peers:
        pairs = [(i, i ^ step) for i in range(peers)]
        value = jnp.maximum(value, lax.ppermute(value, axis, pairs))
        step *= 2
    return value


def per_device(observed, estimate, taps_z, taps_y, taps_x):
    radius = (taps_z.shape[0] - 1) // 2
    forward = jnp.concatenate([taps_z, taps_y, taps_x])
    backward = jnp.concatenate([taps_z[::-1], taps_y[::-1], taps_x[::-1]])
    ratio = split_blur("ratio", forward, estimate, observed, radius)
    updated, local_max = split_blur("update", backward, ratio, estimate, radius)
    projection = butterfly_max(local_max, "gz")
    return (updated, projection)


def solution(mesh):
    return jax.shard_map(
        per_device,
        mesh=mesh,
        in_specs=(P("gz", "gy", None), P("gz", "gy", None), P(), P(), P()),
        out_specs=(P("gz", "gy", None), P("gy", None)),
        check_vma=False,
    )
```

time: 120 us -> 120 us (level); the launches traced: 118 us -> 120 us
  Pallas kernels: 37.8 us -> 42 us
  other arithmetic: 7.4 us -> 3.67 us
  waiting for transfers between devices: 24.7 us -> 27.9 us
  local copies, waits for them, and re-layouts: 6.7 us -> 4.95 us
    pallas_call x4, Pallas kernels: 37.8 us -> 42 us  [the longest x2 29.1 us: inner_blur(): pl.pallas_call(functools.partial(inner_kernel, mode, width), out_shape=tu...]
    ppermute x4, waiting for transfers between devices: 2.26 us -> 6.21 us  [halo_pair(): after = lax.ppermute(first, axis, down)]
    ppermute x4, starting transfers between devices: 21.3 us -> 24.9 us  [halo_pair(): after = lax.ppermute(first, axis, down)]
    concatenate x3 -> x0, other arithmetic: 3.57 us -> none  [the longest x1 2.01 us: split_blur(): jnp.concatenate([edges[0][:width], inner[0], edges[0][width:]], axis=0)]
    ppermute x4, starting transfers between devices: 15.1 us -> 11.5 us  [halo_pair(): before = lax.ppermute(last, axis, up)]
    ppermute x4, waiting for transfers between devices: 13 us -> 10.1 us  [halo_pair(): before = lax.ppermute(last, axis, up)]
    ppermute x3, waiting for transfers between devices: 9.45 us -> 11.6 us  [butterfly_max(): value = jnp.maximum(value, lax.ppermute(value, axis, pairs))]
    slice x3 -> x2, local copies, waits for them, and re-layouts: 2.61 us -> 1.65 us  [halo_pair(): last = lax.slice_in_dim(shard, length - width, length, axis=dim)]
  transfers between devices with their start and end apart: 11 -> 11, of which waited for: 6 -> 6; matrix products, arithmetic and copies ran while one was open for 4% -> 0% of each run, Pallas kernels for 22% -> 24%
where the time goes in v6:
time: 120 us
  Pallas kernels  42 us (35%)
  starting transfers between devices  40.5 us (34%)
  waiting for transfers between devices  27.9 us (23%)
  local copies, waits for them, and re-layouts  4.95 us (4%)
  other arithmetic  3.67 us (3%)
    pallas_call x2, Pallas kernels, inner_blur(): pl.pallas_call(functools.partial(inner_kernel, mode, width), out_shape=tu...  29.1 us
    ppermute x4, starting transfers between devices, halo_pair(): after = lax.ppermute(first, axis, down)  24.9 us
    pallas_call x2, Pallas kernels, edge_blur(): pl.pallas_call(functools.partial(edge_kernel, mode, width), out_shape=tup...  12.9 us
    ppermute x3, waiting for transfers between devices, butterfly_max(): value = jnp.maximum(value, lax.ppermute(value, axis, pairs))  11.6 us
    ppermute x4, starting transfers between devices, halo_pair(): before = lax.ppermute(last, axis, up)  11.5 us
    ppermute x4, waiting for transfers between devices, halo_pair(): before = lax.ppermute(last, axis, up)  10.1 us
    ppermute x4, waiting for transfers between devices, halo_pair(): after = lax.ppermute(first, axis, down)  6.21 us
    ppermute x3, starting transfers between devices, butterfly_max(): value = jnp.maximum(value, lax.ppermute(value, axis, pairs))  4.03 us
  transfers between devices with their start and end apart: 11, of which 6 were waited for; matrix products, arithmetic and copies ran while one was open for 0% of the time, Pallas kernels for 24%

profile of v6, /device:TPU:160, one launch (start us, length us, event | category | flops | bytes accessed | tf_op | source)
XLA Modules:
  0.0 119.9 jit_solution(7053937393751362231)
XLA Ops:
  0.6 1.5 %fusion.3 = (f32[32,4,768]{2,1,0:T(4,128)S(1)}, f32[32,4,768]{2,1,0:T(4,128)S(1)}) fusion(f32[32,32,768]{2,1,0:T(8,128)} %other_ref.7), kind=kLoop, calls=%fused_computation.7 | loop fusion | bytes 1572864 | tf_op jit(solution)/shard_map/slice | solution.py:153
  2.1 1.9 %collective-permute-start = (f32[32,4,768]{2,1,0:T(4,128)S(1)}, f32[32,4,768]{2,1,0:T(4,128)S(1)}, u32[]{:S(2)}, u32[]{:S(2)}) collective-permute-start(f32[32,4,768]{2,1,0:T(4,128)S(1)} %get-tuple-element.16), channel_id=1, source_target_pairs={{0,1},{1,2},{2,3},{3,4},{4,5},{5,6},{6,7},{7,8},{8,9},{9,10},{10,1... | collective-permute-start | bytes 1179656 | tf_op jit(solution)/shard_map/ppermute | solution.py:155
  4.1 0.0 copy-start.3
  4.1 0.0 copy-start.4
  4.1 0.0 copy-start.5
  4.1 8.0 %collective-permute-start.1 = (f32[32,4,768]{2,1,0:T(4,128)S(1)}, f32[32,4,768]{2,1,0:T(4,128)S(1)}, u32[]{:S(2)}, u32[]{:S(2)}) collective-permute-start(f32[32,4,768]{2,1,0:T(4,128)S(1)} %get-tuple-element.17), channel_id=1, source_target_pairs={{1,0},{2,1},{3,2},{4,3},{5,4},{6,5},{7,6},{8,7},{9,8},{10,9},{11,1... | collective-permute-start | bytes 1179656 | tf_op jit(solution)/shard_map/ppermute | solution.py:156
  12.1 5.7 %collective-permute-done = f32[32,4,768]{2,1,0:T(4,128)S(1)} collective-permute-done((f32[32,4,768]{2,1,0:T(4,128)S(1)}, f32[32,4,768]{2,1,0:T(4,128)S(1)}, u32[]{:S(2)}, u32[]{:S(2)}) %collective-permute-start) | collective-permute-done | bytes 393248 | tf_op jit(solution)/shard_map/ppermute | solution.py:155
  17.8 0.0 collective-permute-done.1
  17.8 2.3 %pad_maximum_fusion.pad_ref = f32[32,40,768]{2,1,0:T(8,128)S(1)} fusion(f32[32,4,768]{2,1,0:T(4,128)S(1)} %collective-permute-done.1, f32[32,32,768]{2,1,0:T(8,128)} %other_ref.7, f32[32,4,768]{2,1,0:T(4,128)S(1)} %collective-permute-done), kind=kLoop, calls=%fused_computation | loop fusion | flops 1966080 | bytes 7864320 | tf_op jit(solution)/shard_map/concatenate | solution.py:162
  20.1 0.0 copy-start.2
  20.1 0.1 fusion.1
  20.2 6.7 %collective-permute-start.3 = (f32[4,40,768]{2,1,0:T(8,128)S(1)}, f32[4,40,768]{2,1,0:T(8,128)S(1)}, u32[]{:S(2)}, u32[]{:S(2)}) collective-permute-start(f32[4,40,768]{2,1,0:T(8,128)S(1)} %get-tuple-element.12), channel_id=1, source_target_pairs={{32,0},{64,32},{96,64},{128,96},{160,128},{192,160},{224,192},{33,... | collective-permute-start | bytes 1474568 | tf_op jit(solution)/shard_map/ppermute | solution.py:156
  26.9 2.8 %collective-permute-start.2 = (f32[4,40,768]{2,1,0:T(8,128)S(1)}, f32[4,40,768]{2,1,0:T(8,128)S(1)}, u32[]{:S(2)}, u32[]{:S(2)}) collective-permute-start(f32[4,40,768]{2,1,0:T(8,128)S(1)} %get-tuple-element.13), channel_id=1, source_target_pairs={{0,32},{32,64},{64,96},{96,128},{128,160},{160,192},{192,224},{1,3... | collective-permute-start | bytes 1474568 | tf_op jit(solution)/shard_map/ppermute | solution.py:155
  29.8 0.0 copy-done.3
  29.8 0.0 copy-done.4
  29.8 0.0 copy-done.5
  29.8 0.1 pad_maximum_fusion.3.taps_ref
  29.9 0.0 copy-done.2
  29.9 14.2 %shard_map.68.volume_in = f32[32,32,768]{2,1,0:T(8,128)S(1)} custom-call(f32[27]{0:T(128)S(1)} %pad_maximum_fusion.3.taps_ref, f32[32,40,768]{2,1,0:T(8,128)} %copy-done.2, f32[32,32,768]{2,1,0:T(8,128)} %other_ref.5), custom_call_target="tpu_custom_call" | custom-call | flops 35389440 | bytes 9437184 | tf_op jit(solution)/shard_map/pallas_call | solution.py:112
  44.1 0.0 collective-permute-done.3.above_ref
  44.1 0.0 collective-permute-done.2.below_ref
  44.1 6.6 %shard_map.69 = f32[32,32,768]{2,1,0:T(8,128)S(1)} custom-call(f32[27]{0:T(128)S(1)} %pad_maximum_fusion.3.taps_ref, f32[4,40,768]{2,1,0:T(8,128)S(1)} %collective-permute-done.2.below_ref, f32[32,40,768]{2,1,0:T(8,128)} %copy-done.2, f32[4,40,768]{2,1,0:T(8,128)S(1)} %collective-permute-done.3.above_ref, ...), custom_call_target="tpu_custom_call", output_to_operand_aliasing={{}: (5, {})} | custom-call | flops 11796480 | bytes 3145728 | tf_op jit(solution)/shard_map/pallas_call | solution.py:132
  50.7 0.1 fusion.2
  50.9 1.9 %collective-permute-start.4 = (f32[32,4,768]{2,1,0:T(4,128)S(1)}, f32[32,4,768]{2,1,0:T(4,128)S(1)}, u32[]{:S(2)}, u32[]{:S(2)}) collective-permute-start(f32[32,4,768]{2,1,0:T(4,128)S(1)} %get-tuple-element.14), channel_id=1, source_target_pairs={{0,1},{1,2},{2,3},{3,4},{4,5},{5,6},{6,7},{7,8},{8,9},{9,10},{10,1... | collective-permute-start | bytes 1179656 | tf_op jit(solution)/shard_map/ppermute | solution.py:155
  52.8 0.0 copy-start
  52.8 8.3 %collective-permute-start.5 = (f32[32,4,768]{2,1,0:T(4,128)S(1)}, f32[32,4,768]{2,1,0:T(4,128)S(1)}, u32[]{:S(2)}, u32[]{:S(2)}) collective-permute-start(f32[32,4,768]{2,1,0:T(4,128)S(1)} %get-tuple-element.15), channel_id=1, source_target_pairs={{1,0},{2,1},{3,2},{4,3},{5,4},{6,5},{7,6},{8,7},{9,8},{10,9},{11,1... | collective-permute-start | bytes 1179656 | tf_op jit(solution)/shard_map/ppermute | solution.py:156
  61.2 4.4 %collective-permute-done.4 = f32[32,4,768]{2,1,0:T(4,128)S(1)} collective-permute-done((f32[32,4,768]{2,1,0:T(4,128)S(1)}, f32[32,4,768]{2,1,0:T(4,128)S(1)}, u32[]{:S(2)}, u32[]{:S(2)}) %collective-permute-start.4) | collective-permute-done | bytes 393248 | tf_op jit(solution)/shard_map/ppermute | solution.py:155
  65.6 6.2 %collective-permute-done.5 = f32[32,4,768]{2,1,0:T(4,128)S(1)} collective-permute-done((f32[32,4,768]{2,1,0:T(4,128)S(1)}, f32[32,4,768]{2,1,0:T(4,128)S(1)}, u32[]{:S(2)}, u32[]{:S(2)}) %collective-permute-start.5) | collective-permute-done | bytes 393248 | tf_op jit(solution)/shard_map/ppermute | solution.py:156
  71.8 0.5 pad_maximum_fusion.1.pad_ref
  72.3 0.0 copy-start.1
  72.3 1.9 %copy-done.1 = f32[32,40,768]{2,1,0:T(8,128)} copy-done((f32[32,40,768]{2,1,0:T(8,128)}, f32[32,40,768]{2,1,0:T(8,128)S(1)}, u32[]{:S(2)}) %copy-start.1) | copy-done | bytes 3932184
  74.2 1.1 fusion
  75.2 1.9 %collective-permute-start.7 = (f32[4,40,768]{2,1,0:T(8,128)}, f32[4,40,768]{2,1,0:T(8,128)}, u32[]{:S(2)}, u32[]{:S(2)}) collective-permute-start(f32[4,40,768]{2,1,0:T(8,128)} %get-tuple-element.10), channel_id=1, source_target_pairs={{32,0},{64,32},{96,64},{128,96},{160,128},{192,160},{224,192},{33,... | collective-permute-start | bytes 1474568 | tf_op jit(solution)/shard_map/ppermute | solution.py:156
  77.1 4.8 %collective-permute-start.6 = (f32[4,40,768]{2,1,0:T(8,128)}, f32[4,40,768]{2,1,0:T(8,128)}, u32[]{:S(2)}, u32[]{:S(2)}) collective-permute-start(f32[4,40,768]{2,1,0:T(8,128)} %get-tuple-element.11), channel_id=1, source_target_pairs={{0,32},{32,64},{64,96},{96,128},{128,160},{160,192},{192,224},{1,3... | collective-permute-start | bytes 1474568 | tf_op jit(solution)/shard_map/ppermute | solution.py:155
  82.0 0.1 rev.9
  82.1 0.1 rev.10
  82.1 0.1 rev.11
  82.2 0.1 pad_maximum_fusion.2.taps_ref
  82.3 0.0 copy-done
  82.3 14.9 %shard_map.70 = (f32[32,32,768]{2,1,0:T(8,128)}, f32[32,768]{1,0:T(8,128)S(1)}) custom-call(f32[27]{0:T(128)S(1)} %pad_maximum_fusion.2.taps_ref, f32[32,40,768]{2,1,0:T(8,128)} %copy-done.1, f32[32,32,768]{2,1,0:T(8,128)S(1)} %copy-done), custom_call_target="tpu_custom_call" | custom-call | flops 35389440 | bytes 9437184 | tf_op jit(solution)/shard_map/pallas_call | solution.py:112
  97.2 0.0 collective-permute-done.7.above_ref
  97.2 0.0 collective-permute-done.6.below_ref
  97.2 6.3 %shard_map.71 = (f32[32,32,768]{2,1,0:T(8,128)}, f32[32,768]{1,0:T(8,128)S(1)}) custom-call(f32[27]{0:T(128)S(1)} %pad_maximum_fusion.2.taps_ref, f32[4,40,768]{2,1,0:T(8,128)} %collective-permute-done.6.below_ref, f32[32,40,768]{2,1,0:T(8,128)} %copy-done.1, f32[4,40,768]{2,1,0:T(8,128)} %collective-permute-done.7.above_ref, ...), custom_call_target="tpu_custom_call", output_to_operand_aliasing={{0}: (5, {})} | custom-call | flops 11796480 | bytes 3145728 | tf_op jit(solution)/shard_map/pallas_call | solution.py:132
  103.6 0.1 collective-permute-start.8
  103.7 4.6 %collective-permute-done.8 = f32[32,768]{1,0:T(8,128)S(1)} collective-permute-done((f32[32,768]{1,0:T(8,128)S(1)}, f32[32,768]{1,0:T(8,128)S(1)}, u32[]{:S(2)}, u32[]{:S(2)}) %collective-permute-start.8) | collective-permute-done | bytes 98336 | tf_op jit(solution)/shard_map/ppermute | solution.py:176
  108.3 1.2 %collective-permute-start.9 = (f32[32,768]{1,0:T(8,128)S(1)}, f32[32,768]{1,0:T(8,128)S(1)}, u32[]{:S(2)}, u32[]{:S(2)}) collective-permute-start(f32[32,768]{1,0:T(8,128)S(1)} %max.13), channel_id=1, source_target_pairs={{0,64},{32,96},{64,0},{96,32},{128,192},{160,224},{192,128},{224,1... | collective-permute-start | bytes 294920 | tf_op jit(solution)/shard_map/ppermute | solution.py:176
  109.5 3.5 %collective-permute-done.9 = f32[32,768]{1,0:T(8,128)S(1)} collective-permute-done((f32[32,768]{1,0:T(8,128)S(1)}, f32[32,768]{1,0:T(8,128)S(1)}, u32[]{:S(2)}, u32[]{:S(2)}) %collective-permute-start.9) | collective-permute-done | bytes 98336 | tf_op jit(solution)/shard_map/ppermute | solution.py:176
  113.0 2.7 %collective-permute-start.10 = (f32[32,768]{1,0:T(8,128)S(1)}, f32[32,768]{1,0:T(8,128)S(1)}, u32[]{:S(2)}, u32[]{:S(2)}) collective-permute-start(f32[32,768]{1,0:T(8,128)S(1)} %max.14), channel_id=1, source_target_pairs={{0,128},{32,160},{64,192},{96,224},{128,0},{160,32},{192,64},{224,... | collective-permute-start | bytes 294920 | tf_op jit(solution)/shard_map/ppermute | solution.py:176
  115.7 3.5 %collective-permute-done.10 = f32[32,768]{1,0:T(8,128)S(1)} collective-permute-done((f32[32,768]{1,0:T(8,128)S(1)}, f32[32,768]{1,0:T(8,128)S(1)}, u32[]{:S(2)}, u32[]{:S(2)}) %collective-permute-start.10) | collective-permute-done | bytes 98336 | tf_op jit(solution)/shard_map/ppermute | solution.py:176
  119.2 0.7 max.15
  (3 shorter events, 0.0 us)
Async XLA Ops:
  2.1 15.7 %collective-permute-start = (f32[32,4,768]{2,1,0:T(4,128)S(1)}, f32[32,4,768]{2,1,0:T(4,128)S(1)}, u32[]{:S(2)}, u32[]{:S(2)}) collective-permute-start(f32[32,4,768]{2,1,0:T(4,128)S(1)} %get-tuple-element.16), channel_id=1, source_target_pairs={{0,1},{1,2},{2,3},{3,4},{4,5},{5,6},{6,7},{7,8},{8,9},{9,10},{10,1... | collective-permute-start | bytes 1179656 | tf_op jit(solution)/shard_map/ppermute | solution.py:155
  4.1 25.7 %copy-start.3 = (f32[9]{0:T(128)S(1)}, f32[9]{0:T(128)}, u32[]{:S(2)}) copy-start(f32[9]{0:T(128)} %param.7) | copy-start | bytes 112
  4.1 25.7 %copy-start.4 = (f32[9]{0:T(128)S(1)}, f32[9]{0:T(128)}, u32[]{:S(2)}) copy-start(f32[9]{0:T(128)} %param.8) | copy-start | bytes 112
  4.1 25.7 %copy-start.5 = (f32[9]{0:T(128)S(1)}, f32[9]{0:T(128)}, u32[]{:S(2)}) copy-start(f32[9]{0:T(128)} %param.9) | copy-start | bytes 112
  4.1 13.7 %collective-permute-start.1 = (f32[32,4,768]{2,1,0:T(4,128)S(1)}, f32[32,4,768]{2,1,0:T(4,128)S(1)}, u32[]{:S(2)}, u32[]{:S(2)}) collective-permute-start(f32[32,4,768]{2,1,0:T(4,128)S(1)} %get-tuple-element.17), channel_id=1, source_target_pairs={{1,0},{2,1},{3,2},{4,3},{5,4},{6,5},{7,6},{8,7},{9,8},{10,9},{11,1... | collective-permute-start | bytes 1179656 | tf_op jit(solution)/shard_map/ppermute | solution.py:156
  20.1 9.8 %copy-start.2 = (f32[32,40,768]{2,1,0:T(8,128)}, f32[32,40,768]{2,1,0:T(8,128)S(1)}, u32[]{:S(2)}) copy-start(f32[32,40,768]{2,1,0:T(8,128)S(1)} %pad_maximum_fusion.pad_ref) | copy-start | bytes 11796484
  20.2 23.9 %collective-permute-start.3 = (f32[4,40,768]{2,1,0:T(8,128)S(1)}, f32[4,40,768]{2,1,0:T(8,128)S(1)}, u32[]{:S(2)}, u32[]{:S(2)}) collective-permute-start(f32[4,40,768]{2,1,0:T(8,128)S(1)} %get-tuple-element.12), channel_id=1, source_target_pairs={{32,0},{64,32},{96,64},{128,96},{160,128},{192,160},{224,192},{33,... | collective-permute-start | bytes 1474568 | tf_op jit(solution)/shard_map/ppermute | solution.py:156
  26.9 17.2 %collective-permute-start.2 = (f32[4,40,768]{2,1,0:T(8,128)S(1)}, f32[4,40,768]{2,1,0:T(8,128)S(1)}, u32[]{:S(2)}, u32[]{:S(2)}) collective-permute-start(f32[4,40,768]{2,1,0:T(8,128)S(1)} %get-tuple-element.13), channel_id=1, source_target_pairs={{0,32},{32,64},{64,96},{96,128},{128,160},{160,192},{192,224},{1,3... | collective-permute-start | bytes 1474568 | tf_op jit(solution)/shard_map/ppermute | solution.py:155
  50.9 14.7 %collective-permute-start.4 = (f32[32,4,768]{2,1,0:T(4,128)S(1)}, f32[32,4,768]{2,1,0:T(4,128)S(1)}, u32[]{:S(2)}, u32[]{:S(2)}) collective-permute-start(f32[32,4,768]{2,1,0:T(4,128)S(1)} %get-tuple-element.14), channel_id=1, source_target_pairs={{0,1},{1,2},{2,3},{3,4},{4,5},{5,6},{6,7},{7,8},{8,9},{9,10},{10,1... | collective-permute-start | bytes 1179656 | tf_op jit(solution)/shard_map/ppermute | solution.py:155
  52.8 29.5 %copy-start = (f32[32,32,768]{2,1,0:T(8,128)S(1)}, f32[32,32,768]{2,1,0:T(8,128)}, u32[]{:S(2)}) copy-start(f32[32,32,768]{2,1,0:T(8,128)} %other_ref.7) | copy-start | bytes 9437188
  52.8 19.0 %collective-permute-start.5 = (f32[32,4,768]{2,1,0:T(4,128)S(1)}, f32[32,4,768]{2,1,0:T(4,128)S(1)}, u32[]{:S(2)}, u32[]{:S(2)}) collective-permute-start(f32[32,4,768]{2,1,0:T(4,128)S(1)} %get-tuple-element.15), channel_id=1, source_target_pairs={{1,0},{2,1},{3,2},{4,3},{5,4},{6,5},{7,6},{8,7},{9,8},{10,9},{11,1... | collective-permute-start | bytes 1179656 | tf_op jit(solution)/shard_map/ppermute | solution.py:156
  72.3 1.9 %copy-start.1 = (f32[32,40,768]{2,1,0:T(8,128)}, f32[32,40,768]{2,1,0:T(8,128)S(1)}, u32[]{:S(2)}) copy-start(f32[32,40,768]{2,1,0:T(8,128)S(1)} %pad_maximum_fusion.1.pad_ref) | copy-start | bytes 11796484
  75.2 22.0 %collective-permute-start.7 = (f32[4,40,768]{2,1,0:T(8,128)}, f32[4,40,768]{2,1,0:T(8,128)}, u32[]{:S(2)}, u32[]{:S(2)}) collective-permute-start(f32[4,40,768]{2,1,0:T(8,128)} %get-tuple-element.10), channel_id=1, source_target_pairs={{32,0},{64,32},{96,64},{128,96},{160,128},{192,160},{224,192},{33,... | collective-permute-start | bytes 1474568 | tf_op jit(solution)/shard_map/ppermute | solution.py:156
  77.1 20.1 %collective-permute-start.6 = (f32[4,40,768]{2,1,0:T(8,128)}, f32[4,40,768]{2,1,0:T(8,128)}, u32[]{:S(2)}, u32[]{:S(2)}) collective-permute-start(f32[4,40,768]{2,1,0:T(8,128)} %get-tuple-element.11), channel_id=1, source_target_pairs={{0,32},{32,64},{64,96},{96,128},{128,160},{160,192},{192,224},{1,3... | collective-permute-start | bytes 1474568 | tf_op jit(solution)/shard_map/ppermute | solution.py:155
  103.6 4.7 %collective-permute-start.8 = (f32[32,768]{1,0:T(8,128)S(1)}, f32[32,768]{1,0:T(8,128)S(1)}, u32[]{:S(2)}, u32[]{:S(2)}) collective-permute-start(f32[32,768]{1,0:T(8,128)S(1)} %max.12), channel_id=1, source_target_pairs={{0,32},{32,0},{64,96},{96,64},{128,160},{160,128},{192,224},{224,1... | collective-permute-start | bytes 294920 | tf_op jit(solution)/shard_map/ppermute | solution.py:176
  108.3 4.7 %collective-permute-start.9 = (f32[32,768]{1,0:T(8,128)S(1)}, f32[32,768]{1,0:T(8,128)S(1)}, u32[]{:S(2)}, u32[]{:S(2)}) collective-permute-start(f32[32,768]{1,0:T(8,128)S(1)} %max.13), channel_id=1, source_target_pairs={{0,64},{32,96},{64,0},{96,32},{128,192},{160,224},{192,128},{224,1... | collective-permute-start | bytes 294920 | tf_op jit(solution)/shard_map/ppermute | solution.py:176
  113.0 6.2 %collective-permute-start.10 = (f32[32,768]{1,0:T(8,128)S(1)}, f32[32,768]{1,0:T(8,128)S(1)}, u32[]{:S(2)}, u32[]{:S(2)}) collective-permute-start(f32[32,768]{1,0:T(8,128)S(1)} %max.14), channel_id=1, source_target_pairs={{0,128},{32,160},{64,192},{96,224},{128,0},{160,32},{192,64},{224,... | collective-permute-start | bytes 294920 | tf_op jit(solution)/shard_map/ppermute | solution.py:176

commit v7 on v6

--- a/solution.py
+++ b/solution.py
@@ -158,11 +158,22 @@
 
 
 def split_blur(mode, taps, shard, other, width):
+    ny = shard.shape[1]
     before, after = halo_pair(shard, "gy", 1, width)
+    below, above = halo_pair(shard, "gz", 0, width)
     rows_padded = jnp.concatenate([before, shard, after], axis=1)
-    below, above = halo_pair(rows_padded, "gz", 0, width)
     inner = inner_blur(mode, width, taps, rows_padded, other)
-    edges = edge_blur(mode, width, taps, below, rows_padded, above, other, inner[0])
+    below, above, inner = lax.optimization_barrier((below, above, inner))
+    gy_size = lax.axis_size("gy")
+    up = [(i, i + 1) for i in range(gy_size - 1)]
+    down = [(i + 1, i) for i in range(gy_size - 1)]
+    last_rows = jnp.concatenate([below[:, ny - width :], above[:, ny - width :]], axis=0)
+    first_rows = jnp.concatenate([below[:, :width], above[:, :width]], axis=0)
+    corner_before = lax.ppermute(last_rows, "gy", up)
+    corner_after = lax.ppermute(first_rows, "gy", down)
+    below_padded = jnp.concatenate([corner_before[:width], below, corner_after[:width]], axis=1)
+    above_padded = jnp.concatenate([corner_before[width:], above, corner_after[width:]], axis=1)
+    edges = edge_blur(mode, width, taps, below_padded, rows_padded, above_padded, other, inner[0])
     if mode == "update":
         return edges[0], jnp.maximum(inner[1], edges[1])
     return edges[0]

time: 120 us -> 150 us (1.25)
  starting transfers between devices: 40.5 us -> 57.7 us
  other arithmetic: 3.67 us -> 9.65 us
  waiting for transfers between devices: 27.9 us -> 33.5 us
    ppermute x0 -> x4, starting transfers between devices: none -> 19.9 us  [the longest x2 16.1 us: split_blur(): corner_after = lax.ppermute(first_rows, 'gy', down)]
    ppermute x0 -> x4, waiting for transfers between devices: none -> 16.5 us  [the longest x2 16.1 us: split_blur(): corner_before = lax.ppermute(last_rows, 'gy', up)]
    ppermute x4, waiting for transfers between devices: 10.1 us -> 0.01 us  [halo_pair(): before = lax.ppermute(last, axis, up)]
    ppermute x4, starting transfers between devices: 24.9 us -> 20.5 us  [halo_pair(): after = lax.ppermute(first, axis, down)]
    concatenate x2, other arithmetic: 2.83 us -> 6.77 us  [split_blur(): rows_padded = jnp.concatenate([before, shard, after], axis=1)]
    unnamed x12 -> x10, local copies, waits for them, and re-layouts: 1.89 us -> 0.03 us
  transfers between devices with their start and end apart: 11 -> 15, of which waited for: 6 -> 9; matrix products, arithmetic and copies ran while one was open for 0% -> 7% of each run, Pallas kernels for 24% -> 19%
where the time goes in v7:
time: 150 us
  starting transfers between devices  57.7 us (38%)
  Pallas kernels  41.7 us (28%)
  waiting for transfers between devices  33.5 us (22%)
  other arithmetic  9.65 us (6%)
  local copies, waits for them, and re-layouts  6.37 us (4%)
    pallas_call x2, Pallas kernels, inner_blur(): pl.pallas_call(functools.partial(inner_kernel, mode, width), out_shape=tu...  29.1 us
    ppermute x4, starting transfers between devices, halo_pair(): after = lax.ppermute(first, axis, down)  20.5 us
    ppermute x2, waiting for transfers between devices, split_blur(): corner_before = lax.ppermute(last_rows, 'gy', up)  16.1 us
    ppermute x2, starting transfers between devices, split_blur(): corner_after = lax.ppermute(first_rows, 'gy', down)  16.1 us
    pallas_call x2, Pallas kernels, edge_blur(): pl.pallas_call(functools.partial(edge_kernel, mode, width), out_shape=tup...  12.6 us
    ppermute x4, starting transfers between devices, halo_pair(): before = lax.ppermute(last, axis, up)  12.5 us
    ppermute x3, waiting for transfers between devices, butterfly_max(): value = jnp.maximum(value, lax.ppermute(value, axis, pairs))  10.8 us
    concatenate x2, other arithmetic, split_blur(): rows_padded = jnp.concatenate([before, shard, after], axis=1)  6.77 us
  transfers between devices with their start and end apart: 15, of which 9 were waited for; matrix products, arithmetic and copies ran while one was open for 7% of the time, Pallas kernels for 19%

profile of v7, /device:TPU:160, one launch (start us, length us, event | category | flops | bytes accessed | tf_op | source)
XLA Modules:
  0.0 149.9 jit_solution(14618382943641126243)
XLA Ops:
  0.6 0.0 copy-start
  0.6 1.7 %fusion.2 = (f32[32,4,768]{2,1,0:T(4,128)S(1)}, f32[32,4,768]{2,1,0:T(4,128)S(1)}) fusion(f32[32,32,768]{2,1,0:T(8,128)} %other_ref.7), kind=kLoop, calls=%fused_computation.14 | loop fusion | bytes 1572864 | tf_op jit(solution)/shard_map/slice | solution.py:153
  2.3 1.9 %collective-permute-start.2 = (f32[32,4,768]{2,1,0:T(4,128)S(1)}, f32[32,4,768]{2,1,0:T(4,128)S(1)}, u32[]{:S(2)}, u32[]{:S(2)}) collective-permute-start(f32[32,4,768]{2,1,0:T(4,128)S(1)} %get-tuple-element.28), channel_id=1, source_target_pairs={{0,1},{1,2},{2,3},{3,4},{4,5},{5,6},{6,7},{7,8},{8,9},{9,10},{10,1... | collective-permute-start | bytes 1179656 | tf_op jit(solution)/shard_map/ppermute | solution.py:155
  4.2 7.9 %collective-permute-start.3 = (f32[32,4,768]{2,1,0:T(4,128)S(1)}, f32[32,4,768]{2,1,0:T(4,128)S(1)}, u32[]{:S(2)}, u32[]{:S(2)}) collective-permute-start(f32[32,4,768]{2,1,0:T(4,128)S(1)} %get-tuple-element.29), channel_id=1, source_target_pairs={{1,0},{2,1},{3,2},{4,3},{5,4},{6,5},{7,6},{8,7},{9,8},{10,9},{11,1... | collective-permute-start | bytes 1179656 | tf_op jit(solution)/shard_map/ppermute | solution.py:156
  12.1 1.2 fusion.3
  13.3 2.9 %collective-permute-start.1 = (f32[4,32,768]{2,1,0:T(8,128)S(1)}, f32[4,32,768]{2,1,0:T(8,128)S(1)}, u32[]{:S(2)}, u32[]{:S(2)}) collective-permute-start(f32[4,32,768]{2,1,0:T(8,128)S(1)} %get-tuple-element.30), channel_id=1, source_target_pairs={{32,0},{64,32},{96,64},{128,96},{160,128},{192,160},{224,192},{33,... | collective-permute-start | bytes 1179656 | tf_op jit(solution)/shard_map/ppermute | solution.py:156
  16.2 3.8 %collective-permute-start = (f32[4,32,768]{2,1,0:T(8,128)S(1)}, f32[4,32,768]{2,1,0:T(8,128)S(1)}, u32[]{:S(2)}, u32[]{:S(2)}) collective-permute-start(f32[4,32,768]{2,1,0:T(8,128)S(1)} %get-tuple-element.31), channel_id=1, source_target_pairs={{0,32},{32,64},{64,96},{96,128},{128,160},{160,192},{192,224},{1,3... | collective-permute-start | bytes 1179656 | tf_op jit(solution)/shard_map/ppermute | solution.py:155
  20.0 0.8 pad_maximum_fusion.11.taps_ref
  20.8 0.0 collective-permute-done.2
  20.8 4.4 %collective-permute-done.3 = f32[32,4,768]{2,1,0:T(4,128)S(1)} collective-permute-done((f32[32,4,768]{2,1,0:T(4,128)S(1)}, f32[32,4,768]{2,1,0:T(4,128)S(1)}, u32[]{:S(2)}, u32[]{:S(2)}) %collective-permute-start.3) | collective-permute-done | bytes 393248 | tf_op jit(solution)/shard_map/ppermute | solution.py:156
  25.2 0.0 copy-done
  25.2 2.4 %pad_maximum_fusion.pad_ref = f32[32,40,768]{2,1,0:T(8,128)} fusion(f32[32,4,768]{2,1,0:T(4,128)S(1)} %collective-permute-done.3, f32[32,32,768]{2,1,0:T(8,128)S(1)} %copy-done, f32[32,4,768]{2,1,0:T(4,128)S(1)} %collective-permute-done.2), kind=kLoop, calls=%fused_computation | loop fusion | flops 1966080 | bytes 7864320 | tf_op jit(solution)/shard_map/concatenate | solution.py:164
  27.6 14.2 %shard_map.68.volume_in = f32[32,32,768]{2,1,0:T(8,128)S(1)} custom-call(f32[27]{0:T(128)S(1)} %pad_maximum_fusion.11.taps_ref, f32[32,40,768]{2,1,0:T(8,128)} %pad_maximum_fusion.pad_ref, f32[32,32,768]{2,1,0:T(8,128)} %other_ref.5), custom_call_target="tpu_custom_call" | custom-call | flops 35389440 | bytes 9437184 | tf_op jit(solution)/shard_map/pallas_call | solution.py:112
  41.8 0.0 collective-permute-done.1
  41.9 0.0 collective-permute-done
  41.9 8.0 %collective-permute-start.5 = (f32[8,4,768]{2,1,0:T(4,128)S(1)}, f32[8,4,768]{2,1,0:T(4,128)S(1)}, u32[]{:S(2)}, u32[]{:S(2)}) collective-permute-start(f32[8,4,768]{2,1,0:T(4,128)S(1)} %pad_maximum_fusion.7), channel_id=1, source_target_pairs={{1,0},{2,1},{3,2},{4,3},{5,4},{6,5},{7,6},{8,7},{9,8},{10,9},{11,1... | collective-permute-start | bytes 294920 | tf_op jit(solution)/shard_map/ppermute | solution.py:173
  50.0 1.9 %collective-permute-start.4 = (f32[8,4,768]{2,1,0:T(4,128)S(1)}, f32[8,4,768]{2,1,0:T(4,128)S(1)}, u32[]{:S(2)}, u32[]{:S(2)}) collective-permute-start(f32[8,4,768]{2,1,0:T(4,128)S(1)} %pad_maximum_fusion.6), channel_id=1, source_target_pairs={{0,1},{1,2},{2,3},{3,4},{4,5},{5,6},{6,7},{7,8},{8,9},{9,10},{10,1... | collective-permute-start | bytes 294920 | tf_op jit(solution)/shard_map/ppermute | solution.py:172
  52.0 0.2 collective-permute-done.5
  52.2 8.0 %collective-permute-done.4 = f32[8,4,768]{2,1,0:T(4,128)S(1)} collective-permute-done((f32[8,4,768]{2,1,0:T(4,128)S(1)}, f32[8,4,768]{2,1,0:T(4,128)S(1)}, u32[]{:S(2)}, u32[]{:S(2)}) %collective-permute-start.4) | collective-permute-done | bytes 98336 | tf_op jit(solution)/shard_map/ppermute | solution.py:172
  60.2 0.1 pad_maximum_fusion.2
  60.3 0.0 copy-start.2
  60.3 0.0 copy-start.3
  60.3 0.0 copy-start.4
  60.4 6.6 %shard_map.69 = f32[32,32,768]{2,1,0:T(8,128)S(1)} custom-call(f32[27]{0:T(128)S(1)} %pad_maximum_fusion.11.taps_ref, f32[4,40,768]{2,1,0:T(8,128)S(1)} %get-tuple-element.48.below_ref, f32[32,40,768]{2,1,0:T(8,128)} %pad_maximum_fusion.pad_ref, f32[4,40,768]{2,1,0:T(8,128)S(1)} %get-tuple-element.49.above_ref, ...), custom_call_target="tpu_custom_call", output_to_operand_aliasing={{}: (5, {})} | custom-call | flops 11796480 | bytes 3145728 | tf_op jit(solution)/shard_map/pallas_call | solution.py:132
  66.9 0.0 copy-start.1
  66.9 1.2 fusion
  68.1 1.9 %collective-permute-start.8 = (f32[32,4,768]{2,1,0:T(4,128)}, f32[32,4,768]{2,1,0:T(4,128)}, u32[]{:S(2)}, u32[]{:S(2)}) collective-permute-start(f32[32,4,768]{2,1,0:T(4,128)} %get-tuple-element.24), channel_id=1, source_target_pairs={{0,1},{1,2},{2,3},{3,4},{4,5},{5,6},{6,7},{7,8},{8,9},{9,10},{10,1... | collective-permute-start | bytes 1179656 | tf_op jit(solution)/shard_map/ppermute | solution.py:155
  70.1 7.9 %collective-permute-start.9 = (f32[32,4,768]{2,1,0:T(4,128)}, f32[32,4,768]{2,1,0:T(4,128)}, u32[]{:S(2)}, u32[]{:S(2)}) collective-permute-start(f32[32,4,768]{2,1,0:T(4,128)} %get-tuple-element.25), channel_id=1, source_target_pairs={{1,0},{2,1},{3,2},{4,3},{5,4},{6,5},{7,6},{8,7},{9,8},{10,9},{11,1... | collective-permute-start | bytes 1179656 | tf_op jit(solution)/shard_map/ppermute | solution.py:156
  77.9 0.0 copy-done.1
  77.9 1.0 fusion.1
  78.9 1.9 %collective-permute-start.7 = (f32[4,32,768]{2,1,0:T(8,128)}, f32[4,32,768]{2,1,0:T(8,128)}, u32[]{:S(2)}, u32[]{:S(2)}) collective-permute-start(f32[4,32,768]{2,1,0:T(8,128)} %get-tuple-element.26), channel_id=1, source_target_pairs={{32,0},{64,32},{96,64},{128,96},{160,128},{192,160},{224,192},{33,... | collective-permute-start | bytes 1179656 | tf_op jit(solution)/shard_map/ppermute | solution.py:156
  80.8 4.8 %collective-permute-start.6 = (f32[4,32,768]{2,1,0:T(8,128)}, f32[4,32,768]{2,1,0:T(8,128)S(1)}, u32[]{:S(2)}, u32[]{:S(2)}) collective-permute-start(f32[4,32,768]{2,1,0:T(8,128)} %get-tuple-element.27), channel_id=1, source_target_pairs={{0,32},{32,64},{64,96},{96,128},{128,160},{160,192},{192,224},{1,3... | collective-permute-start | bytes 1179656 | tf_op jit(solution)/shard_map/ppermute | solution.py:155
  85.6 0.0 copy-done.2
  85.6 0.1 rev.9
  85.7 0.0 copy-done.3
  85.7 0.1 rev.10
  85.8 0.0 copy-done.4
  85.8 0.1 rev.11
  85.9 0.1 pad_maximum_fusion.10.taps_ref
  86.0 0.0 collective-permute-done.8
  86.0 1.7 %collective-permute-done.9 = f32[32,4,768]{2,1,0:T(4,128)} collective-permute-done((f32[32,4,768]{2,1,0:T(4,128)}, f32[32,4,768]{2,1,0:T(4,128)}, u32[]{:S(2)}, u32[]{:S(2)}) %collective-permute-start.9) | collective-permute-done | bytes 393248 | tf_op jit(solution)/shard_map/ppermute | solution.py:156
  87.7 4.4 %pad_maximum_fusion.1.pad_ref = f32[32,40,768]{2,1,0:T(8,128)} fusion(f32[32,4,768]{2,1,0:T(4,128)} %collective-permute-done.9, f32[32,32,768]{2,1,0:T(8,128)} %copy-done.1, f32[32,4,768]{2,1,0:T(4,128)} %collective-permute-done.8), kind=kLoop, calls=%fused_computation.1 | loop fusion | flops 1966080 | bytes 7864320 | tf_op jit(solution)/shard_map/concatenate | solution.py:164
  92.1 14.9 %shard_map.70 = (f32[32,32,768]{2,1,0:T(8,128)}, f32[32,768]{1,0:T(8,128)S(1)}) custom-call(f32[27]{0:T(128)S(1)} %pad_maximum_fusion.10.taps_ref, f32[32,40,768]{2,1,0:T(8,128)} %pad_maximum_fusion.1.pad_ref, f32[32,32,768]{2,1,0:T(8,128)S(1)} %copy-done), custom_call_target="tpu_custom_call" | custom-call | flops 35389440 | bytes 9437184 | tf_op jit(solution)/shard_map/pallas_call | solution.py:112
  107.0 0.0 collective-permute-done.7
  107.0 0.0 collective-permute-done.6
  107.0 1.0 fusion.5
  108.0 8.0 %collective-permute-start.11 = (f32[8,4,768]{2,1,0:T(4,128)S(1)}, f32[8,4,768]{2,1,0:T(4,128)S(1)}, u32[]{:S(2)}, u32[]{:S(2)}) collective-permute-start(f32[8,4,768]{2,1,0:T(4,128)S(1)} %pad_maximum_fusion.9), channel_id=1, source_target_pairs={{1,0},{2,1},{3,2},{4,3},{5,4},{6,5},{7,6},{8,7},{9,8},{10,9},{11,1... | collective-permute-start | bytes 294920 | tf_op jit(solution)/shard_map/ppermute | solution.py:173
  116.1 1.9 %collective-permute-start.10 = (f32[8,4,768]{2,1,0:T(4,128)S(1)}, f32[8,4,768]{2,1,0:T(4,128)S(1)}, u32[]{:S(2)}, u32[]{:S(2)}) collective-permute-start(f32[8,4,768]{2,1,0:T(4,128)S(1)} %pad_maximum_fusion.8), channel_id=1, source_target_pairs={{0,1},{1,2},{2,3},{3,4},{4,5},{5,6},{6,7},{7,8},{8,9},{9,10},{10,1... | collective-permute-start | bytes 294920 | tf_op jit(solution)/shard_map/ppermute | solution.py:172
  118.0 0.2 collective-permute-done.11
  118.2 8.1 %collective-permute-done.10 = f32[8,4,768]{2,1,0:T(4,128)S(1)} collective-permute-done((f32[8,4,768]{2,1,0:T(4,128)S(1)}, f32[8,4,768]{2,1,0:T(4,128)S(1)}, u32[]{:S(2)}, u32[]{:S(2)}) %collective-permute-start.10) | collective-permute-done | bytes 98336 | tf_op jit(solution)/shard_map/ppermute | solution.py:172
  126.3 1.1 pad_maximum_fusion.5.above_ref
  127.4 0.1 pad_maximum_fusion.4.below_ref
  127.5 6.1 %shard_map.71 = (f32[32,32,768]{2,1,0:T(8,128)}, f32[32,768]{1,0:T(8,128)S(1)}) custom-call(f32[27]{0:T(128)S(1)} %pad_maximum_fusion.10.taps_ref, f32[4,40,768]{2,1,0:T(8,128)S(1)} %pad_maximum_fusion.4.below_ref, f32[32,40,768]{2,1,0:T(8,128)} %pad_maximum_fusion.1.pad_ref, ...), custom_call_target="tpu_custom_call", output_to_operand_aliasing={{0}: (5, {})} | custom-call | flops 11796480 | bytes 3145728 | tf_op jit(solution)/shard_map/pallas_call | solution.py:132
  133.6 0.1 collective-permute-start.12
  133.7 4.6 %collective-permute-done.12 = f32[32,768]{1,0:T(8,128)S(1)} collective-permute-done((f32[32,768]{1,0:T(8,128)S(1)}, f32[32,768]{1,0:T(8,128)S(1)}, u32[]{:S(2)}, u32[]{:S(2)}) %collective-permute-start.12) | collective-permute-done | bytes 98336 | tf_op jit(solution)/shard_map/ppermute | solution.py:187
  138.3 1.6 %collective-permute-start.13 = (f32[32,768]{1,0:T(8,128)S(1)}, f32[32,768]{1,0:T(8,128)S(1)}, u32[]{:S(2)}, u32[]{:S(2)}) collective-permute-start(f32[32,768]{1,0:T(8,128)S(1)} %max.13), channel_id=1, source_target_pairs={{0,64},{32,96},{64,0},{96,32},{128,192},{160,224},{192,128},{224,1... | collective-permute-start | bytes 294920 | tf_op jit(solution)/shard_map/ppermute | solution.py:187
  139.9 3.1 %collective-permute-done.13 = f32[32,768]{1,0:T(8,128)S(1)} collective-permute-done((f32[32,768]{1,0:T(8,128)S(1)}, f32[32,768]{1,0:T(8,128)S(1)}, u32[]{:S(2)}, u32[]{:S(2)}) %collective-permute-start.13) | collective-permute-done | bytes 98336 | tf_op jit(solution)/shard_map/ppermute | solution.py:187
  143.0 3.1 %collective-permute-start.14 = (f32[32,768]{1,0:T(8,128)S(1)}, f32[32,768]{1,0:T(8,128)S(1)}, u32[]{:S(2)}, u32[]{:S(2)}) collective-permute-start(f32[32,768]{1,0:T(8,128)S(1)} %max.14), channel_id=1, source_target_pairs={{0,128},{32,160},{64,192},{96,224},{128,0},{160,32},{192,64},{224,... | collective-permute-start | bytes 294920 | tf_op jit(solution)/shard_map/ppermute | solution.py:187
  146.1 3.1 %collective-permute-done.14 = f32[32,768]{1,0:T(8,128)S(1)} collective-permute-done((f32[32,768]{1,0:T(8,128)S(1)}, f32[32,768]{1,0:T(8,128)S(1)}, u32[]{:S(2)}, u32[]{:S(2)}) %collective-permute-start.14) | collective-permute-done | bytes 98336 | tf_op jit(solution)/shard_map/ppermute | solution.py:187
  149.2 0.7 max.15
  (14 shorter events, 0.2 us)
Async XLA Ops:
  0.6 24.6 %copy-start = (f32[32,32,768]{2,1,0:T(8,128)S(1)}, f32[32,32,768]{2,1,0:T(8,128)}, u32[]{:S(2)}) copy-start(f32[32,32,768]{2,1,0:T(8,128)} %other_ref.7) | copy-start | bytes 9437188
  2.3 18.5 %collective-permute-start.2 = (f32[32,4,768]{2,1,0:T(4,128)S(1)}, f32[32,4,768]{2,1,0:T(4,128)S(1)}, u32[]{:S(2)}, u32[]{:S(2)}) collective-permute-start(f32[32,4,768]{2,1,0:T(4,128)S(1)} %get-tuple-element.28), channel_id=1, source_target_pairs={{0,1},{1,2},{2,3},{3,4},{4,5},{5,6},{6,7},{7,8},{8,9},{9,10},{10,1... | collective-permute-start | bytes 1179656 | tf_op jit(solution)/shard_map/ppermute | solution.py:155
  4.2 21.0 %collective-permute-start.3 = (f32[32,4,768]{2,1,0:T(4,128)S(1)}, f32[32,4,768]{2,1,0:T(4,128)S(1)}, u32[]{:S(2)}, u32[]{:S(2)}) collective-permute-start(f32[32,4,768]{2,1,0:T(4,128)S(1)} %get-tuple-element.29), channel_id=1, source_target_pairs={{1,0},{2,1},{3,2},{4,3},{5,4},{6,5},{7,6},{8,7},{9,8},{10,9},{11,1... | collective-permute-start | bytes 1179656 | tf_op jit(solution)/shard_map/ppermute | solution.py:156
  13.3 28.6 %collective-permute-start.1 = (f32[4,32,768]{2,1,0:T(8,128)S(1)}, f32[4,32,768]{2,1,0:T(8,128)S(1)}, u32[]{:S(2)}, u32[]{:S(2)}) collective-permute-start(f32[4,32,768]{2,1,0:T(8,128)S(1)} %get-tuple-element.30), channel_id=1, source_target_pairs={{32,0},{64,32},{96,64},{128,96},{160,128},{192,160},{224,192},{33,... | collective-permute-start | bytes 1179656 | tf_op jit(solution)/shard_map/ppermute | solution.py:156
  16.2 25.6 %collective-permute-start = (f32[4,32,768]{2,1,0:T(8,128)S(1)}, f32[4,32,768]{2,1,0:T(8,128)S(1)}, u32[]{:S(2)}, u32[]{:S(2)}) collective-permute-start(f32[4,32,768]{2,1,0:T(8,128)S(1)} %get-tuple-element.31), channel_id=1, source_target_pairs={{0,32},{32,64},{64,96},{96,128},{128,160},{160,192},{192,224},{1,3... | collective-permute-start | bytes 1179656 | tf_op jit(solution)/shard_map/ppermute | solution.py:155
  41.9 10.2 %collective-permute-start.5 = (f32[8,4,768]{2,1,0:T(4,128)S(1)}, f32[8,4,768]{2,1,0:T(4,128)S(1)}, u32[]{:S(2)}, u32[]{:S(2)}) collective-permute-start(f32[8,4,768]{2,1,0:T(4,128)S(1)} %pad_maximum_fusion.7), channel_id=1, source_target_pairs={{1,0},{2,1},{3,2},{4,3},{5,4},{6,5},{7,6},{8,7},{9,8},{10,9},{11,1... | collective-permute-start | bytes 294920 | tf_op jit(solution)/shard_map/ppermute | solution.py:173
  50.0 10.2 %collective-permute-start.4 = (f32[8,4,768]{2,1,0:T(4,128)S(1)}, f32[8,4,768]{2,1,0:T(4,128)S(1)}, u32[]{:S(2)}, u32[]{:S(2)}) collective-permute-start(f32[8,4,768]{2,1,0:T(4,128)S(1)} %pad_maximum_fusion.6), channel_id=1, source_target_pairs={{0,1},{1,2},{2,3},{3,4},{4,5},{5,6},{6,7},{7,8},{8,9},{9,10},{10,1... | collective-permute-start | bytes 294920 | tf_op jit(solution)/shard_map/ppermute | solution.py:172
  60.3 25.3 %copy-start.2 = (f32[9]{0:T(128)S(1)}, f32[9]{0:T(128)}, u32[]{:S(2)}) copy-start(f32[9]{0:T(128)} %param.7) | copy-start | bytes 112
  60.3 25.4 %copy-start.3 = (f32[9]{0:T(128)S(1)}, f32[9]{0:T(128)}, u32[]{:S(2)}) copy-start(f32[9]{0:T(128)} %param.8) | copy-start | bytes 112
  60.3 25.5 %copy-start.4 = (f32[9]{0:T(128)S(1)}, f32[9]{0:T(128)}, u32[]{:S(2)}) copy-start(f32[9]{0:T(128)} %param.9) | copy-start | bytes 112
  66.9 11.0 %copy-start.1 = (f32[32,32,768]{2,1,0:T(8,128)}, f32[32,32,768]{2,1,0:T(8,128)S(1)}, u32[]{:S(2)}) copy-start(f32[32,32,768]{2,1,0:T(8,128)S(1)} %shard_map.69) | copy-start | bytes 9437188
  68.1 17.9 %collective-permute-start.8 = (f32[32,4,768]{2,1,0:T(4,128)}, f32[32,4,768]{2,1,0:T(4,128)}, u32[]{:S(2)}, u32[]{:S(2)}) collective-permute-start(f32[32,4,768]{2,1,0:T(4,128)} %get-tuple-element.24), channel_id=1, source_target_pairs={{0,1},{1,2},{2,3},{3,4},{4,5},{5,6},{6,7},{7,8},{8,9},{9,10},{10,1... | collective-permute-start | bytes 1179656 | tf_op jit(solution)/shard_map/ppermute | solution.py:155
  70.1 17.7 %collective-permute-start.9 = (f32[32,4,768]{2,1,0:T(4,128)}, f32[32,4,768]{2,1,0:T(4,128)}, u32[]{:S(2)}, u32[]{:S(2)}) collective-permute-start(f32[32,4,768]{2,1,0:T(4,128)} %get-tuple-element.25), channel_id=1, source_target_pairs={{1,0},{2,1},{3,2},{4,3},{5,4},{6,5},{7,6},{8,7},{9,8},{10,9},{11,1... | collective-permute-start | bytes 1179656 | tf_op jit(solution)/shard_map/ppermute | solution.py:156
  78.9 28.1 %collective-permute-start.7 = (f32[4,32,768]{2,1,0:T(8,128)}, f32[4,32,768]{2,1,0:T(8,128)}, u32[]{:S(2)}, u32[]{:S(2)}) collective-permute-start(f32[4,32,768]{2,1,0:T(8,128)} %get-tuple-element.26), channel_id=1, source_target_pairs={{32,0},{64,32},{96,64},{128,96},{160,128},{192,160},{224,192},{33,... | collective-permute-start | bytes 1179656 | tf_op jit(solution)/shard_map/ppermute | solution.py:156
  80.8 26.2 %collective-permute-start.6 = (f32[4,32,768]{2,1,0:T(8,128)}, f32[4,32,768]{2,1,0:T(8,128)S(1)}, u32[]{:S(2)}, u32[]{:S(2)}) collective-permute-start(f32[4,32,768]{2,1,0:T(8,128)} %get-tuple-element.27), channel_id=1, source_target_pairs={{0,32},{32,64},{64,96},{96,128},{128,160},{160,192},{192,224},{1,3... | collective-permute-start | bytes 1179656 | tf_op jit(solution)/shard_map/ppermute | solution.py:155
  108.0 10.2 %collective-permute-start.11 = (f32[8,4,768]{2,1,0:T(4,128)S(1)}, f32[8,4,768]{2,1,0:T(4,128)S(1)}, u32[]{:S(2)}, u32[]{:S(2)}) collective-permute-start(f32[8,4,768]{2,1,0:T(4,128)S(1)} %pad_maximum_fusion.9), channel_id=1, source_target_pairs={{1,0},{2,1},{3,2},{4,3},{5,4},{6,5},{7,6},{8,7},{9,8},{10,9},{11,1... | collective-permute-start | bytes 294920 | tf_op jit(solution)/shard_map/ppermute | solution.py:173
  116.1 10.3 %collective-permute-start.10 = (f32[8,4,768]{2,1,0:T(4,128)S(1)}, f32[8,4,768]{2,1,0:T(4,128)S(1)}, u32[]{:S(2)}, u32[]{:S(2)}) collective-permute-start(f32[8,4,768]{2,1,0:T(4,128)S(1)} %pad_maximum_fusion.8), channel_id=1, source_target_pairs={{0,1},{1,2},{2,3},{3,4},{4,5},{5,6},{6,7},{7,8},{8,9},{9,10},{10,1... | collective-permute-start | bytes 294920 | tf_op jit(solution)/shard_map/ppermute | solution.py:172
  133.6 4.7 %collective-permute-start.12 = (f32[32,768]{1,0:T(8,128)S(1)}, f32[32,768]{1,0:T(8,128)S(1)}, u32[]{:S(2)}, u32[]{:S(2)}) collective-permute-start(f32[32,768]{1,0:T(8,128)S(1)} %max.12), channel_id=1, source_target_pairs={{0,32},{32,0},{64,96},{96,64},{128,160},{160,128},{192,224},{224,1... | collective-permute-start | bytes 294920 | tf_op jit(solution)/shard_map/ppermute | solution.py:187
  138.3 4.7 %collective-permute-start.13 = (f32[32,768]{1,0:T(8,128)S(1)}, f32[32,768]{1,0:T(8,128)S(1)}, u32[]{:S(2)}, u32[]{:S(2)}) collective-permute-start(f32[32,768]{1,0:T(8,128)S(1)} %max.13), channel_id=1, source_target_pairs={{0,64},{32,96},{64,0},{96,32},{128,192},{160,224},{192,128},{224,1... | collective-permute-start | bytes 294920 | tf_op jit(solution)/shard_map/ppermute | solution.py:187
  143.0 6.2 %collective-permute-start.14 = (f32[32,768]{1,0:T(8,128)S(1)}, f32[32,768]{1,0:T(8,128)S(1)}, u32[]{:S(2)}, u32[]{:S(2)}) collective-permute-start(f32[32,768]{1,0:T(8,128)S(1)} %max.14), channel_id=1, source_target_pairs={{0,128},{32,160},{64,192},{96,224},{128,0},{160,32},{192,64},{224,... | collective-permute-start | bytes 294920 | tf_op jit(solution)/shard_map/ppermute | solution.py:187

commit v8 on v6

--- a/solution.py
+++ b/solution.py
@@ -7,23 +7,26 @@
 from jax.experimental.pallas import tpu as pltpu
 
 
-def plane_blur(mode, taps_ref, load, zbuf, ybuf, lanes, store, other_plane, max_ref):
+def plane_blur(mode, taps_ref, load, zbuf, ybuf, lanes, store, other_plane, max_ref, out_chunks=None):
     ntap = 9
     r = 4
     ny, nx = ybuf.shape
     py = ny + 2 * r
-    for c in range(py // 8):
+    if out_chunks is None:
+        out_chunks = range(ny // 8)
+    z_chunks = sorted({c for o in out_chunks for c in (o, o + 1)})
+    for c in z_chunks:
         rows = pl.ds(c * 8, 8)
         acc = taps_ref[0] * load(0, rows)
         for k in range(1, ntap):
             acc = acc + taps_ref[k] * load(k, rows)
         zbuf[rows, :] = acc
-    for c in range(ny // 8):
+    for c in out_chunks:
         acc = taps_ref[ntap] * zbuf[pl.ds(c * 8, 8), :]
         for k in range(1, ntap):
             acc = acc + taps_ref[ntap + k] * zbuf[pl.ds(c * 8 + k, 8), :]
         ybuf[pl.ds(c * 8, 8), :] = acc
-    for c in range(ny // 8):
+    for c in out_chunks:
         rows = pl.ds(c * 8, 8)
         v = ybuf[rows, :]
         acc = None
@@ -45,7 +48,12 @@
             max_ref[rows, :] = jnp.maximum(max_ref[rows, :], upd)
 
 
-def inner_kernel(mode, width, taps_ref, pad_ref, other_ref, out_ref, *rest):
+def inner_kernel(mode, width, out_chunks, row_shift, taps_ref, pad_ref, other_ref, *rest):
+    prev_ref = None
+    if len(rest) == 5 or (mode == "ratio" and len(rest) == 4):
+        prev_ref, rest = rest[0], rest[1:]
+    out_ref = rest[0]
+    rest = rest[1:]
     if mode == "update":
         max_ref, zbuf, ybuf = rest
         max_ref[...] = jnp.full(max_ref.shape, -jnp.inf, max_ref.dtype)
@@ -58,12 +66,16 @@
         zo = width + j
 
         def load(k, rows):
-            return pad_ref[j + k, rows, :]
+            return pad_ref[j + k, pl.ds(rows.start - row_shift, 8), :]
 
         def store(rows, value):
             out_ref[zo, rows, :] = value
 
-        plane_blur(mode, taps_ref, load, zbuf, ybuf, lanes, store, lambda rows: other_ref[zo, rows, :], max_ref)
+        plane_blur(mode, taps_ref, load, zbuf, ybuf, lanes, store, lambda rows: other_ref[zo, rows, :], max_ref, out_chunks)
+        if prev_ref is not None:
+            for c in range(out_ref.shape[1] // 8):
+                if c not in out_chunks:
+                    out_ref[zo, pl.ds(c * 8, 8), :] = prev_ref[zo, pl.ds(c * 8, 8), :]
         return carry
 
     lax.fori_loop(0, nz - 2 * width, body, 0)
@@ -100,7 +112,7 @@
     high.wait()
 
 
-def inner_blur(mode, width, taps, padded, other):
+def inner_blur(mode, width, out_chunks, row_shift, taps, padded, other, prev=None):
     nz, ny, nx = other.shape
     vmem = pltpu.VMEM
     outs = [jax.ShapeDtypeStruct((nz, ny, nx), jnp.float32)]
@@ -108,16 +120,21 @@
     if mode == "update":
         outs.append(jax.ShapeDtypeStruct((ny, nx), jnp.float32))
         out_specs.append(pl.BlockSpec(memory_space=vmem))
-    elems = (nz - 2 * width) * ny * nx
+    operands = [taps, padded, other]
+    aliases = {}
+    if prev is not None:
+        operands.append(prev)
+    elems = (nz - 2 * width) * 8 * len(out_chunks) * nx
     return pl.pallas_call(
-        functools.partial(inner_kernel, mode, width),
+        functools.partial(inner_kernel, mode, width, tuple(out_chunks), row_shift),
         out_shape=tuple(outs),
-        in_specs=[pl.BlockSpec(memory_space=pltpu.SMEM), pl.BlockSpec(memory_space=vmem), pl.BlockSpec(memory_space=vmem)],
+        in_specs=[pl.BlockSpec(memory_space=pltpu.SMEM)] + [pl.BlockSpec(memory_space=vmem)] * (len(operands) - 1),
         out_specs=tuple(out_specs),
         scratch_shapes=[pltpu.VMEM((ny + 8, nx), jnp.float32), pltpu.VMEM((ny, nx), jnp.float32)],
+        input_output_aliases=aliases,
         compiler_params=pltpu.CompilerParams(vmem_limit_bytes=48 * 1024 * 1024),
         cost_estimate=pl.CostEstimate(flops=elems * 60, bytes_accessed=elems * 4 * 4, transcendentals=0),
-    )(taps, padded, other)
+    )(*operands)
 
 
 def edge_blur(mode, width, taps, below, padded, above, other, volume):
@@ -158,13 +175,17 @@
 
 
 def split_blur(mode, taps, shard, other, width):
+    ny = shard.shape[1]
+    chunks = ny // 8
     before, after = halo_pair(shard, "gy", 1, width)
+    middle = inner_blur(mode, width, range(1, chunks - 1), width, taps, shard, other)
+    before, after, middle = lax.optimization_barrier((before, after, middle))
     rows_padded = jnp.concatenate([before, shard, after], axis=1)
     below, above = halo_pair(rows_padded, "gz", 0, width)
-    inner = inner_blur(mode, width, taps, rows_padded, other)
+    inner = inner_blur(mode, width, (0, chunks - 1), 0, taps, rows_padded, other, middle[0])
     edges = edge_blur(mode, width, taps, below, rows_padded, above, other, inner[0])
     if mode == "update":
-        return edges[0], jnp.maximum(inner[1], edges[1])
+        return edges[0], jnp.maximum(jnp.maximum(middle[1], inner[1]), edges[1])
     return edges[0]
 
 

time: 120 us -> 125 us (1.042); the launches traced: 120 us -> 122 us
  Pallas kernels: 42 us -> 58.2 us
  waiting for transfers between devices: 27.9 us -> 21.2 us
  starting transfers between devices: 40.5 us -> 34.4 us
  local copies, waits for them, and re-layouts: 4.95 us -> 3 us
    pallas_call x2 -> x4, Pallas kernels: 29.1 us -> 45.6 us  [inner_blur(): pl.pallas_call(functools.partial(inner_kernel, mode, width, tuple(out_chu...]
    ppermute x4, starting transfers between devices: 24.9 us -> 12.2 us  [halo_pair(): after = lax.ppermute(first, axis, down)]
    ppermute x4, waiting for transfers between devices: 6.21 us -> 0.01 us  [halo_pair(): after = lax.ppermute(first, axis, down)]
    ppermute x3, starting transfers between devices: 4.03 us -> 8.01 us  [butterfly_max(): value = jnp.maximum(value, lax.ppermute(value, axis, pairs))]
    ppermute x4, starting transfers between devices: 11.5 us -> 14.1 us  [halo_pair(): before = lax.ppermute(last, axis, up)]
    unnamed x12 -> x20, local copies, waits for them, and re-layouts: 1.89 us -> 0.05 us
    slice x2 -> x0, local copies, waits for them, and re-layouts: 1.65 us -> none  [halo_pair(): last = lax.slice_in_dim(shard, length - width, length, axis=dim)]
    slice x2 -> x4, local copies, waits for them, and re-layouts: 1.12 us -> 2.66 us  [halo_pair(): first = lax.slice_in_dim(shard, 0, width, axis=dim)]
  transfers between devices with their start and end apart: 11 -> 11, of which waited for: 6 -> 7; matrix products, arithmetic and copies ran while one was open for 0% -> 1% of each run, Pallas kernels for 24% -> 37%
where the time goes in v8:
time: 125 us; the launch traced here: 122 us
  Pallas kernels  58.2 us (47%)
  starting transfers between devices  34.4 us (28%)
  waiting for transfers between devices  21.2 us (17%)
  other arithmetic  4.71 us (4%)
  local copies, waits for them, and re-layouts  3 us (2%)
    pallas_call x4, Pallas kernels, inner_blur(): pl.pallas_call(functools.partial(inner_kernel, mode, width, tuple(out_chu...  45.6 us
    ppermute x4, starting transfers between devices, halo_pair(): before = lax.ppermute(last, axis, up)  14.1 us
    pallas_call x2, Pallas kernels, edge_blur(): pl.pallas_call(functools.partial(edge_kernel, mode, width), out_shape=tup...  12.7 us
    ppermute x4, starting transfers between devices, halo_pair(): after = lax.ppermute(first, axis, down)  12.2 us
    ppermute x3, waiting for transfers between devices, butterfly_max(): value = jnp.maximum(value, lax.ppermute(value, axis, pairs))  10.9 us
    ppermute x4, waiting for transfers between devices, halo_pair(): before = lax.ppermute(last, axis, up)  10.3 us
    ppermute x3, starting transfers between devices, butterfly_max(): value = jnp.maximum(value, lax.ppermute(value, axis, pairs))  8.01 us
    concatenate x2, other arithmetic, split_blur(): rows_padded = jnp.concatenate([before, shard, after], axis=1)  3.17 us
  transfers between devices with their start and end apart: 11, of which 7 were waited for; matrix products, arithmetic and copies ran while one was open for 1% of the time, Pallas kernels for 37%

profile of v8, /device:TPU:160, one launch (start us, length us, event | category | flops | bytes accessed | tf_op | source)
XLA Modules:
  0.0 122.4 jit_solution(12880458392678676793)
XLA Ops:
  0.6 1.5 %fusion.3 = (f32[32,4,768]{2,1,0:T(4,128)S(1)}, f32[32,4,768]{2,1,0:T(4,128)S(1)}) fusion(f32[32,32,768]{2,1,0:T(8,128)} %other_ref.11), kind=kLoop, calls=%fused_computation.8 | loop fusion | bytes 1572864 | tf_op jit(solution)/shard_map/slice | solution.py:171
  2.1 4.4 %collective-permute-start.1 = (f32[32,4,768]{2,1,0:T(4,128)S(1)}, f32[32,4,768]{2,1,0:T(4,128)S(1)}, u32[]{:S(2)}, u32[]{:S(2)}) collective-permute-start(f32[32,4,768]{2,1,0:T(4,128)S(1)} %get-tuple-element.34), channel_id=1, source_target_pairs={{1,0},{2,1},{3,2},{4,3},{5,4},{6,5},{7,6},{8,7},{9,8},{10,9},{11,1... | collective-permute-start | bytes 1179656 | tf_op jit(solution)/shard_map/ppermute | solution.py:173
  6.5 1.9 %collective-permute-start = (f32[32,4,768]{2,1,0:T(4,128)S(1)}, f32[32,4,768]{2,1,0:T(4,128)S(1)}, u32[]{:S(2)}, u32[]{:S(2)}) collective-permute-start(f32[32,4,768]{2,1,0:T(4,128)S(1)} %get-tuple-element.35), channel_id=1, source_target_pairs={{0,1},{1,2},{2,3},{3,4},{4,5},{5,6},{6,7},{7,8},{8,9},{9,10},{10,1... | collective-permute-start | bytes 1179656 | tf_op jit(solution)/shard_map/ppermute | solution.py:172
  8.4 0.8 pad_maximum_fusion.3.taps_ref
  9.2 0.0 copy-start
  9.2 11.2 %shard_map.68.rest_0_ = f32[32,32,768]{2,1,0:T(8,128)S(1)} custom-call(f32[27]{0:T(128)S(1)} %pad_maximum_fusion.3.taps_ref, f32[32,32,768]{2,1,0:T(8,128)} %other_ref.11, f32[32,32,768]{2,1,0:T(8,128)} %other_ref.8), custom_call_target="tpu_custom_call" | custom-call | flops 17694720 | bytes 4718592 | tf_op jit(solution)/shard_map/pallas_call | solution.py:128
  20.4 0.0 copy-start.3
  20.4 0.0 collective-permute-done.1
  20.4 3.2 %collective-permute-done = f32[32,4,768]{2,1,0:T(4,128)S(1)} collective-permute-done((f32[32,4,768]{2,1,0:T(4,128)S(1)}, f32[32,4,768]{2,1,0:T(4,128)S(1)}, u32[]{:S(2)}, u32[]{:S(2)}) %collective-permute-start) | collective-permute-done | bytes 393248 | tf_op jit(solution)/shard_map/ppermute | solution.py:172
  23.6 0.0 copy-done
  23.6 0.5 pad_maximum_fusion.pad_ref
  24.2 0.0 copy-done.3
  24.2 0.0 copy-start.6
  24.2 0.1 fusion.1
  24.3 2.5 %collective-permute-start.3 = (f32[4,40,768]{2,1,0:T(8,128)S(1)}, f32[4,40,768]{2,1,0:T(8,128)S(1)}, u32[]{:S(2)}, u32[]{:S(2)}) collective-permute-start(f32[4,40,768]{2,1,0:T(8,128)S(1)} %get-tuple-element.30), channel_id=1, source_target_pairs={{32,0},{64,32},{96,64},{128,96},{160,128},{192,160},{224,192},{33,... | collective-permute-start | bytes 1474568 | tf_op jit(solution)/shard_map/ppermute | solution.py:173
  26.7 4.3 %collective-permute-start.2 = (f32[4,40,768]{2,1,0:T(8,128)S(1)}, f32[4,40,768]{2,1,0:T(8,128)S(1)}, u32[]{:S(2)}, u32[]{:S(2)}) collective-permute-start(f32[4,40,768]{2,1,0:T(8,128)S(1)} %get-tuple-element.31), channel_id=1, source_target_pairs={{0,32},{32,64},{64,96},{96,128},{128,160},{160,192},{192,224},{1,3... | collective-permute-start | bytes 1474568 | tf_op jit(solution)/shard_map/ppermute | solution.py:172
  31.0 0.0 copy-done.6
  31.0 11.4 %shard_map.69.volume_in = f32[32,32,768]{2,1,0:T(8,128)S(1)} custom-call(f32[27]{0:T(128)S(1)} %pad_maximum_fusion.3.taps_ref, f32[32,40,768]{2,1,0:T(8,128)} %copy-done.6, f32[32,32,768]{2,1,0:T(8,128)} %other_ref.8, f32[32,32,768]{2,1,0:T(8,128)} %copy-done.3), custom_call_target="tpu_custom_call" | custom-call | flops 17694720 | bytes 4718592 | tf_op jit(solution)/shard_map/pallas_call | solution.py:128
  42.4 0.0 copy-start.7
  42.4 0.0 copy-start.8
  42.4 0.0 copy-start.9
  42.5 0.0 collective-permute-done.3.above_ref
  42.5 3.0 %collective-permute-done.2.below_ref = f32[4,40,768]{2,1,0:T(8,128)S(1)} collective-permute-done((f32[4,40,768]{2,1,0:T(8,128)S(1)}, f32[4,40,768]{2,1,0:T(8,128)S(1)}, u32[]{:S(2)}, u32[]{:S(2)}) %collective-permute-start.2) | collective-permute-done | bytes 491552 | tf_op jit(solution)/shard_map/ppermute | solution.py:172
  45.5 6.6 %shard_map.70.pad_ref = f32[32,32,768]{2,1,0:T(8,128)S(1)} custom-call(f32[27]{0:T(128)S(1)} %pad_maximum_fusion.3.taps_ref, f32[4,40,768]{2,1,0:T(8,128)S(1)} %collective-permute-done.2.below_ref, f32[32,40,768]{2,1,0:T(8,128)} %copy-done.6, f32[4,40,768]{2,1,0:T(8,128)S(1)} %collective-permute-done.3.above_ref, ...), custom_call_target="tpu_custom_call", output_to_operand_aliasing={{}: (5, {})} | custom-call | flops 11796480 | bytes 3145728 | tf_op jit(solution)/shard_map/pallas_call | solution.py:149
  52.1 0.0 copy-start.2
  52.1 1.0 fusion.2
  53.1 3.5 %collective-permute-start.5 = (f32[32,4,768]{2,1,0:T(4,128)}, f32[32,4,768]{2,1,0:T(4,128)}, u32[]{:S(2)}, u32[]{:S(2)}) collective-permute-start(f32[32,4,768]{2,1,0:T(4,128)} %get-tuple-element.32), channel_id=1, source_target_pairs={{1,0},{2,1},{3,2},{4,3},{5,4},{6,5},{7,6},{8,7},{9,8},{10,9},{11,1... | collective-permute-start | bytes 1179656 | tf_op jit(solution)/shard_map/ppermute | solution.py:173
  56.6 1.9 %collective-permute-start.4 = (f32[32,4,768]{2,1,0:T(4,128)S(1)}, f32[32,4,768]{2,1,0:T(4,128)}, u32[]{:S(2)}, u32[]{:S(2)}) collective-permute-start(f32[32,4,768]{2,1,0:T(4,128)S(1)} %get-tuple-element.33), channel_id=1, source_target_pairs={{0,1},{1,2},{2,3},{3,4},{4,5},{5,6},{6,7},{7,8},{8,9},{9,10},{10,1... | collective-permute-start | bytes 1179656 | tf_op jit(solution)/shard_map/ppermute | solution.py:172
  58.5 0.0 copy-done.7
  58.5 0.1 rev.9
  58.6 0.0 copy-done.8
  58.6 0.1 rev.10
  58.7 0.0 copy-done.9
  58.7 0.1 rev.11
  58.8 0.1 pad_maximum_fusion.2.taps_ref
  58.9 0.0 copy-done.2
  58.9 11.0 %shard_map.71 = (f32[32,32,768]{2,1,0:T(8,128)S(1)}, f32[32,768]{1,0:T(8,128)S(1)}) custom-call(f32[27]{0:T(128)S(1)} %pad_maximum_fusion.2.taps_ref, f32[32,32,768]{2,1,0:T(8,128)} %copy-done.2, f32[32,32,768]{2,1,0:T(8,128)} %other_ref.11), custom_call_target="tpu_custom_call" | custom-call | flops 17694720 | bytes 4718592 | tf_op jit(solution)/shard_map/pallas_call | solution.py:128
  69.9 0.0 copy-start.4
  69.9 0.0 collective-permute-done.5
  69.9 3.4 %collective-permute-done.4 = f32[32,4,768]{2,1,0:T(4,128)} collective-permute-done((f32[32,4,768]{2,1,0:T(4,128)S(1)}, f32[32,4,768]{2,1,0:T(4,128)}, u32[]{:S(2)}, u32[]{:S(2)}) %collective-permute-start.4) | collective-permute-done | bytes 393248 | tf_op jit(solution)/shard_map/ppermute | solution.py:172
  73.3 0.0 copy-start.1
  73.3 2.6 %pad_maximum_fusion.1.pad_ref = f32[32,40,768]{2,1,0:T(8,128)S(1)} fusion(f32[32,4,768]{2,1,0:T(4,128)} %collective-permute-done.5, f32[32,32,768]{2,1,0:T(8,128)} %copy-done.2, f32[32,4,768]{2,1,0:T(4,128)} %collective-permute-done.4), kind=kLoop, calls=%fused_computation.1 | loop fusion | flops 1966080 | bytes 7864320 | tf_op jit(solution)/shard_map/concatenate | solution.py:183
  75.9 0.0 copy-done.4
  75.9 0.0 copy-start.5
  75.9 0.1 fusion
  76.0 1.9 %collective-permute-start.7 = (f32[4,40,768]{2,1,0:T(8,128)S(1)}, f32[4,40,768]{2,1,0:T(8,128)S(1)}, u32[]{:S(2)}, u32[]{:S(2)}) collective-permute-start(f32[4,40,768]{2,1,0:T(8,128)S(1)} %get-tuple-element.28), channel_id=1, source_target_pairs={{32,0},{64,32},{96,64},{128,96},{160,128},{192,160},{224,192},{33,... | collective-permute-start | bytes 1474568 | tf_op jit(solution)/shard_map/ppermute | solution.py:173
  77.9 6.0 %collective-permute-start.6 = (f32[4,40,768]{2,1,0:T(8,128)S(1)}, f32[4,40,768]{2,1,0:T(8,128)S(1)}, u32[]{:S(2)}, u32[]{:S(2)}) collective-permute-start(f32[4,40,768]{2,1,0:T(8,128)S(1)} %get-tuple-element.29), channel_id=1, source_target_pairs={{0,32},{32,64},{64,96},{96,128},{128,160},{160,192},{192,224},{1,3... | collective-permute-start | bytes 1474568 | tf_op jit(solution)/shard_map/ppermute | solution.py:172
  83.9 0.0 copy-done.5
  83.9 0.0 copy-done.1
  83.9 12.0 %shard_map.72 = (f32[32,32,768]{2,1,0:T(8,128)}, f32[32,768]{1,0:T(8,128)S(1)}) custom-call(f32[27]{0:T(128)S(1)} %pad_maximum_fusion.2.taps_ref, f32[32,40,768]{2,1,0:T(8,128)} %copy-done.5, f32[32,32,768]{2,1,0:T(8,128)S(1)} %copy-done.1, f32[32,32,768]{2,1,0:T(8,128)} %copy-done.4), custom_call_target="tpu_custom_call" | custom-call | flops 17694720 | bytes 4718592 | tf_op jit(solution)/shard_map/pallas_call | solution.py:128
  96.0 0.0 collective-permute-done.7.above_ref
  96.0 0.7 collective-permute-done.6.below_ref
  96.7 6.1 %shard_map.73 = (f32[32,32,768]{2,1,0:T(8,128)}, f32[32,768]{1,0:T(8,128)S(1)}) custom-call(f32[27]{0:T(128)S(1)} %pad_maximum_fusion.2.taps_ref, f32[4,40,768]{2,1,0:T(8,128)S(1)} %collective-permute-done.6.below_ref, f32[32,40,768]{2,1,0:T(8,128)} %copy-done.5, ...), custom_call_target="tpu_custom_call", output_to_operand_aliasing={{0}: (5, {})} | custom-call | flops 11796480 | bytes 3145728 | tf_op jit(solution)/shard_map/pallas_call | solution.py:149
  102.8 0.1 collective-permute-start.8
  102.9 4.6 %collective-permute-done.8 = f32[32,768]{1,0:T(8,128)S(1)} collective-permute-done((f32[32,768]{1,0:T(8,128)S(1)}, f32[32,768]{1,0:T(8,128)S(1)}, u32[]{:S(2)}, u32[]{:S(2)}) %collective-permute-start.8) | collective-permute-done | bytes 98336 | tf_op jit(solution)/shard_map/ppermute | solution.py:197
  107.5 4.5 %collective-permute-start.9 = (f32[32,768]{1,0:T(8,128)S(1)}, f32[32,768]{1,0:T(8,128)S(1)}, u32[]{:S(2)}, u32[]{:S(2)}) collective-permute-start(f32[32,768]{1,0:T(8,128)S(1)} %max.17), channel_id=1, source_target_pairs={{0,64},{32,96},{64,0},{96,32},{128,192},{160,224},{192,128},{224,1... | collective-permute-start | bytes 294920 | tf_op jit(solution)/shard_map/ppermute | solution.py:197
  112.0 3.5 %collective-permute-done.9 = f32[32,768]{1,0:T(8,128)S(1)} collective-permute-done((f32[32,768]{1,0:T(8,128)S(1)}, f32[32,768]{1,0:T(8,128)S(1)}, u32[]{:S(2)}, u32[]{:S(2)}) %collective-permute-start.9) | collective-permute-done | bytes 98336 | tf_op jit(solution)/shard_map/ppermute | solution.py:197
  115.5 3.4 %collective-permute-start.10 = (f32[32,768]{1,0:T(8,128)S(1)}, f32[32,768]{1,0:T(8,128)S(1)}, u32[]{:S(2)}, u32[]{:S(2)}) collective-permute-start(f32[32,768]{1,0:T(8,128)S(1)} %max.18), channel_id=1, source_target_pairs={{0,128},{32,160},{64,192},{96,224},{128,0},{160,32},{192,64},{224,... | collective-permute-start | bytes 294920 | tf_op jit(solution)/shard_map/ppermute | solution.py:197
  119.0 2.8 %collective-permute-done.10 = f32[32,768]{1,0:T(8,128)S(1)} collective-permute-done((f32[32,768]{1,0:T(8,128)S(1)}, f32[32,768]{1,0:T(8,128)S(1)}, u32[]{:S(2)}, u32[]{:S(2)}) %collective-permute-start.10) | collective-permute-done | bytes 98336 | tf_op jit(solution)/shard_map/ppermute | solution.py:197
  121.7 0.7 max.19
  (3 shorter events, 0.0 us)
Async XLA Ops:
  2.1 18.3 %collective-permute-start.1 = (f32[32,4,768]{2,1,0:T(4,128)S(1)}, f32[32,4,768]{2,1,0:T(4,128)S(1)}, u32[]{:S(2)}, u32[]{:S(2)}) collective-permute-start(f32[32,4,768]{2,1,0:T(4,128)S(1)} %get-tuple-element.34), channel_id=1, source_target_pairs={{1,0},{2,1},{3,2},{4,3},{5,4},{6,5},{7,6},{8,7},{9,8},{10,9},{11,1... | collective-permute-start | bytes 1179656 | tf_op jit(solution)/shard_map/ppermute | solution.py:173
  6.5 17.1 %collective-permute-start = (f32[32,4,768]{2,1,0:T(4,128)S(1)}, f32[32,4,768]{2,1,0:T(4,128)S(1)}, u32[]{:S(2)}, u32[]{:S(2)}) collective-permute-start(f32[32,4,768]{2,1,0:T(4,128)S(1)} %get-tuple-element.35), channel_id=1, source_target_pairs={{0,1},{1,2},{2,3},{3,4},{4,5},{5,6},{6,7},{7,8},{8,9},{9,10},{10,1... | collective-permute-start | bytes 1179656 | tf_op jit(solution)/shard_map/ppermute | solution.py:172
  9.2 14.4 %copy-start = (f32[32,32,768]{2,1,0:T(8,128)S(1)}, f32[32,32,768]{2,1,0:T(8,128)}, u32[]{:S(2)}) copy-start(f32[32,32,768]{2,1,0:T(8,128)} %other_ref.11) | copy-start | bytes 9437188
  20.4 3.8 %copy-start.3 = (f32[32,32,768]{2,1,0:T(8,128)}, f32[32,32,768]{2,1,0:T(8,128)S(1)}, u32[]{:S(2)}) copy-start(f32[32,32,768]{2,1,0:T(8,128)S(1)} %shard_map.68.rest_0_) | copy-start | bytes 9437188
  24.2 6.8 %copy-start.6 = (f32[32,40,768]{2,1,0:T(8,128)}, f32[32,40,768]{2,1,0:T(8,128)S(1)}, u32[]{:S(2)}) copy-start(f32[32,40,768]{2,1,0:T(8,128)S(1)} %pad_maximum_fusion.pad_ref) | copy-start | bytes 11796484
  24.3 18.2 %collective-permute-start.3 = (f32[4,40,768]{2,1,0:T(8,128)S(1)}, f32[4,40,768]{2,1,0:T(8,128)S(1)}, u32[]{:S(2)}, u32[]{:S(2)}) collective-permute-start(f32[4,40,768]{2,1,0:T(8,128)S(1)} %get-tuple-element.30), channel_id=1, source_target_pairs={{32,0},{64,32},{96,64},{128,96},{160,128},{192,160},{224,192},{33,... | collective-permute-start | bytes 1474568 | tf_op jit(solution)/shard_map/ppermute | solution.py:173
  26.7 18.7 %collective-permute-start.2 = (f32[4,40,768]{2,1,0:T(8,128)S(1)}, f32[4,40,768]{2,1,0:T(8,128)S(1)}, u32[]{:S(2)}, u32[]{:S(2)}) collective-permute-start(f32[4,40,768]{2,1,0:T(8,128)S(1)} %get-tuple-element.31), channel_id=1, source_target_pairs={{0,32},{32,64},{64,96},{96,128},{128,160},{160,192},{192,224},{1,3... | collective-permute-start | bytes 1474568 | tf_op jit(solution)/shard_map/ppermute | solution.py:172
  42.4 16.1 %copy-start.7 = (f32[9]{0:T(128)S(1)}, f32[9]{0:T(128)}, u32[]{:S(2)}) copy-start(f32[9]{0:T(128)} %param.7) | copy-start | bytes 112
  42.4 16.2 %copy-start.8 = (f32[9]{0:T(128)S(1)}, f32[9]{0:T(128)}, u32[]{:S(2)}) copy-start(f32[9]{0:T(128)} %param.8) | copy-start | bytes 112
  42.4 16.3 %copy-start.9 = (f32[9]{0:T(128)S(1)}, f32[9]{0:T(128)}, u32[]{:S(2)}) copy-start(f32[9]{0:T(128)} %param.9) | copy-start | bytes 112
  52.1 6.9 %copy-start.2 = (f32[32,32,768]{2,1,0:T(8,128)}, f32[32,32,768]{2,1,0:T(8,128)S(1)}, u32[]{:S(2)}) copy-start(f32[32,32,768]{2,1,0:T(8,128)S(1)} %shard_map.70.pad_ref) | copy-start | bytes 9437188
  53.1 16.8 %collective-permute-start.5 = (f32[32,4,768]{2,1,0:T(4,128)}, f32[32,4,768]{2,1,0:T(4,128)}, u32[]{:S(2)}, u32[]{:S(2)}) collective-permute-start(f32[32,4,768]{2,1,0:T(4,128)} %get-tuple-element.32), channel_id=1, source_target_pairs={{1,0},{2,1},{3,2},{4,3},{5,4},{6,5},{7,6},{8,7},{9,8},{10,9},{11,1... | collective-permute-start | bytes 1179656 | tf_op jit(solution)/shard_map/ppermute | solution.py:173
  56.6 16.7 %collective-permute-start.4 = (f32[32,4,768]{2,1,0:T(4,128)S(1)}, f32[32,4,768]{2,1,0:T(4,128)}, u32[]{:S(2)}, u32[]{:S(2)}) collective-permute-start(f32[32,4,768]{2,1,0:T(4,128)S(1)} %get-tuple-element.33), channel_id=1, source_target_pairs={{0,1},{1,2},{2,3},{3,4},{4,5},{5,6},{6,7},{7,8},{8,9},{9,10},{10,1... | collective-permute-start | bytes 1179656 | tf_op jit(solution)/shard_map/ppermute | solution.py:172
  69.9 6.0 %copy-start.4 = (f32[32,32,768]{2,1,0:T(8,128)}, f32[32,32,768]{2,1,0:T(8,128)S(1)}, u32[]{:S(2)}) copy-start(f32[32,32,768]{2,1,0:T(8,128)S(1)} %get-tuple-element.22.rest_0_) | copy-start | bytes 9437188
  73.3 10.7 %copy-start.1 = (f32[32,32,768]{2,1,0:T(8,128)S(1)}, f32[32,32,768]{2,1,0:T(8,128)}, u32[]{:S(2)}) copy-start(f32[32,32,768]{2,1,0:T(8,128)} %other_ref.11) | copy-start | bytes 9437188
  75.9 8.0 %copy-start.5 = (f32[32,40,768]{2,1,0:T(8,128)}, f32[32,40,768]{2,1,0:T(8,128)S(1)}, u32[]{:S(2)}) copy-start(f32[32,40,768]{2,1,0:T(8,128)S(1)} %pad_maximum_fusion.1.pad_ref) | copy-start | bytes 11796484
  76.0 20.0 %collective-permute-start.7 = (f32[4,40,768]{2,1,0:T(8,128)S(1)}, f32[4,40,768]{2,1,0:T(8,128)S(1)}, u32[]{:S(2)}, u32[]{:S(2)}) collective-permute-start(f32[4,40,768]{2,1,0:T(8,128)S(1)} %get-tuple-element.28), channel_id=1, source_target_pairs={{32,0},{64,32},{96,64},{128,96},{160,128},{192,160},{224,192},{33,... | collective-permute-start | bytes 1474568 | tf_op jit(solution)/shard_map/ppermute | solution.py:173
  77.9 18.7 %collective-permute-start.6 = (f32[4,40,768]{2,1,0:T(8,128)S(1)}, f32[4,40,768]{2,1,0:T(8,128)S(1)}, u32[]{:S(2)}, u32[]{:S(2)}) collective-permute-start(f32[4,40,768]{2,1,0:T(8,128)S(1)} %get-tuple-element.29), channel_id=1, source_target_pairs={{0,32},{32,64},{64,96},{96,128},{128,160},{160,192},{192,224},{1,3... | collective-permute-start | bytes 1474568 | tf_op jit(solution)/shard_map/ppermute | solution.py:172
  102.8 4.7 %collective-permute-start.8 = (f32[32,768]{1,0:T(8,128)S(1)}, f32[32,768]{1,0:T(8,128)S(1)}, u32[]{:S(2)}, u32[]{:S(2)}) collective-permute-start(f32[32,768]{1,0:T(8,128)S(1)} %maximum_maximum_fusion), channel_id=1, source_target_pairs={{0,32},{32,0},{64,96},{96,64},{128,160},{160,128},{192,224},{224,1... | collective-permute-start | bytes 294920 | tf_op jit(solution)/shard_map/ppermute | solution.py:197
  107.5 8.0 %collective-permute-start.9 = (f32[32,768]{1,0:T(8,128)S(1)}, f32[32,768]{1,0:T(8,128)S(1)}, u32[]{:S(2)}, u32[]{:S(2)}) collective-permute-start(f32[32,768]{1,0:T(8,128)S(1)} %max.17), channel_id=1, source_target_pairs={{0,64},{32,96},{64,0},{96,32},{128,192},{160,224},{192,128},{224,1... | collective-permute-start | bytes 294920 | tf_op jit(solution)/shard_map/ppermute | solution.py:197
  115.5 6.2 %collective-permute-start.10 = (f32[32,768]{1,0:T(8,128)S(1)}, f32[32,768]{1,0:T(8,128)S(1)}, u32[]{:S(2)}, u32[]{:S(2)}) collective-permute-start(f32[32,768]{1,0:T(8,128)S(1)} %max.18), channel_id=1, source_target_pairs={{0,128},{32,160},{64,192},{96,224},{128,0},{160,32},{192,64},{224,... | collective-permute-start | bytes 294920 | tf_op jit(solution)/shard_map/ppermute | solution.py:197

commit v9 on v4

--- a/solution.py
+++ b/solution.py
@@ -99,11 +99,13 @@
     rows_padded = jnp.concatenate([before, shard, after], axis=1)
     below, above = halo_pair(rows_padded, "gz", 0, width)
     inner = fused_blur(mode, [(0, nz - 2 * width, 0, width)], taps, rows_padded, other)
-    slabs = jnp.concatenate([below, rows_padded[: 2 * width], rows_padded[nz - 2 * width :], above], axis=0)
-    edges = fused_blur(mode, [(0, width, 0, 0), (width, width, 3 * width, nz - width)], taps, slabs, other)
-    volume = jnp.concatenate([edges[0][:width], inner[0], edges[0][width:]], axis=0)
+    low_slab = jnp.concatenate([below, rows_padded[: 2 * width]], axis=0)
+    high_slab = jnp.concatenate([rows_padded[nz - 2 * width :], above], axis=0)
+    low = fused_blur(mode, [(0, width, 0, 0)], taps, low_slab, other)
+    high = fused_blur(mode, [(0, width, 0, nz - width)], taps, high_slab, other)
+    volume = jnp.concatenate([low[0], inner[0], high[0]], axis=0)
     if mode == "update":
-        return volume, jnp.maximum(inner[1], edges[1])
+        return volume, jnp.maximum(jnp.maximum(inner[1], low[1]), high[1])
     return volume
 
 

time: 120 us -> 117 us (0.975)
  waiting for transfers between devices: 24.7 us -> 22.2 us
  starting transfers between devices: 40.5 us -> 42.8 us
  Pallas kernels: 37.8 us -> 36.2 us
    ppermute x3, starting transfers between devices: 4.09 us -> 6.43 us  [butterfly_max(): value = jnp.maximum(value, lax.ppermute(value, axis, pairs))]
    pallas_call x4 -> x6, Pallas kernels: 37.8 us -> 36.2 us  [fused_blur(): pl.pallas_call(functools.partial(blur_kernel, mode, tuple(segments)), out...]
    ppermute x4, waiting for transfers between devices: 13 us -> 11.6 us  [halo_pair(): before = lax.ppermute(last, axis, up)]
    concatenate x3 -> x4, other arithmetic: 3.57 us -> 3.62 us  [the longest x1 2.01 us: split_blur(): volume = jnp.concatenate([low[0], inner[0], high[0]], axis=0)]
  transfers between devices with their start and end apart: 11 -> 11, of which waited for: 6 -> 6; matrix products, arithmetic and copies ran while one was open for 4% -> 4% of each run, Pallas kernels for 22% -> 25%
where the time goes in v9:
time: 117 us; the launch traced here: 116 us
  starting transfers between devices  42.8 us (37%)
  Pallas kernels  36.2 us (31%)
  waiting for transfers between devices  22.2 us (19%)
  other arithmetic  7.41 us (6%)
  local copies, waits for them, and re-layouts  6.59 us (6%)
    pallas_call x6, Pallas kernels, fused_blur(): pl.pallas_call(functools.partial(blur_kernel, mode, tuple(segments)), out...  36.2 us
    ppermute x4, starting transfers between devices, halo_pair(): after = lax.ppermute(first, axis, down)  20.5 us
    ppermute x4, starting transfers between devices, halo_pair(): before = lax.ppermute(last, axis, up)  15.9 us
    ppermute x4, waiting for transfers between devices, halo_pair(): before = lax.ppermute(last, axis, up)  11.6 us
    ppermute x3, waiting for transfers between devices, butterfly_max(): value = jnp.maximum(value, lax.ppermute(value, axis, pairs))  8.28 us
    ppermute x3, starting transfers between devices, butterfly_max(): value = jnp.maximum(value, lax.ppermute(value, axis, pairs))  6.43 us
    concatenate x2, other arithmetic, split_blur(): rows_padded = jnp.concatenate([before, shard, after], axis=1)  2.79 us
    slice x3, local copies, waits for them, and re-layouts, halo_pair(): last = lax.slice_in_dim(shard, length - width, length, axis=dim)  2.61 us
  transfers between devices with their start and end apart: 11, of which 6 were waited for; matrix products, arithmetic and copies ran while one was open for 4% of the time, Pallas kernels for 25%

profile of v9, /device:TPU:160, one launch (start us, length us, event | category | flops | bytes accessed | tf_op | source)
XLA Modules:
  0.0 116.1 jit_solution(17861755576133024496)
XLA Ops:
  0.6 1.5 %fusion.4 = (f32[32,4,768]{2,1,0:T(4,128)S(1)}, f32[32,4,768]{2,1,0:T(4,128)S(1)}) fusion(f32[32,32,768]{2,1,0:T(8,128)} %other_ref.11), kind=kLoop, calls=%fused_computation.17 | loop fusion | bytes 1572864 | tf_op jit(solution)/shard_map/slice | solution.py:89
  2.1 1.9 %collective-permute-start = (f32[32,4,768]{2,1,0:T(4,128)S(1)}, f32[32,4,768]{2,1,0:T(4,128)S(1)}, u32[]{:S(2)}, u32[]{:S(2)}) collective-permute-start(f32[32,4,768]{2,1,0:T(4,128)S(1)} %get-tuple-element.24), channel_id=1, source_target_pairs={{0,1},{1,2},{2,3},{3,4},{4,5},{5,6},{6,7},{7,8},{8,9},{9,10},{10,1... | collective-permute-start | bytes 1179656 | tf_op jit(solution)/shard_map/ppermute | solution.py:91
  4.1 0.0 copy-start.5
  4.1 0.0 copy-start.6
  4.1 0.0 copy-start.7
  4.1 0.0 copy-start.1
  4.1 8.1 %collective-permute-start.1 = (f32[32,4,768]{2,1,0:T(4,128)S(1)}, f32[32,4,768]{2,1,0:T(4,128)S(1)}, u32[]{:S(2)}, u32[]{:S(2)}) collective-permute-start(f32[32,4,768]{2,1,0:T(4,128)S(1)} %get-tuple-element.25), channel_id=1, source_target_pairs={{1,0},{2,1},{3,2},{4,3},{5,4},{6,5},{7,6},{8,7},{9,8},{10,9},{11,1... | collective-permute-start | bytes 1179656 | tf_op jit(solution)/shard_map/ppermute | solution.py:92
  12.3 5.6 %collective-permute-done = f32[32,4,768]{2,1,0:T(4,128)S(1)} collective-permute-done((f32[32,4,768]{2,1,0:T(4,128)S(1)}, f32[32,4,768]{2,1,0:T(4,128)S(1)}, u32[]{:S(2)}, u32[]{:S(2)}) %collective-permute-start) | collective-permute-done | bytes 393248 | tf_op jit(solution)/shard_map/ppermute | solution.py:91
  17.8 0.0 collective-permute-done.1
  17.8 2.3 %pad_maximum_fusion.pad_ref = f32[32,40,768]{2,1,0:T(8,128)S(1)} fusion(f32[32,4,768]{2,1,0:T(4,128)S(1)} %collective-permute-done.1, f32[32,32,768]{2,1,0:T(8,128)} %other_ref.11, f32[32,4,768]{2,1,0:T(4,128)S(1)} %collective-permute-done), kind=kLoop, calls=%fused_computation | loop fusion | flops 1966080 | bytes 7864320 | tf_op jit(solution)/shard_map/concatenate | solution.py:99
  20.1 0.0 copy-start.4
  20.1 0.1 fusion.2
  20.2 7.8 %collective-permute-start.2 = (f32[4,40,768]{2,1,0:T(8,128)S(1)}, f32[4,40,768]{2,1,0:T(8,128)S(1)}, u32[]{:S(2)}, u32[]{:S(2)}) collective-permute-start(f32[4,40,768]{2,1,0:T(8,128)S(1)} %get-tuple-element.18), channel_id=1, source_target_pairs={{0,32},{32,64},{64,96},{96,128},{128,160},{160,192},{192,224},{1,3... | collective-permute-start | bytes 1474568 | tf_op jit(solution)/shard_map/ppermute | solution.py:91
  28.0 1.9 %collective-permute-start.3 = (f32[4,40,768]{2,1,0:T(8,128)S(1)}, f32[4,40,768]{2,1,0:T(8,128)S(1)}, u32[]{:S(2)}, u32[]{:S(2)}) collective-permute-start(f32[4,40,768]{2,1,0:T(8,128)S(1)} %get-tuple-element.19), channel_id=1, source_target_pairs={{32,0},{64,32},{96,64},{128,96},{160,128},{192,160},{224,192},{33,... | collective-permute-start | bytes 1474568 | tf_op jit(solution)/shard_map/ppermute | solution.py:92
  29.9 0.0 copy-done.5
  29.9 0.0 copy-done.6
  30.0 0.0 copy-done.7
  30.0 0.1 pad_maximum_fusion.11.taps_ref
  30.0 0.0 copy-done.4
  30.0 0.0 copy-done.1
  30.1 13.2 %shard_map.69 = f32[24,32,768]{2,1,0:T(8,128)S(1)} custom-call(f32[27]{0:T(128)S(1)} %pad_maximum_fusion.11.taps_ref, f32[32,40,768]{2,1,0:T(8,128)} %copy-done.4, f32[32,32,768]{2,1,0:T(8,128)S(1)} %copy-done.1), custom_call_target="tpu_custom_call" | custom-call | flops 35389440 | bytes 9437184 | tf_op jit(solution)/shard_map/pallas_call | solution.py:74
  43.2 1.6 %fusion.3 = (f32[8,40,768]{2,1,0:T(8,128)S(1)}, f32[8,40,768]{2,1,0:T(8,128)S(1)}) fusion(f32[32,40,768]{2,1,0:T(8,128)} %copy-done.4), kind=kLoop, calls=%fused_computation.16 | loop fusion | bytes 3932160 | tf_op jit(solution)/shard_map/slice | solution.py:102
  44.9 0.0 collective-permute-done.2
  44.9 0.1 pad_maximum_fusion.3.pad_ref
  45.0 2.4 %shard_map.68 = f32[4,32,768]{2,1,0:T(8,128)S(1)} custom-call(f32[27]{0:T(128)S(1)} %pad_maximum_fusion.11.taps_ref, f32[12,40,768]{2,1,0:T(8,128)S(1)} %pad_maximum_fusion.3.pad_ref, f32[32,32,768]{2,1,0:T(8,128)S(1)} %copy-done.1), custom_call_target="tpu_custom_call" | custom-call | flops 5898240 | bytes 1572864 | tf_op jit(solution)/shard_map/pallas_call | solution.py:74
  47.4 0.0 collective-permute-done.3
  47.5 0.1 pad_maximum_fusion.4.pad_ref
  47.6 2.4 %shard_map.70 = f32[4,32,768]{2,1,0:T(8,128)S(1)} custom-call(f32[27]{0:T(128)S(1)} %pad_maximum_fusion.11.taps_ref, f32[12,40,768]{2,1,0:T(8,128)S(1)} %pad_maximum_fusion.4.pad_ref, f32[32,32,768]{2,1,0:T(8,128)S(1)} %copy-done.1), custom_call_target="tpu_custom_call" | custom-call | flops 5898240 | bytes 1572864 | tf_op jit(solution)/shard_map/pallas_call | solution.py:74
  50.0 0.1 pad_maximum_fusion.9
  50.1 1.9 %collective-permute-start.4 = (f32[32,4,768]{2,1,0:T(4,128)S(1)}, f32[32,4,768]{2,1,0:T(4,128)S(1)}, u32[]{:S(2)}, u32[]{:S(2)}) collective-permute-start(f32[32,4,768]{2,1,0:T(4,128)S(1)} %get-tuple-element.22), channel_id=1, source_target_pairs={{0,1},{1,2},{2,3},{3,4},{4,5},{5,6},{6,7},{7,8},{8,9},{9,10},{10,1... | collective-permute-start | bytes 1179656 | tf_op jit(solution)/shard_map/ppermute | solution.py:91
  52.1 0.0 copy-start
  52.1 8.1 %collective-permute-start.5 = (f32[32,4,768]{2,1,0:T(4,128)S(1)}, f32[32,4,768]{2,1,0:T(4,128)S(1)}, u32[]{:S(2)}, u32[]{:S(2)}) collective-permute-start(f32[32,4,768]{2,1,0:T(4,128)S(1)} %get-tuple-element.23), channel_id=1, source_target_pairs={{1,0},{2,1},{3,2},{4,3},{5,4},{6,5},{7,6},{8,7},{9,8},{10,9},{11,1... | collective-permute-start | bytes 1179656 | tf_op jit(solution)/shard_map/ppermute | solution.py:92
  60.2 6.0 %collective-permute-done.4 = f32[32,4,768]{2,1,0:T(4,128)S(1)} collective-permute-done((f32[32,4,768]{2,1,0:T(4,128)S(1)}, f32[32,4,768]{2,1,0:T(4,128)S(1)}, u32[]{:S(2)}, u32[]{:S(2)}) %collective-permute-start.4) | collective-permute-done | bytes 393248 | tf_op jit(solution)/shard_map/ppermute | solution.py:91
  66.2 2.3 %collective-permute-done.5 = f32[32,4,768]{2,1,0:T(4,128)S(1)} collective-permute-done((f32[32,4,768]{2,1,0:T(4,128)S(1)}, f32[32,4,768]{2,1,0:T(4,128)S(1)}, u32[]{:S(2)}, u32[]{:S(2)}) %collective-permute-start.5) | collective-permute-done | bytes 393248 | tf_op jit(solution)/shard_map/ppermute | solution.py:92
  68.6 0.5 pad_maximum_fusion.1.pad_ref
  69.0 0.0 copy-start.2
  69.1 1.9 %copy-done.2 = f32[32,40,768]{2,1,0:T(8,128)} copy-done((f32[32,40,768]{2,1,0:T(8,128)}, f32[32,40,768]{2,1,0:T(8,128)S(1)}, u32[]{:S(2)}) %copy-start.2) | copy-done | bytes 3932184
  70.9 1.0 fusion
  71.9 4.3 %collective-permute-start.6 = (f32[4,40,768]{2,1,0:T(8,128)}, f32[4,40,768]{2,1,0:T(8,128)}, u32[]{:S(2)}, u32[]{:S(2)}) collective-permute-start(f32[4,40,768]{2,1,0:T(8,128)} %get-tuple-element.14), channel_id=1, source_target_pairs={{0,32},{32,64},{64,96},{96,128},{128,160},{160,192},{192,224},{1,3... | collective-permute-start | bytes 1474568 | tf_op jit(solution)/shard_map/ppermute | solution.py:91
  76.2 2.3 %collective-permute-start.7 = (f32[4,40,768]{2,1,0:T(8,128)}, f32[4,40,768]{2,1,0:T(8,128)}, u32[]{:S(2)}, u32[]{:S(2)}) collective-permute-start(f32[4,40,768]{2,1,0:T(8,128)} %get-tuple-element.15), channel_id=1, source_target_pairs={{32,0},{64,32},{96,64},{128,96},{160,128},{192,160},{224,192},{33,... | collective-permute-start | bytes 1474568 | tf_op jit(solution)/shard_map/ppermute | solution.py:92
  78.6 0.1 rev.9
  78.7 0.1 rev.10
  78.8 0.1 rev.11
  78.8 0.1 pad_maximum_fusion.10.taps_ref
  78.9 0.0 copy-done
  78.9 0.0 copy-start.3
  78.9 13.3 %shard_map.72 = (f32[24,32,768]{2,1,0:T(8,128)S(1)}, f32[32,768]{1,0:T(8,128)S(1)}) custom-call(f32[27]{0:T(128)S(1)} %pad_maximum_fusion.10.taps_ref, f32[32,40,768]{2,1,0:T(8,128)} %copy-done.2, f32[32,32,768]{2,1,0:T(8,128)S(1)} %copy-done), custom_call_target="tpu_custom_call" | custom-call | flops 35389440 | bytes 9437184 | tf_op jit(solution)/shard_map/pallas_call | solution.py:74
  92.3 0.0 copy-done.3
  92.3 0.2 fusion.1
  92.4 0.0 collective-permute-done.6
  92.4 0.0 collective-permute-done.7
  92.5 1.4 %pad_maximum_fusion.5 = (f32[12,40,768]{2,1,0:T(8,128)S(1)}, f32[12,40,768]{2,1,0:T(8,128)S(1)}) fusion(f32[8,40,768]{2,1,0:T(8,128)S(1)} %get-tuple-element.16, f32[4,40,768]{2,1,0:T(8,128)} %collective-permute-done.6, f32[4,40,768]{2,1,0:T(8,128)} %collective-permute-done.7, f32[8,40,768]{2,1,0:T(8,128)S(1)} %get-tuple-element.17), kind=kLoop, calls=%fused_computation.5 | loop fusion | flops 737280 | bytes 5898240 | tf_op jit(solution)/shard_map/concatenate | solution.py:102
  93.9 2.4 %shard_map.71 = (f32[4,32,768]{2,1,0:T(8,128)S(1)}, f32[32,768]{1,0:T(8,128)S(1)}) custom-call(f32[27]{0:T(128)S(1)} %pad_maximum_fusion.10.taps_ref, f32[12,40,768]{2,1,0:T(8,128)S(1)} %get-tuple-element.26.pad_ref, f32[32,32,768]{2,1,0:T(8,128)S(1)} %copy-done), custom_call_target="tpu_custom_call" | custom-call | flops 5898240 | bytes 1572864 | tf_op jit(solution)/shard_map/pallas_call | solution.py:74
  96.3 2.4 %shard_map.73 = (f32[4,32,768]{2,1,0:T(8,128)S(1)}, f32[32,768]{1,0:T(8,128)S(1)}) custom-call(f32[27]{0:T(128)S(1)} %pad_maximum_fusion.10.taps_ref, f32[12,40,768]{2,1,0:T(8,128)S(1)} %get-tuple-element.27.pad_ref, f32[32,32,768]{2,1,0:T(8,128)S(1)} %copy-done), custom_call_target="tpu_custom_call" | custom-call | flops 5898240 | bytes 1572864 | tf_op jit(solution)/shard_map/pallas_call | solution.py:74
  98.7 0.1 collective-permute-start.8
  98.8 4.6 %collective-permute-done.8 = f32[32,768]{1,0:T(8,128)S(1)} collective-permute-done((f32[32,768]{1,0:T(8,128)S(1)}, f32[32,768]{1,0:T(8,128)S(1)}, u32[]{:S(2)}, u32[]{:S(2)}) %collective-permute-start.8) | collective-permute-done | bytes 98336 | tf_op jit(solution)/shard_map/ppermute | solution.py:117
  103.4 3.2 %collective-permute-start.9 = (f32[32,768]{1,0:T(8,128)S(1)}, f32[32,768]{1,0:T(8,128)S(1)}, u32[]{:S(2)}, u32[]{:S(2)}) collective-permute-start(f32[32,768]{1,0:T(8,128)S(1)} %max.17), channel_id=1, source_target_pairs={{0,64},{32,96},{64,0},{96,32},{128,192},{160,224},{192,128},{224,1... | collective-permute-start | bytes 294920 | tf_op jit(solution)/shard_map/ppermute | solution.py:117
  106.6 2.6 %collective-permute-done.9 = f32[32,768]{1,0:T(8,128)S(1)} collective-permute-done((f32[32,768]{1,0:T(8,128)S(1)}, f32[32,768]{1,0:T(8,128)S(1)}, u32[]{:S(2)}, u32[]{:S(2)}) %collective-permute-start.9) | collective-permute-done | bytes 98336 | tf_op jit(solution)/shard_map/ppermute | solution.py:117
  109.3 3.1 %collective-permute-start.10 = (f32[32,768]{1,0:T(8,128)S(1)}, f32[32,768]{1,0:T(8,128)S(1)}, u32[]{:S(2)}, u32[]{:S(2)}) collective-permute-start(f32[32,768]{1,0:T(8,128)S(1)} %max.18), channel_id=1, source_target_pairs={{0,128},{32,160},{64,192},{96,224},{128,0},{160,32},{192,64},{224,... | collective-permute-start | bytes 294920 | tf_op jit(solution)/shard_map/ppermute | solution.py:117
  112.4 2.0 %pad_maximum_fusion.2 = f32[32,32,768]{2,1,0:T(8,128)} fusion(f32[4,32,768]{2,1,0:T(8,128)S(1)} %get-tuple-element.10, f32[24,32,768]{2,1,0:T(8,128)S(1)} %get-tuple-element.9, f32[4,32,768]{2,1,0:T(8,128)S(1)} %get-tuple-element.8), kind=kLoop, calls=%fused_computation.2 | loop fusion | flops 1572864 | bytes 6291456 | tf_op jit(solution)/shard_map/concatenate | solution.py:106
  114.4 1.1 collective-permute-done.10
  115.5 0.7 max.19
  (3 shorter events, 0.1 us)
Async XLA Ops:
  2.1 15.7 %collective-permute-start = (f32[32,4,768]{2,1,0:T(4,128)S(1)}, f32[32,4,768]{2,1,0:T(4,128)S(1)}, u32[]{:S(2)}, u32[]{:S(2)}) collective-permute-start(f32[32,4,768]{2,1,0:T(4,128)S(1)} %get-tuple-element.24), channel_id=1, source_target_pairs={{0,1},{1,2},{2,3},{3,4},{4,5},{5,6},{6,7},{7,8},{8,9},{9,10},{10,1... | collective-permute-start | bytes 1179656 | tf_op jit(solution)/shard_map/ppermute | solution.py:91
  4.1 25.9 %copy-start.5 = (f32[9]{0:T(128)S(1)}, f32[9]{0:T(128)}, u32[]{:S(2)}) copy-start(f32[9]{0:T(128)} %param.7) | copy-start | bytes 112
  4.1 25.9 %copy-start.6 = (f32[9]{0:T(128)S(1)}, f32[9]{0:T(128)}, u32[]{:S(2)}) copy-start(f32[9]{0:T(128)} %param.8) | copy-start | bytes 112
  4.1 25.9 %copy-start.7 = (f32[9]{0:T(128)S(1)}, f32[9]{0:T(128)}, u32[]{:S(2)}) copy-start(f32[9]{0:T(128)} %param.9) | copy-start | bytes 112
  4.1 25.9 %copy-start.1 = (f32[32,32,768]{2,1,0:T(8,128)S(1)}, f32[32,32,768]{2,1,0:T(8,128)}, u32[]{:S(2)}) copy-start(f32[32,32,768]{2,1,0:T(8,128)} %other_ref.8) | copy-start | bytes 9437188
  4.1 13.7 %collective-permute-start.1 = (f32[32,4,768]{2,1,0:T(4,128)S(1)}, f32[32,4,768]{2,1,0:T(4,128)S(1)}, u32[]{:S(2)}, u32[]{:S(2)}) collective-permute-start(f32[32,4,768]{2,1,0:T(4,128)S(1)} %get-tuple-element.25), channel_id=1, source_target_pairs={{1,0},{2,1},{3,2},{4,3},{5,4},{6,5},{7,6},{8,7},{9,8},{10,9},{11,1... | collective-permute-start | bytes 1179656 | tf_op jit(solution)/shard_map/ppermute | solution.py:92
  20.1 9.9 %copy-start.4 = (f32[32,40,768]{2,1,0:T(8,128)}, f32[32,40,768]{2,1,0:T(8,128)S(1)}, u32[]{:S(2)}) copy-start(f32[32,40,768]{2,1,0:T(8,128)S(1)} %pad_maximum_fusion.pad_ref) | copy-start | bytes 11796484
  20.2 24.7 %collective-permute-start.2 = (f32[4,40,768]{2,1,0:T(8,128)S(1)}, f32[4,40,768]{2,1,0:T(8,128)S(1)}, u32[]{:S(2)}, u32[]{:S(2)}) collective-permute-start(f32[4,40,768]{2,1,0:T(8,128)S(1)} %get-tuple-element.18), channel_id=1, source_target_pairs={{0,32},{32,64},{64,96},{96,128},{128,160},{160,192},{192,224},{1,3... | collective-permute-start | bytes 1474568 | tf_op jit(solution)/shard_map/ppermute | solution.py:91
  28.0 19.4 %collective-permute-start.3 = (f32[4,40,768]{2,1,0:T(8,128)S(1)}, f32[4,40,768]{2,1,0:T(8,128)S(1)}, u32[]{:S(2)}, u32[]{:S(2)}) collective-permute-start(f32[4,40,768]{2,1,0:T(8,128)S(1)} %get-tuple-element.19), channel_id=1, source_target_pairs={{32,0},{64,32},{96,64},{128,96},{160,128},{192,160},{224,192},{33,... | collective-permute-start | bytes 1474568 | tf_op jit(solution)/shard_map/ppermute | solution.py:92
  50.1 16.1 %collective-permute-start.4 = (f32[32,4,768]{2,1,0:T(4,128)S(1)}, f32[32,4,768]{2,1,0:T(4,128)S(1)}, u32[]{:S(2)}, u32[]{:S(2)}) collective-permute-start(f32[32,4,768]{2,1,0:T(4,128)S(1)} %get-tuple-element.22), channel_id=1, source_target_pairs={{0,1},{1,2},{2,3},{3,4},{4,5},{5,6},{6,7},{7,8},{8,9},{9,10},{10,1... | collective-permute-start | bytes 1179656 | tf_op jit(solution)/shard_map/ppermute | solution.py:91
  52.1 26.9 %copy-start = (f32[32,32,768]{2,1,0:T(8,128)S(1)}, f32[32,32,768]{2,1,0:T(8,128)}, u32[]{:S(2)}) copy-start(f32[32,32,768]{2,1,0:T(8,128)} %other_ref.11) | copy-start | bytes 9437188
  52.1 16.5 %collective-permute-start.5 = (f32[32,4,768]{2,1,0:T(4,128)S(1)}, f32[32,4,768]{2,1,0:T(4,128)S(1)}, u32[]{:S(2)}, u32[]{:S(2)}) collective-permute-start(f32[32,4,768]{2,1,0:T(4,128)S(1)} %get-tuple-element.23), channel_id=1, source_target_pairs={{1,0},{2,1},{3,2},{4,3},{5,4},{6,5},{7,6},{8,7},{9,8},{10,9},{11,1... | collective-permute-start | bytes 1179656 | tf_op jit(solution)/shard_map/ppermute | solution.py:92
  69.0 1.9 %copy-start.2 = (f32[32,40,768]{2,1,0:T(8,128)}, f32[32,40,768]{2,1,0:T(8,128)S(1)}, u32[]{:S(2)}) copy-start(f32[32,40,768]{2,1,0:T(8,128)S(1)} %pad_maximum_fusion.1.pad_ref) | copy-start | bytes 11796484
  71.9 20.5 %collective-permute-start.6 = (f32[4,40,768]{2,1,0:T(8,128)}, f32[4,40,768]{2,1,0:T(8,128)}, u32[]{:S(2)}, u32[]{:S(2)}) collective-permute-start(f32[4,40,768]{2,1,0:T(8,128)} %get-tuple-element.14), channel_id=1, source_target_pairs={{0,32},{32,64},{64,96},{96,128},{128,160},{160,192},{192,224},{1,3... | collective-permute-start | bytes 1474568 | tf_op jit(solution)/shard_map/ppermute | solution.py:91
  76.2 16.2 %collective-permute-start.7 = (f32[4,40,768]{2,1,0:T(8,128)}, f32[4,40,768]{2,1,0:T(8,128)}, u32[]{:S(2)}, u32[]{:S(2)}) collective-permute-start(f32[4,40,768]{2,1,0:T(8,128)} %get-tuple-element.15), channel_id=1, source_target_pairs={{32,0},{64,32},{96,64},{128,96},{160,128},{192,160},{224,192},{33,... | collective-permute-start | bytes 1474568 | tf_op jit(solution)/shard_map/ppermute | solution.py:92
  78.9 13.3 %copy-start.3 = (f32[32,40,768]{2,1,0:T(8,128)S(1)}, f32[32,40,768]{2,1,0:T(8,128)}, u32[]{:S(2)}) copy-start(f32[32,40,768]{2,1,0:T(8,128)} %copy-done.2) | copy-start | bytes 11796484
  98.7 4.7 %collective-permute-start.8 = (f32[32,768]{1,0:T(8,128)S(1)}, f32[32,768]{1,0:T(8,128)S(1)}, u32[]{:S(2)}, u32[]{:S(2)}) collective-permute-start(f32[32,768]{1,0:T(8,128)S(1)} %maximum_maximum_fusion), channel_id=1, source_target_pairs={{0,32},{32,0},{64,96},{96,64},{128,160},{160,128},{192,224},{224,1... | collective-permute-start | bytes 294920 | tf_op jit(solution)/shard_map/ppermute | solution.py:117
  103.4 5.8 %collective-permute-start.9 = (f32[32,768]{1,0:T(8,128)S(1)}, f32[32,768]{1,0:T(8,128)S(1)}, u32[]{:S(2)}, u32[]{:S(2)}) collective-permute-start(f32[32,768]{1,0:T(8,128)S(1)} %max.17), channel_id=1, source_target_pairs={{0,64},{32,96},{64,0},{96,32},{128,192},{160,224},{192,128},{224,1... | collective-permute-start | bytes 294920 | tf_op jit(solution)/shard_map/ppermute | solution.py:117
  109.3 6.2 %collective-permute-start.10 = (f32[32,768]{1,0:T(8,128)S(1)}, f32[32,768]{1,0:T(8,128)S(1)}, u32[]{:S(2)}, u32[]{:S(2)}) collective-permute-start(f32[32,768]{1,0:T(8,128)S(1)} %max.18), channel_id=1, source_target_pairs={{0,128},{32,160},{64,192},{96,224},{128,0},{160,32},{192,64},{224,... | collective-permute-start | bytes 294920 | tf_op jit(solution)/shard_map/ppermute | solution.py:117

commit v10 on v9

--- a/solution.py
+++ b/solution.py
@@ -100,8 +100,9 @@
     below, above = halo_pair(rows_padded, "gz", 0, width)
     inner = fused_blur(mode, [(0, nz - 2 * width, 0, width)], taps, rows_padded, other)
     low_slab = jnp.concatenate([below, rows_padded[: 2 * width]], axis=0)
+    low = fused_blur(mode, [(0, width, 0, 0)], taps, low_slab, other)
+    above, low = lax.optimization_barrier((above, low))
     high_slab = jnp.concatenate([rows_padded[nz - 2 * width :], above], axis=0)
-    low = fused_blur(mode, [(0, width, 0, 0)], taps, low_slab, other)
     high = fused_blur(mode, [(0, width, 0, nz - width)], taps, high_slab, other)
     volume = jnp.concatenate([low[0], inner[0], high[0]], axis=0)
     if mode == "update":

time: 117 us -> 117 us (level)
  transfers between devices with their start and end apart: 11 -> 11, of which waited for: 6 -> 6; matrix products, arithmetic and copies ran while one was open for 4% -> 5% of each run, Pallas kernels for 25% -> 27%
where the time goes in v10:
time: 117 us; the launch traced here: 116 us
  starting transfers between devices  42.8 us (37%)
  Pallas kernels  36.1 us (31%)
  waiting for transfers between devices  22.2 us (19%)
  other arithmetic  7.27 us (6%)
  local copies, waits for them, and re-layouts  6.6 us (6%)
    pallas_call x6, Pallas kernels, fused_blur(): pl.pallas_call(functools.partial(blur_kernel, mode, tuple(segments)), out...  36.1 us
    ppermute x4, starting transfers between devices, halo_pair(): after = lax.ppermute(first, axis, down)  20.5 us
    ppermute x4, starting transfers between devices, halo_pair(): before = lax.ppermute(last, axis, up)  15.9 us
    ppermute x4, waiting for transfers between devices, halo_pair(): before = lax.ppermute(last, axis, up)  11.6 us
    ppermute x3, waiting for transfers between devices, butterfly_max(): value = jnp.maximum(value, lax.ppermute(value, axis, pairs))  8.28 us
    ppermute x3, starting transfers between devices, butterfly_max(): value = jnp.maximum(value, lax.ppermute(value, axis, pairs))  6.43 us
    concatenate x2, other arithmetic, split_blur(): rows_padded = jnp.concatenate([before, shard, after], axis=1)  2.83 us
    slice x3, local copies, waits for them, and re-layouts, halo_pair(): last = lax.slice_in_dim(shard, length - width, length, axis=dim)  2.61 us
  transfers between devices with their start and end apart: 11, of which 6 were waited for; matrix products, arithmetic and copies ran while one was open for 5% of the time, Pallas kernels for 27%

profile of v10, /device:TPU:160, one launch (start us, length us, event | category | flops | bytes accessed | tf_op | source)
XLA Modules:
  0.0 116.0 jit_solution(14907926389856789811)
XLA Ops:
  0.6 1.5 %fusion.4 = (f32[32,4,768]{2,1,0:T(4,128)S(1)}, f32[32,4,768]{2,1,0:T(4,128)S(1)}) fusion(f32[32,32,768]{2,1,0:T(8,128)} %other_ref.11), kind=kLoop, calls=%fused_computation.17 | loop fusion | bytes 1572864 | tf_op jit(solution)/shard_map/slice | solution.py:89
  2.1 1.9 %collective-permute-start = (f32[32,4,768]{2,1,0:T(4,128)S(1)}, f32[32,4,768]{2,1,0:T(4,128)S(1)}, u32[]{:S(2)}, u32[]{:S(2)}) collective-permute-start(f32[32,4,768]{2,1,0:T(4,128)S(1)} %get-tuple-element.34), channel_id=1, source_target_pairs={{0,1},{1,2},{2,3},{3,4},{4,5},{5,6},{6,7},{7,8},{8,9},{9,10},{10,1... | collective-permute-start | bytes 1179656 | tf_op jit(solution)/shard_map/ppermute | solution.py:91
  4.1 0.0 copy-start.5
  4.1 0.0 copy-start.6
  4.1 0.0 copy-start.7
  4.1 0.0 copy-start.1
  4.1 8.1 %collective-permute-start.1 = (f32[32,4,768]{2,1,0:T(4,128)S(1)}, f32[32,4,768]{2,1,0:T(4,128)S(1)}, u32[]{:S(2)}, u32[]{:S(2)}) collective-permute-start(f32[32,4,768]{2,1,0:T(4,128)S(1)} %get-tuple-element.35), channel_id=1, source_target_pairs={{1,0},{2,1},{3,2},{4,3},{5,4},{6,5},{7,6},{8,7},{9,8},{10,9},{11,1... | collective-permute-start | bytes 1179656 | tf_op jit(solution)/shard_map/ppermute | solution.py:92
  12.3 5.6 %collective-permute-done = f32[32,4,768]{2,1,0:T(4,128)S(1)} collective-permute-done((f32[32,4,768]{2,1,0:T(4,128)S(1)}, f32[32,4,768]{2,1,0:T(4,128)S(1)}, u32[]{:S(2)}, u32[]{:S(2)}) %collective-permute-start) | collective-permute-done | bytes 393248 | tf_op jit(solution)/shard_map/ppermute | solution.py:91
  17.8 0.0 collective-permute-done.1
  17.8 2.3 %pad_maximum_fusion.pad_ref = f32[32,40,768]{2,1,0:T(8,128)S(1)} fusion(f32[32,4,768]{2,1,0:T(4,128)S(1)} %collective-permute-done.1, f32[32,32,768]{2,1,0:T(8,128)} %other_ref.11, f32[32,4,768]{2,1,0:T(4,128)S(1)} %collective-permute-done), kind=kLoop, calls=%fused_computation | loop fusion | flops 1966080 | bytes 7864320 | tf_op jit(solution)/shard_map/concatenate | solution.py:99
  20.1 0.0 copy-start.4
  20.1 0.1 fusion.3
  20.2 7.8 %collective-permute-start.3 = (f32[4,40,768]{2,1,0:T(8,128)S(1)}, f32[4,40,768]{2,1,0:T(8,128)S(1)}, u32[]{:S(2)}, u32[]{:S(2)}) collective-permute-start(f32[4,40,768]{2,1,0:T(8,128)S(1)} %get-tuple-element.30), channel_id=1, source_target_pairs={{0,32},{32,64},{64,96},{96,128},{128,160},{160,192},{192,224},{1,3... | collective-permute-start | bytes 1474568 | tf_op jit(solution)/shard_map/ppermute | solution.py:91
  28.0 1.9 %collective-permute-start.2 = (f32[4,40,768]{2,1,0:T(8,128)S(1)}, f32[4,40,768]{2,1,0:T(8,128)S(1)}, u32[]{:S(2)}, u32[]{:S(2)}) collective-permute-start(f32[4,40,768]{2,1,0:T(8,128)S(1)} %get-tuple-element.31), channel_id=1, source_target_pairs={{32,0},{64,32},{96,64},{128,96},{160,128},{192,160},{224,192},{33,... | collective-permute-start | bytes 1474568 | tf_op jit(solution)/shard_map/ppermute | solution.py:92
  29.9 0.0 copy-done.5
  29.9 0.0 copy-done.6
  30.0 0.0 copy-done.7
  30.0 0.1 pad_maximum_fusion.10.taps_ref
  30.0 0.0 copy-done.4
  30.0 0.0 copy-done.1
  30.1 13.2 %shard_map.69 = f32[24,32,768]{2,1,0:T(8,128)S(1)} custom-call(f32[27]{0:T(128)S(1)} %pad_maximum_fusion.10.taps_ref, f32[32,40,768]{2,1,0:T(8,128)} %copy-done.4, f32[32,32,768]{2,1,0:T(8,128)S(1)} %copy-done.1), custom_call_target="tpu_custom_call" | custom-call | flops 35389440 | bytes 9437184 | tf_op jit(solution)/shard_map/pallas_call | solution.py:74
  43.2 1.6 %fusion.2 = (f32[8,40,768]{2,1,0:T(8,128)S(1)}, f32[8,40,768]{2,1,0:T(8,128)S(1)}) fusion(f32[32,40,768]{2,1,0:T(8,128)} %copy-done.4), kind=kLoop, calls=%fused_computation.15 | loop fusion | bytes 3932160 | tf_op jit(solution)/shard_map/slice | solution.py:105
  44.9 0.0 collective-permute-done.3
  44.9 0.1 pad_maximum_fusion.3.pad_ref
  45.0 2.4 %shard_map.68 = f32[4,32,768]{2,1,0:T(8,128)S(1)} custom-call(f32[27]{0:T(128)S(1)} %pad_maximum_fusion.10.taps_ref, f32[12,40,768]{2,1,0:T(8,128)S(1)} %pad_maximum_fusion.3.pad_ref, f32[32,32,768]{2,1,0:T(8,128)S(1)} %copy-done.1), custom_call_target="tpu_custom_call" | custom-call | flops 5898240 | bytes 1572864 | tf_op jit(solution)/shard_map/pallas_call | solution.py:74
  47.4 0.0 collective-permute-done.2
  47.5 0.1 pad_maximum_fusion.4.pad_ref
  47.6 2.4 %shard_map.70 = f32[4,32,768]{2,1,0:T(8,128)S(1)} custom-call(f32[27]{0:T(128)S(1)} %pad_maximum_fusion.10.taps_ref, f32[12,40,768]{2,1,0:T(8,128)S(1)} %pad_maximum_fusion.4.pad_ref, f32[32,32,768]{2,1,0:T(8,128)S(1)} %copy-done.1), custom_call_target="tpu_custom_call" | custom-call | flops 5898240 | bytes 1572864 | tf_op jit(solution)/shard_map/pallas_call | solution.py:74
  50.0 0.1 pad_maximum_fusion.9
  50.1 1.9 %collective-permute-start.4 = (f32[32,4,768]{2,1,0:T(4,128)S(1)}, f32[32,4,768]{2,1,0:T(4,128)S(1)}, u32[]{:S(2)}, u32[]{:S(2)}) collective-permute-start(f32[32,4,768]{2,1,0:T(4,128)S(1)} %get-tuple-element.32), channel_id=1, source_target_pairs={{0,1},{1,2},{2,3},{3,4},{4,5},{5,6},{6,7},{7,8},{8,9},{9,10},{10,1... | collective-permute-start | bytes 1179656 | tf_op jit(solution)/shard_map/ppermute | solution.py:91
  52.1 0.0 copy-start
  52.1 8.1 %collective-permute-start.5 = (f32[32,4,768]{2,1,0:T(4,128)S(1)}, f32[32,4,768]{2,1,0:T(4,128)S(1)}, u32[]{:S(2)}, u32[]{:S(2)}) collective-permute-start(f32[32,4,768]{2,1,0:T(4,128)S(1)} %get-tuple-element.33), channel_id=1, source_target_pairs={{1,0},{2,1},{3,2},{4,3},{5,4},{6,5},{7,6},{8,7},{9,8},{10,9},{11,1... | collective-permute-start | bytes 1179656 | tf_op jit(solution)/shard_map/ppermute | solution.py:92
  60.2 6.0 %collective-permute-done.4 = f32[32,4,768]{2,1,0:T(4,128)S(1)} collective-permute-done((f32[32,4,768]{2,1,0:T(4,128)S(1)}, f32[32,4,768]{2,1,0:T(4,128)S(1)}, u32[]{:S(2)}, u32[]{:S(2)}) %collective-permute-start.4) | collective-permute-done | bytes 393248 | tf_op jit(solution)/shard_map/ppermute | solution.py:91
  66.2 2.3 %collective-permute-done.5 = f32[32,4,768]{2,1,0:T(4,128)S(1)} collective-permute-done((f32[32,4,768]{2,1,0:T(4,128)S(1)}, f32[32,4,768]{2,1,0:T(4,128)S(1)}, u32[]{:S(2)}, u32[]{:S(2)}) %collective-permute-start.5) | collective-permute-done | bytes 393248 | tf_op jit(solution)/shard_map/ppermute | solution.py:92
  68.6 0.5 pad_maximum_fusion.1.pad_ref
  69.1 0.0 copy-start.2
  69.1 1.9 %copy-done.2 = f32[32,40,768]{2,1,0:T(8,128)} copy-done((f32[32,40,768]{2,1,0:T(8,128)}, f32[32,40,768]{2,1,0:T(8,128)S(1)}, u32[]{:S(2)}) %copy-start.2) | copy-done | bytes 3932184
  71.0 1.0 fusion.1
  72.0 4.3 %collective-permute-start.7 = (f32[4,40,768]{2,1,0:T(8,128)}, f32[4,40,768]{2,1,0:T(8,128)}, u32[]{:S(2)}, u32[]{:S(2)}) collective-permute-start(f32[4,40,768]{2,1,0:T(8,128)} %get-tuple-element.26), channel_id=1, source_target_pairs={{0,32},{32,64},{64,96},{96,128},{128,160},{160,192},{192,224},{1,3... | collective-permute-start | bytes 1474568 | tf_op jit(solution)/shard_map/ppermute | solution.py:91
  76.3 0.1 rev.10
  76.4 0.1 rev.11
  76.5 0.1 rev.9
  76.5 2.3 %collective-permute-start.6 = (f32[4,40,768]{2,1,0:T(8,128)}, f32[4,40,768]{2,1,0:T(8,128)S(1)}, u32[]{:S(2)}, u32[]{:S(2)}) collective-permute-start(f32[4,40,768]{2,1,0:T(8,128)} %get-tuple-element.27), channel_id=1, source_target_pairs={{32,0},{64,32},{96,64},{128,96},{160,128},{192,160},{224,192},{33,... | collective-permute-start | bytes 1474568 | tf_op jit(solution)/shard_map/ppermute | solution.py:92
  78.9 0.1 pad_maximum_fusion.11.taps_ref
  79.0 0.0 copy-done
  79.0 0.0 copy-start.3
  79.0 13.3 %shard_map.72 = (f32[24,32,768]{2,1,0:T(8,128)S(1)}, f32[32,768]{1,0:T(8,128)S(1)}) custom-call(f32[27]{0:T(128)S(1)} %pad_maximum_fusion.11.taps_ref, f32[32,40,768]{2,1,0:T(8,128)} %copy-done.2, f32[32,32,768]{2,1,0:T(8,128)S(1)} %copy-done), custom_call_target="tpu_custom_call" | custom-call | flops 35389440 | bytes 9437184 | tf_op jit(solution)/shard_map/pallas_call | solution.py:74
  92.3 0.0 copy-done.3
  92.3 0.2 fusion
  92.5 0.0 collective-permute-done.7
  92.5 1.1 pad_maximum_fusion.5.pad_ref
  93.6 2.4 %shard_map.71 = (f32[4,32,768]{2,1,0:T(8,128)S(1)}, f32[32,768]{1,0:T(8,128)S(1)}) custom-call(f32[27]{0:T(128)S(1)} %pad_maximum_fusion.11.taps_ref, f32[12,40,768]{2,1,0:T(8,128)S(1)} %pad_maximum_fusion.5.pad_ref, f32[32,32,768]{2,1,0:T(8,128)S(1)} %copy-done), custom_call_target="tpu_custom_call" | custom-call | flops 5898240 | bytes 1572864 | tf_op jit(solution)/shard_map/pallas_call | solution.py:74
  96.0 0.0 collective-permute-done.6
  96.0 0.1 pad_maximum_fusion.6.pad_ref
  96.1 2.4 %shard_map.73 = (f32[4,32,768]{2,1,0:T(8,128)S(1)}, f32[32,768]{1,0:T(8,128)S(1)}) custom-call(f32[27]{0:T(128)S(1)} %pad_maximum_fusion.11.taps_ref, f32[12,40,768]{2,1,0:T(8,128)S(1)} %pad_maximum_fusion.6.pad_ref, f32[32,32,768]{2,1,0:T(8,128)S(1)} %copy-done), custom_call_target="tpu_custom_call" | custom-call | flops 5898240 | bytes 1572864 | tf_op jit(solution)/shard_map/pallas_call | solution.py:74
  98.6 0.1 collective-permute-start.8
  98.7 4.6 %collective-permute-done.8 = f32[32,768]{1,0:T(8,128)S(1)} collective-permute-done((f32[32,768]{1,0:T(8,128)S(1)}, f32[32,768]{1,0:T(8,128)S(1)}, u32[]{:S(2)}, u32[]{:S(2)}) %collective-permute-start.8) | collective-permute-done | bytes 98336 | tf_op jit(solution)/shard_map/ppermute | solution.py:118
  103.3 3.2 %collective-permute-start.9 = (f32[32,768]{1,0:T(8,128)S(1)}, f32[32,768]{1,0:T(8,128)S(1)}, u32[]{:S(2)}, u32[]{:S(2)}) collective-permute-start(f32[32,768]{1,0:T(8,128)S(1)} %max.17), channel_id=1, source_target_pairs={{0,64},{32,96},{64,0},{96,32},{128,192},{160,224},{192,128},{224,1... | collective-permute-start | bytes 294920 | tf_op jit(solution)/shard_map/ppermute | solution.py:118
  106.5 2.6 %collective-permute-done.9 = f32[32,768]{1,0:T(8,128)S(1)} collective-permute-done((f32[32,768]{1,0:T(8,128)S(1)}, f32[32,768]{1,0:T(8,128)S(1)}, u32[]{:S(2)}, u32[]{:S(2)}) %collective-permute-start.9) | collective-permute-done | bytes 98336 | tf_op jit(solution)/shard_map/ppermute | solution.py:118
  109.1 3.1 %collective-permute-start.10 = (f32[32,768]{1,0:T(8,128)S(1)}, f32[32,768]{1,0:T(8,128)S(1)}, u32[]{:S(2)}, u32[]{:S(2)}) collective-permute-start(f32[32,768]{1,0:T(8,128)S(1)} %max.18), channel_id=1, source_target_pairs={{0,128},{32,160},{64,192},{96,224},{128,0},{160,32},{192,64},{224,... | collective-permute-start | bytes 294920 | tf_op jit(solution)/shard_map/ppermute | solution.py:118
  112.2 2.0 %pad_maximum_fusion.2 = f32[32,32,768]{2,1,0:T(8,128)} fusion(f32[4,32,768]{2,1,0:T(8,128)S(1)} %get-tuple-element.20, f32[24,32,768]{2,1,0:T(8,128)S(1)} %get-tuple-element.18, f32[4,32,768]{2,1,0:T(8,128)S(1)} %get-tuple-element.17), kind=kLoop, calls=%fused_computation.2 | loop fusion | flops 1572864 | bytes 6291456 | tf_op jit(solution)/shard_map/concatenate | solution.py:107
  114.2 1.1 collective-permute-done.10
  115.3 0.7 max.19
  (3 shorter events, 0.1 us)
Async XLA Ops:
  2.1 15.7 %collective-permute-start = (f32[32,4,768]{2,1,0:T(4,128)S(1)}, f32[32,4,768]{2,1,0:T(4,128)S(1)}, u32[]{:S(2)}, u32[]{:S(2)}) collective-permute-start(f32[32,4,768]{2,1,0:T(4,128)S(1)} %get-tuple-element.34), channel_id=1, source_target_pairs={{0,1},{1,2},{2,3},{3,4},{4,5},{5,6},{6,7},{7,8},{8,9},{9,10},{10,1... | collective-permute-start | bytes 1179656 | tf_op jit(solution)/shard_map/ppermute | solution.py:91
  4.1 25.9 %copy-start.5 = (f32[9]{0:T(128)S(1)}, f32[9]{0:T(128)}, u32[]{:S(2)}) copy-start(f32[9]{0:T(128)} %param.8) | copy-start | bytes 112
  4.1 25.9 %copy-start.6 = (f32[9]{0:T(128)S(1)}, f32[9]{0:T(128)}, u32[]{:S(2)}) copy-start(f32[9]{0:T(128)} %param.9) | copy-start | bytes 112
  4.1 25.9 %copy-start.7 = (f32[9]{0:T(128)S(1)}, f32[9]{0:T(128)}, u32[]{:S(2)}) copy-start(f32[9]{0:T(128)} %param.7) | copy-start | bytes 112
  4.1 25.9 %copy-start.1 = (f32[32,32,768]{2,1,0:T(8,128)S(1)}, f32[32,32,768]{2,1,0:T(8,128)}, u32[]{:S(2)}) copy-start(f32[32,32,768]{2,1,0:T(8,128)} %other_ref.8) | copy-start | bytes 9437188
  4.1 13.7 %collective-permute-start.1 = (f32[32,4,768]{2,1,0:T(4,128)S(1)}, f32[32,4,768]{2,1,0:T(4,128)S(1)}, u32[]{:S(2)}, u32[]{:S(2)}) collective-permute-start(f32[32,4,768]{2,1,0:T(4,128)S(1)} %get-tuple-element.35), channel_id=1, source_target_pairs={{1,0},{2,1},{3,2},{4,3},{5,4},{6,5},{7,6},{8,7},{9,8},{10,9},{11,1... | collective-permute-start | bytes 1179656 | tf_op jit(solution)/shard_map/ppermute | solution.py:92
  20.1 9.9 %copy-start.4 = (f32[32,40,768]{2,1,0:T(8,128)}, f32[32,40,768]{2,1,0:T(8,128)S(1)}, u32[]{:S(2)}) copy-start(f32[32,40,768]{2,1,0:T(8,128)S(1)} %pad_maximum_fusion.pad_ref) | copy-start | bytes 11796484
  20.2 24.7 %collective-permute-start.3 = (f32[4,40,768]{2,1,0:T(8,128)S(1)}, f32[4,40,768]{2,1,0:T(8,128)S(1)}, u32[]{:S(2)}, u32[]{:S(2)}) collective-permute-start(f32[4,40,768]{2,1,0:T(8,128)S(1)} %get-tuple-element.30), channel_id=1, source_target_pairs={{0,32},{32,64},{64,96},{96,128},{128,160},{160,192},{192,224},{1,3... | collective-permute-start | bytes 1474568 | tf_op jit(solution)/shard_map/ppermute | solution.py:91
  28.0 19.4 %collective-permute-start.2 = (f32[4,40,768]{2,1,0:T(8,128)S(1)}, f32[4,40,768]{2,1,0:T(8,128)S(1)}, u32[]{:S(2)}, u32[]{:S(2)}) collective-permute-start(f32[4,40,768]{2,1,0:T(8,128)S(1)} %get-tuple-element.31), channel_id=1, source_target_pairs={{32,0},{64,32},{96,64},{128,96},{160,128},{192,160},{224,192},{33,... | collective-permute-start | bytes 1474568 | tf_op jit(solution)/shard_map/ppermute | solution.py:92
  50.1 16.1 %collective-permute-start.4 = (f32[32,4,768]{2,1,0:T(4,128)S(1)}, f32[32,4,768]{2,1,0:T(4,128)S(1)}, u32[]{:S(2)}, u32[]{:S(2)}) collective-permute-start(f32[32,4,768]{2,1,0:T(4,128)S(1)} %get-tuple-element.32), channel_id=1, source_target_pairs={{0,1},{1,2},{2,3},{3,4},{4,5},{5,6},{6,7},{7,8},{8,9},{9,10},{10,1... | collective-permute-start | bytes 1179656 | tf_op jit(solution)/shard_map/ppermute | solution.py:91
  52.1 26.9 %copy-start = (f32[32,32,768]{2,1,0:T(8,128)S(1)}, f32[32,32,768]{2,1,0:T(8,128)}, u32[]{:S(2)}) copy-start(f32[32,32,768]{2,1,0:T(8,128)} %other_ref.11) | copy-start | bytes 9437188
  52.1 16.5 %collective-permute-start.5 = (f32[32,4,768]{2,1,0:T(4,128)S(1)}, f32[32,4,768]{2,1,0:T(4,128)S(1)}, u32[]{:S(2)}, u32[]{:S(2)}) collective-permute-start(f32[32,4,768]{2,1,0:T(4,128)S(1)} %get-tuple-element.33), channel_id=1, source_target_pairs={{1,0},{2,1},{3,2},{4,3},{5,4},{6,5},{7,6},{8,7},{9,8},{10,9},{11,1... | collective-permute-start | bytes 1179656 | tf_op jit(solution)/shard_map/ppermute | solution.py:92
  69.1 1.9 %copy-start.2 = (f32[32,40,768]{2,1,0:T(8,128)}, f32[32,40,768]{2,1,0:T(8,128)S(1)}, u32[]{:S(2)}) copy-start(f32[32,40,768]{2,1,0:T(8,128)S(1)} %pad_maximum_fusion.1.pad_ref) | copy-start | bytes 11796484
  72.0 20.5 %collective-permute-start.7 = (f32[4,40,768]{2,1,0:T(8,128)}, f32[4,40,768]{2,1,0:T(8,128)}, u32[]{:S(2)}, u32[]{:S(2)}) collective-permute-start(f32[4,40,768]{2,1,0:T(8,128)} %get-tuple-element.26), channel_id=1, source_target_pairs={{0,32},{32,64},{64,96},{96,128},{128,160},{160,192},{192,224},{1,3... | collective-permute-start | bytes 1474568 | tf_op jit(solution)/shard_map/ppermute | solution.py:91
  76.5 19.5 %collective-permute-start.6 = (f32[4,40,768]{2,1,0:T(8,128)}, f32[4,40,768]{2,1,0:T(8,128)S(1)}, u32[]{:S(2)}, u32[]{:S(2)}) collective-permute-start(f32[4,40,768]{2,1,0:T(8,128)} %get-tuple-element.27), channel_id=1, source_target_pairs={{32,0},{64,32},{96,64},{128,96},{160,128},{192,160},{224,192},{33,... | collective-permute-start | bytes 1474568 | tf_op jit(solution)/shard_map/ppermute | solution.py:92
  79.0 13.3 %copy-start.3 = (f32[32,40,768]{2,1,0:T(8,128)S(1)}, f32[32,40,768]{2,1,0:T(8,128)}, u32[]{:S(2)}) copy-start(f32[32,40,768]{2,1,0:T(8,128)} %copy-done.2) | copy-start | bytes 11796484
  98.6 4.7 %collective-permute-start.8 = (f32[32,768]{1,0:T(8,128)S(1)}, f32[32,768]{1,0:T(8,128)S(1)}, u32[]{:S(2)}, u32[]{:S(2)}) collective-permute-start(f32[32,768]{1,0:T(8,128)S(1)} %maximum_maximum_fusion), channel_id=1, source_target_pairs={{0,32},{32,0},{64,96},{96,64},{128,160},{160,128},{192,224},{224,1... | collective-permute-start | bytes 294920 | tf_op jit(solution)/shard_map/ppermute | solution.py:118
  103.3 5.8 %collective-permute-start.9 = (f32[32,768]{1,0:T(8,128)S(1)}, f32[32,768]{1,0:T(8,128)S(1)}, u32[]{:S(2)}, u32[]{:S(2)}) collective-permute-start(f32[32,768]{1,0:T(8,128)S(1)} %max.17), channel_id=1, source_target_pairs={{0,64},{32,96},{64,0},{96,32},{128,192},{160,224},{192,128},{224,1... | collective-permute-start | bytes 294920 | tf_op jit(solution)/shard_map/ppermute | solution.py:118
  109.1 6.2 %collective-permute-start.10 = (f32[32,768]{1,0:T(8,128)S(1)}, f32[32,768]{1,0:T(8,128)S(1)}, u32[]{:S(2)}, u32[]{:S(2)}) collective-permute-start(f32[32,768]{1,0:T(8,128)S(1)} %max.18), channel_id=1, source_target_pairs={{0,128},{32,160},{64,192},{96,224},{128,0},{160,32},{192,64},{224,... | collective-permute-start | bytes 294920 | tf_op jit(solution)/shard_map/ppermute | solution.py:118

commit v11 on v9

--- a/solution.py
+++ b/solution.py
@@ -111,11 +111,11 @@
 
 def butterfly_max(value, axis):
     peers = lax.axis_size(axis)
-    step = 1
-    while step < peers:
+    step = peers // 2
+    while step >= 1:
         pairs = [(i, i ^ step) for i in range(peers)]
         value = jnp.maximum(value, lax.ppermute(value, axis, pairs))
-        step *= 2
+        step //= 2
     return value
 
 

time: 117 us -> 117 us (level)
  no operation moved by 1% of the time
where the time goes in v11:
time: 117 us; the launch traced here: 116 us
  starting transfers between devices  43.3 us (37%)
  Pallas kernels  36.2 us (31%)
  waiting for transfers between devices  21.7 us (19%)
  other arithmetic  7.41 us (6%)
  local copies, waits for them, and re-layouts  6.59 us (6%)
    pallas_call x6, Pallas kernels, fused_blur(): pl.pallas_call(functools.partial(blur_kernel, mode, tuple(segments)), out...  36.2 us
    ppermute x4, starting transfers between devices, halo_pair(): after = lax.ppermute(first, axis, down)  20.5 us
    ppermute x4, starting transfers between devices, halo_pair(): before = lax.ppermute(last, axis, up)  15.9 us
    ppermute x4, waiting for transfers between devices, halo_pair(): before = lax.ppermute(last, axis, up)  11.6 us
    ppermute x3, waiting for transfers between devices, butterfly_max(): value = jnp.maximum(value, lax.ppermute(value, axis, pairs))  7.79 us
    ppermute x3, starting transfers between devices, butterfly_max(): value = jnp.maximum(value, lax.ppermute(value, axis, pairs))  6.93 us
    concatenate x2, other arithmetic, split_blur(): rows_padded = jnp.concatenate([before, shard, after], axis=1)  2.79 us
    slice x3, local copies, waits for them, and re-layouts, halo_pair(): last = lax.slice_in_dim(shard, length - width, length, axis=dim)  2.61 us
  transfers between devices with their start and end apart: 11, of which 6 were waited for; matrix products, arithmetic and copies ran while one was open for 4% of the time, Pallas kernels for 25%

profile of v11, /device:TPU:160, one launch (start us, length us, event | category | flops | bytes accessed | tf_op | source)
XLA Modules:
  0.0 116.1 jit_solution(11120456934186474395)
XLA Ops:
  0.6 1.5 %fusion.4 = (f32[32,4,768]{2,1,0:T(4,128)S(1)}, f32[32,4,768]{2,1,0:T(4,128)S(1)}) fusion(f32[32,32,768]{2,1,0:T(8,128)} %other_ref.11), kind=kLoop, calls=%fused_computation.17 | loop fusion | bytes 1572864 | tf_op jit(solution)/shard_map/slice | solution.py:89
  2.1 1.9 %collective-permute-start = (f32[32,4,768]{2,1,0:T(4,128)S(1)}, f32[32,4,768]{2,1,0:T(4,128)S(1)}, u32[]{:S(2)}, u32[]{:S(2)}) collective-permute-start(f32[32,4,768]{2,1,0:T(4,128)S(1)} %get-tuple-element.24), channel_id=1, source_target_pairs={{0,1},{1,2},{2,3},{3,4},{4,5},{5,6},{6,7},{7,8},{8,9},{9,10},{10,1... | collective-permute-start | bytes 1179656 | tf_op jit(solution)/shard_map/ppermute | solution.py:91
  4.1 0.0 copy-start.5
  4.1 0.0 copy-start.6
  4.1 0.0 copy-start.7
  4.1 0.0 copy-start.1
  4.1 8.1 %collective-permute-start.1 = (f32[32,4,768]{2,1,0:T(4,128)S(1)}, f32[32,4,768]{2,1,0:T(4,128)S(1)}, u32[]{:S(2)}, u32[]{:S(2)}) collective-permute-start(f32[32,4,768]{2,1,0:T(4,128)S(1)} %get-tuple-element.25), channel_id=1, source_target_pairs={{1,0},{2,1},{3,2},{4,3},{5,4},{6,5},{7,6},{8,7},{9,8},{10,9},{11,1... | collective-permute-start | bytes 1179656 | tf_op jit(solution)/shard_map/ppermute | solution.py:92
  12.3 5.6 %collective-permute-done = f32[32,4,768]{2,1,0:T(4,128)S(1)} collective-permute-done((f32[32,4,768]{2,1,0:T(4,128)S(1)}, f32[32,4,768]{2,1,0:T(4,128)S(1)}, u32[]{:S(2)}, u32[]{:S(2)}) %collective-permute-start) | collective-permute-done | bytes 393248 | tf_op jit(solution)/shard_map/ppermute | solution.py:91
  17.8 0.0 collective-permute-done.1
  17.8 2.3 %pad_maximum_fusion.pad_ref = f32[32,40,768]{2,1,0:T(8,128)S(1)} fusion(f32[32,4,768]{2,1,0:T(4,128)S(1)} %collective-permute-done.1, f32[32,32,768]{2,1,0:T(8,128)} %other_ref.11, f32[32,4,768]{2,1,0:T(4,128)S(1)} %collective-permute-done), kind=kLoop, calls=%fused_computation | loop fusion | flops 1966080 | bytes 7864320 | tf_op jit(solution)/shard_map/concatenate | solution.py:99
  20.1 0.0 copy-start.4
  20.1 0.1 fusion.2
  20.2 7.8 %collective-permute-start.2 = (f32[4,40,768]{2,1,0:T(8,128)S(1)}, f32[4,40,768]{2,1,0:T(8,128)S(1)}, u32[]{:S(2)}, u32[]{:S(2)}) collective-permute-start(f32[4,40,768]{2,1,0:T(8,128)S(1)} %get-tuple-element.18), channel_id=1, source_target_pairs={{0,32},{32,64},{64,96},{96,128},{128,160},{160,192},{192,224},{1,3... | collective-permute-start | bytes 1474568 | tf_op jit(solution)/shard_map/ppermute | solution.py:91
  28.0 1.9 %collective-permute-start.3 = (f32[4,40,768]{2,1,0:T(8,128)S(1)}, f32[4,40,768]{2,1,0:T(8,128)S(1)}, u32[]{:S(2)}, u32[]{:S(2)}) collective-permute-start(f32[4,40,768]{2,1,0:T(8,128)S(1)} %get-tuple-element.19), channel_id=1, source_target_pairs={{32,0},{64,32},{96,64},{128,96},{160,128},{192,160},{224,192},{33,... | collective-permute-start | bytes 1474568 | tf_op jit(solution)/shard_map/ppermute | solution.py:92
  29.9 0.0 copy-done.5
  29.9 0.0 copy-done.6
  30.0 0.0 copy-done.7
  30.0 0.1 pad_maximum_fusion.11.taps_ref
  30.0 0.0 copy-done.4
  30.0 0.0 copy-done.1
  30.1 13.2 %shard_map.69 = f32[24,32,768]{2,1,0:T(8,128)S(1)} custom-call(f32[27]{0:T(128)S(1)} %pad_maximum_fusion.11.taps_ref, f32[32,40,768]{2,1,0:T(8,128)} %copy-done.4, f32[32,32,768]{2,1,0:T(8,128)S(1)} %copy-done.1), custom_call_target="tpu_custom_call" | custom-call | flops 35389440 | bytes 9437184 | tf_op jit(solution)/shard_map/pallas_call | solution.py:74
  43.2 1.6 %fusion.3 = (f32[8,40,768]{2,1,0:T(8,128)S(1)}, f32[8,40,768]{2,1,0:T(8,128)S(1)}) fusion(f32[32,40,768]{2,1,0:T(8,128)} %copy-done.4), kind=kLoop, calls=%fused_computation.16 | loop fusion | bytes 3932160 | tf_op jit(solution)/shard_map/slice | solution.py:102
  44.9 0.0 collective-permute-done.2
  44.9 0.1 pad_maximum_fusion.3.pad_ref
  45.0 2.4 %shard_map.68 = f32[4,32,768]{2,1,0:T(8,128)S(1)} custom-call(f32[27]{0:T(128)S(1)} %pad_maximum_fusion.11.taps_ref, f32[12,40,768]{2,1,0:T(8,128)S(1)} %pad_maximum_fusion.3.pad_ref, f32[32,32,768]{2,1,0:T(8,128)S(1)} %copy-done.1), custom_call_target="tpu_custom_call" | custom-call | flops 5898240 | bytes 1572864 | tf_op jit(solution)/shard_map/pallas_call | solution.py:74
  47.4 0.0 collective-permute-done.3
  47.5 0.1 pad_maximum_fusion.4.pad_ref
  47.6 2.4 %shard_map.70 = f32[4,32,768]{2,1,0:T(8,128)S(1)} custom-call(f32[27]{0:T(128)S(1)} %pad_maximum_fusion.11.taps_ref, f32[12,40,768]{2,1,0:T(8,128)S(1)} %pad_maximum_fusion.4.pad_ref, f32[32,32,768]{2,1,0:T(8,128)S(1)} %copy-done.1), custom_call_target="tpu_custom_call" | custom-call | flops 5898240 | bytes 1572864 | tf_op jit(solution)/shard_map/pallas_call | solution.py:74
  50.0 0.1 pad_maximum_fusion.9
  50.1 1.9 %collective-permute-start.4 = (f32[32,4,768]{2,1,0:T(4,128)S(1)}, f32[32,4,768]{2,1,0:T(4,128)S(1)}, u32[]{:S(2)}, u32[]{:S(2)}) collective-permute-start(f32[32,4,768]{2,1,0:T(4,128)S(1)} %get-tuple-element.22), channel_id=1, source_target_pairs={{0,1},{1,2},{2,3},{3,4},{4,5},{5,6},{6,7},{7,8},{8,9},{9,10},{10,1... | collective-permute-start | bytes 1179656 | tf_op jit(solution)/shard_map/ppermute | solution.py:91
  52.1 0.0 copy-start
  52.1 8.1 %collective-permute-start.5 = (f32[32,4,768]{2,1,0:T(4,128)S(1)}, f32[32,4,768]{2,1,0:T(4,128)S(1)}, u32[]{:S(2)}, u32[]{:S(2)}) collective-permute-start(f32[32,4,768]{2,1,0:T(4,128)S(1)} %get-tuple-element.23), channel_id=1, source_target_pairs={{1,0},{2,1},{3,2},{4,3},{5,4},{6,5},{7,6},{8,7},{9,8},{10,9},{11,1... | collective-permute-start | bytes 1179656 | tf_op jit(solution)/shard_map/ppermute | solution.py:92
  60.2 6.0 %collective-permute-done.4 = f32[32,4,768]{2,1,0:T(4,128)S(1)} collective-permute-done((f32[32,4,768]{2,1,0:T(4,128)S(1)}, f32[32,4,768]{2,1,0:T(4,128)S(1)}, u32[]{:S(2)}, u32[]{:S(2)}) %collective-permute-start.4) | collective-permute-done | bytes 393248 | tf_op jit(solution)/shard_map/ppermute | solution.py:91
  66.2 2.3 %collective-permute-done.5 = f32[32,4,768]{2,1,0:T(4,128)S(1)} collective-permute-done((f32[32,4,768]{2,1,0:T(4,128)S(1)}, f32[32,4,768]{2,1,0:T(4,128)S(1)}, u32[]{:S(2)}, u32[]{:S(2)}) %collective-permute-start.5) | collective-permute-done | bytes 393248 | tf_op jit(solution)/shard_map/ppermute | solution.py:92
  68.6 0.5 pad_maximum_fusion.1.pad_ref
  69.0 0.0 copy-start.2
  69.1 1.9 %copy-done.2 = f32[32,40,768]{2,1,0:T(8,128)} copy-done((f32[32,40,768]{2,1,0:T(8,128)}, f32[32,40,768]{2,1,0:T(8,128)S(1)}, u32[]{:S(2)}) %copy-start.2) | copy-done | bytes 3932184
  70.9 1.0 fusion
  71.9 4.3 %collective-permute-start.6 = (f32[4,40,768]{2,1,0:T(8,128)}, f32[4,40,768]{2,1,0:T(8,128)}, u32[]{:S(2)}, u32[]{:S(2)}) collective-permute-start(f32[4,40,768]{2,1,0:T(8,128)} %get-tuple-element.14), channel_id=1, source_target_pairs={{0,32},{32,64},{64,96},{96,128},{128,160},{160,192},{192,224},{1,3... | collective-permute-start | bytes 1474568 | tf_op jit(solution)/shard_map/ppermute | solution.py:91
  76.2 2.3 %collective-permute-start.7 = (f32[4,40,768]{2,1,0:T(8,128)}, f32[4,40,768]{2,1,0:T(8,128)}, u32[]{:S(2)}, u32[]{:S(2)}) collective-permute-start(f32[4,40,768]{2,1,0:T(8,128)} %get-tuple-element.15), channel_id=1, source_target_pairs={{32,0},{64,32},{96,64},{128,96},{160,128},{192,160},{224,192},{33,... | collective-permute-start | bytes 1474568 | tf_op jit(solution)/shard_map/ppermute | solution.py:92
  78.6 0.1 rev.9
  78.7 0.1 rev.10
  78.8 0.1 rev.11
  78.8 0.1 pad_maximum_fusion.10.taps_ref
  78.9 0.0 copy-done
  78.9 0.0 copy-start.3
  78.9 13.3 %shard_map.72 = (f32[24,32,768]{2,1,0:T(8,128)S(1)}, f32[32,768]{1,0:T(8,128)S(1)}) custom-call(f32[27]{0:T(128)S(1)} %pad_maximum_fusion.10.taps_ref, f32[32,40,768]{2,1,0:T(8,128)} %copy-done.2, f32[32,32,768]{2,1,0:T(8,128)S(1)} %copy-done), custom_call_target="tpu_custom_call" | custom-call | flops 35389440 | bytes 9437184 | tf_op jit(solution)/shard_map/pallas_call | solution.py:74
  92.3 0.0 copy-done.3
  92.3 0.2 fusion.1
  92.4 0.0 collective-permute-done.6
  92.4 0.0 collective-permute-done.7
  92.5 1.4 %pad_maximum_fusion.5 = (f32[12,40,768]{2,1,0:T(8,128)S(1)}, f32[12,40,768]{2,1,0:T(8,128)S(1)}) fusion(f32[8,40,768]{2,1,0:T(8,128)S(1)} %get-tuple-element.16, f32[4,40,768]{2,1,0:T(8,128)} %collective-permute-done.6, f32[4,40,768]{2,1,0:T(8,128)} %collective-permute-done.7, f32[8,40,768]{2,1,0:T(8,128)S(1)} %get-tuple-element.17), kind=kLoop, calls=%fused_computation.5 | loop fusion | flops 737280 | bytes 5898240 | tf_op jit(solution)/shard_map/concatenate | solution.py:102
  93.9 2.4 %shard_map.71 = (f32[4,32,768]{2,1,0:T(8,128)S(1)}, f32[32,768]{1,0:T(8,128)S(1)}) custom-call(f32[27]{0:T(128)S(1)} %pad_maximum_fusion.10.taps_ref, f32[12,40,768]{2,1,0:T(8,128)S(1)} %get-tuple-element.26.pad_ref, f32[32,32,768]{2,1,0:T(8,128)S(1)} %copy-done), custom_call_target="tpu_custom_call" | custom-call | flops 5898240 | bytes 1572864 | tf_op jit(solution)/shard_map/pallas_call | solution.py:74
  96.3 2.4 %shard_map.73 = (f32[4,32,768]{2,1,0:T(8,128)S(1)}, f32[32,768]{1,0:T(8,128)S(1)}) custom-call(f32[27]{0:T(128)S(1)} %pad_maximum_fusion.10.taps_ref, f32[12,40,768]{2,1,0:T(8,128)S(1)} %get-tuple-element.27.pad_ref, f32[32,32,768]{2,1,0:T(8,128)S(1)} %copy-done), custom_call_target="tpu_custom_call" | custom-call | flops 5898240 | bytes 1572864 | tf_op jit(solution)/shard_map/pallas_call | solution.py:74
  98.7 4.2 %collective-permute-start.8 = (f32[32,768]{1,0:T(8,128)S(1)}, f32[32,768]{1,0:T(8,128)S(1)}, u32[]{:S(2)}, u32[]{:S(2)}) collective-permute-start(f32[32,768]{1,0:T(8,128)S(1)} %maximum_maximum_fusion), channel_id=1, source_target_pairs={{0,128},{32,160},{64,192},{96,224},{128,0},{160,32},{192,64},{224,... | collective-permute-start | bytes 294920 | tf_op jit(solution)/shard_map/ppermute | solution.py:117
  102.9 2.6 %collective-permute-done.8 = f32[32,768]{1,0:T(8,128)S(1)} collective-permute-done((f32[32,768]{1,0:T(8,128)S(1)}, f32[32,768]{1,0:T(8,128)S(1)}, u32[]{:S(2)}, u32[]{:S(2)}) %collective-permute-start.8) | collective-permute-done | bytes 98336 | tf_op jit(solution)/shard_map/ppermute | solution.py:117
  105.5 2.6 %collective-permute-start.9 = (f32[32,768]{1,0:T(8,128)S(1)}, f32[32,768]{1,0:T(8,128)S(1)}, u32[]{:S(2)}, u32[]{:S(2)}) collective-permute-start(f32[32,768]{1,0:T(8,128)S(1)} %max.17), channel_id=1, source_target_pairs={{0,64},{32,96},{64,0},{96,32},{128,192},{160,224},{192,128},{224,1... | collective-permute-start | bytes 294920 | tf_op jit(solution)/shard_map/ppermute | solution.py:117
  108.1 2.6 %collective-permute-done.9 = f32[32,768]{1,0:T(8,128)S(1)} collective-permute-done((f32[32,768]{1,0:T(8,128)S(1)}, f32[32,768]{1,0:T(8,128)S(1)}, u32[]{:S(2)}, u32[]{:S(2)}) %collective-permute-start.9) | collective-permute-done | bytes 98336 | tf_op jit(solution)/shard_map/ppermute | solution.py:117
  110.8 0.1 collective-permute-start.10
  110.9 2.0 %pad_maximum_fusion.2 = f32[32,32,768]{2,1,0:T(8,128)} fusion(f32[4,32,768]{2,1,0:T(8,128)S(1)} %get-tuple-element.10, f32[24,32,768]{2,1,0:T(8,128)S(1)} %get-tuple-element.9, f32[4,32,768]{2,1,0:T(8,128)S(1)} %get-tuple-element.8), kind=kLoop, calls=%fused_computation.2 | loop fusion | flops 1572864 | bytes 6291456 | tf_op jit(solution)/shard_map/concatenate | solution.py:106
  112.9 2.6 %collective-permute-done.10 = f32[32,768]{1,0:T(8,128)S(1)} collective-permute-done((f32[32,768]{1,0:T(8,128)S(1)}, f32[32,768]{1,0:T(8,128)S(1)}, u32[]{:S(2)}, u32[]{:S(2)}) %collective-permute-start.10) | collective-permute-done | bytes 98336 | tf_op jit(solution)/shard_map/ppermute | solution.py:117
  115.5 0.7 max.19
  (3 shorter events, 0.1 us)
Async XLA Ops:
  2.1 15.7 %collective-permute-start = (f32[32,4,768]{2,1,0:T(4,128)S(1)}, f32[32,4,768]{2,1,0:T(4,128)S(1)}, u32[]{:S(2)}, u32[]{:S(2)}) collective-permute-start(f32[32,4,768]{2,1,0:T(4,128)S(1)} %get-tuple-element.24), channel_id=1, source_target_pairs={{0,1},{1,2},{2,3},{3,4},{4,5},{5,6},{6,7},{7,8},{8,9},{9,10},{10,1... | collective-permute-start | bytes 1179656 | tf_op jit(solution)/shard_map/ppermute | solution.py:91
  4.1 25.9 %copy-start.5 = (f32[9]{0:T(128)S(1)}, f32[9]{0:T(128)}, u32[]{:S(2)}) copy-start(f32[9]{0:T(128)} %param.7) | copy-start | bytes 112
  4.1 25.9 %copy-start.6 = (f32[9]{0:T(128)S(1)}, f32[9]{0:T(128)}, u32[]{:S(2)}) copy-start(f32[9]{0:T(128)} %param.8) | copy-start | bytes 112
  4.1 25.9 %copy-start.7 = (f32[9]{0:T(128)S(1)}, f32[9]{0:T(128)}, u32[]{:S(2)}) copy-start(f32[9]{0:T(128)} %param.9) | copy-start | bytes 112
  4.1 25.9 %copy-start.1 = (f32[32,32,768]{2,1,0:T(8,128)S(1)}, f32[32,32,768]{2,1,0:T(8,128)}, u32[]{:S(2)}) copy-start(f32[32,32,768]{2,1,0:T(8,128)} %other_ref.8) | copy-start | bytes 9437188
  4.1 13.7 %collective-permute-start.1 = (f32[32,4,768]{2,1,0:T(4,128)S(1)}, f32[32,4,768]{2,1,0:T(4,128)S(1)}, u32[]{:S(2)}, u32[]{:S(2)}) collective-permute-start(f32[32,4,768]{2,1,0:T(4,128)S(1)} %get-tuple-element.25), channel_id=1, source_target_pairs={{1,0},{2,1},{3,2},{4,3},{5,4},{6,5},{7,6},{8,7},{9,8},{10,9},{11,1... | collective-permute-start | bytes 1179656 | tf_op jit(solution)/shard_map/ppermute | solution.py:92
  20.1 9.9 %copy-start.4 = (f32[32,40,768]{2,1,0:T(8,128)}, f32[32,40,768]{2,1,0:T(8,128)S(1)}, u32[]{:S(2)}) copy-start(f32[32,40,768]{2,1,0:T(8,128)S(1)} %pad_maximum_fusion.pad_ref) | copy-start | bytes 11796484
  20.2 24.7 %collective-permute-start.2 = (f32[4,40,768]{2,1,0:T(8,128)S(1)}, f32[4,40,768]{2,1,0:T(8,128)S(1)}, u32[]{:S(2)}, u32[]{:S(2)}) collective-permute-start(f32[4,40,768]{2,1,0:T(8,128)S(1)} %get-tuple-element.18), channel_id=1, source_target_pairs={{0,32},{32,64},{64,96},{96,128},{128,160},{160,192},{192,224},{1,3... | collective-permute-start | bytes 1474568 | tf_op jit(solution)/shard_map/ppermute | solution.py:91
  28.0 19.4 %collective-permute-start.3 = (f32[4,40,768]{2,1,0:T(8,128)S(1)}, f32[4,40,768]{2,1,0:T(8,128)S(1)}, u32[]{:S(2)}, u32[]{:S(2)}) collective-permute-start(f32[4,40,768]{2,1,0:T(8,128)S(1)} %get-tuple-element.19), channel_id=1, source_target_pairs={{32,0},{64,32},{96,64},{128,96},{160,128},{192,160},{224,192},{33,... | collective-permute-start | bytes 1474568 | tf_op jit(solution)/shard_map/ppermute | solution.py:92
  50.1 16.1 %collective-permute-start.4 = (f32[32,4,768]{2,1,0:T(4,128)S(1)}, f32[32,4,768]{2,1,0:T(4,128)S(1)}, u32[]{:S(2)}, u32[]{:S(2)}) collective-permute-start(f32[32,4,768]{2,1,0:T(4,128)S(1)} %get-tuple-element.22), channel_id=1, source_target_pairs={{0,1},{1,2},{2,3},{3,4},{4,5},{5,6},{6,7},{7,8},{8,9},{9,10},{10,1... | collective-permute-start | bytes 1179656 | tf_op jit(solution)/shard_map/ppermute | solution.py:91
  52.1 26.9 %copy-start = (f32[32,32,768]{2,1,0:T(8,128)S(1)}, f32[32,32,768]{2,1,0:T(8,128)}, u32[]{:S(2)}) copy-start(f32[32,32,768]{2,1,0:T(8,128)} %other_ref.11) | copy-start | bytes 9437188
  52.1 16.5 %collective-permute-start.5 = (f32[32,4,768]{2,1,0:T(4,128)S(1)}, f32[32,4,768]{2,1,0:T(4,128)S(1)}, u32[]{:S(2)}, u32[]{:S(2)}) collective-permute-start(f32[32,4,768]{2,1,0:T(4,128)S(1)} %get-tuple-element.23), channel_id=1, source_target_pairs={{1,0},{2,1},{3,2},{4,3},{5,4},{6,5},{7,6},{8,7},{9,8},{10,9},{11,1... | collective-permute-start | bytes 1179656 | tf_op jit(solution)/shard_map/ppermute | solution.py:92
  69.0 1.9 %copy-start.2 = (f32[32,40,768]{2,1,0:T(8,128)}, f32[32,40,768]{2,1,0:T(8,128)S(1)}, u32[]{:S(2)}) copy-start(f32[32,40,768]{2,1,0:T(8,128)S(1)} %pad_maximum_fusion.1.pad_ref) | copy-start | bytes 11796484
  71.9 20.5 %collective-permute-start.6 = (f32[4,40,768]{2,1,0:T(8,128)}, f32[4,40,768]{2,1,0:T(8,128)}, u32[]{:S(2)}, u32[]{:S(2)}) collective-permute-start(f32[4,40,768]{2,1,0:T(8,128)} %get-tuple-element.14), channel_id=1, source_target_pairs={{0,32},{32,64},{64,96},{96,128},{128,160},{160,192},{192,224},{1,3... | collective-permute-start | bytes 1474568 | tf_op jit(solution)/shard_map/ppermute | solution.py:91
  76.2 16.2 %collective-permute-start.7 = (f32[4,40,768]{2,1,0:T(8,128)}, f32[4,40,768]{2,1,0:T(8,128)}, u32[]{:S(2)}, u32[]{:S(2)}) collective-permute-start(f32[4,40,768]{2,1,0:T(8,128)} %get-tuple-element.15), channel_id=1, source_target_pairs={{32,0},{64,32},{96,64},{128,96},{160,128},{192,160},{224,192},{33,... | collective-permute-start | bytes 1474568 | tf_op jit(solution)/shard_map/ppermute | solution.py:92
  78.9 13.3 %copy-start.3 = (f32[32,40,768]{2,1,0:T(8,128)S(1)}, f32[32,40,768]{2,1,0:T(8,128)}, u32[]{:S(2)}) copy-start(f32[32,40,768]{2,1,0:T(8,128)} %copy-done.2) | copy-start | bytes 11796484
  98.7 6.8 %collective-permute-start.8 = (f32[32,768]{1,0:T(8,128)S(1)}, f32[32,768]{1,0:T(8,128)S(1)}, u32[]{:S(2)}, u32[]{:S(2)}) collective-permute-start(f32[32,768]{1,0:T(8,128)S(1)} %maximum_maximum_fusion), channel_id=1, source_target_pairs={{0,128},{32,160},{64,192},{96,224},{128,0},{160,32},{192,64},{224,... | collective-permute-start | bytes 294920 | tf_op jit(solution)/shard_map/ppermute | solution.py:117
  105.5 5.2 %collective-permute-start.9 = (f32[32,768]{1,0:T(8,128)S(1)}, f32[32,768]{1,0:T(8,128)S(1)}, u32[]{:S(2)}, u32[]{:S(2)}) collective-permute-start(f32[32,768]{1,0:T(8,128)S(1)} %max.17), channel_id=1, source_target_pairs={{0,64},{32,96},{64,0},{96,32},{128,192},{160,224},{192,128},{224,1... | collective-permute-start | bytes 294920 | tf_op jit(solution)/shard_map/ppermute | solution.py:117
  110.8 4.7 %collective-permute-start.10 = (f32[32,768]{1,0:T(8,128)S(1)}, f32[32,768]{1,0:T(8,128)S(1)}, u32[]{:S(2)}, u32[]{:S(2)}) collective-permute-start(f32[32,768]{1,0:T(8,128)S(1)} %max.18), channel_id=1, source_target_pairs={{0,32},{32,0},{64,96},{96,64},{128,160},{160,128},{192,224},{224,1... | collective-permute-start | bytes 294920 | tf_op jit(solution)/shard_map/ppermute | solution.py:117

commit v12 on v11

--- a/solution.py
+++ b/solution.py
@@ -96,8 +96,14 @@
 def split_blur(mode, taps, shard, other, width):
     nz = shard.shape[0]
     before, after = halo_pair(shard, "gy", 1, width)
+    peers = lax.axis_size("gz")
+    up = [(i, i + 1) for i in range(peers - 1)]
+    down = [(i + 1, i) for i in range(peers - 1)]
+    first = jnp.concatenate([before[:width], shard[:width], after[:width]], axis=1)
+    last = jnp.concatenate([before[nz - width :], shard[nz - width :], after[nz - width :]], axis=1)
+    below = lax.ppermute(last, "gz", up)
+    above = lax.ppermute(first, "gz", down)
     rows_padded = jnp.concatenate([before, shard, after], axis=1)
-    below, above = halo_pair(rows_padded, "gz", 0, width)
     inner = fused_blur(mode, [(0, nz - 2 * width, 0, width)], taps, rows_padded, other)
     low_slab = jnp.concatenate([below, rows_padded[: 2 * width]], axis=0)
     high_slab = jnp.concatenate([rows_padded[nz - 2 * width :], above], axis=0)

time: 117 us -> 122 us (1.043)
  other arithmetic: 7.41 us -> 12.5 us
  waiting for transfers between devices: 21.7 us -> 26.6 us
  starting transfers between devices: 43.3 us -> 40 us
  local copies, waits for them, and re-layouts: 6.59 us -> 5.13 us
    ppermute x0 -> x4, starting transfers between devices: none -> 16.4 us  [the longest x2 8.44 us: split_blur(): above = lax.ppermute(first, 'gz', down)]
    ppermute x4 -> x2, starting transfers between devices: 15.9 us -> 3.83 us  [halo_pair(): before = lax.ppermute(last, axis, up)]
    ppermute x4 -> x2, waiting for transfers between devices: 2.35 us -> 7.54 us  [halo_pair(): after = lax.ppermute(first, axis, down)]
    ppermute x4 -> x2, starting transfers between devices: 20.5 us -> 15.9 us  [halo_pair(): after = lax.ppermute(first, axis, down)]
    concatenate x2, other arithmetic: 2.79 us -> 6.08 us  [split_blur(): rows_padded = jnp.concatenate([before, shard, after], axis=1)]
    ppermute x3, starting transfers between devices: 6.93 us -> 3.91 us  [butterfly_max(): value = jnp.maximum(value, lax.ppermute(value, axis, pairs))]
    slice x0 -> x5, local copies, waits for them, and re-layouts: none -> 2.85 us  [the longest x1 1.17 us: split_blur(): shard[nz - width:]]
    ppermute x4 -> x2, waiting for transfers between devices: 11.6 us -> 9.21 us  [halo_pair(): before = lax.ppermute(last, axis, up)]
  transfers between devices with their start and end apart: 11 -> 11, of which waited for: 6 -> 6; matrix products, arithmetic and copies ran while one was open for 4% -> 10% of each run, Pallas kernels for 25% -> 24%
where the time goes in v12:
time: 122 us; the launch traced here: 121 us
  starting transfers between devices  40 us (33%)
  Pallas kernels  36.2 us (30%)
  waiting for transfers between devices  26.6 us (22%)
  other arithmetic  12.5 us (10%)
  local copies, waits for them, and re-layouts  5.13 us (4%)
    pallas_call x6, Pallas kernels, fused_blur(): pl.pallas_call(functools.partial(blur_kernel, mode, tuple(segments)), out...  36.2 us
    ppermute x2, starting transfers between devices, halo_pair(): after = lax.ppermute(first, axis, down)  15.9 us
    ppermute x3, waiting for transfers between devices, butterfly_max(): value = jnp.maximum(value, lax.ppermute(value, axis, pairs))  9.8 us
    ppermute x2, waiting for transfers between devices, halo_pair(): before = lax.ppermute(last, axis, up)  9.21 us
    ppermute x2, starting transfers between devices, split_blur(): above = lax.ppermute(first, 'gz', down)  8.44 us
    ppermute x2, starting transfers between devices, split_blur(): below = lax.ppermute(last, 'gz', up)  7.93 us
    ppermute x2, waiting for transfers between devices, halo_pair(): after = lax.ppermute(first, axis, down)  7.54 us
    concatenate x2, other arithmetic, split_blur(): rows_padded = jnp.concatenate([before, shard, after], axis=1)  6.08 us
  transfers between devices with their start and end apart: 11, of which 6 were waited for; matrix products, arithmetic and copies ran while one was open for 10% of the time, Pallas kernels for 24%

profile of v12, /device:TPU:160, one launch (start us, length us, event | category | flops | bytes accessed | tf_op | source)
XLA Modules:
  0.0 121.5 jit_solution(15925558021503148984)
XLA Ops:
  0.6 0.0 copy-start
  0.6 0.0 copy-start.9
  0.7 0.0 copy-start.8
  0.7 0.0 copy-start.7
  0.7 1.7 %fusion.3 = (f32[32,4,768]{2,1,0:T(4,128)S(1)}, f32[32,4,768]{2,1,0:T(4,128)S(1)}) fusion(f32[32,32,768]{2,1,0:T(8,128)} %other_ref.11), kind=kLoop, calls=%fused_computation.20 | loop fusion | bytes 1572864 | tf_op jit(solution)/shard_map/slice | solution.py:89
  2.3 1.9 %collective-permute-start = (f32[32,4,768]{2,1,0:T(4,128)S(1)}, f32[32,4,768]{2,1,0:T(4,128)S(1)}, u32[]{:S(2)}, u32[]{:S(2)}) collective-permute-start(f32[32,4,768]{2,1,0:T(4,128)S(1)} %get-tuple-element.22), channel_id=1, source_target_pairs={{0,1},{1,2},{2,3},{3,4},{4,5},{5,6},{6,7},{7,8},{8,9},{9,10},{10,1... | collective-permute-start | bytes 1179656 | tf_op jit(solution)/shard_map/ppermute | solution.py:91
  4.3 7.9 %collective-permute-start.1 = (f32[32,4,768]{2,1,0:T(4,128)S(1)}, f32[32,4,768]{2,1,0:T(4,128)S(1)}, u32[]{:S(2)}, u32[]{:S(2)}) collective-permute-start(f32[32,4,768]{2,1,0:T(4,128)S(1)} %get-tuple-element.23), channel_id=1, source_target_pairs={{1,0},{2,1},{3,2},{4,3},{5,4},{6,5},{7,6},{8,7},{9,8},{10,9},{11,1... | collective-permute-start | bytes 1179656 | tf_op jit(solution)/shard_map/ppermute | solution.py:92
  12.1 1.2 fusion.2
  13.3 0.0 copy-done.9
  13.3 0.0 copy-done.8
  13.3 0.0 copy-done.7
  13.3 0.1 pad_maximum_fusion.15.taps_ref
  13.4 4.6 %collective-permute-done = f32[32,4,768]{2,1,0:T(4,128)S(1)} collective-permute-done((f32[32,4,768]{2,1,0:T(4,128)S(1)}, f32[32,4,768]{2,1,0:T(4,128)S(1)}, u32[]{:S(2)}, u32[]{:S(2)}) %collective-permute-start) | collective-permute-done | bytes 393248 | tf_op jit(solution)/shard_map/ppermute | solution.py:91
  18.0 0.0 collective-permute-done.1
  18.0 0.1 pad_maximum_fusion.8
  18.1 6.5 %collective-permute-start.3 = (f32[4,40,768]{2,1,0:T(8,128)S(1)}, f32[4,40,768]{2,1,0:T(8,128)}, u32[]{:S(2)}, u32[]{:S(2)}) collective-permute-start(f32[4,40,768]{2,1,0:T(8,128)S(1)} %pad_maximum_fusion.8), channel_id=1, source_target_pairs={{32,0},{64,32},{96,64},{128,96},{160,128},{192,160},{224,192},{33,... | collective-permute-start | bytes 1474568 | tf_op jit(solution)/shard_map/ppermute | solution.py:105
  24.6 0.1 pad_maximum_fusion.7
  24.7 0.0 copy-start.1
  24.7 3.1 %collective-permute-start.2 = (f32[4,40,768]{2,1,0:T(8,128)S(1)}, f32[4,40,768]{2,1,0:T(8,128)S(1)}, u32[]{:S(2)}, u32[]{:S(2)}) collective-permute-start(f32[4,40,768]{2,1,0:T(8,128)S(1)} %pad_maximum_fusion.7), channel_id=1, source_target_pairs={{0,32},{32,64},{64,96},{96,128},{128,160},{160,192},{192,224},{1,3... | collective-permute-start | bytes 1474568 | tf_op jit(solution)/shard_map/ppermute | solution.py:104
  27.8 0.0 copy-done
  27.9 2.4 %pad_maximum_fusion.pad_ref = f32[32,40,768]{2,1,0:T(8,128)} fusion(f32[32,4,768]{2,1,0:T(4,128)S(1)} %collective-permute-done.1, f32[32,32,768]{2,1,0:T(8,128)S(1)} %copy-done, f32[32,4,768]{2,1,0:T(4,128)S(1)} %collective-permute-done), kind=kLoop, calls=%fused_computation | loop fusion | flops 1966080 | bytes 7864320 | tf_op jit(solution)/shard_map/concatenate | solution.py:106
  30.3 0.0 copy-done.1
  30.3 13.3 %shard_map.69 = f32[24,32,768]{2,1,0:T(8,128)S(1)} custom-call(f32[27]{0:T(128)S(1)} %pad_maximum_fusion.15.taps_ref, f32[32,40,768]{2,1,0:T(8,128)} %pad_maximum_fusion.pad_ref, f32[32,32,768]{2,1,0:T(8,128)S(1)} %copy-done.1), custom_call_target="tpu_custom_call" | custom-call | flops 35389440 | bytes 9437184 | tf_op jit(solution)/shard_map/pallas_call | solution.py:74
  43.6 0.0 copy-start.2
  43.6 0.1 fusion.1
  43.8 0.0 collective-permute-done.2
  43.8 0.1 pad_maximum_fusion.3.pad_ref
  43.9 2.4 %shard_map.68 = f32[4,32,768]{2,1,0:T(8,128)S(1)} custom-call(f32[27]{0:T(128)S(1)} %pad_maximum_fusion.15.taps_ref, f32[12,40,768]{2,1,0:T(8,128)S(1)} %pad_maximum_fusion.3.pad_ref, f32[32,32,768]{2,1,0:T(8,128)S(1)} %copy-done.1), custom_call_target="tpu_custom_call" | custom-call | flops 5898240 | bytes 1572864 | tf_op jit(solution)/shard_map/pallas_call | solution.py:74
  46.3 0.0 collective-permute-done.3
  46.3 1.1 pad_maximum_fusion.4.pad_ref
  47.4 2.4 %shard_map.70 = f32[4,32,768]{2,1,0:T(8,128)S(1)} custom-call(f32[27]{0:T(128)S(1)} %pad_maximum_fusion.15.taps_ref, f32[12,40,768]{2,1,0:T(8,128)S(1)} %pad_maximum_fusion.4.pad_ref, f32[32,32,768]{2,1,0:T(8,128)S(1)} %copy-done.1), custom_call_target="tpu_custom_call" | custom-call | flops 5898240 | bytes 1572864 | tf_op jit(solution)/shard_map/pallas_call | solution.py:74
  49.8 0.0 copy-done.2
  49.8 0.0 copy-start.4
  49.8 1.1 pad_maximum_fusion.13
  50.9 1.9 %collective-permute-start.4 = (f32[32,4,768]{2,1,0:T(4,128)}, f32[32,4,768]{2,1,0:T(4,128)}, u32[]{:S(2)}, u32[]{:S(2)}) collective-permute-start(f32[32,4,768]{2,1,0:T(4,128)} %get-tuple-element.18), channel_id=1, source_target_pairs={{0,1},{1,2},{2,3},{3,4},{4,5},{5,6},{6,7},{7,8},{8,9},{9,10},{10,1... | collective-permute-start | bytes 1179656 | tf_op jit(solution)/shard_map/ppermute | solution.py:91
  52.8 8.1 %collective-permute-start.5 = (f32[32,4,768]{2,1,0:T(4,128)}, f32[32,4,768]{2,1,0:T(4,128)}, u32[]{:S(2)}, u32[]{:S(2)}) collective-permute-start(f32[32,4,768]{2,1,0:T(4,128)} %get-tuple-element.19), channel_id=1, source_target_pairs={{1,0},{2,1},{3,2},{4,3},{5,4},{6,5},{7,6},{8,7},{9,8},{10,9},{11,1... | collective-permute-start | bytes 1179656 | tf_op jit(solution)/shard_map/ppermute | solution.py:92
  60.9 0.1 rev.9
  61.0 0.1 rev.10
  61.1 0.1 rev.11
  61.2 0.1 pad_maximum_fusion.14.taps_ref
  61.2 4.6 %collective-permute-done.4 = f32[32,4,768]{2,1,0:T(4,128)} collective-permute-done((f32[32,4,768]{2,1,0:T(4,128)}, f32[32,4,768]{2,1,0:T(4,128)}, u32[]{:S(2)}, u32[]{:S(2)}) %collective-permute-start.4) | collective-permute-done | bytes 393248 | tf_op jit(solution)/shard_map/ppermute | solution.py:91
  65.9 0.8 fusion.4
  66.7 7.5 %collective-permute-done.5 = f32[32,4,768]{2,1,0:T(4,128)} collective-permute-done((f32[32,4,768]{2,1,0:T(4,128)}, f32[32,4,768]{2,1,0:T(4,128)}, u32[]{:S(2)}, u32[]{:S(2)}) %collective-permute-start.5) | collective-permute-done | bytes 393248 | tf_op jit(solution)/shard_map/ppermute | solution.py:92
  74.2 0.8 fusion.5
  75.1 0.1 pad_maximum_fusion.10
  75.1 1.9 %collective-permute-start.7 = (f32[4,40,768]{2,1,0:T(8,128)S(1)}, f32[4,40,768]{2,1,0:T(8,128)S(1)}, u32[]{:S(2)}, u32[]{:S(2)}) collective-permute-start(f32[4,40,768]{2,1,0:T(8,128)S(1)} %pad_maximum_fusion.10), channel_id=1, source_target_pairs={{32,0},{64,32},{96,64},{128,96},{160,128},{192,160},{224,192},{33,... | collective-permute-start | bytes 1474568 | tf_op jit(solution)/shard_map/ppermute | solution.py:105
  77.1 1.1 pad_maximum_fusion.9
  78.1 4.8 %collective-permute-start.6 = (f32[4,40,768]{2,1,0:T(8,128)S(1)}, f32[4,40,768]{2,1,0:T(8,128)S(1)}, u32[]{:S(2)}, u32[]{:S(2)}) collective-permute-start(f32[4,40,768]{2,1,0:T(8,128)S(1)} %pad_maximum_fusion.9), channel_id=1, source_target_pairs={{0,32},{32,64},{64,96},{96,128},{128,160},{160,192},{192,224},{1,3... | collective-permute-start | bytes 1474568 | tf_op jit(solution)/shard_map/ppermute | solution.py:104
  83.0 3.7 %pad_maximum_fusion.1.pad_ref = f32[32,40,768]{2,1,0:T(8,128)} fusion(f32[32,4,768]{2,1,0:T(4,128)} %collective-permute-done.5, f32[4,32,768]{2,1,0:T(8,128)} %copy-done.4, f32[24,32,768]{2,1,0:T(8,128)S(1)} %copy-done.3, f32[4,32,768]{2,1,0:T(8,128)S(1)} %shard_map.68, f32[32,4,768]{2,1,0:T(4,128)} %collective-permute-done.4), kind=kLoop, calls=%fused_computation.1 | loop fusion | flops 3932160 | bytes 7864320 | tf_op jit(solution)/shard_map/concatenate | solution.py:106
  86.6 13.3 %shard_map.72 = (f32[24,32,768]{2,1,0:T(8,128)S(1)}, f32[32,768]{1,0:T(8,128)S(1)}) custom-call(f32[27]{0:T(128)S(1)} %pad_maximum_fusion.14.taps_ref, f32[32,40,768]{2,1,0:T(8,128)} %pad_maximum_fusion.1.pad_ref, f32[32,32,768]{2,1,0:T(8,128)S(1)} %copy-done), custom_call_target="tpu_custom_call" | custom-call | flops 35389440 | bytes 9437184 | tf_op jit(solution)/shard_map/pallas_call | solution.py:74
  100.0 0.2 fusion
  100.1 0.0 collective-permute-done.7
  100.1 0.0 collective-permute-done.6
  100.2 0.2 pad_maximum_fusion.5
  100.4 2.4 %shard_map.71 = (f32[4,32,768]{2,1,0:T(8,128)S(1)}, f32[32,768]{1,0:T(8,128)S(1)}) custom-call(f32[27]{0:T(128)S(1)} %pad_maximum_fusion.14.taps_ref, f32[12,40,768]{2,1,0:T(8,128)S(1)} %get-tuple-element.32.pad_ref, f32[32,32,768]{2,1,0:T(8,128)S(1)} %copy-done), custom_call_target="tpu_custom_call" | custom-call | flops 5898240 | bytes 1572864 | tf_op jit(solution)/shard_map/pallas_call | solution.py:74
  102.7 2.4 %shard_map.73 = (f32[4,32,768]{2,1,0:T(8,128)S(1)}, f32[32,768]{1,0:T(8,128)S(1)}) custom-call(f32[27]{0:T(128)S(1)} %pad_maximum_fusion.14.taps_ref, f32[12,40,768]{2,1,0:T(8,128)S(1)} %get-tuple-element.33.pad_ref, f32[32,32,768]{2,1,0:T(8,128)S(1)} %copy-done), custom_call_target="tpu_custom_call" | custom-call | flops 5898240 | bytes 1572864 | tf_op jit(solution)/shard_map/pallas_call | solution.py:74
  105.2 2.8 %collective-permute-start.8 = (f32[32,768]{1,0:T(8,128)S(1)}, f32[32,768]{1,0:T(8,128)S(1)}, u32[]{:S(2)}, u32[]{:S(2)}) collective-permute-start(f32[32,768]{1,0:T(8,128)S(1)} %maximum_maximum_fusion), channel_id=1, source_target_pairs={{0,128},{32,160},{64,192},{96,224},{128,0},{160,32},{192,64},{224,... | collective-permute-start | bytes 294920 | tf_op jit(solution)/shard_map/ppermute | solution.py:123
  108.0 3.4 %collective-permute-done.8 = f32[32,768]{1,0:T(8,128)S(1)} collective-permute-done((f32[32,768]{1,0:T(8,128)S(1)}, f32[32,768]{1,0:T(8,128)S(1)}, u32[]{:S(2)}, u32[]{:S(2)}) %collective-permute-start.8) | collective-permute-done | bytes 98336 | tf_op jit(solution)/shard_map/ppermute | solution.py:123
  111.4 1.0 collective-permute-start.9
  112.4 3.7 %collective-permute-done.9 = f32[32,768]{1,0:T(8,128)S(1)} collective-permute-done((f32[32,768]{1,0:T(8,128)S(1)}, f32[32,768]{1,0:T(8,128)S(1)}, u32[]{:S(2)}, u32[]{:S(2)}) %collective-permute-start.9) | collective-permute-done | bytes 98336 | tf_op jit(solution)/shard_map/ppermute | solution.py:123
  116.1 0.1 collective-permute-start.10
  116.2 1.9 %pad_maximum_fusion.2 = f32[32,32,768]{2,1,0:T(8,128)} fusion(f32[4,32,768]{2,1,0:T(8,128)S(1)} %get-tuple-element.10, f32[24,32,768]{2,1,0:T(8,128)S(1)} %get-tuple-element.9, f32[4,32,768]{2,1,0:T(8,128)S(1)} %get-tuple-element.8), kind=kLoop, calls=%fused_computation.2 | loop fusion | flops 1572864 | bytes 6291456 | tf_op jit(solution)/shard_map/concatenate | solution.py:112
  118.1 2.7 %collective-permute-done.10 = f32[32,768]{1,0:T(8,128)S(1)} collective-permute-done((f32[32,768]{1,0:T(8,128)S(1)}, f32[32,768]{1,0:T(8,128)S(1)}, u32[]{:S(2)}, u32[]{:S(2)}) %collective-permute-start.10) | collective-permute-done | bytes 98336 | tf_op jit(solution)/shard_map/ppermute | solution.py:123
  120.8 0.7 max.19
  (12 shorter events, 0.1 us)
Async XLA Ops:
  0.6 27.2 %copy-start = (f32[32,32,768]{2,1,0:T(8,128)S(1)}, f32[32,32,768]{2,1,0:T(8,128)}, u32[]{:S(2)}) copy-start(f32[32,32,768]{2,1,0:T(8,128)} %other_ref.11) | copy-start | bytes 9437188
  0.6 12.7 %copy-start.9 = (f32[9]{0:T(128)S(1)}, f32[9]{0:T(128)}, u32[]{:S(2)}) copy-start(f32[9]{0:T(128)} %param.9) | copy-start | bytes 112
  0.7 12.7 %copy-start.8 = (f32[9]{0:T(128)S(1)}, f32[9]{0:T(128)}, u32[]{:S(2)}) copy-start(f32[9]{0:T(128)} %param.8) | copy-start | bytes 112
  0.7 12.7 %copy-start.7 = (f32[9]{0:T(128)S(1)}, f32[9]{0:T(128)}, u32[]{:S(2)}) copy-start(f32[9]{0:T(128)} %param.7) | copy-start | bytes 112
  2.3 15.7 %collective-permute-start = (f32[32,4,768]{2,1,0:T(4,128)S(1)}, f32[32,4,768]{2,1,0:T(4,128)S(1)}, u32[]{:S(2)}, u32[]{:S(2)}) collective-permute-start(f32[32,4,768]{2,1,0:T(4,128)S(1)} %get-tuple-element.22), channel_id=1, source_target_pairs={{0,1},{1,2},{2,3},{3,4},{4,5},{5,6},{6,7},{7,8},{8,9},{9,10},{10,1... | collective-permute-start | bytes 1179656 | tf_op jit(solution)/shard_map/ppermute | solution.py:91
  4.3 13.7 %collective-permute-start.1 = (f32[32,4,768]{2,1,0:T(4,128)S(1)}, f32[32,4,768]{2,1,0:T(4,128)S(1)}, u32[]{:S(2)}, u32[]{:S(2)}) collective-permute-start(f32[32,4,768]{2,1,0:T(4,128)S(1)} %get-tuple-element.23), channel_id=1, source_target_pairs={{1,0},{2,1},{3,2},{4,3},{5,4},{6,5},{7,6},{8,7},{9,8},{10,9},{11,1... | collective-permute-start | bytes 1179656 | tf_op jit(solution)/shard_map/ppermute | solution.py:92
  18.1 28.2 %collective-permute-start.3 = (f32[4,40,768]{2,1,0:T(8,128)S(1)}, f32[4,40,768]{2,1,0:T(8,128)}, u32[]{:S(2)}, u32[]{:S(2)}) collective-permute-start(f32[4,40,768]{2,1,0:T(8,128)S(1)} %pad_maximum_fusion.8), channel_id=1, source_target_pairs={{32,0},{64,32},{96,64},{128,96},{160,128},{192,160},{224,192},{33,... | collective-permute-start | bytes 1474568 | tf_op jit(solution)/shard_map/ppermute | solution.py:105
  24.7 5.5 %copy-start.1 = (f32[32,32,768]{2,1,0:T(8,128)S(1)}, f32[32,32,768]{2,1,0:T(8,128)}, u32[]{:S(2)}) copy-start(f32[32,32,768]{2,1,0:T(8,128)} %other_ref.8) | copy-start | bytes 9437188
  24.7 19.0 %collective-permute-start.2 = (f32[4,40,768]{2,1,0:T(8,128)S(1)}, f32[4,40,768]{2,1,0:T(8,128)S(1)}, u32[]{:S(2)}, u32[]{:S(2)}) collective-permute-start(f32[4,40,768]{2,1,0:T(8,128)S(1)} %pad_maximum_fusion.7), channel_id=1, source_target_pairs={{0,32},{32,64},{64,96},{96,128},{128,160},{160,192},{192,224},{1,3... | collective-permute-start | bytes 1474568 | tf_op jit(solution)/shard_map/ppermute | solution.py:104
  30.3 13.3 %copy-start.6 = (f32[32,40,768]{2,1,0:T(8,128)S(1)}, f32[32,40,768]{2,1,0:T(8,128)}, u32[]{:S(2)}) copy-start(f32[32,40,768]{2,1,0:T(8,128)} %pad_maximum_fusion.pad_ref) | copy-start | bytes 11796484
  43.6 6.2 %copy-start.2 = (f32[24,32,768]{2,1,0:T(8,128)}, f32[24,32,768]{2,1,0:T(8,128)S(1)}, u32[]{:S(2)}) copy-start(f32[24,32,768]{2,1,0:T(8,128)S(1)} %shard_map.69) | copy-start | bytes 7077892
  49.8 1.1 copy-start.4
  50.9 15.0 %collective-permute-start.4 = (f32[32,4,768]{2,1,0:T(4,128)}, f32[32,4,768]{2,1,0:T(4,128)}, u32[]{:S(2)}, u32[]{:S(2)}) collective-permute-start(f32[32,4,768]{2,1,0:T(4,128)} %get-tuple-element.18), channel_id=1, source_target_pairs={{0,1},{1,2},{2,3},{3,4},{4,5},{5,6},{6,7},{7,8},{8,9},{9,10},{10,1... | collective-permute-start | bytes 1179656 | tf_op jit(solution)/shard_map/ppermute | solution.py:91
  52.8 21.4 %collective-permute-start.5 = (f32[32,4,768]{2,1,0:T(4,128)}, f32[32,4,768]{2,1,0:T(4,128)}, u32[]{:S(2)}, u32[]{:S(2)}) collective-permute-start(f32[32,4,768]{2,1,0:T(4,128)} %get-tuple-element.19), channel_id=1, source_target_pairs={{1,0},{2,1},{3,2},{4,3},{5,4},{6,5},{7,6},{8,7},{9,8},{10,9},{11,1... | collective-permute-start | bytes 1179656 | tf_op jit(solution)/shard_map/ppermute | solution.py:92
  61.2 21.8 %copy-start.3 = (f32[24,32,768]{2,1,0:T(8,128)S(1)}, f32[24,32,768]{2,1,0:T(8,128)}, u32[]{:S(2)}) copy-start(f32[24,32,768]{2,1,0:T(8,128)} %copy-done.2) | copy-start | bytes 7077892
  75.1 25.0 %collective-permute-start.7 = (f32[4,40,768]{2,1,0:T(8,128)S(1)}, f32[4,40,768]{2,1,0:T(8,128)S(1)}, u32[]{:S(2)}, u32[]{:S(2)}) collective-permute-start(f32[4,40,768]{2,1,0:T(8,128)S(1)} %pad_maximum_fusion.10), channel_id=1, source_target_pairs={{32,0},{64,32},{96,64},{128,96},{160,128},{192,160},{224,192},{33,... | collective-permute-start | bytes 1474568 | tf_op jit(solution)/shard_map/ppermute | solution.py:105
  78.1 22.0 %collective-permute-start.6 = (f32[4,40,768]{2,1,0:T(8,128)S(1)}, f32[4,40,768]{2,1,0:T(8,128)S(1)}, u32[]{:S(2)}, u32[]{:S(2)}) collective-permute-start(f32[4,40,768]{2,1,0:T(8,128)S(1)} %pad_maximum_fusion.9), channel_id=1, source_target_pairs={{0,32},{32,64},{64,96},{96,128},{128,160},{160,192},{192,224},{1,3... | collective-permute-start | bytes 1474568 | tf_op jit(solution)/shard_map/ppermute | solution.py:104
  86.6 13.3 %copy-start.5 = (f32[32,40,768]{2,1,0:T(8,128)S(1)}, f32[32,40,768]{2,1,0:T(8,128)}, u32[]{:S(2)}) copy-start(f32[32,40,768]{2,1,0:T(8,128)} %pad_maximum_fusion.1.pad_ref) | copy-start | bytes 11796484
  105.2 6.2 %collective-permute-start.8 = (f32[32,768]{1,0:T(8,128)S(1)}, f32[32,768]{1,0:T(8,128)S(1)}, u32[]{:S(2)}, u32[]{:S(2)}) collective-permute-start(f32[32,768]{1,0:T(8,128)S(1)} %maximum_maximum_fusion), channel_id=1, source_target_pairs={{0,128},{32,160},{64,192},{96,224},{128,0},{160,32},{192,64},{224,... | collective-permute-start | bytes 294920 | tf_op jit(solution)/shard_map/ppermute | solution.py:123
  111.4 4.7 %collective-permute-start.9 = (f32[32,768]{1,0:T(8,128)S(1)}, f32[32,768]{1,0:T(8,128)S(1)}, u32[]{:S(2)}, u32[]{:S(2)}) collective-permute-start(f32[32,768]{1,0:T(8,128)S(1)} %max.17), channel_id=1, source_target_pairs={{0,64},{32,96},{64,0},{96,32},{128,192},{160,224},{192,128},{224,1... | collective-permute-start | bytes 294920 | tf_op jit(solution)/shard_map/ppermute | solution.py:123
  116.1 4.7 %collective-permute-start.10 = (f32[32,768]{1,0:T(8,128)S(1)}, f32[32,768]{1,0:T(8,128)S(1)}, u32[]{:S(2)}, u32[]{:S(2)}) collective-permute-start(f32[32,768]{1,0:T(8,128)S(1)} %max.18), channel_id=1, source_target_pairs={{0,32},{32,0},{64,96},{96,64},{128,160},{160,128},{192,224},{224,1... | collective-permute-start | bytes 294920 | tf_op jit(solution)/shard_map/ppermute | solution.py:123

commit v13 on v11

--- a/solution.py
+++ b/solution.py
@@ -101,8 +101,8 @@
     inner = fused_blur(mode, [(0, nz - 2 * width, 0, width)], taps, rows_padded, other)
     low_slab = jnp.concatenate([below, rows_padded[: 2 * width]], axis=0)
     high_slab = jnp.concatenate([rows_padded[nz - 2 * width :], above], axis=0)
-    low = fused_blur(mode, [(0, width, 0, 0)], taps, low_slab, other)
-    high = fused_blur(mode, [(0, width, 0, nz - width)], taps, high_slab, other)
+    low = fused_blur(mode, [(0, width, 0, 0)], taps, low_slab, other[:width])
+    high = fused_blur(mode, [(0, width, 0, 0)], taps, high_slab, other[nz - width :])
     volume = jnp.concatenate([low[0], inner[0], high[0]], axis=0)
     if mode == "update":
         return volume, jnp.maximum(jnp.maximum(inner[1], low[1]), high[1])

time: 117 us -> 116 us (level)
  local copies, waits for them, and re-layouts: 6.59 us -> 3.88 us
    unnamed x16, local copies, waits for them, and re-layouts: 1.9 us -> 0.04 us
    ppermute x4, starting transfers between devices: 15.9 us -> 14.6 us  [halo_pair(): before = lax.ppermute(last, axis, up)]
    concatenate x2, other arithmetic: 1.52 us -> 0.31 us  [split_blur(): low_slab = jnp.concatenate([below, rows_padded[:2 * width]], axis=0)]
  transfers between devices with their start and end apart: 11 -> 11, of which waited for: 6 -> 7; matrix products, arithmetic and copies ran while one was open for 4% -> 4% of each run, Pallas kernels for 25% -> 25%
where the time goes in v13:
time: 116 us; the launch traced here: 115 us
  starting transfers between devices  43.4 us (37%)
  Pallas kernels  36.2 us (31%)
  waiting for transfers between devices  22.6 us (19%)
  other arithmetic  8.05 us (7%)
  local copies, waits for them, and re-layouts  3.88 us (3%)
    pallas_call x6, Pallas kernels, fused_blur(): pl.pallas_call(functools.partial(blur_kernel, mode, tuple(segments)), out...  36.2 us
    ppermute x4, starting transfers between devices, halo_pair(): after = lax.ppermute(first, axis, down)  20.8 us
    ppermute x4, starting transfers between devices, halo_pair(): before = lax.ppermute(last, axis, up)  14.6 us
    ppermute x4, waiting for transfers between devices, halo_pair(): before = lax.ppermute(last, axis, up)  11.6 us
    ppermute x3, waiting for transfers between devices, butterfly_max(): value = jnp.maximum(value, lax.ppermute(value, axis, pairs))  7.91 us
    ppermute x3, starting transfers between devices, butterfly_max(): value = jnp.maximum(value, lax.ppermute(value, axis, pairs))  7.88 us
    concatenate x2, other arithmetic, split_blur(): rows_padded = jnp.concatenate([before, shard, after], axis=1)  3.79 us
    ppermute x4, waiting for transfers between devices, halo_pair(): after = lax.ppermute(first, axis, down)  3.14 us
  transfers between devices with their start and end apart: 11, of which 7 were waited for; matrix products, arithmetic and copies ran while one was open for 4% of the time, Pallas kernels for 25%

profile of v13, /device:TPU:160, one launch (start us, length us, event | category | flops | bytes accessed | tf_op | source)
XLA Modules:
  0.0 115.1 jit_solution(13328504445366291634)
XLA Ops:
  0.6 1.5 %fusion.6 = (f32[32,4,768]{2,1,0:T(4,128)S(1)}, f32[32,4,768]{2,1,0:T(4,128)S(1)}) fusion(f32[32,32,768]{2,1,0:T(8,128)} %other_ref.3), kind=kLoop, calls=%fused_computation.19 | loop fusion | bytes 1572864 | tf_op jit(solution)/shard_map/slice | solution.py:89
  2.1 1.9 %collective-permute-start = (f32[32,4,768]{2,1,0:T(4,128)S(1)}, f32[32,4,768]{2,1,0:T(4,128)S(1)}, u32[]{:S(2)}, u32[]{:S(2)}) collective-permute-start(f32[32,4,768]{2,1,0:T(4,128)S(1)} %get-tuple-element.28), channel_id=1, source_target_pairs={{0,1},{1,2},{2,3},{3,4},{4,5},{5,6},{6,7},{7,8},{8,9},{9,10},{10,1... | collective-permute-start | bytes 1179656 | tf_op jit(solution)/shard_map/ppermute | solution.py:91
  4.1 0.0 copy-start.1
  4.1 8.1 %collective-permute-start.1 = (f32[32,4,768]{2,1,0:T(4,128)S(1)}, f32[32,4,768]{2,1,0:T(4,128)S(1)}, u32[]{:S(2)}, u32[]{:S(2)}) collective-permute-start(f32[32,4,768]{2,1,0:T(4,128)S(1)} %get-tuple-element.29), channel_id=1, source_target_pairs={{1,0},{2,1},{3,2},{4,3},{5,4},{6,5},{7,6},{8,7},{9,8},{10,9},{11,1... | collective-permute-start | bytes 1179656 | tf_op jit(solution)/shard_map/ppermute | solution.py:92
  12.2 5.6 %collective-permute-done = f32[32,4,768]{2,1,0:T(4,128)S(1)} collective-permute-done((f32[32,4,768]{2,1,0:T(4,128)S(1)}, f32[32,4,768]{2,1,0:T(4,128)S(1)}, u32[]{:S(2)}, u32[]{:S(2)}) %collective-permute-start) | collective-permute-done | bytes 393248 | tf_op jit(solution)/shard_map/ppermute | solution.py:91
  17.8 0.0 collective-permute-done.1
  17.8 2.3 %pad_maximum_fusion.pad_ref = f32[32,40,768]{2,1,0:T(8,128)S(1)} fusion(f32[32,4,768]{2,1,0:T(4,128)S(1)} %collective-permute-done.1, f32[32,32,768]{2,1,0:T(8,128)} %other_ref.3, f32[32,4,768]{2,1,0:T(4,128)S(1)} %collective-permute-done), kind=kLoop, calls=%fused_computation | loop fusion | flops 1966080 | bytes 7864320 | tf_op jit(solution)/shard_map/concatenate | solution.py:99
  20.2 0.0 copy-start.4
  20.2 0.0 copy-start.5
  20.2 0.0 copy-start.6
  20.2 0.0 copy-start.7
  20.2 0.1 fusion.2
  20.3 7.9 %collective-permute-start.2 = (f32[4,40,768]{2,1,0:T(8,128)S(1)}, f32[4,40,768]{2,1,0:T(8,128)S(1)}, u32[]{:S(2)}, u32[]{:S(2)}) collective-permute-start(f32[4,40,768]{2,1,0:T(8,128)S(1)} %get-tuple-element.18), channel_id=1, source_target_pairs={{0,32},{32,64},{64,96},{96,128},{128,160},{160,192},{192,224},{1,3... | collective-permute-start | bytes 1474568 | tf_op jit(solution)/shard_map/ppermute | solution.py:91
  28.2 0.0 copy-done.1
  28.2 0.1 fusion.5
  28.2 1.9 %collective-permute-start.3 = (f32[4,40,768]{2,1,0:T(8,128)S(1)}, f32[4,40,768]{2,1,0:T(8,128)S(1)}, u32[]{:S(2)}, u32[]{:S(2)}) collective-permute-start(f32[4,40,768]{2,1,0:T(8,128)S(1)} %get-tuple-element.19), channel_id=1, source_target_pairs={{32,0},{64,32},{96,64},{128,96},{160,128},{192,160},{224,192},{33,... | collective-permute-start | bytes 1474568 | tf_op jit(solution)/shard_map/ppermute | solution.py:92
  30.2 0.0 copy-done.5
  30.2 0.0 copy-done.6
  30.2 0.0 copy-done.7
  30.2 0.1 pad_maximum_fusion.11.taps_ref
  30.3 0.0 copy-done.4
  30.3 13.2 %shard_map.69 = f32[24,32,768]{2,1,0:T(8,128)S(1)} custom-call(f32[27]{0:T(128)S(1)} %pad_maximum_fusion.11.taps_ref, f32[32,40,768]{2,1,0:T(8,128)} %copy-done.4, f32[32,32,768]{2,1,0:T(8,128)S(1)} %copy-done.1), custom_call_target="tpu_custom_call" | custom-call | flops 35389440 | bytes 9437184 | tf_op jit(solution)/shard_map/pallas_call | solution.py:74
  43.5 1.6 %fusion.3 = (f32[8,40,768]{2,1,0:T(8,128)S(1)}, f32[8,40,768]{2,1,0:T(8,128)S(1)}) fusion(f32[32,40,768]{2,1,0:T(8,128)} %copy-done.4), kind=kLoop, calls=%fused_computation.16 | loop fusion | bytes 3932160 | tf_op jit(solution)/shard_map/slice | solution.py:102
  45.2 0.0 collective-permute-done.2
  45.2 0.1 pad_maximum_fusion.3.pad_ref
  45.3 2.4 %shard_map.68 = f32[4,32,768]{2,1,0:T(8,128)S(1)} custom-call(f32[27]{0:T(128)S(1)} %pad_maximum_fusion.11.taps_ref, f32[12,40,768]{2,1,0:T(8,128)S(1)} %pad_maximum_fusion.3.pad_ref, f32[4,32,768]{2,1,0:T(8,128)S(1)} %get-tuple-element.26.other_ref), custom_call_target="tpu_custom_call" | custom-call | flops 5898240 | bytes 1572864 | tf_op jit(solution)/shard_map/pallas_call | solution.py:74
  47.7 0.0 collective-permute-done.3
  47.7 0.1 pad_maximum_fusion.4.pad_ref
  47.8 2.4 %shard_map.70 = f32[4,32,768]{2,1,0:T(8,128)S(1)} custom-call(f32[27]{0:T(128)S(1)} %pad_maximum_fusion.11.taps_ref, f32[12,40,768]{2,1,0:T(8,128)S(1)} %pad_maximum_fusion.4.pad_ref, f32[4,32,768]{2,1,0:T(8,128)S(1)} %get-tuple-element.27.other_ref), custom_call_target="tpu_custom_call" | custom-call | flops 5898240 | bytes 1572864 | tf_op jit(solution)/shard_map/pallas_call | solution.py:74
  50.2 1.0 pad_maximum_fusion.9
  51.3 1.9 %collective-permute-start.4 = (f32[32,4,768]{2,1,0:T(4,128)}, f32[32,4,768]{2,1,0:T(4,128)S(1)}, u32[]{:S(2)}, u32[]{:S(2)}) collective-permute-start(f32[32,4,768]{2,1,0:T(4,128)} %get-tuple-element.24), channel_id=1, source_target_pairs={{0,1},{1,2},{2,3},{3,4},{4,5},{5,6},{6,7},{7,8},{8,9},{9,10},{10,1... | collective-permute-start | bytes 1179656 | tf_op jit(solution)/shard_map/ppermute | solution.py:91
  53.2 7.9 %collective-permute-start.5 = (f32[32,4,768]{2,1,0:T(4,128)}, f32[32,4,768]{2,1,0:T(4,128)}, u32[]{:S(2)}, u32[]{:S(2)}) collective-permute-start(f32[32,4,768]{2,1,0:T(4,128)} %get-tuple-element.25), channel_id=1, source_target_pairs={{1,0},{2,1},{3,2},{4,3},{5,4},{6,5},{7,6},{8,7},{9,8},{10,9},{11,1... | collective-permute-start | bytes 1179656 | tf_op jit(solution)/shard_map/ppermute | solution.py:92
  61.0 0.1 rev.10
  61.1 0.1 rev.11
  61.2 0.1 rev.9
  61.3 0.1 pad_maximum_fusion.10.taps_ref
  61.4 0.0 copy-start
  61.4 6.0 %collective-permute-done.4 = f32[32,4,768]{2,1,0:T(4,128)S(1)} collective-permute-done((f32[32,4,768]{2,1,0:T(4,128)}, f32[32,4,768]{2,1,0:T(4,128)S(1)}, u32[]{:S(2)}, u32[]{:S(2)}) %collective-permute-start.4) | collective-permute-done | bytes 393248 | tf_op jit(solution)/shard_map/ppermute | solution.py:91
  67.4 3.0 %collective-permute-done.5 = f32[32,4,768]{2,1,0:T(4,128)} collective-permute-done((f32[32,4,768]{2,1,0:T(4,128)}, f32[32,4,768]{2,1,0:T(4,128)}, u32[]{:S(2)}, u32[]{:S(2)}) %collective-permute-start.5) | collective-permute-done | bytes 393248 | tf_op jit(solution)/shard_map/ppermute | solution.py:92
  70.4 1.4 %pad_maximum_fusion.1.pad_ref = f32[32,40,768]{2,1,0:T(8,128)S(1)} fusion(f32[32,4,768]{2,1,0:T(4,128)} %collective-permute-done.5, f32[4,32,768]{2,1,0:T(8,128)S(1)} %shard_map.70, f32[24,32,768]{2,1,0:T(8,128)S(1)} %shard_map.69, f32[4,32,768]{2,1,0:T(8,128)S(1)} %shard_map.68, f32[32,4,768]{2,1,0:T(4,128)S(1)} %collective-permute-done.4), kind=kLoop, calls=%fused_computation.1 | loop fusion | flops 3932160 | bytes 7864320 | tf_op jit(solution)/shard_map/concatenate | solution.py:99
  71.9 0.0 copy-start.2
  71.9 0.1 fusion
  71.9 2.9 %collective-permute-start.6 = (f32[4,40,768]{2,1,0:T(8,128)S(1)}, f32[4,40,768]{2,1,0:T(8,128)S(1)}, u32[]{:S(2)}, u32[]{:S(2)}) collective-permute-start(f32[4,40,768]{2,1,0:T(8,128)S(1)} %get-tuple-element.14), channel_id=1, source_target_pairs={{0,32},{32,64},{64,96},{96,128},{128,160},{160,192},{192,224},{1,3... | collective-permute-start | bytes 1474568 | tf_op jit(solution)/shard_map/ppermute | solution.py:91
  74.9 2.9 %collective-permute-start.7 = (f32[4,40,768]{2,1,0:T(8,128)S(1)}, f32[4,40,768]{2,1,0:T(8,128)S(1)}, u32[]{:S(2)}, u32[]{:S(2)}) collective-permute-start(f32[4,40,768]{2,1,0:T(8,128)S(1)} %get-tuple-element.15), channel_id=1, source_target_pairs={{32,0},{64,32},{96,64},{128,96},{160,128},{192,160},{224,192},{33,... | collective-permute-start | bytes 1474568 | tf_op jit(solution)/shard_map/ppermute | solution.py:92
  77.8 0.0 copy-done.2
  77.8 0.0 copy-done
  77.8 0.1 fusion.4
  77.9 0.0 copy-start.3
  77.9 13.4 %shard_map.72 = (f32[24,32,768]{2,1,0:T(8,128)S(1)}, f32[32,768]{1,0:T(8,128)S(1)}) custom-call(f32[27]{0:T(128)S(1)} %pad_maximum_fusion.10.taps_ref, f32[32,40,768]{2,1,0:T(8,128)} %copy-done.2, f32[32,32,768]{2,1,0:T(8,128)S(1)} %copy-done), custom_call_target="tpu_custom_call" | custom-call | flops 35389440 | bytes 9437184 | tf_op jit(solution)/shard_map/pallas_call | solution.py:74
  91.3 0.0 copy-done.3
  91.3 0.2 fusion.1
  91.5 0.0 collective-permute-done.6
  91.5 0.1 collective-permute-done.7
  91.6 0.2 pad_maximum_fusion.5
  91.8 2.4 %shard_map.71 = (f32[4,32,768]{2,1,0:T(8,128)S(1)}, f32[32,768]{1,0:T(8,128)S(1)}) custom-call(f32[27]{0:T(128)S(1)} %pad_maximum_fusion.10.taps_ref, f32[12,40,768]{2,1,0:T(8,128)S(1)} %get-tuple-element.30.pad_ref, f32[4,32,768]{2,1,0:T(8,128)S(1)} %get-tuple-element.22.other_ref), custom_call_target="tpu_custom_call" | custom-call | flops 5898240 | bytes 1572864 | tf_op jit(solution)/shard_map/pallas_call | solution.py:74
  94.2 2.4 %shard_map.73 = (f32[4,32,768]{2,1,0:T(8,128)S(1)}, f32[32,768]{1,0:T(8,128)S(1)}) custom-call(f32[27]{0:T(128)S(1)} %pad_maximum_fusion.10.taps_ref, f32[12,40,768]{2,1,0:T(8,128)S(1)} %get-tuple-element.31.pad_ref, f32[4,32,768]{2,1,0:T(8,128)S(1)} %get-tuple-element.23.other_ref), custom_call_target="tpu_custom_call" | custom-call | flops 5898240 | bytes 1572864 | tf_op jit(solution)/shard_map/pallas_call | solution.py:74
  96.6 5.8 %collective-permute-start.8 = (f32[32,768]{1,0:T(8,128)S(1)}, f32[32,768]{1,0:T(8,128)S(1)}, u32[]{:S(2)}, u32[]{:S(2)}) collective-permute-start(f32[32,768]{1,0:T(8,128)S(1)} %maximum_maximum_fusion), channel_id=1, source_target_pairs={{0,128},{32,160},{64,192},{96,224},{128,0},{160,32},{192,64},{224,... | collective-permute-start | bytes 294920 | tf_op jit(solution)/shard_map/ppermute | solution.py:117
  102.4 2.6 %collective-permute-done.8 = f32[32,768]{1,0:T(8,128)S(1)} collective-permute-done((f32[32,768]{1,0:T(8,128)S(1)}, f32[32,768]{1,0:T(8,128)S(1)}, u32[]{:S(2)}, u32[]{:S(2)}) %collective-permute-start.8) | collective-permute-done | bytes 98336 | tf_op jit(solution)/shard_map/ppermute | solution.py:117
  105.0 2.0 %collective-permute-start.9 = (f32[32,768]{1,0:T(8,128)S(1)}, f32[32,768]{1,0:T(8,128)S(1)}, u32[]{:S(2)}, u32[]{:S(2)}) collective-permute-start(f32[32,768]{1,0:T(8,128)S(1)} %max.17), channel_id=1, source_target_pairs={{0,64},{32,96},{64,0},{96,32},{128,192},{160,224},{192,128},{224,1... | collective-permute-start | bytes 294920 | tf_op jit(solution)/shard_map/ppermute | solution.py:117
  107.0 2.7 %collective-permute-done.9 = f32[32,768]{1,0:T(8,128)S(1)} collective-permute-done((f32[32,768]{1,0:T(8,128)S(1)}, f32[32,768]{1,0:T(8,128)S(1)}, u32[]{:S(2)}, u32[]{:S(2)}) %collective-permute-start.9) | collective-permute-done | bytes 98336 | tf_op jit(solution)/shard_map/ppermute | solution.py:117
  109.8 0.1 collective-permute-start.10
  109.9 2.0 %pad_maximum_fusion.2 = f32[32,32,768]{2,1,0:T(8,128)} fusion(f32[4,32,768]{2,1,0:T(8,128)S(1)} %get-tuple-element.10, f32[24,32,768]{2,1,0:T(8,128)S(1)} %get-tuple-element.9, f32[4,32,768]{2,1,0:T(8,128)S(1)} %get-tuple-element.8), kind=kLoop, calls=%fused_computation.2 | loop fusion | flops 1572864 | bytes 6291456 | tf_op jit(solution)/shard_map/concatenate | solution.py:106
  111.8 2.6 %collective-permute-done.10 = f32[32,768]{1,0:T(8,128)S(1)} collective-permute-done((f32[32,768]{1,0:T(8,128)S(1)}, f32[32,768]{1,0:T(8,128)S(1)}, u32[]{:S(2)}, u32[]{:S(2)}) %collective-permute-start.10) | collective-permute-done | bytes 98336 | tf_op jit(solution)/shard_map/ppermute | solution.py:117
  114.5 0.7 max.19
  (3 shorter events, 0.0 us)
Async XLA Ops:
  2.1 15.7 %collective-permute-start = (f32[32,4,768]{2,1,0:T(4,128)S(1)}, f32[32,4,768]{2,1,0:T(4,128)S(1)}, u32[]{:S(2)}, u32[]{:S(2)}) collective-permute-start(f32[32,4,768]{2,1,0:T(4,128)S(1)} %get-tuple-element.28), channel_id=1, source_target_pairs={{0,1},{1,2},{2,3},{3,4},{4,5},{5,6},{6,7},{7,8},{8,9},{9,10},{10,1... | collective-permute-start | bytes 1179656 | tf_op jit(solution)/shard_map/ppermute | solution.py:91
  4.1 24.1 %copy-start.1 = (f32[32,32,768]{2,1,0:T(8,128)S(1)}, f32[32,32,768]{2,1,0:T(8,128)}, u32[]{:S(2)}) copy-start(f32[32,32,768]{2,1,0:T(8,128)} %other_ref.2) | copy-start | bytes 9437188
  4.1 13.7 %collective-permute-start.1 = (f32[32,4,768]{2,1,0:T(4,128)S(1)}, f32[32,4,768]{2,1,0:T(4,128)S(1)}, u32[]{:S(2)}, u32[]{:S(2)}) collective-permute-start(f32[32,4,768]{2,1,0:T(4,128)S(1)} %get-tuple-element.29), channel_id=1, source_target_pairs={{1,0},{2,1},{3,2},{4,3},{5,4},{6,5},{7,6},{8,7},{9,8},{10,9},{11,1... | collective-permute-start | bytes 1179656 | tf_op jit(solution)/shard_map/ppermute | solution.py:92
  20.2 10.1 %copy-start.4 = (f32[32,40,768]{2,1,0:T(8,128)}, f32[32,40,768]{2,1,0:T(8,128)S(1)}, u32[]{:S(2)}) copy-start(f32[32,40,768]{2,1,0:T(8,128)S(1)} %pad_maximum_fusion.pad_ref) | copy-start | bytes 11796484
  20.2 10.0 %copy-start.5 = (f32[9]{0:T(128)S(1)}, f32[9]{0:T(128)}, u32[]{:S(2)}) copy-start(f32[9]{0:T(128)} %param.8) | copy-start | bytes 112
  20.2 10.0 %copy-start.6 = (f32[9]{0:T(128)S(1)}, f32[9]{0:T(128)}, u32[]{:S(2)}) copy-start(f32[9]{0:T(128)} %param.9) | copy-start | bytes 112
  20.2 10.0 %copy-start.7 = (f32[9]{0:T(128)S(1)}, f32[9]{0:T(128)}, u32[]{:S(2)}) copy-start(f32[9]{0:T(128)} %param.7) | copy-start | bytes 112
  20.3 24.9 %collective-permute-start.2 = (f32[4,40,768]{2,1,0:T(8,128)S(1)}, f32[4,40,768]{2,1,0:T(8,128)S(1)}, u32[]{:S(2)}, u32[]{:S(2)}) collective-permute-start(f32[4,40,768]{2,1,0:T(8,128)S(1)} %get-tuple-element.18), channel_id=1, source_target_pairs={{0,32},{32,64},{64,96},{96,128},{128,160},{160,192},{192,224},{1,3... | collective-permute-start | bytes 1474568 | tf_op jit(solution)/shard_map/ppermute | solution.py:91
  28.2 19.5 %collective-permute-start.3 = (f32[4,40,768]{2,1,0:T(8,128)S(1)}, f32[4,40,768]{2,1,0:T(8,128)S(1)}, u32[]{:S(2)}, u32[]{:S(2)}) collective-permute-start(f32[4,40,768]{2,1,0:T(8,128)S(1)} %get-tuple-element.19), channel_id=1, source_target_pairs={{32,0},{64,32},{96,64},{128,96},{160,128},{192,160},{224,192},{33,... | collective-permute-start | bytes 1474568 | tf_op jit(solution)/shard_map/ppermute | solution.py:92
  51.3 16.1 %collective-permute-start.4 = (f32[32,4,768]{2,1,0:T(4,128)}, f32[32,4,768]{2,1,0:T(4,128)S(1)}, u32[]{:S(2)}, u32[]{:S(2)}) collective-permute-start(f32[32,4,768]{2,1,0:T(4,128)} %get-tuple-element.24), channel_id=1, source_target_pairs={{0,1},{1,2},{2,3},{3,4},{4,5},{5,6},{6,7},{7,8},{8,9},{9,10},{10,1... | collective-permute-start | bytes 1179656 | tf_op jit(solution)/shard_map/ppermute | solution.py:91
  53.2 17.2 %collective-permute-start.5 = (f32[32,4,768]{2,1,0:T(4,128)}, f32[32,4,768]{2,1,0:T(4,128)}, u32[]{:S(2)}, u32[]{:S(2)}) collective-permute-start(f32[32,4,768]{2,1,0:T(4,128)} %get-tuple-element.25), channel_id=1, source_target_pairs={{1,0},{2,1},{3,2},{4,3},{5,4},{6,5},{7,6},{8,7},{9,8},{10,9},{11,1... | collective-permute-start | bytes 1179656 | tf_op jit(solution)/shard_map/ppermute | solution.py:92
  61.4 16.4 %copy-start = (f32[32,32,768]{2,1,0:T(8,128)S(1)}, f32[32,32,768]{2,1,0:T(8,128)}, u32[]{:S(2)}) copy-start(f32[32,32,768]{2,1,0:T(8,128)} %other_ref.3) | copy-start | bytes 9437188
  71.9 6.0 %copy-start.2 = (f32[32,40,768]{2,1,0:T(8,128)}, f32[32,40,768]{2,1,0:T(8,128)S(1)}, u32[]{:S(2)}) copy-start(f32[32,40,768]{2,1,0:T(8,128)S(1)} %pad_maximum_fusion.1.pad_ref) | copy-start | bytes 11796484
  71.9 19.5 %collective-permute-start.6 = (f32[4,40,768]{2,1,0:T(8,128)S(1)}, f32[4,40,768]{2,1,0:T(8,128)S(1)}, u32[]{:S(2)}, u32[]{:S(2)}) collective-permute-start(f32[4,40,768]{2,1,0:T(8,128)S(1)} %get-tuple-element.14), channel_id=1, source_target_pairs={{0,32},{32,64},{64,96},{96,128},{128,160},{160,192},{192,224},{1,3... | collective-permute-start | bytes 1474568 | tf_op jit(solution)/shard_map/ppermute | solution.py:91
  74.9 16.7 %collective-permute-start.7 = (f32[4,40,768]{2,1,0:T(8,128)S(1)}, f32[4,40,768]{2,1,0:T(8,128)S(1)}, u32[]{:S(2)}, u32[]{:S(2)}) collective-permute-start(f32[4,40,768]{2,1,0:T(8,128)S(1)} %get-tuple-element.15), channel_id=1, source_target_pairs={{32,0},{64,32},{96,64},{128,96},{160,128},{192,160},{224,192},{33,... | collective-permute-start | bytes 1474568 | tf_op jit(solution)/shard_map/ppermute | solution.py:92
  77.9 13.4 %copy-start.3 = (f32[32,40,768]{2,1,0:T(8,128)S(1)}, f32[32,40,768]{2,1,0:T(8,128)}, u32[]{:S(2)}) copy-start(f32[32,40,768]{2,1,0:T(8,128)} %copy-done.2) | copy-start | bytes 11796484
  96.6 8.4 %collective-permute-start.8 = (f32[32,768]{1,0:T(8,128)S(1)}, f32[32,768]{1,0:T(8,128)S(1)}, u32[]{:S(2)}, u32[]{:S(2)}) collective-permute-start(f32[32,768]{1,0:T(8,128)S(1)} %maximum_maximum_fusion), channel_id=1, source_target_pairs={{0,128},{32,160},{64,192},{96,224},{128,0},{160,32},{192,64},{224,... | collective-permute-start | bytes 294920 | tf_op jit(solution)/shard_map/ppermute | solution.py:117
  105.0 4.7 %collective-permute-start.9 = (f32[32,768]{1,0:T(8,128)S(1)}, f32[32,768]{1,0:T(8,128)S(1)}, u32[]{:S(2)}, u32[]{:S(2)}) collective-permute-start(f32[32,768]{1,0:T(8,128)S(1)} %max.17), channel_id=1, source_target_pairs={{0,64},{32,96},{64,0},{96,32},{128,192},{160,224},{192,128},{224,1... | collective-permute-start | bytes 294920 | tf_op jit(solution)/shard_map/ppermute | solution.py:117
  109.8 4.7 %collective-permute-start.10 = (f32[32,768]{1,0:T(8,128)S(1)}, f32[32,768]{1,0:T(8,128)S(1)}, u32[]{:S(2)}, u32[]{:S(2)}) collective-permute-start(f32[32,768]{1,0:T(8,128)S(1)} %max.18), channel_id=1, source_target_pairs={{0,32},{32,0},{64,96},{96,64},{128,160},{160,128},{192,224},{224,1... | collective-permute-start | bytes 294920 | tf_op jit(solution)/shard_map/ppermute | solution.py:117

commit v14 on v13

--- a/solution.py
+++ b/solution.py
@@ -82,6 +82,77 @@
     )(taps, padded, other)
 
 
+def edge_kernel(mode, width, halo_first, taps_ref, halo_ref, own_ref, other_ref, out_ref, *rest):
+    if mode == "update":
+        max_ref, zbuf, ybuf = rest
+        max_ref[...] = jnp.full(max_ref.shape, -jnp.inf, max_ref.dtype)
+    else:
+        (zbuf, ybuf), max_ref = rest, None
+    ntap = 9
+    r = 4
+    ny, nx = out_ref.shape[1], out_ref.shape[2]
+    py = ny + 2 * r
+    lanes = lax.broadcasted_iota(jnp.int32, (8, nx), 1)
+    for zo in range(width):
+
+        def load(q, rows):
+            if halo_first:
+                return halo_ref[q, rows, :] if q < width else own_ref[q - width, rows, :]
+            return own_ref[q, rows, :] if q < 2 * width else halo_ref[q - 2 * width, rows, :]
+
+        for c in range(py // 8):
+            rows = pl.ds(c * 8, 8)
+            acc = taps_ref[0] * load(zo, rows)
+            for k in range(1, ntap):
+                acc = acc + taps_ref[k] * load(zo + k, rows)
+            zbuf[rows, :] = acc
+        for c in range(ny // 8):
+            acc = taps_ref[ntap] * zbuf[pl.ds(c * 8, 8), :]
+            for k in range(1, ntap):
+                acc = acc + taps_ref[ntap + k] * zbuf[pl.ds(c * 8 + k, 8), :]
+            ybuf[pl.ds(c * 8, 8), :] = acc
+        for c in range(ny // 8):
+            rows = pl.ds(c * 8, 8)
+            v = ybuf[rows, :]
+            acc = None
+            for k in range(ntap):
+                d = k - r
+                if d == 0:
+                    t = v
+                else:
+                    t = pltpu.roll(v, (-d) % nx, 1)
+                    keep = (lanes >= -d) if d < 0 else (lanes < nx - d)
+                    t = jnp.where(keep, t, 0.0)
+                term = taps_ref[2 * ntap + k] * t
+                acc = term if acc is None else acc + term
+            if mode == "ratio":
+                out_ref[zo, rows, :] = other_ref[zo, rows, :] / acc
+            else:
+                upd = other_ref[zo, rows, :] * acc
+                out_ref[zo, rows, :] = upd
+                max_ref[rows, :] = jnp.maximum(max_ref[rows, :], upd)
+
+
+def edge_blur(mode, width, halo_first, taps, halo, own, other):
+    nzo, ny, nx = other.shape
+    vmem = pltpu.VMEM
+    outs = [jax.ShapeDtypeStruct((nzo, ny, nx), jnp.float32)]
+    out_specs = [pl.BlockSpec(memory_space=vmem)]
+    if mode == "update":
+        outs.append(jax.ShapeDtypeStruct((ny, nx), jnp.float32))
+        out_specs.append(pl.BlockSpec(memory_space=vmem))
+    elems = nzo * ny * nx
+    return pl.pallas_call(
+        functools.partial(edge_kernel, mode, width, halo_first),
+        out_shape=tuple(outs),
+        in_specs=[pl.BlockSpec(memory_space=pltpu.SMEM)] + [pl.BlockSpec(memory_space=vmem)] * 3,
+        out_specs=tuple(out_specs),
+        scratch_shapes=[pltpu.VMEM((ny + 8, nx), jnp.float32), pltpu.VMEM((ny, nx), jnp.float32)],
+        compiler_params=pltpu.CompilerParams(vmem_limit_bytes=48 * 1024 * 1024),
+        cost_estimate=pl.CostEstimate(flops=elems * 60, bytes_accessed=elems * 4 * 4, transcendentals=0),
+    )(taps, halo, own, other)
+
+
 def halo_pair(shard, axis, dim, width):
     peers, length = (lax.axis_size(axis), shard.shape[dim])
     up = [(i, (i + 1) % peers) for i in range(peers - 1)]
@@ -99,10 +170,8 @@
     rows_padded = jnp.concatenate([before, shard, after], axis=1)
     below, above = halo_pair(rows_padded, "gz", 0, width)
     inner = fused_blur(mode, [(0, nz - 2 * width, 0, width)], taps, rows_padded, other)
-    low_slab = jnp.concatenate([below, rows_padded[: 2 * width]], axis=0)
-    high_slab = jnp.concatenate([rows_padded[nz - 2 * width :], above], axis=0)
-    low = fused_blur(mode, [(0, width, 0, 0)], taps, low_slab, other[:width])
-    high = fused_blur(mode, [(0, width, 0, 0)], taps, high_slab, other[nz - width :])
+    low = edge_blur(mode, width, True, taps, below, rows_padded[: 2 * width], other[:width])
+    high = edge_blur(mode, width, False, taps, above, rows_padded[nz - 2 * width :], other[nz - width :])
     volume = jnp.concatenate([low[0], inner[0], high[0]], axis=0)
     if mode == "update":
         return volume, jnp.maximum(jnp.maximum(inner[1], low[1]), high[1])

time: 116 us -> 114 us (0.983)
    pallas_call x6 -> x2, Pallas kernels: 36.2 us -> 26.6 us  [fused_blur(): pl.pallas_call(functools.partial(blur_kernel, mode, tuple(segments)), out...]
    pallas_call x0 -> x4, Pallas kernels: none -> 8.55 us  [edge_blur(): pl.pallas_call(functools.partial(edge_kernel, mode, width, halo_first), o...]
  transfers between devices with their start and end apart: 11 -> 11, of which waited for: 7 -> 6; matrix products, arithmetic and copies ran while one was open for 4% -> 4% of each run, Pallas kernels for 25% -> 27%
where the time goes in v14:
time: 114 us; the launch traced here: 113 us
  starting transfers between devices  42.4 us (37%)
  Pallas kernels  35.1 us (31%)
  waiting for transfers between devices  22.4 us (20%)
  other arithmetic  8.33 us (7%)
  local copies, waits for them, and re-layouts  3.87 us (3%)
    pallas_call x2, Pallas kernels, fused_blur(): pl.pallas_call(functools.partial(blur_kernel, mode, tuple(segments)), out...  26.6 us
    ppermute x4, starting transfers between devices, halo_pair(): after = lax.ppermute(first, axis, down)  20.4 us
    ppermute x4, starting transfers between devices, halo_pair(): before = lax.ppermute(last, axis, up)  14.4 us
    ppermute x4, waiting for transfers between devices, halo_pair(): before = lax.ppermute(last, axis, up)  11.6 us
    pallas_call x4, Pallas kernels, edge_blur(): pl.pallas_call(functools.partial(edge_kernel, mode, width, halo_first), o...  8.55 us
    ppermute x3, waiting for transfers between devices, butterfly_max(): value = jnp.maximum(value, lax.ppermute(value, axis, pairs))  8.31 us
    ppermute x3, starting transfers between devices, butterfly_max(): value = jnp.maximum(value, lax.ppermute(value, axis, pairs))  7.58 us
    concatenate x2, other arithmetic, split_blur(): rows_padded = jnp.concatenate([before, shard, after], axis=1)  3.79 us
  transfers between devices with their start and end apart: 11, of which 6 were waited for; matrix products, arithmetic and copies ran while one was open for 4% of the time, Pallas kernels for 27%

profile of v14, /device:TPU:160, one launch (start us, length us, event | category | flops | bytes accessed | tf_op | source)
XLA Modules:
  0.0 113.1 jit_solution(3323569106542176332)
XLA Ops:
  0.6 1.5 %fusion.6 = (f32[32,4,768]{2,1,0:T(4,128)S(1)}, f32[32,4,768]{2,1,0:T(4,128)S(1)}) fusion(f32[32,32,768]{2,1,0:T(8,128)} %other_ref.3), kind=kLoop, calls=%fused_computation.15 | loop fusion | bytes 1572864 | tf_op jit(solution)/shard_map/slice | solution.py:160
  2.1 1.9 %collective-permute-start = (f32[32,4,768]{2,1,0:T(4,128)S(1)}, f32[32,4,768]{2,1,0:T(4,128)S(1)}, u32[]{:S(2)}, u32[]{:S(2)}) collective-permute-start(f32[32,4,768]{2,1,0:T(4,128)S(1)} %get-tuple-element.28), channel_id=1, source_target_pairs={{0,1},{1,2},{2,3},{3,4},{4,5},{5,6},{6,7},{7,8},{8,9},{9,10},{10,1... | collective-permute-start | bytes 1179656 | tf_op jit(solution)/shard_map/ppermute | solution.py:162
  4.1 7.9 %collective-permute-start.1 = (f32[32,4,768]{2,1,0:T(4,128)S(1)}, f32[32,4,768]{2,1,0:T(4,128)S(1)}, u32[]{:S(2)}, u32[]{:S(2)}) collective-permute-start(f32[32,4,768]{2,1,0:T(4,128)S(1)} %get-tuple-element.29), channel_id=1, source_target_pairs={{1,0},{2,1},{3,2},{4,3},{5,4},{6,5},{7,6},{8,7},{9,8},{10,9},{11,1... | collective-permute-start | bytes 1179656 | tf_op jit(solution)/shard_map/ppermute | solution.py:163
  11.9 0.8 pad_maximum_fusion.7.taps_ref
  12.7 0.0 copy-start.1
  12.7 5.1 %collective-permute-done = f32[32,4,768]{2,1,0:T(4,128)S(1)} collective-permute-done((f32[32,4,768]{2,1,0:T(4,128)S(1)}, f32[32,4,768]{2,1,0:T(4,128)S(1)}, u32[]{:S(2)}, u32[]{:S(2)}) %collective-permute-start) | collective-permute-done | bytes 393248 | tf_op jit(solution)/shard_map/ppermute | solution.py:162
  17.8 0.0 collective-permute-done.1
  17.8 2.3 %pad_maximum_fusion.pad_ref = f32[32,40,768]{2,1,0:T(8,128)S(1)} fusion(f32[32,4,768]{2,1,0:T(4,128)S(1)} %collective-permute-done.1, f32[32,32,768]{2,1,0:T(8,128)} %other_ref.3, f32[32,4,768]{2,1,0:T(4,128)S(1)} %collective-permute-done), kind=kLoop, calls=%fused_computation | loop fusion | flops 1966080 | bytes 7864320 | tf_op jit(solution)/shard_map/concatenate | solution.py:170
  20.2 0.0 copy-start.4
  20.2 0.1 fusion.3
  20.2 7.5 %collective-permute-start.2 = (f32[4,40,768]{2,1,0:T(8,128)S(1)}, f32[4,40,768]{2,1,0:T(8,128)S(1)}, u32[]{:S(2)}, u32[]{:S(2)}) collective-permute-start(f32[4,40,768]{2,1,0:T(8,128)S(1)} %get-tuple-element.20), channel_id=1, source_target_pairs={{0,32},{32,64},{64,96},{96,128},{128,160},{160,192},{192,224},{1,3... | collective-permute-start | bytes 1474568 | tf_op jit(solution)/shard_map/ppermute | solution.py:162
  27.7 1.9 %collective-permute-start.3 = (f32[4,40,768]{2,1,0:T(8,128)S(1)}, f32[4,40,768]{2,1,0:T(8,128)S(1)}, u32[]{:S(2)}, u32[]{:S(2)}) collective-permute-start(f32[4,40,768]{2,1,0:T(8,128)S(1)} %get-tuple-element.21), channel_id=1, source_target_pairs={{32,0},{64,32},{96,64},{128,96},{160,128},{192,160},{224,192},{33,... | collective-permute-start | bytes 1474568 | tf_op jit(solution)/shard_map/ppermute | solution.py:163
  29.7 0.0 copy-done.1
  29.7 0.1 fusion.5
  29.7 0.0 copy-done.4
  29.7 13.2 %shard_map.69 = f32[24,32,768]{2,1,0:T(8,128)S(1)} custom-call(f32[27]{0:T(128)S(1)} %pad_maximum_fusion.7.taps_ref, f32[32,40,768]{2,1,0:T(8,128)} %copy-done.4, f32[32,32,768]{2,1,0:T(8,128)S(1)} %copy-done.1), custom_call_target="tpu_custom_call" | custom-call | flops 35389440 | bytes 9437184 | tf_op jit(solution)/shard_map/pallas_call | solution.py:74
  43.0 1.6 %fusion.2 = (f32[8,40,768]{2,1,0:T(8,128)S(1)}, f32[8,40,768]{2,1,0:T(8,128)S(1)}) fusion(f32[32,40,768]{2,1,0:T(8,128)} %copy-done.4), kind=kLoop, calls=%fused_computation.11 | loop fusion | bytes 3932160 | tf_op jit(solution)/shard_map/slice | solution.py:173
  44.6 0.0 collective-permute-done.2.halo_ref
  44.6 0.0 copy-start.5
  44.6 0.0 copy-start.6
  44.6 0.0 copy-start.7
  44.7 2.1 %shard_map.68 = f32[4,32,768]{2,1,0:T(8,128)S(1)} custom-call(f32[27]{0:T(128)S(1)} %pad_maximum_fusion.7.taps_ref, f32[4,40,768]{2,1,0:T(8,128)S(1)} %collective-permute-done.2.halo_ref, f32[8,40,768]{2,1,0:T(8,128)S(1)} %get-tuple-element.18.own_ref, f32[4,32,768]{2,1,0:T(8,128)S(1)} %get-tuple-element.26.other_ref), custom_call_target="tpu_custom_call" | custom-call | flops 5898240 | bytes 1572864 | tf_op jit(solution)/shard_map/pallas_call | solution.py:145
  46.8 0.0 collective-permute-done.3.halo_ref
  46.8 2.1 %shard_map.70 = f32[4,32,768]{2,1,0:T(8,128)S(1)} custom-call(f32[27]{0:T(128)S(1)} %pad_maximum_fusion.7.taps_ref, f32[4,40,768]{2,1,0:T(8,128)S(1)} %collective-permute-done.3.halo_ref, f32[8,40,768]{2,1,0:T(8,128)S(1)} %get-tuple-element.19.own_ref, f32[4,32,768]{2,1,0:T(8,128)S(1)} %get-tuple-element.27.other_ref), custom_call_target="tpu_custom_call" | custom-call | flops 5898240 | bytes 1572864 | tf_op jit(solution)/shard_map/pallas_call | solution.py:145
  49.0 1.0 pad_maximum_fusion.5
  50.0 1.9 %collective-permute-start.4 = (f32[32,4,768]{2,1,0:T(4,128)}, f32[32,4,768]{2,1,0:T(4,128)S(1)}, u32[]{:S(2)}, u32[]{:S(2)}) collective-permute-start(f32[32,4,768]{2,1,0:T(4,128)} %get-tuple-element.24), channel_id=1, source_target_pairs={{0,1},{1,2},{2,3},{3,4},{4,5},{5,6},{6,7},{7,8},{8,9},{9,10},{10,1... | collective-permute-start | bytes 1179656 | tf_op jit(solution)/shard_map/ppermute | solution.py:162
  51.9 7.9 %collective-permute-start.5 = (f32[32,4,768]{2,1,0:T(4,128)}, f32[32,4,768]{2,1,0:T(4,128)}, u32[]{:S(2)}, u32[]{:S(2)}) collective-permute-start(f32[32,4,768]{2,1,0:T(4,128)} %get-tuple-element.25), channel_id=1, source_target_pairs={{1,0},{2,1},{3,2},{4,3},{5,4},{6,5},{7,6},{8,7},{9,8},{10,9},{11,1... | collective-permute-start | bytes 1179656 | tf_op jit(solution)/shard_map/ppermute | solution.py:163
  59.8 0.0 copy-done.5
  59.8 0.1 rev.10
  59.9 0.0 copy-done.6
  59.9 0.1 rev.11
  60.0 0.0 copy-done.7
  60.0 0.1 rev.9
  60.1 0.1 pad_maximum_fusion.6.taps_ref
  60.2 0.0 copy-start
  60.2 6.4 %collective-permute-done.4 = f32[32,4,768]{2,1,0:T(4,128)S(1)} collective-permute-done((f32[32,4,768]{2,1,0:T(4,128)}, f32[32,4,768]{2,1,0:T(4,128)S(1)}, u32[]{:S(2)}, u32[]{:S(2)}) %collective-permute-start.4) | collective-permute-done | bytes 393248 | tf_op jit(solution)/shard_map/ppermute | solution.py:162
  66.6 2.5 %collective-permute-done.5 = f32[32,4,768]{2,1,0:T(4,128)} collective-permute-done((f32[32,4,768]{2,1,0:T(4,128)}, f32[32,4,768]{2,1,0:T(4,128)}, u32[]{:S(2)}, u32[]{:S(2)}) %collective-permute-start.5) | collective-permute-done | bytes 393248 | tf_op jit(solution)/shard_map/ppermute | solution.py:163
  69.1 1.4 %pad_maximum_fusion.1.pad_ref = f32[32,40,768]{2,1,0:T(8,128)S(1)} fusion(f32[32,4,768]{2,1,0:T(4,128)} %collective-permute-done.5, f32[4,32,768]{2,1,0:T(8,128)S(1)} %shard_map.70, f32[24,32,768]{2,1,0:T(8,128)S(1)} %shard_map.69, f32[4,32,768]{2,1,0:T(8,128)S(1)} %shard_map.68, f32[32,4,768]{2,1,0:T(4,128)S(1)} %collective-permute-done.4), kind=kLoop, calls=%fused_computation.1 | loop fusion | flops 3932160 | bytes 7864320 | tf_op jit(solution)/shard_map/concatenate | solution.py:170
  70.6 0.0 copy-start.2
  70.6 0.1 fusion.1
  70.7 3.1 %collective-permute-start.6 = (f32[4,40,768]{2,1,0:T(8,128)S(1)}, f32[4,40,768]{2,1,0:T(8,128)S(1)}, u32[]{:S(2)}, u32[]{:S(2)}) collective-permute-start(f32[4,40,768]{2,1,0:T(8,128)S(1)} %get-tuple-element.16), channel_id=1, source_target_pairs={{0,32},{32,64},{64,96},{96,128},{128,160},{160,192},{192,224},{1,3... | collective-permute-start | bytes 1474568 | tf_op jit(solution)/shard_map/ppermute | solution.py:162
  73.8 2.7 %collective-permute-start.7 = (f32[4,40,768]{2,1,0:T(8,128)S(1)}, f32[4,40,768]{2,1,0:T(8,128)S(1)}, u32[]{:S(2)}, u32[]{:S(2)}) collective-permute-start(f32[4,40,768]{2,1,0:T(8,128)S(1)} %get-tuple-element.17), channel_id=1, source_target_pairs={{32,0},{64,32},{96,64},{128,96},{160,128},{192,160},{224,192},{33,... | collective-permute-start | bytes 1474568 | tf_op jit(solution)/shard_map/ppermute | solution.py:163
  76.5 0.0 copy-done.2
  76.6 0.0 copy-done
  76.6 0.1 fusion.4
  76.6 0.0 copy-start.3
  76.6 13.4 %shard_map.72 = (f32[24,32,768]{2,1,0:T(8,128)S(1)}, f32[32,768]{1,0:T(8,128)S(1)}) custom-call(f32[27]{0:T(128)S(1)} %pad_maximum_fusion.6.taps_ref, f32[32,40,768]{2,1,0:T(8,128)} %copy-done.2, f32[32,32,768]{2,1,0:T(8,128)S(1)} %copy-done), custom_call_target="tpu_custom_call" | custom-call | flops 35389440 | bytes 9437184 | tf_op jit(solution)/shard_map/pallas_call | solution.py:74
  90.0 0.0 copy-done.3
  90.0 0.2 fusion
  90.2 0.0 collective-permute-done.6.halo_ref
  90.2 2.1 %shard_map.71 = (f32[4,32,768]{2,1,0:T(8,128)S(1)}, f32[32,768]{1,0:T(8,128)S(1)}) custom-call(f32[27]{0:T(128)S(1)} %pad_maximum_fusion.6.taps_ref, f32[4,40,768]{2,1,0:T(8,128)S(1)} %collective-permute-done.6.halo_ref, f32[8,40,768]{2,1,0:T(8,128)S(1)} %get-tuple-element.14.own_ref, f32[4,32,768]{2,1,0:T(8,128)S(1)} %get-tuple-element.22.other_ref), custom_call_target="tpu_custom_call" | custom-call | flops 5898240 | bytes 1572864 | tf_op jit(solution)/shard_map/pallas_call | solution.py:145
  92.3 0.0 collective-permute-done.7.halo_ref
  92.3 2.1 %shard_map.73 = (f32[4,32,768]{2,1,0:T(8,128)S(1)}, f32[32,768]{1,0:T(8,128)S(1)}) custom-call(f32[27]{0:T(128)S(1)} %pad_maximum_fusion.6.taps_ref, f32[4,40,768]{2,1,0:T(8,128)S(1)} %collective-permute-done.7.halo_ref, f32[8,40,768]{2,1,0:T(8,128)S(1)} %get-tuple-element.15.own_ref, f32[4,32,768]{2,1,0:T(8,128)S(1)} %get-tuple-element.23.other_ref), custom_call_target="tpu_custom_call" | custom-call | flops 5898240 | bytes 1572864 | tf_op jit(solution)/shard_map/pallas_call | solution.py:145
  94.5 5.9 %collective-permute-start.8 = (f32[32,768]{1,0:T(8,128)S(1)}, f32[32,768]{1,0:T(8,128)S(1)}, u32[]{:S(2)}, u32[]{:S(2)}) collective-permute-start(f32[32,768]{1,0:T(8,128)S(1)} %maximum_maximum_fusion), channel_id=1, source_target_pairs={{0,128},{32,160},{64,192},{96,224},{128,0},{160,32},{192,64},{224,... | collective-permute-start | bytes 294920 | tf_op jit(solution)/shard_map/ppermute | solution.py:186
  100.4 2.6 %collective-permute-done.8 = f32[32,768]{1,0:T(8,128)S(1)} collective-permute-done((f32[32,768]{1,0:T(8,128)S(1)}, f32[32,768]{1,0:T(8,128)S(1)}, u32[]{:S(2)}, u32[]{:S(2)}) %collective-permute-start.8) | collective-permute-done | bytes 98336 | tf_op jit(solution)/shard_map/ppermute | solution.py:186
  103.0 1.6 %collective-permute-start.9 = (f32[32,768]{1,0:T(8,128)S(1)}, f32[32,768]{1,0:T(8,128)S(1)}, u32[]{:S(2)}, u32[]{:S(2)}) collective-permute-start(f32[32,768]{1,0:T(8,128)S(1)} %max.17), channel_id=1, source_target_pairs={{0,64},{32,96},{64,0},{96,32},{128,192},{160,224},{192,128},{224,1... | collective-permute-start | bytes 294920 | tf_op jit(solution)/shard_map/ppermute | solution.py:186
  104.6 3.1 %collective-permute-done.9 = f32[32,768]{1,0:T(8,128)S(1)} collective-permute-done((f32[32,768]{1,0:T(8,128)S(1)}, f32[32,768]{1,0:T(8,128)S(1)}, u32[]{:S(2)}, u32[]{:S(2)}) %collective-permute-start.9) | collective-permute-done | bytes 98336 | tf_op jit(solution)/shard_map/ppermute | solution.py:186
  107.7 0.1 collective-permute-start.10
  107.8 2.0 %pad_maximum_fusion.2 = f32[32,32,768]{2,1,0:T(8,128)} fusion(f32[4,32,768]{2,1,0:T(8,128)S(1)} %get-tuple-element.10, f32[24,32,768]{2,1,0:T(8,128)S(1)} %get-tuple-element.9, f32[4,32,768]{2,1,0:T(8,128)S(1)} %get-tuple-element.8), kind=kLoop, calls=%fused_computation.2 | loop fusion | flops 1572864 | bytes 6291456 | tf_op jit(solution)/shard_map/concatenate | solution.py:175
  109.8 2.6 %collective-permute-done.10 = f32[32,768]{1,0:T(8,128)S(1)} collective-permute-done((f32[32,768]{1,0:T(8,128)S(1)}, f32[32,768]{1,0:T(8,128)S(1)}, u32[]{:S(2)}, u32[]{:S(2)}) %collective-permute-start.10) | collective-permute-done | bytes 98336 | tf_op jit(solution)/shard_map/ppermute | solution.py:186
  112.4 0.7 max.19
  (3 shorter events, 0.0 us)
Async XLA Ops:
  2.1 15.7 %collective-permute-start = (f32[32,4,768]{2,1,0:T(4,128)S(1)}, f32[32,4,768]{2,1,0:T(4,128)S(1)}, u32[]{:S(2)}, u32[]{:S(2)}) collective-permute-start(f32[32,4,768]{2,1,0:T(4,128)S(1)} %get-tuple-element.28), channel_id=1, source_target_pairs={{0,1},{1,2},{2,3},{3,4},{4,5},{5,6},{6,7},{7,8},{8,9},{9,10},{10,1... | collective-permute-start | bytes 1179656 | tf_op jit(solution)/shard_map/ppermute | solution.py:162
  4.1 13.7 %collective-permute-start.1 = (f32[32,4,768]{2,1,0:T(4,128)S(1)}, f32[32,4,768]{2,1,0:T(4,128)S(1)}, u32[]{:S(2)}, u32[]{:S(2)}) collective-permute-start(f32[32,4,768]{2,1,0:T(4,128)S(1)} %get-tuple-element.29), channel_id=1, source_target_pairs={{1,0},{2,1},{3,2},{4,3},{5,4},{6,5},{7,6},{8,7},{9,8},{10,9},{11,1... | collective-permute-start | bytes 1179656 | tf_op jit(solution)/shard_map/ppermute | solution.py:163
  12.7 16.9 %copy-start.1 = (f32[32,32,768]{2,1,0:T(8,128)S(1)}, f32[32,32,768]{2,1,0:T(8,128)}, u32[]{:S(2)}) copy-start(f32[32,32,768]{2,1,0:T(8,128)} %other_ref.2) | copy-start | bytes 9437188
  20.2 9.6 %copy-start.4 = (f32[32,40,768]{2,1,0:T(8,128)}, f32[32,40,768]{2,1,0:T(8,128)S(1)}, u32[]{:S(2)}) copy-start(f32[32,40,768]{2,1,0:T(8,128)S(1)} %pad_maximum_fusion.pad_ref) | copy-start | bytes 11796484
  20.2 24.4 %collective-permute-start.2 = (f32[4,40,768]{2,1,0:T(8,128)S(1)}, f32[4,40,768]{2,1,0:T(8,128)S(1)}, u32[]{:S(2)}, u32[]{:S(2)}) collective-permute-start(f32[4,40,768]{2,1,0:T(8,128)S(1)} %get-tuple-element.20), channel_id=1, source_target_pairs={{0,32},{32,64},{64,96},{96,128},{128,160},{160,192},{192,224},{1,3... | collective-permute-start | bytes 1474568 | tf_op jit(solution)/shard_map/ppermute | solution.py:162
  27.7 19.1 %collective-permute-start.3 = (f32[4,40,768]{2,1,0:T(8,128)S(1)}, f32[4,40,768]{2,1,0:T(8,128)S(1)}, u32[]{:S(2)}, u32[]{:S(2)}) collective-permute-start(f32[4,40,768]{2,1,0:T(8,128)S(1)} %get-tuple-element.21), channel_id=1, source_target_pairs={{32,0},{64,32},{96,64},{128,96},{160,128},{192,160},{224,192},{33,... | collective-permute-start | bytes 1474568 | tf_op jit(solution)/shard_map/ppermute | solution.py:163
  44.6 15.1 %copy-start.5 = (f32[9]{0:T(128)S(1)}, f32[9]{0:T(128)}, u32[]{:S(2)}) copy-start(f32[9]{0:T(128)} %param.8) | copy-start | bytes 112
  44.6 15.2 %copy-start.6 = (f32[9]{0:T(128)S(1)}, f32[9]{0:T(128)}, u32[]{:S(2)}) copy-start(f32[9]{0:T(128)} %param.9) | copy-start | bytes 112
  44.6 15.3 %copy-start.7 = (f32[9]{0:T(128)S(1)}, f32[9]{0:T(128)}, u32[]{:S(2)}) copy-start(f32[9]{0:T(128)} %param.7) | copy-start | bytes 112
  50.0 16.6 %collective-permute-start.4 = (f32[32,4,768]{2,1,0:T(4,128)}, f32[32,4,768]{2,1,0:T(4,128)S(1)}, u32[]{:S(2)}, u32[]{:S(2)}) collective-permute-start(f32[32,4,768]{2,1,0:T(4,128)} %get-tuple-element.24), channel_id=1, source_target_pairs={{0,1},{1,2},{2,3},{3,4},{4,5},{5,6},{6,7},{7,8},{8,9},{9,10},{10,1... | collective-permute-start | bytes 1179656 | tf_op jit(solution)/shard_map/ppermute | solution.py:162
  51.9 17.2 %collective-permute-start.5 = (f32[32,4,768]{2,1,0:T(4,128)}, f32[32,4,768]{2,1,0:T(4,128)}, u32[]{:S(2)}, u32[]{:S(2)}) collective-permute-start(f32[32,4,768]{2,1,0:T(4,128)} %get-tuple-element.25), channel_id=1, source_target_pairs={{1,0},{2,1},{3,2},{4,3},{5,4},{6,5},{7,6},{8,7},{9,8},{10,9},{11,1... | collective-permute-start | bytes 1179656 | tf_op jit(solution)/shard_map/ppermute | solution.py:163
  60.2 16.4 %copy-start = (f32[32,32,768]{2,1,0:T(8,128)S(1)}, f32[32,32,768]{2,1,0:T(8,128)}, u32[]{:S(2)}) copy-start(f32[32,32,768]{2,1,0:T(8,128)} %other_ref.3) | copy-start | bytes 9437188
  70.6 6.0 %copy-start.2 = (f32[32,40,768]{2,1,0:T(8,128)}, f32[32,40,768]{2,1,0:T(8,128)S(1)}, u32[]{:S(2)}) copy-start(f32[32,40,768]{2,1,0:T(8,128)S(1)} %pad_maximum_fusion.1.pad_ref) | copy-start | bytes 11796484
  70.7 19.5 %collective-permute-start.6 = (f32[4,40,768]{2,1,0:T(8,128)S(1)}, f32[4,40,768]{2,1,0:T(8,128)S(1)}, u32[]{:S(2)}, u32[]{:S(2)}) collective-permute-start(f32[4,40,768]{2,1,0:T(8,128)S(1)} %get-tuple-element.16), channel_id=1, source_target_pairs={{0,32},{32,64},{64,96},{96,128},{128,160},{160,192},{192,224},{1,3... | collective-permute-start | bytes 1474568 | tf_op jit(solution)/shard_map/ppermute | solution.py:162
  73.8 18.5 %collective-permute-start.7 = (f32[4,40,768]{2,1,0:T(8,128)S(1)}, f32[4,40,768]{2,1,0:T(8,128)S(1)}, u32[]{:S(2)}, u32[]{:S(2)}) collective-permute-start(f32[4,40,768]{2,1,0:T(8,128)S(1)} %get-tuple-element.17), channel_id=1, source_target_pairs={{32,0},{64,32},{96,64},{128,96},{160,128},{192,160},{224,192},{33,... | collective-permute-start | bytes 1474568 | tf_op jit(solution)/shard_map/ppermute | solution.py:163
  76.6 13.4 %copy-start.3 = (f32[32,40,768]{2,1,0:T(8,128)S(1)}, f32[32,40,768]{2,1,0:T(8,128)}, u32[]{:S(2)}) copy-start(f32[32,40,768]{2,1,0:T(8,128)} %copy-done.2) | copy-start | bytes 11796484
  94.5 8.5 %collective-permute-start.8 = (f32[32,768]{1,0:T(8,128)S(1)}, f32[32,768]{1,0:T(8,128)S(1)}, u32[]{:S(2)}, u32[]{:S(2)}) collective-permute-start(f32[32,768]{1,0:T(8,128)S(1)} %maximum_maximum_fusion), channel_id=1, source_target_pairs={{0,128},{32,160},{64,192},{96,224},{128,0},{160,32},{192,64},{224,... | collective-permute-start | bytes 294920 | tf_op jit(solution)/shard_map/ppermute | solution.py:186
  103.0 4.7 %collective-permute-start.9 = (f32[32,768]{1,0:T(8,128)S(1)}, f32[32,768]{1,0:T(8,128)S(1)}, u32[]{:S(2)}, u32[]{:S(2)}) collective-permute-start(f32[32,768]{1,0:T(8,128)S(1)} %max.17), channel_id=1, source_target_pairs={{0,64},{32,96},{64,0},{96,32},{128,192},{160,224},{192,128},{224,1... | collective-permute-start | bytes 294920 | tf_op jit(solution)/shard_map/ppermute | solution.py:186
  107.7 4.7 %collective-permute-start.10 = (f32[32,768]{1,0:T(8,128)S(1)}, f32[32,768]{1,0:T(8,128)S(1)}, u32[]{:S(2)}, u32[]{:S(2)}) collective-permute-start(f32[32,768]{1,0:T(8,128)S(1)} %max.18), channel_id=1, source_target_pairs={{0,32},{32,0},{64,96},{96,64},{128,160},{160,128},{192,224},{224,1... | collective-permute-start | bytes 294920 | tf_op jit(solution)/shard_map/ppermute | solution.py:186

commit v15 on v14

--- a/solution.py
+++ b/solution.py
@@ -169,7 +169,7 @@
     before, after = halo_pair(shard, "gy", 1, width)
     rows_padded = jnp.concatenate([before, shard, after], axis=1)
     below, above = halo_pair(rows_padded, "gz", 0, width)
-    inner = fused_blur(mode, [(0, nz - 2 * width, 0, width)], taps, rows_padded, other)
+    inner = fused_blur(mode, [(0, nz - 2 * width, 0, 0)], taps, rows_padded, other[width : nz - width])
     low = edge_blur(mode, width, True, taps, below, rows_padded[: 2 * width], other[:width])
     high = edge_blur(mode, width, False, taps, above, rows_padded[nz - 2 * width :], other[nz - width :])
     volume = jnp.concatenate([low[0], inner[0], high[0]], axis=0)

time: 114 us -> 116 us (1.018)
  local copies, waits for them, and re-layouts: 3.87 us -> 11.4 us
  waiting for transfers between devices: 22.4 us -> 18.5 us
  other arithmetic: 8.33 us -> 5.78 us
    slice x0 -> x2, local copies, waits for them, and re-layouts: none -> 3.64 us  [split_blur(): other[width:nz - width]]
    ppermute x4, waiting for transfers between devices: 11.6 us -> 8.13 us  [halo_pair(): before = lax.ppermute(last, axis, up)]
    slice x2, local copies, waits for them, and re-layouts: 0.11 us -> 2.34 us  [split_blur(): other[:width]]
    concatenate x2, other arithmetic: 3.79 us -> 1.93 us  [split_blur(): rows_padded = jnp.concatenate([before, shard, after], axis=1)]
    slice x2, local copies, waits for them, and re-layouts: 1.8 us -> 3.28 us  [split_blur(): rows_padded[:2 * width]]
  transfers between devices with their start and end apart: 11 -> 11, of which waited for: 6 -> 6; matrix products, arithmetic and copies ran while one was open for 4% -> 10% of each run, Pallas kernels for 27% -> 27%
where the time goes in v15:
time: 116 us; the launch traced here: 115 us
  starting transfers between devices  43.1 us (37%)
  Pallas kernels  35 us (30%)
  waiting for transfers between devices  18.5 us (16%)
  local copies, waits for them, and re-layouts  11.4 us (10%)
  other arithmetic  5.78 us (5%)
    pallas_call x2, Pallas kernels, fused_blur(): pl.pallas_call(functools.partial(blur_kernel, mode, tuple(segments)), out...  26.4 us
    ppermute x4, starting transfers between devices, halo_pair(): after = lax.ppermute(first, axis, down)  20.1 us
    ppermute x4, starting transfers between devices, halo_pair(): before = lax.ppermute(last, axis, up)  14.7 us
    pallas_call x4, Pallas kernels, edge_blur(): pl.pallas_call(functools.partial(edge_kernel, mode, width, halo_first), o...  8.55 us
    ppermute x3, starting transfers between devices, butterfly_max(): value = jnp.maximum(value, lax.ppermute(value, axis, pairs))  8.3 us
    ppermute x4, waiting for transfers between devices, halo_pair(): before = lax.ppermute(last, axis, up)  8.13 us
    ppermute x3, waiting for transfers between devices, butterfly_max(): value = jnp.maximum(value, lax.ppermute(value, axis, pairs))  7.8 us
    slice x2, local copies, waits for them, and re-layouts, split_blur(): other[width:nz - width]  3.64 us
  transfers between devices with their start and end apart: 11, of which 6 were waited for; matrix products, arithmetic and copies ran while one was open for 10% of the time, Pallas kernels for 27%

profile of v15, /device:TPU:160, one launch (start us, length us, event | category | flops | bytes accessed | tf_op | source)
XLA Modules:
  0.0 114.7 jit_solution(18079022279077133257)
XLA Ops:
  0.6 0.0 copy-start.2
  0.6 0.0 copy-start.5
  0.7 0.0 copy-start.3
  0.7 0.0 copy-start.4
  0.7 1.7 %fusion.6 = (f32[32,4,768]{2,1,0:T(4,128)S(1)}, f32[32,4,768]{2,1,0:T(4,128)S(1)}) fusion(f32[32,32,768]{2,1,0:T(8,128)} %param.6), kind=kLoop, calls=%fused_computation.15 | loop fusion | bytes 1572864 | tf_op jit(solution)/shard_map/slice | solution.py:160
  2.3 1.9 %collective-permute-start = (f32[32,4,768]{2,1,0:T(4,128)S(1)}, f32[32,4,768]{2,1,0:T(4,128)S(1)}, u32[]{:S(2)}, u32[]{:S(2)}) collective-permute-start(f32[32,4,768]{2,1,0:T(4,128)S(1)} %get-tuple-element.28), channel_id=1, source_target_pairs={{0,1},{1,2},{2,3},{3,4},{4,5},{5,6},{6,7},{7,8},{8,9},{9,10},{10,1... | collective-permute-start | bytes 1179656 | tf_op jit(solution)/shard_map/ppermute | solution.py:162
  4.3 7.9 %collective-permute-start.1 = (f32[32,4,768]{2,1,0:T(4,128)S(1)}, f32[32,4,768]{2,1,0:T(4,128)S(1)}, u32[]{:S(2)}, u32[]{:S(2)}) collective-permute-start(f32[32,4,768]{2,1,0:T(4,128)S(1)} %get-tuple-element.29), channel_id=1, source_target_pairs={{1,0},{2,1},{3,2},{4,3},{5,4},{6,5},{7,6},{8,7},{9,8},{10,9},{11,1... | collective-permute-start | bytes 1179656 | tf_op jit(solution)/shard_map/ppermute | solution.py:163
  12.1 1.8 %slice.59.other_ref = f32[24,32,768]{2,1,0:T(8,128)S(1)} slice(f32[32,32,768]{2,1,0:T(8,128)} %param.5), slice={[4:28], [0:32], [0:768]} | slice | bytes 4718592 | tf_op jit(solution)/shard_map/slice | solution.py:172
  14.0 0.0 copy-done.5
  14.0 0.0 copy-done.3
  14.0 0.0 copy-done.4
  14.0 0.1 pad_maximum_fusion.7.taps_ref
  14.1 3.9 %collective-permute-done = f32[32,4,768]{2,1,0:T(4,128)S(1)} collective-permute-done((f32[32,4,768]{2,1,0:T(4,128)S(1)}, f32[32,4,768]{2,1,0:T(4,128)S(1)}, u32[]{:S(2)}, u32[]{:S(2)}) %collective-permute-start) | collective-permute-done | bytes 393248 | tf_op jit(solution)/shard_map/ppermute | solution.py:162
  18.0 0.0 collective-permute-done.1
  18.0 0.0 copy-done.2
  18.0 0.5 pad_maximum_fusion.pad_ref
  18.5 0.0 copy-start.1
  18.5 0.1 fusion.3
  18.6 7.5 %collective-permute-start.2 = (f32[4,40,768]{2,1,0:T(8,128)S(1)}, f32[4,40,768]{2,1,0:T(8,128)S(1)}, u32[]{:S(2)}, u32[]{:S(2)}) collective-permute-start(f32[4,40,768]{2,1,0:T(8,128)S(1)} %get-tuple-element.20), channel_id=1, source_target_pairs={{0,32},{32,64},{64,96},{96,128},{128,160},{160,192},{192,224},{1,3... | collective-permute-start | bytes 1474568 | tf_op jit(solution)/shard_map/ppermute | solution.py:162
  26.1 1.9 %collective-permute-start.3 = (f32[4,40,768]{2,1,0:T(8,128)S(1)}, f32[4,40,768]{2,1,0:T(8,128)S(1)}, u32[]{:S(2)}, u32[]{:S(2)}) collective-permute-start(f32[4,40,768]{2,1,0:T(8,128)S(1)} %get-tuple-element.21), channel_id=1, source_target_pairs={{32,0},{64,32},{96,64},{128,96},{160,128},{192,160},{224,192},{33,... | collective-permute-start | bytes 1474568 | tf_op jit(solution)/shard_map/ppermute | solution.py:163
  28.0 1.2 %fusion.5 = (f32[4,32,768]{2,1,0:T(8,128)S(1)}, f32[4,32,768]{2,1,0:T(8,128)S(1)}) fusion(f32[32,32,768]{2,1,0:T(8,128)} %param.5), kind=kLoop, calls=%fused_computation.14 | loop fusion | bytes 1572864 | tf_op jit(solution)/shard_map/slice | solution.py:173
  29.2 0.0 copy-done.1
  29.2 13.2 %shard_map.69 = f32[24,32,768]{2,1,0:T(8,128)S(1)} custom-call(f32[27]{0:T(128)S(1)} %pad_maximum_fusion.7.taps_ref, f32[32,40,768]{2,1,0:T(8,128)} %copy-done.1, f32[24,32,768]{2,1,0:T(8,128)S(1)} %slice.59.other_ref), custom_call_target="tpu_custom_call" | custom-call | flops 35389440 | bytes 9437184 | tf_op jit(solution)/shard_map/pallas_call | solution.py:74
  42.4 1.6 %fusion.2 = (f32[8,40,768]{2,1,0:T(8,128)S(1)}, f32[8,40,768]{2,1,0:T(8,128)S(1)}) fusion(f32[32,40,768]{2,1,0:T(8,128)} %copy-done.1), kind=kLoop, calls=%fused_computation.11 | loop fusion | bytes 3932160 | tf_op jit(solution)/shard_map/slice | solution.py:173
  44.1 0.0 collective-permute-done.2.halo_ref
  44.1 2.1 %shard_map.68 = f32[4,32,768]{2,1,0:T(8,128)S(1)} custom-call(f32[27]{0:T(128)S(1)} %pad_maximum_fusion.7.taps_ref, f32[4,40,768]{2,1,0:T(8,128)S(1)} %collective-permute-done.2.halo_ref, f32[8,40,768]{2,1,0:T(8,128)S(1)} %get-tuple-element.18.own_ref, f32[4,32,768]{2,1,0:T(8,128)S(1)} %get-tuple-element.26.other_ref), custom_call_target="tpu_custom_call" | custom-call | flops 5898240 | bytes 1572864 | tf_op jit(solution)/shard_map/pallas_call | solution.py:145
  46.2 0.0 collective-permute-done.3.halo_ref
  46.2 2.1 %shard_map.70 = f32[4,32,768]{2,1,0:T(8,128)S(1)} custom-call(f32[27]{0:T(128)S(1)} %pad_maximum_fusion.7.taps_ref, f32[4,40,768]{2,1,0:T(8,128)S(1)} %collective-permute-done.3.halo_ref, f32[8,40,768]{2,1,0:T(8,128)S(1)} %get-tuple-element.19.own_ref, f32[4,32,768]{2,1,0:T(8,128)S(1)} %get-tuple-element.27.other_ref), custom_call_target="tpu_custom_call" | custom-call | flops 5898240 | bytes 1572864 | tf_op jit(solution)/shard_map/pallas_call | solution.py:145
  48.4 1.0 pad_maximum_fusion.5
  49.4 1.9 %collective-permute-start.4 = (f32[32,4,768]{2,1,0:T(4,128)}, f32[32,4,768]{2,1,0:T(4,128)S(1)}, u32[]{:S(2)}, u32[]{:S(2)}) collective-permute-start(f32[32,4,768]{2,1,0:T(4,128)} %get-tuple-element.24), channel_id=1, source_target_pairs={{0,1},{1,2},{2,3},{3,4},{4,5},{5,6},{6,7},{7,8},{8,9},{9,10},{10,1... | collective-permute-start | bytes 1179656 | tf_op jit(solution)/shard_map/ppermute | solution.py:162
  51.3 7.9 %collective-permute-start.5 = (f32[32,4,768]{2,1,0:T(4,128)}, f32[32,4,768]{2,1,0:T(4,128)}, u32[]{:S(2)}, u32[]{:S(2)}) collective-permute-start(f32[32,4,768]{2,1,0:T(4,128)} %get-tuple-element.25), channel_id=1, source_target_pairs={{1,0},{2,1},{3,2},{4,3},{5,4},{6,5},{7,6},{8,7},{9,8},{10,9},{11,1... | collective-permute-start | bytes 1179656 | tf_op jit(solution)/shard_map/ppermute | solution.py:163
  59.2 0.1 rev.10
  59.3 0.1 rev.11
  59.4 0.1 rev.9
  59.5 1.8 %slice.68.other_ref = f32[24,32,768]{2,1,0:T(8,128)S(1)} slice(f32[32,32,768]{2,1,0:T(8,128)} %param.6), slice={[4:28], [0:32], [0:768]} | slice | bytes 4718592 | tf_op jit(solution)/shard_map/slice | solution.py:172
  61.3 0.1 pad_maximum_fusion.6.taps_ref
  61.4 4.2 %collective-permute-done.4 = f32[32,4,768]{2,1,0:T(4,128)S(1)} collective-permute-done((f32[32,4,768]{2,1,0:T(4,128)}, f32[32,4,768]{2,1,0:T(4,128)S(1)}, u32[]{:S(2)}, u32[]{:S(2)}) %collective-permute-start.4) | collective-permute-done | bytes 393248 | tf_op jit(solution)/shard_map/ppermute | solution.py:162
  65.5 2.6 %collective-permute-done.5 = f32[32,4,768]{2,1,0:T(4,128)} collective-permute-done((f32[32,4,768]{2,1,0:T(4,128)}, f32[32,4,768]{2,1,0:T(4,128)}, u32[]{:S(2)}, u32[]{:S(2)}) %collective-permute-start.5) | collective-permute-done | bytes 393248 | tf_op jit(solution)/shard_map/ppermute | solution.py:163
  68.1 1.4 %pad_maximum_fusion.1.pad_ref = f32[32,40,768]{2,1,0:T(8,128)S(1)} fusion(f32[32,4,768]{2,1,0:T(4,128)} %collective-permute-done.5, f32[4,32,768]{2,1,0:T(8,128)S(1)} %shard_map.70, f32[24,32,768]{2,1,0:T(8,128)S(1)} %shard_map.69, f32[4,32,768]{2,1,0:T(8,128)S(1)} %shard_map.68, f32[32,4,768]{2,1,0:T(4,128)S(1)} %collective-permute-done.4), kind=kLoop, calls=%fused_computation.1 | loop fusion | flops 3932160 | bytes 7864320 | tf_op jit(solution)/shard_map/concatenate | solution.py:170
  69.6 0.0 copy-start
  69.6 0.1 fusion.1
  69.7 3.4 %collective-permute-start.6 = (f32[4,40,768]{2,1,0:T(8,128)S(1)}, f32[4,40,768]{2,1,0:T(8,128)S(1)}, u32[]{:S(2)}, u32[]{:S(2)}) collective-permute-start(f32[4,40,768]{2,1,0:T(8,128)S(1)} %get-tuple-element.16), channel_id=1, source_target_pairs={{0,32},{32,64},{64,96},{96,128},{128,160},{160,192},{192,224},{1,3... | collective-permute-start | bytes 1474568 | tf_op jit(solution)/shard_map/ppermute | solution.py:162
  73.0 2.5 %collective-permute-start.7 = (f32[4,40,768]{2,1,0:T(8,128)S(1)}, f32[4,40,768]{2,1,0:T(8,128)S(1)}, u32[]{:S(2)}, u32[]{:S(2)}) collective-permute-start(f32[4,40,768]{2,1,0:T(8,128)S(1)} %get-tuple-element.17), channel_id=1, source_target_pairs={{32,0},{64,32},{96,64},{128,96},{160,128},{192,160},{224,192},{33,... | collective-permute-start | bytes 1474568 | tf_op jit(solution)/shard_map/ppermute | solution.py:163
  75.5 1.2 %fusion.4 = (f32[4,32,768]{2,1,0:T(8,128)S(1)}, f32[4,32,768]{2,1,0:T(8,128)S(1)}) fusion(f32[32,32,768]{2,1,0:T(8,128)} %param.6), kind=kLoop, calls=%fused_computation.13 | loop fusion | bytes 1572864 | tf_op jit(solution)/shard_map/slice | solution.py:173
  76.7 0.0 copy-done
  76.7 13.2 %shard_map.72 = (f32[24,32,768]{2,1,0:T(8,128)S(1)}, f32[32,768]{1,0:T(8,128)S(1)}) custom-call(f32[27]{0:T(128)S(1)} %pad_maximum_fusion.6.taps_ref, f32[32,40,768]{2,1,0:T(8,128)} %copy-done, f32[24,32,768]{2,1,0:T(8,128)S(1)} %slice.68.other_ref), custom_call_target="tpu_custom_call" | custom-call | flops 35389440 | bytes 9437184 | tf_op jit(solution)/shard_map/pallas_call | solution.py:74
  89.9 1.6 %fusion = (f32[8,40,768]{2,1,0:T(8,128)S(1)}, f32[8,40,768]{2,1,0:T(8,128)S(1)}) fusion(f32[32,40,768]{2,1,0:T(8,128)} %copy-done), kind=kLoop, calls=%fused_computation.9 | loop fusion | bytes 3932160 | tf_op jit(solution)/shard_map/slice | solution.py:173
  91.6 0.0 collective-permute-done.6.halo_ref
  91.6 2.1 %shard_map.71 = (f32[4,32,768]{2,1,0:T(8,128)S(1)}, f32[32,768]{1,0:T(8,128)S(1)}) custom-call(f32[27]{0:T(128)S(1)} %pad_maximum_fusion.6.taps_ref, f32[4,40,768]{2,1,0:T(8,128)S(1)} %collective-permute-done.6.halo_ref, f32[8,40,768]{2,1,0:T(8,128)S(1)} %get-tuple-element.14.own_ref, f32[4,32,768]{2,1,0:T(8,128)S(1)} %get-tuple-element.22.other_ref), custom_call_target="tpu_custom_call" | custom-call | flops 5898240 | bytes 1572864 | tf_op jit(solution)/shard_map/pallas_call | solution.py:145
  93.7 0.0 collective-permute-done.7.halo_ref
  93.8 2.1 %shard_map.73 = (f32[4,32,768]{2,1,0:T(8,128)S(1)}, f32[32,768]{1,0:T(8,128)S(1)}) custom-call(f32[27]{0:T(128)S(1)} %pad_maximum_fusion.6.taps_ref, f32[4,40,768]{2,1,0:T(8,128)S(1)} %collective-permute-done.7.halo_ref, f32[8,40,768]{2,1,0:T(8,128)S(1)} %get-tuple-element.15.own_ref, f32[4,32,768]{2,1,0:T(8,128)S(1)} %get-tuple-element.23.other_ref), custom_call_target="tpu_custom_call" | custom-call | flops 5898240 | bytes 1572864 | tf_op jit(solution)/shard_map/pallas_call | solution.py:145
  95.9 5.8 %collective-permute-start.8 = (f32[32,768]{1,0:T(8,128)S(1)}, f32[32,768]{1,0:T(8,128)S(1)}, u32[]{:S(2)}, u32[]{:S(2)}) collective-permute-start(f32[32,768]{1,0:T(8,128)S(1)} %maximum_maximum_fusion), channel_id=1, source_target_pairs={{0,128},{32,160},{64,192},{96,224},{128,0},{160,32},{192,64},{224,... | collective-permute-start | bytes 294920 | tf_op jit(solution)/shard_map/ppermute | solution.py:186
  101.7 2.6 %collective-permute-done.8 = f32[32,768]{1,0:T(8,128)S(1)} collective-permute-done((f32[32,768]{1,0:T(8,128)S(1)}, f32[32,768]{1,0:T(8,128)S(1)}, u32[]{:S(2)}, u32[]{:S(2)}) %collective-permute-start.8) | collective-permute-done | bytes 98336 | tf_op jit(solution)/shard_map/ppermute | solution.py:186
  104.3 2.4 %collective-permute-start.9 = (f32[32,768]{1,0:T(8,128)S(1)}, f32[32,768]{1,0:T(8,128)S(1)}, u32[]{:S(2)}, u32[]{:S(2)}) collective-permute-start(f32[32,768]{1,0:T(8,128)S(1)} %max.17), channel_id=1, source_target_pairs={{0,64},{32,96},{64,0},{96,32},{128,192},{160,224},{192,128},{224,1... | collective-permute-start | bytes 294920 | tf_op jit(solution)/shard_map/ppermute | solution.py:186
  106.7 2.6 %collective-permute-done.9 = f32[32,768]{1,0:T(8,128)S(1)} collective-permute-done((f32[32,768]{1,0:T(8,128)S(1)}, f32[32,768]{1,0:T(8,128)S(1)}, u32[]{:S(2)}, u32[]{:S(2)}) %collective-permute-start.9) | collective-permute-done | bytes 98336 | tf_op jit(solution)/shard_map/ppermute | solution.py:186
  109.3 0.1 collective-permute-start.10
  109.5 2.0 %pad_maximum_fusion.2 = f32[32,32,768]{2,1,0:T(8,128)} fusion(f32[4,32,768]{2,1,0:T(8,128)S(1)} %get-tuple-element.10, f32[24,32,768]{2,1,0:T(8,128)S(1)} %get-tuple-element.9, f32[4,32,768]{2,1,0:T(8,128)S(1)} %get-tuple-element.8), kind=kLoop, calls=%fused_computation.2 | loop fusion | flops 1572864 | bytes 6291456 | tf_op jit(solution)/shard_map/concatenate | solution.py:175
  111.4 2.6 %collective-permute-done.10 = f32[32,768]{1,0:T(8,128)S(1)} collective-permute-done((f32[32,768]{1,0:T(8,128)S(1)}, f32[32,768]{1,0:T(8,128)S(1)}, u32[]{:S(2)}, u32[]{:S(2)}) %collective-permute-start.10) | collective-permute-done | bytes 98336 | tf_op jit(solution)/shard_map/ppermute | solution.py:186
  114.1 0.7 max.19
  (3 shorter events, 0.0 us)
Async XLA Ops:
  0.6 17.4 %copy-start.2 = (f32[32,32,768]{2,1,0:T(8,128)S(1)}, f32[32,32,768]{2,1,0:T(8,128)}, u32[]{:S(2)}) copy-start(f32[32,32,768]{2,1,0:T(8,128)} %param.6) | copy-start | bytes 9437188
  0.6 13.3 %copy-start.5 = (f32[9]{0:T(128)S(1)}, f32[9]{0:T(128)}, u32[]{:S(2)}) copy-start(f32[9]{0:T(128)} %param.7) | copy-start | bytes 112
  0.7 13.3 %copy-start.3 = (f32[9]{0:T(128)S(1)}, f32[9]{0:T(128)}, u32[]{:S(2)}) copy-start(f32[9]{0:T(128)} %param.8) | copy-start | bytes 112
  0.7 13.3 %copy-start.4 = (f32[9]{0:T(128)S(1)}, f32[9]{0:T(128)}, u32[]{:S(2)}) copy-start(f32[9]{0:T(128)} %param.9) | copy-start | bytes 112
  2.3 15.7 %collective-permute-start = (f32[32,4,768]{2,1,0:T(4,128)S(1)}, f32[32,4,768]{2,1,0:T(4,128)S(1)}, u32[]{:S(2)}, u32[]{:S(2)}) collective-permute-start(f32[32,4,768]{2,1,0:T(4,128)S(1)} %get-tuple-element.28), channel_id=1, source_target_pairs={{0,1},{1,2},{2,3},{3,4},{4,5},{5,6},{6,7},{7,8},{8,9},{9,10},{10,1... | collective-permute-start | bytes 1179656 | tf_op jit(solution)/shard_map/ppermute | solution.py:162
  4.3 13.7 %collective-permute-start.1 = (f32[32,4,768]{2,1,0:T(4,128)S(1)}, f32[32,4,768]{2,1,0:T(4,128)S(1)}, u32[]{:S(2)}, u32[]{:S(2)}) collective-permute-start(f32[32,4,768]{2,1,0:T(4,128)S(1)} %get-tuple-element.29), channel_id=1, source_target_pairs={{1,0},{2,1},{3,2},{4,3},{5,4},{6,5},{7,6},{8,7},{9,8},{10,9},{11,1... | collective-permute-start | bytes 1179656 | tf_op jit(solution)/shard_map/ppermute | solution.py:163
  18.5 10.7 %copy-start.1 = (f32[32,40,768]{2,1,0:T(8,128)}, f32[32,40,768]{2,1,0:T(8,128)S(1)}, u32[]{:S(2)}) copy-start(f32[32,40,768]{2,1,0:T(8,128)S(1)} %pad_maximum_fusion.pad_ref) | copy-start | bytes 11796484
  18.6 25.5 %collective-permute-start.2 = (f32[4,40,768]{2,1,0:T(8,128)S(1)}, f32[4,40,768]{2,1,0:T(8,128)S(1)}, u32[]{:S(2)}, u32[]{:S(2)}) collective-permute-start(f32[4,40,768]{2,1,0:T(8,128)S(1)} %get-tuple-element.20), channel_id=1, source_target_pairs={{0,32},{32,64},{64,96},{96,128},{128,160},{160,192},{192,224},{1,3... | collective-permute-start | bytes 1474568 | tf_op jit(solution)/shard_map/ppermute | solution.py:162
  26.1 20.2 %collective-permute-start.3 = (f32[4,40,768]{2,1,0:T(8,128)S(1)}, f32[4,40,768]{2,1,0:T(8,128)S(1)}, u32[]{:S(2)}, u32[]{:S(2)}) collective-permute-start(f32[4,40,768]{2,1,0:T(8,128)S(1)} %get-tuple-element.21), channel_id=1, source_target_pairs={{32,0},{64,32},{96,64},{128,96},{160,128},{192,160},{224,192},{33,... | collective-permute-start | bytes 1474568 | tf_op jit(solution)/shard_map/ppermute | solution.py:163
  49.4 16.2 %collective-permute-start.4 = (f32[32,4,768]{2,1,0:T(4,128)}, f32[32,4,768]{2,1,0:T(4,128)S(1)}, u32[]{:S(2)}, u32[]{:S(2)}) collective-permute-start(f32[32,4,768]{2,1,0:T(4,128)} %get-tuple-element.24), channel_id=1, source_target_pairs={{0,1},{1,2},{2,3},{3,4},{4,5},{5,6},{6,7},{7,8},{8,9},{9,10},{10,1... | collective-permute-start | bytes 1179656 | tf_op jit(solution)/shard_map/ppermute | solution.py:162
  51.3 16.8 %collective-permute-start.5 = (f32[32,4,768]{2,1,0:T(4,128)}, f32[32,4,768]{2,1,0:T(4,128)}, u32[]{:S(2)}, u32[]{:S(2)}) collective-permute-start(f32[32,4,768]{2,1,0:T(4,128)} %get-tuple-element.25), channel_id=1, source_target_pairs={{1,0},{2,1},{3,2},{4,3},{5,4},{6,5},{7,6},{8,7},{9,8},{10,9},{11,1... | collective-permute-start | bytes 1179656 | tf_op jit(solution)/shard_map/ppermute | solution.py:163
  69.6 7.1 %copy-start = (f32[32,40,768]{2,1,0:T(8,128)}, f32[32,40,768]{2,1,0:T(8,128)S(1)}, u32[]{:S(2)}) copy-start(f32[32,40,768]{2,1,0:T(8,128)S(1)} %pad_maximum_fusion.1.pad_ref) | copy-start | bytes 11796484
  69.7 21.9 %collective-permute-start.6 = (f32[4,40,768]{2,1,0:T(8,128)S(1)}, f32[4,40,768]{2,1,0:T(8,128)S(1)}, u32[]{:S(2)}, u32[]{:S(2)}) collective-permute-start(f32[4,40,768]{2,1,0:T(8,128)S(1)} %get-tuple-element.16), channel_id=1, source_target_pairs={{0,32},{32,64},{64,96},{96,128},{128,160},{160,192},{192,224},{1,3... | collective-permute-start | bytes 1474568 | tf_op jit(solution)/shard_map/ppermute | solution.py:162
  73.0 20.7 %collective-permute-start.7 = (f32[4,40,768]{2,1,0:T(8,128)S(1)}, f32[4,40,768]{2,1,0:T(8,128)S(1)}, u32[]{:S(2)}, u32[]{:S(2)}) collective-permute-start(f32[4,40,768]{2,1,0:T(8,128)S(1)} %get-tuple-element.17), channel_id=1, source_target_pairs={{32,0},{64,32},{96,64},{128,96},{160,128},{192,160},{224,192},{33,... | collective-permute-start | bytes 1474568 | tf_op jit(solution)/shard_map/ppermute | solution.py:163
  95.9 8.4 %collective-permute-start.8 = (f32[32,768]{1,0:T(8,128)S(1)}, f32[32,768]{1,0:T(8,128)S(1)}, u32[]{:S(2)}, u32[]{:S(2)}) collective-permute-start(f32[32,768]{1,0:T(8,128)S(1)} %maximum_maximum_fusion), channel_id=1, source_target_pairs={{0,128},{32,160},{64,192},{96,224},{128,0},{160,32},{192,64},{224,... | collective-permute-start | bytes 294920 | tf_op jit(solution)/shard_map/ppermute | solution.py:186
  104.3 5.0 %collective-permute-start.9 = (f32[32,768]{1,0:T(8,128)S(1)}, f32[32,768]{1,0:T(8,128)S(1)}, u32[]{:S(2)}, u32[]{:S(2)}) collective-permute-start(f32[32,768]{1,0:T(8,128)S(1)} %max.17), channel_id=1, source_target_pairs={{0,64},{32,96},{64,0},{96,32},{128,192},{160,224},{192,128},{224,1... | collective-permute-start | bytes 294920 | tf_op jit(solution)/shard_map/ppermute | solution.py:186
  109.3 4.7 %collective-permute-start.10 = (f32[32,768]{1,0:T(8,128)S(1)}, f32[32,768]{1,0:T(8,128)S(1)}, u32[]{:S(2)}, u32[]{:S(2)}) collective-permute-start(f32[32,768]{1,0:T(8,128)S(1)} %max.18), channel_id=1, source_target_pairs={{0,32},{32,0},{64,96},{96,64},{128,160},{160,128},{192,224},{224,1... | collective-permute-start | bytes 294920 | tf_op jit(solution)/shard_map/ppermute | solution.py:186
